TPU v7x, 32 devices: a whole 2x2x4 slice. The times are simulated.
32 devices in a mesh: kv: 4 (over x, core), blk: 8 (over z, y).
Axes of the slice: x: 2, y: 2, z: 4, core: 2. Of those that a mesh axis runs over, the one named last changes fastest.
Arguments:
- patches: bfloat16 [24, 256, 1408], P('blk'), may hold values from -6 to 6
- merged_grid: int32 [24, 2], P('blk'), may hold values from 1 to 8, as said below
- picture_start: int32 [24], P('blk'), may hold values from 0 to 4095, as said below
- vis_gain: float32 [1408], replicated, may hold values from 0.5 to 2
- vis_qkv: bfloat16 [1408, 3, 1408], P(None, None, 'kv'), may hold values from -2 to 2
- vis_out: bfloat16 [1408, 1408], P('kv'), may hold values from -0.15625 to 0.15625
- merge_weight: bfloat16 [1408, 4096], P(None, 'kv'), may hold values from -0.15625 to 0.15625
- text_embed: bfloat16 [4096, 4096], P('blk', 'kv'), may hold values from -6 to 6
- dec_gain: float32 [4096], replicated, may hold values from 0.1 to 1.9
- w_query: bfloat16 [4096, 2048], P(None, 'kv'), may hold values from -2 to 2
- w_keyval: bfloat16 [4096, 2, 1024], P(None, None, 'kv'), may hold values from -2 to 2
- w_out: bfloat16 [2048, 4096], P('kv'), may hold values from -0.5 to 0.5
- req_lengths: int32 [8], replicated, may hold values from 1 to 2048, as said below
- final_gain: float32 [4096], P('kv'), may hold values from 0.1 to 1.9
- table: bfloat16 [8192, 4096], P('blk', 'kv'), may hold values from -0.25 to 0.25
Outputs:
- hidden: bfloat16 [4096, 4096], P('blk', 'kv')
- last_norm: bfloat16 [8, 4096], P(None, 'kv')
- max_logit: float32 [8], replicated
Inputs may be any that keep to these rules, and one draw needn't show every extreme that they name: `merged_grid`: some picture has a grid of 8 x 8 merged cells. Picture p's merged rows go to consecutive positions from picture_start[p] on, all inside the block of 512 positions with block index p // 3; pictures never share a position. `req_lengths`: the first request ends inside positions 512 to 1023; the second request holds 2048 positions, more than any other.
All inputs are finite; a program needn't handle non-finite values.
Results may differ from a plain program's by a relative error of at most 0.017.
Values may be sent and summed in bfloat16 or wider, within the bound.
No kernel may reach another device: no remote copies, remote signals or barrier semaphores. Data moves between devices by JAX's collectives and lax.ppermute only.
A program may use at most 128 MiB of HBM per device.

v0:
```python
import math

import jax
import jax.numpy as jnp
from jax import lax
from jax.sharding import PartitionSpec as P

VHD = 88
D = 4096
QHEADS = 16
KVHEADS = 8
HD = 128


def layer_norm(inputs, gain):
    centre = jnp.mean(inputs, axis=-1, keepdims=True)
    centred = inputs - centre
    spread = jnp.mean(centred * centred, axis=-1, keepdims=True)
    return centred * lax.rsqrt(spread + 1e-06) * gain


def rotate(inputs, position):
    half_width = inputs.shape[-1] // 2
    inverse = 500000.0 ** (-jnp.arange(half_width, dtype=jnp.float32) * 2.0 / inputs.shape[-1])
    angles = position.astype(jnp.float32)[:, None] * inverse[None, :]
    cosine = jnp.cos(angles)[:, None, :]
    sine = jnp.sin(angles)[:, None, :]
    first = inputs[..., :half_width]
    second = inputs[..., half_width:]
    return jnp.concatenate(
        [first * cosine - second * sine, second * cosine + first * sine], axis=-1
    )


def request_info(row_index, req_lengths):
    ends_at = jnp.cumsum(req_lengths)
    starts_at = ends_at - req_lengths
    request_id = jnp.sum((row_index[:, None] >= ends_at[None, :]).astype(jnp.int32), axis=1)
    choose = request_id[:, None] == jnp.arange(req_lengths.shape[0], dtype=jnp.int32)[None, :]
    request_begin = jnp.sum(jnp.where(choose, starts_at[None, :], 0), axis=1)
    return (request_id, request_begin)


def attend(state, queries, query_ids, query_req, key_part, value_part, key_ids, key_req, root):
    run_max, weight_sum, running = state
    scores = (
        jnp.einsum("tgqd,kgd->tgqk", queries, key_part, preferred_element_type=jnp.float32) / root
    )
    allowed = (key_ids[None, :] <= query_ids[:, None]) & (key_req[None, :] == query_req[:, None])
    allowed = allowed[:, None, None, :]
    scores = jnp.where(allowed, scores, -1e30)
    new_max = jnp.maximum(run_max, jnp.max(scores, axis=-1))
    weights = jnp.where(allowed, jnp.exp(scores - new_max[..., None]), 0.0)
    weight_sum = jnp.sum(weights, axis=-1)
    running = jnp.einsum(
        "tgqk,kgd->tgqd",
        weights.astype(jnp.bfloat16),
        value_part,
        preferred_element_type=jnp.float32,
    )
    return (new_max, weight_sum, running)


def on_device(
    patches,
    merged_grid,
    picture_start,
    vis_gain,
    vis_qkv,
    vis_out,
    merge_weight,
    text_embed,
    dec_gain,
    w_query,
    w_keyval,
    w_out,
    req_lengths,
    final_gain,
    table,
):
    pictures, patch_max, vis_width = patches.shape
    merged_max = patch_max // 4
    vis_cols = vis_qkv.shape[2]
    vis_heads = vis_cols // VHD
    tok_rows, feat_dev = text_embed.shape
    inputs = patches.astype(jnp.float32)
    normed = layer_norm(inputs, vis_gain).astype(jnp.bfloat16)
    packed = jnp.einsum(
        "pnd,dce->pnce", normed, vis_qkv, preferred_element_type=jnp.float32
    ).astype(jnp.bfloat16)
    packed = packed.reshape(pictures, patch_max, 3, vis_heads, VHD)
    scores = jnp.einsum(
        "pqhd,pkhd->phqk", packed[:, :, 0], packed[:, :, 1], preferred_element_type=jnp.float32
    ) / math.sqrt(VHD)
    cell_count = merged_grid[:, 0] * merged_grid[:, 1]
    valid_cols = jnp.arange(patch_max, dtype=jnp.int32)[None, :] < 4 * cell_count[:, None]
    scores = jnp.where(valid_cols[:, None, None, :], scores, -1e30)
    weights = jnp.exp(scores - jnp.max(scores, axis=-1, keepdims=True))
    weight_sum = jnp.sum(weights, axis=-1)
    mixed_rows = jnp.einsum(
        "phqk,pkhd->pqhd",
        weights.astype(jnp.bfloat16),
        packed[:, :, 2],
        preferred_element_type=jnp.float32,
    )
    mixed_rows = (
        (mixed_rows / jnp.transpose(weight_sum, (0, 2, 1))[..., None])
        .astype(jnp.bfloat16)
        .reshape(pictures, patch_max, vis_cols)
    )
    head_part = jnp.einsum("pnc,cd->pnd", mixed_rows, vis_out, preferred_element_type=jnp.float32)
    head_pooled = jnp.mean(head_part.reshape(pictures, merged_max, 4, vis_width), axis=2)
    head_total = lax.psum(head_pooled.astype(jnp.bfloat16), "kv").astype(jnp.float32)
    input_pooled = jnp.mean(inputs.reshape(pictures, merged_max, 4, vis_width), axis=2)
    pooled = (input_pooled + head_total).astype(jnp.bfloat16)
    merged = jnp.einsum(
        "pmd,de->pme", pooled, merge_weight, preferred_element_type=jnp.float32
    ).astype(jnp.bfloat16)
    block_base = lax.axis_index("blk") * tok_rows
    slot_index = jnp.arange(merged_max, dtype=jnp.int32)
    target = picture_start[:, None] + slot_index[None, :] - block_base
    target = jnp.where(slot_index[None, :] < cell_count[:, None], target, -1).reshape(-1)
    local_rows = jnp.arange(tok_rows, dtype=jnp.int32)
    one_hot = local_rows[:, None] == target[None, :]
    placed = jnp.dot(
        one_hot.astype(jnp.bfloat16),
        merged.reshape(pictures * merged_max, feat_dev),
        preferred_element_type=jnp.float32,
    )
    is_vision = jnp.any(one_hot, axis=1)
    seq_in = jnp.where(is_vision[:, None], placed.astype(jnp.bfloat16), text_embed)
    full_rows = lax.all_gather(seq_in, "kv", axis=1, tiled=True)
    full_float = full_rows.astype(jnp.float32)
    dec_normed = (
        full_float
        * lax.rsqrt(jnp.mean(full_float * full_float, axis=-1, keepdims=True) + 1e-05)
        * dec_gain
    ).astype(jnp.bfloat16)
    per_group = QHEADS // KVHEADS
    kv_heads = w_keyval.shape[2] // HD
    row_ids = block_base + local_rows
    request_id, request_begin = request_info(row_ids, req_lengths)
    position = row_ids - request_begin
    query_proj = jnp.dot(dec_normed, w_query, preferred_element_type=jnp.float32).reshape(
        tok_rows, kv_heads * per_group, HD
    )
    query_proj = (
        rotate(query_proj, position)
        .astype(jnp.bfloat16)
        .reshape(tok_rows, kv_heads * per_group * HD)
    )
    key_value = jnp.einsum("td,dce->tce", dec_normed, w_keyval, preferred_element_type=jnp.float32)
    key_rows = (
        rotate(key_value[:, 0].reshape(tok_rows, kv_heads, HD), position)
        .astype(jnp.bfloat16)
        .reshape(tok_rows, kv_heads * HD)
    )
    value_rows = key_value[:, 1].astype(jnp.bfloat16)
    queries = query_proj
    query_req, query_begin = request_info(row_ids, req_lengths)
    queries = queries.reshape(tok_rows, kv_heads, per_group, HD)
    half_rows = tok_rows // 2
    root = math.sqrt(HD)

    def empty_state():
        return (
            jnp.full((half_rows, kv_heads, per_group), -1e30, jnp.float32),
            jnp.zeros((half_rows, kv_heads, per_group), jnp.float32),
            jnp.zeros((half_rows, kv_heads, per_group, HD), jnp.float32),
        )

    carry = (empty_state(), empty_state())
    first_row = jnp.int32(0)
    reqs = req_lengths.shape[0]
    ends_at = jnp.cumsum(req_lengths)
    last_ids = ends_at - 1
    picker = (local_rows[None, :] == (last_ids - block_base)[:, None]).astype(jnp.bfloat16)
    query_last = jnp.dot(picker, query_proj, preferred_element_type=jnp.float32)
    seq_last = jnp.dot(picker, seq_in, preferred_element_type=jnp.float32)
    extras = jnp.concatenate([query_last, seq_last], axis=1).astype(jnp.bfloat16).reshape(-1)
    kv_width = 2 * key_rows.shape[1]
    extra_rows = -(-extras.shape[0] // kv_width)
    extras = jnp.pad(extras, (0, extra_rows * kv_width - extras.shape[0]))
    shipped = jnp.concatenate(
        [key_rows, value_rows, ], axis=1
    )
    shipped = jnp.concatenate([shipped, extras.reshape(extra_rows, kv_width)], axis=0)
    gathered = lax.all_gather(shipped, "blk", axis=0, tiled=False)
    blocks = gathered.shape[0]
    key_part = gathered[:, :tok_rows, : kv_width // 2].reshape(blocks * tok_rows, kv_width // 2)
    value_part = gathered[:, :tok_rows, kv_width // 2 :].reshape(blocks * tok_rows, kv_width // 2)
    extras_all = gathered[:, tok_rows:].reshape(blocks, -1)[:, : reqs * (query_last.shape[1] + feat_dev)]
    extras_all = jnp.sum(extras_all.astype(jnp.float32).reshape(blocks, reqs, -1), axis=0)
    query_last = extras_all[:, : query_last.shape[1]].astype(jnp.bfloat16)
    seq_last = extras_all[:, query_last.shape[1] :]
    piece_rows = key_part.shape[0]
    key_ids = jnp.arange(piece_rows, dtype=jnp.int32)
    key_req, unused_begin = request_info(key_ids, req_lengths)
    key_part = key_part.reshape(piece_rows, kv_heads, HD)
    value_part = value_part.reshape(piece_rows, kv_heads, HD)
    result = []
    for part_index in range(2):
        lower = part_index * half_rows
        sub_ids = row_ids[lower : lower + half_rows]
        sub_req = query_req[lower : lower + half_rows]
        sub_queries = queries[lower : lower + half_rows]
        needed = (jnp.max(sub_ids) >= first_row) & (
            first_row + piece_rows - 1 >= jnp.min(query_begin[lower : lower + half_rows])
        )

        def compute(state):
            return attend(
                state, sub_queries, sub_ids, sub_req, key_part, value_part, key_ids, key_req, root
            )

        def keep_state(state):
            return state

        result.append(lax.cond(needed, compute, keep_state, carry[part_index]))
    states = tuple(result)
    context = jnp.concatenate(
        [states[0][2] / states[0][1][..., None], states[1][2] / states[1][1][..., None]], axis=0
    )
    context = context.astype(jnp.bfloat16).reshape(tok_rows, kv_heads * per_group * HD)
    last_begin = ends_at - req_lengths
    last_allowed = (key_ids[None, :] >= last_begin[:, None]) & (key_ids[None, :] <= last_ids[:, None])
    last_allowed = last_allowed[:, None, None, :]
    last_q = query_last.reshape(reqs, kv_heads, per_group, HD)
    last_scores = (
        jnp.einsum("tgqd,kgd->tgqk", last_q, key_part, preferred_element_type=jnp.float32) / root
    )
    last_scores = jnp.where(last_allowed, last_scores, -1e30)
    last_max = jnp.max(last_scores, axis=-1)
    last_weights = jnp.where(last_allowed, jnp.exp(last_scores - last_max[..., None]), 0.0)
    last_sum = jnp.sum(last_weights, axis=-1)
    last_mix = jnp.einsum(
        "tgqk,kgd->tgqd",
        last_weights.astype(jnp.bfloat16),
        value_part,
        preferred_element_type=jnp.float32,
    )
    last_context = (last_mix / last_sum[..., None]).astype(jnp.bfloat16).reshape(reqs, -1)
    out_rows = jnp.concatenate([context, last_context], axis=0)
    head_sum = lax.psum_scatter(
        jnp.dot(out_rows, w_out, preferred_element_type=jnp.float32).astype(jnp.bfloat16),
        "kv",
        scatter_dimension=1,
        tiled=True,
    ).astype(jnp.float32)
    hidden = (seq_in.astype(jnp.float32) + head_sum[:tok_rows]).astype(jnp.bfloat16)
    chosen = (seq_last + head_sum[tok_rows:]).astype(jnp.bfloat16).astype(jnp.float32)
    square_part = jnp.sum(chosen * chosen, axis=-1)
    scaled = (chosen * final_gain).astype(jnp.bfloat16)
    logit_part = lax.dot_general(
        scaled, table, (((1,), (1,)), ((), ())), preferred_element_type=jnp.float32
    )
    logit_sum, square_sum = (
        lax.psum(logit_part.astype(jnp.bfloat16), "kv").astype(jnp.float32),
        lax.psum(square_part.astype(jnp.bfloat16), "kv").astype(jnp.float32),
    )
    inv_rms = lax.rsqrt(square_sum / D + 1e-05)
    last_norm = (chosen * inv_rms[:, None] * final_gain).astype(jnp.bfloat16)
    local_max = jnp.max(inv_rms[:, None] * logit_sum, axis=-1)
    max_logit = lax.pmax(local_max, "blk")
    return (hidden, last_norm, max_logit)


def solution(mesh):
    placed = (
        P("blk", None, None),
        P("blk", None),
        P("blk"),
        P(),
        P(None, None, "kv"),
        P("kv", None),
        P(None, "kv"),
        P("blk", "kv"),
        P(),
        P(None, "kv"),
        P(None, None, "kv"),
        P("kv", None),
        P(),
        P("kv"),
        P("blk", "kv"),
    )
    return jax.shard_map(
        on_device,
        mesh=mesh,
        in_specs=placed,
        out_specs=(P("blk", "kv"), P(None, "kv"), P()),
        check_vma=False,
    )
```

profile of v0, /device:TPU:0, one launch (start us, length us, event | category | flops | bytes accessed | tf_op | source)
XLA Modules:
  0.0 349.7 jit_solution(14714282198440879519)
XLA Ops:
  7.2 0.9 fusion.125
  8.2 2.5 convert_reduce_fusion
  10.7 2.3 multiply_reduce_fusion
  13.0 2.9 fusion.62
  15.9 0.8 fusion.50
  17.5 1.0 fusion.95
  19.1 1.6 dot_general.59
  20.7 2.8 convolution_reduce_fusion
  23.5 0.9 multiply_convert_fusion.1
  24.6 2.9 reshape.361
  27.7 4.9 %reduce_sum.136 = f32[3,64,1408]{2,1,0:T(8,128)S(1)} reduce(f32[3,64,4,1408]{3,2,1,0:T(4,128)} %reshape.361, f32[]{:T(128)} %constant.33.clone.1), dimensions={2}, to_apply=%region_1.0 | reduce | flops 811008 | bytes 5406724 | tf_op jit(solution)/shard_map/reduce_sum | solution.py:114
  32.7 27.6 %all-reduce.3.cloned.1.call-done = bf16[3,64,1408]{2,1,0:T(8,128)(2,1)} async-done(((bf16[3,64,1408]{2,1,0:T(8,128)(2,1)}), bf16[3,64,1408]{2,1,0:T(8,128)(2,1)}) %all-reduce.3.cloned.1.call-update) | async-done | bytes 540688 | tf_op jit(solution)/shard_map/psum | solution.py:113
  60.3 2.8 fusion.77
  63.1 1.6 fusion.76
  65.7 1.5 convolution_convert_fusion.3
  67.2 32.3 %all-gather.4.cloned.1.call-done = bf16[512,4096]{1,0:T(8,128)(2,1)} async-done(((bf16[512,1024]{1,0:T(8,128)(2,1)}), bf16[512,4096]{1,0:T(8,128)(2,1)}) %all-gather.4.cloned.1.call-update) | async-done | bytes 4194320 | tf_op jit(solution)/shard_map/all_gather | solution.py:132
  99.5 3.2 fusion.35
  102.9 4.9 %fusion.43 = f32[512,2,256]{0,2,1:T(8,128)S(1)} fusion(bf16[4096,2,256]{2,1,0:T(2,128)(2,1)} %param.29, bf16[512,4096]{1,0:T(8,128)(2,1)S(1)} %copy-done.4, f32[4096]{0:T(1024)S(1)} %copy-done.11, f32[512]{0:T(512)S(1)} %add_rsqrt_fusion.1), kind=kOutput, calls=%fused_computation.47 | convolution fusion | flops 2155872256 | bytes 9455616 | tf_op jit(solution)/shard_map/td,dce->tce/dot_general | solution.py:152
  107.9 2.6 fusion.81
  111.4 1.0 copy.115
  116.8 71.6 %all-gather.6.cloned.1.call-done = bf16[4288,512]{1,0:T(8,128)(2,1)} async-done(((bf16[536,512]{1,0:T(8,128)(2,1)}), bf16[4288,512]{1,0:T(8,128)(2,1)}) %all-gather.6.cloned.1.call-update) | async-done | bytes 4390928 | tf_op jit(solution)/shard_map/all_gather | solution.py:188
  188.4 1.0 convert_reduce_fusion.1
  189.4 3.9 %fusion.127 = (bf16[8,512,256]{2,1,0:T(8,128)(2,1)S(1)}, bf16[8,512,256]{2,1,0:T(8,128)(2,1)}) fusion(bf16[8,536,512]{2,1,0:T(8,128)(2,1)} %bitcast.162), kind=kLoop, calls=%fused_computation.169 | loop fusion | bytes 8388608 | tf_op jit(solution)/shard_map/slice | solution.py:190
  193.3 2.1 reshape.381
  195.4 4.7 %copy.148 = bf16[4096,2,128]{0,2,1:T(8,128)(2,1)S(1)} copy(bf16[4096,2,128]{2,1,0:T(2,128)(2,1)} %reshape.381) | data formatting | bytes 4194304 | tf_op jit(solution)/shard_map/reshape;reshape | solution.py:199
  200.1 4.0 %reshape.382 = bf16[4096,2,128]{2,1,0:T(2,128)(2,1)} reshape(bf16[8,512,256]{2,1,0:T(8,128)(2,1)} %get-tuple-element.130) | data formatting | bytes 4194304 | tf_op jit(solution)/shard_map/reshape;reshape | solution.py:200
  204.1 6.3 %copy.149 = bf16[4096,2,128]{0,2,1:T(8,128)(2,1)} copy(bf16[4096,2,128]{2,1,0:T(2,128)(2,1)} %reshape.382) | data formatting | bytes 4194304 | tf_op jit(solution)/shard_map/reshape;reshape | solution.py:200
  210.4 2.5 fusion.128
  212.9 2.0 fusion.89
  214.9 0.8 copy.128
  215.7 20.1 %conditional.2 = (f32[256,2,2]{0,2,1:T(2,128)S(1)}, f32[256,2,2,128]{0,3,2,1:T(8,128)}) conditional(s32[]{:T(128)} %convert_element_type.148, () %tuple.24, (s32[4096]{0:T(1024)S(1)}, s32[256]{0:T(256)S(1)}, s32[4096]{0:T(1024)S(1)}, s32[512]{0:T(512)S(1)}, bf16[512,4,128]{0,2,1:T(8,128)(2,1)S(1)}, /*index=5*/bf16[4096,2,128]{0,2,1:T(8,128)(2,1)S(1)}, ...), branch_computations={%region_15.16_spmd, %region_16.19_spmd} | conditional | flops 2205154304 | bytes 62189584 | solution.py:219
  216.0 1.4 compare_and_fusion
  217.4 3.8 %fusion = (f32[256,2,2]{0,2,1:T(2,128)S(1)}, f32[2,4096,256,2]{2,1,3,0:T(8,128)S(1)}) fusion(pred[256,4096]{0,1:T(8,128)(4,1)S(1)} %compare_and_fusion, bf16[256,2,2,128]{3,0,2,1:T(8,128)(2,1)S(1)} %bitcast.164, bf16[4096,2,128]{0,2,1:T(8,128)(2,1)S(1)} %get-tuple-element.106), kind=kOutput, calls=%fused_computation.2 | convolution fusion | flops 1086323712 | bytes 20189184 | tf_op jit(solution)/shard_map/cond/branch_1_fun/tgqd,kgd->tgqk/dot_general | solution.py:47
  221.2 8.4 %fusion.9 = f32[256,2,2,128]{3,0,2,1:T(8,128)} fusion(bf16[4096,2,128]{0,2,1:T(8,128)(2,1)} %get-tuple-element.107, f32[2,4096,256,2]{2,1,3,0:T(8,128)S(1)} %get-tuple-element.126, f32[256,2,2]{0,2,1:T(2,128)S(1)} %broadcast_maximum_fusion, pred[256,4096]{0,1:T(8,128)(4,1)S(1)} %compare_and_fusion), kind=kOutput, calls=%fused_computation.11 | convolution fusion | flops 1094713344 | bytes 20451328 | tf_op jit(solution)/shard_map/cond/branch_1_fun/tgqk,kgd->tgqd/dot_general | solution.py:55
  229.6 4.2 %fusion.2 = f32[256,2,2]{0,2,1:T(2,128)S(1)} fusion(f32[2,4096,256,2]{2,1,3,0:T(8,128)S(1)} %get-tuple-element.126, f32[256,2,2]{0,2,1:T(2,128)S(1)} %broadcast_maximum_fusion, pred[256,4096]{0,1:T(8,128)(4,1)S(1)} %compare_and_fusion), kind=kLoop, calls=%fused_computation.4 | loop fusion | flops 20970496 | bytes 17833984 | tf_op jit(solution)/shard_map/cond/branch_1_fun/reduce_sum | solution.py:54
  233.7 2.0 copy.157
  235.8 1.1 divide_convert_fusion.1
  236.9 17.8 %conditional.3 = (f32[256,2,2]{0,2,1:T(2,128)S(1)}, f32[256,2,2,128]{0,3,2,1:T(8,128)S(1)}) conditional(s32[]{:T(128)} %convert_element_type.158, () %tuple.26, (s32[4096]{0:T(1024)S(1)}, s32[256]{0:T(256)S(1)}, s32[4096]{0:T(1024)S(1)}, s32[512]{0:T(512)S(1)}, bf16[512,4,128]{0,2,1:T(8,128)(2,1)S(1)}, ...), branch_computations={%region_21.22_spmd, %region_22.25_spmd} | conditional | flops 2205154304 | bytes 62189584 | solution.py:219
  237.5 1.4 compare_and_fusion.1
  238.9 3.8 %fusion.17 = (f32[256,2,2]{0,2,1:T(2,128)S(1)}, f32[2,4096,256,2]{2,1,3,0:T(8,128)S(1)}) fusion(pred[256,4096]{0,1:T(8,128)(4,1)S(1)} %compare_and_fusion.1, bf16[256,2,2,128]{3,0,2,1:T(8,128)(2,1)S(1)} %bitcast.165, bf16[4096,2,128]{0,2,1:T(8,128)(2,1)S(1)} %get-tuple-element.113), kind=kOutput, calls=%fused_computation.18 | convolution fusion | flops 1086323712 | bytes 20189184 | tf_op jit(solution)/shard_map/cond/branch_1_fun/tgqd,kgd->tgqk/dot_general | solution.py:47
  242.7 7.6 %fusion.26 = f32[256,2,2,128]{3,0,2,1:T(8,128)S(1)} fusion(bf16[4096,2,128]{0,2,1:T(8,128)(2,1)} %get-tuple-element.114, f32[2,4096,256,2]{2,1,3,0:T(8,128)S(1)} %get-tuple-element.128, f32[256,2,2]{0,2,1:T(2,128)S(1)} %broadcast_maximum_fusion.1, pred[256,4096]{0,1:T(8,128)(4,1)S(1)} %compare_and_fusion.1), kind=kOutput, calls=%fused_computation.27 | convolution fusion | flops 1094713344 | bytes 20451328 | tf_op jit(solution)/shard_map/cond/branch_1_fun/tgqk,kgd->tgqd/dot_general | solution.py:55
  250.3 4.2 %fusion.19 = f32[256,2,2]{0,2,1:T(2,128)S(1)} fusion(f32[2,4096,256,2]{2,1,3,0:T(8,128)S(1)} %get-tuple-element.128, f32[256,2,2]{0,2,1:T(2,128)S(1)} %broadcast_maximum_fusion.1, pred[256,4096]{0,1:T(8,128)(4,1)S(1)} %compare_and_fusion.1), kind=kLoop, calls=%fused_computation.20 | loop fusion | flops 20970496 | bytes 17833984 | tf_op jit(solution)/shard_map/cond/branch_1_fun/reduce_sum | solution.py:54
  254.7 6.7 %convolution_convert_fusion = bf16[520,4096]{1,0:T(8,128)(2,1)} fusion(bf16[512,4096]{1,0:T(8,128)(2,1)} %param.30, bf16[8,512]{0,1:T(8,128)(2,1)} %copy.128, bf16[256,512]{0,1:T(8,128)(2,1)S(1)} %bitcast.167, bf16[256,512]{0,1:T(8,128)(2,1)S(1)} %bitcast.166), kind=kOutput, calls=%fused_computation.38 | convolution fusion | flops 2184765440 | bytes 8986624 | tf_op jit(solution)/shard_map/dot_general | solution.py:245
  261.5 43.3 %reduce-scatter.2.cloned.1.call-done = bf16[520,1024]{1,0:T(8,128)(2,1)} async-done(((bf16[520,4096]{1,0:T(8,128)(2,1)}), bf16[520,1024]{1,0:T(8,128)(2,1)}) %reduce-scatter.2.cloned.1.call-update) | async-done | bytes 1064976 | tf_op jit(solution)/shard_map/reduce_scatter | solution.py:244
  304.8 1.6 convert_element_type.163
  306.5 2.5 fusion.58
  309.7 10.3 %all-reduce = (bf16[8]{0:T(256)(128)(2,1)S(1)}, bf16[8,1024]{1,0:T(8,128)(2,1)S(1)}) all-reduce(bf16[8]{0:T(256)(128)(2,1)S(1)} %get-tuple-element.123, bf16[8,1024]{1,0:T(8,128)(2,1)S(1)} %convolution_convert_fusion.2), channel_id=1, replica_groups=mesh['kv'=4,'blk'=8] {'kv'}, use_global_device_ids=true, to_apply=%region_30.31 | all-reduce | flops 8200 | bytes 32800 | tf_op jit(solution)/shard_map/psum | solution.py:259
  320.8 22.0 %pmax.7 = f32[8]{0:T(128)} all-reduce(f32[8]{0:T(128)S(1)} %get-tuple-element.141), channel_id=1, replica_groups=mesh['kv'=4,'blk'=8] {'blk'}, use_global_device_ids=true, to_apply=%region_33.34 | all-reduce | flops 8 | bytes 64 | tf_op jit(solution)/shard_map/pmax | solution.py:264
  (84 shorter events, 8.3 us)
Async XLA Ops:
  7.2 5.8 %copy-start = (bf16[1408,3,352]{0,2,1:T(8,128)(2,1)S(1)}, bf16[1408,3,352]{0,2,1:T(8,128)(2,1)}, u32[]{:S(2)}) copy-start(bf16[1408,3,352]{0,2,1:T(8,128)(2,1)} %param.23) | copy-start | bytes 8921092
  7.2 5.8 %copy-start.12 = (f32[1408]{0:T(1024)S(1)}, f32[1408]{0:T(1024)}, u32[]{:S(2)}) copy-start(f32[1408]{0:T(1024)} %param.22) | copy-start | bytes 16900
  7.2 53.1 %all-reduce.3.cloned.1.call-start = ((), (), s32[]{:S(2)}) async-start(), calls=%async_computation.1 | async-start | bytes 1081344 | tf_op jit(solution)/shard_map/psum | solution.py:113
  7.2 5.8 %copy-start.2 = (bf16[3,256,1408]{2,1,0:T(8,128)(2,1)S(1)}, bf16[3,256,1408]{2,1,0:T(8,128)(2,1)}, u32[]{:S(2)}) copy-start(bf16[3,256,1408]{2,1,0:T(8,128)(2,1)} %param.19) | copy-start | bytes 6488068
  19.1 5.5 %copy-start.3 = (bf16[3,256,1408]{2,1,0:T(8,128)(2,1)S(1)}, bf16[3,256,1408]{2,1,0:T(8,128)(2,1)}, u32[]{:S(2)}) copy-start(bf16[3,256,1408]{2,1,0:T(8,128)(2,1)} %param.19) | copy-start | bytes 6488068
  23.5 4.1 %copy-start.7 = (s32[3]{0:T(128)S(1)}, s32[3]{0:T(128)}, u32[]{:S(2)}) copy-start(s32[3]{0:T(128)} %param.21) | copy-start | bytes 40
  24.4 75.1 %all-gather.4.cloned.1.call-start = ((), (), s32[]{:S(2)}) async-start(), calls=%async_computation.2 | async-start | bytes 5242880 | tf_op jit(solution)/shard_map/all_gather | solution.py:132
  27.7 35.4 %copy-start.10 = (bf16[512,1024]{1,0:T(8,128)(2,1)S(1)}, bf16[512,1024]{1,0:T(8,128)(2,1)}, u32[]{:S(2)}) copy-start(bf16[512,1024]{1,0:T(8,128)(2,1)} %param.26) | copy-start | bytes 3145732
  32.7 32.0 %copy-start.8 = (s32[8]{0:T(128)S(1)}, s32[8]{0:T(128)}, u32[]{:S(2)}) copy-start(s32[8]{0:T(128)} %param.31) | copy-start | bytes 100
  63.1 39.6 %copy-start.11 = (f32[4096]{0:T(1024)S(1)}, f32[4096]{0:T(1024)}, u32[]{:S(2)}) copy-start(f32[4096]{0:T(1024)} %param.27) | copy-start | bytes 49156
  64.7 123.7 %all-gather.6.cloned.1.call-start = ((), (), s32[]{:S(2)}) async-start(), calls=%async_computation.4 | async-start | bytes 4939776 | tf_op jit(solution)/shard_map/all_gather | solution.py:188
  99.5 3.4 copy-start.4
  102.9 5.0 %copy-start.9 = (bf16[4096,512]{1,0:T(8,128)(2,1)S(1)}, bf16[4096,512]{1,0:T(8,128)(2,1)}, u32[]{:S(2)}) copy-start(bf16[4096,512]{1,0:T(8,128)(2,1)} %param.28) | copy-start | bytes 12582916
  112.4 192.3 %reduce-scatter.2.cloned.1.call-start = ((), (), s32[]{:S(2)}) async-start(), calls=%async_computation.3 | async-start | bytes 5324800 | tf_op jit(solution)/shard_map/reduce_scatter | solution.py:244
  261.5 47.6 %copy-start.6 = (f32[1024]{0:T(1024)S(1)}, f32[1024]{0:T(1024)}, u32[]{:S(2)}) copy-start(f32[1024]{0:T(1024)} %param.32) | copy-start | bytes 12292
  261.5 81.3 %copy-start.1 = (bf16[1408,3,352]{0,2,1:T(8,128)(2,1)S(1)}, bf16[1408,3,352]{0,2,1:T(8,128)(2,1)}, u32[]{:S(2)}) copy-start(bf16[1408,3,352]{0,2,1:T(8,128)(2,1)} %param.23) | copy-start | bytes 8921092
  304.8 4.3 %copy-start.5 = (bf16[1024,1024]{1,0:T(8,128)(2,1)S(1)}, bf16[1024,1024]{1,0:T(8,128)(2,1)}, u32[]{:S(2)}) copy-start(bf16[1024,1024]{1,0:T(8,128)(2,1)} %param.33) | copy-start | bytes 6291460
Sparse Core Ops, SparseCore 0:
  24.5 35.7 all-reduce.2
  64.8 34.6 all-gather.3
  112.6 75.8 all-gather.5
  261.6 43.1 reduce-scatter.1
where the time goes:
time: 356 us; the launch traced here: 350 us
  waiting for transfers between devices  175 us (49%)
  matrix products  56.4 us (16%)
  other arithmetic  36.8 us (10%)
  blocking collectives  32.2 us (9%)
  local copies, waits for them, and re-layouts  31.4 us (9%)
  between operations  17.2 us (5%)
    all_gather x1, waiting for transfers between devices, on_device(): gathered = lax.all_gather(shipped, 'blk', axis=0, tiled=False)  71.6 us
    reduce_scatter x1, waiting for transfers between devices, on_device(): lax.psum_scatter(jnp.dot(out_rows, w_out, preferred_element_type=jnp.floa...  43.3 us
    all_gather x1, waiting for transfers between devices, on_device(): full_rows = lax.all_gather(seq_in, 'kv', axis=1, tiled=True)  32.3 us
    psum x1, waiting for transfers between devices, on_device(): lax.psum(head_pooled.astype(jnp.bfloat16), 'kv').astype(jnp.float32)  27.6 us
    pmax x1, blocking collectives, on_device(): max_logit = lax.pmax(local_max, 'blk')  22 us
    dot_general x2, matrix products, attend(): jnp.einsum('tgqk,kgd->tgqd', weights.astype(jnp.bfloat16), value_part, pr...  16 us
    psum x1, blocking collectives, on_device(): lax.psum(square_part.astype(jnp.bfloat16), 'kv').astype(jnp.float32)  10.3 us
    another operation x2, local copies, waits for them, and re-layouts, on_device(): value_part = value_part.reshape(piece_rows, kv_heads, HD)  10.3 us
  transfers between devices with their start and end apart: 4, of which 4 were waited for; matrix products, arithmetic and copies ran while one was open for 3% of the time, Pallas kernels for 0%

commit v1 on v0

--- a/solution.py
+++ b/solution.py
@@ -39,26 +39,6 @@
     choose = request_id[:, None] == jnp.arange(req_lengths.shape[0], dtype=jnp.int32)[None, :]
     request_begin = jnp.sum(jnp.where(choose, starts_at[None, :], 0), axis=1)
     return (request_id, request_begin)
-
-
-def attend(state, queries, query_ids, query_req, key_part, value_part, key_ids, key_req, root):
-    run_max, weight_sum, running = state
-    scores = (
-        jnp.einsum("tgqd,kgd->tgqk", queries, key_part, preferred_element_type=jnp.float32) / root
-    )
-    allowed = (key_ids[None, :] <= query_ids[:, None]) & (key_req[None, :] == query_req[:, None])
-    allowed = allowed[:, None, None, :]
-    scores = jnp.where(allowed, scores, -1e30)
-    new_max = jnp.maximum(run_max, jnp.max(scores, axis=-1))
-    weights = jnp.where(allowed, jnp.exp(scores - new_max[..., None]), 0.0)
-    weight_sum = jnp.sum(weights, axis=-1)
-    running = jnp.einsum(
-        "tgqk,kgd->tgqd",
-        weights.astype(jnp.bfloat16),
-        value_part,
-        preferred_element_type=jnp.float32,
-    )
-    return (new_max, weight_sum, running)
 
 
 def on_device(
@@ -83,6 +63,7 @@
     vis_cols = vis_qkv.shape[2]
     vis_heads = vis_cols // VHD
     tok_rows, feat_dev = text_embed.shape
+    text_rows = lax.all_gather(text_embed, "kv", axis=1, tiled=True)
     inputs = patches.astype(jnp.float32)
     normed = layer_norm(inputs, vis_gain).astype(jnp.bfloat16)
     packed = jnp.einsum(
@@ -129,7 +110,11 @@
     )
     is_vision = jnp.any(one_hot, axis=1)
     seq_in = jnp.where(is_vision[:, None], placed.astype(jnp.bfloat16), text_embed)
-    full_rows = lax.all_gather(seq_in, "kv", axis=1, tiled=True)
+    merged_rows = lax.all_gather(
+        merged.reshape(pictures * merged_max, feat_dev), "kv", axis=1, tiled=True
+    )
+    placed_rows = jnp.dot(one_hot.astype(jnp.bfloat16), merged_rows, preferred_element_type=jnp.float32)
+    full_rows = jnp.where(is_vision[:, None], placed_rows.astype(jnp.bfloat16), text_rows)
     full_float = full_rows.astype(jnp.float32)
     dec_normed = (
         full_float
@@ -156,21 +141,8 @@
         .reshape(tok_rows, kv_heads * HD)
     )
     value_rows = key_value[:, 1].astype(jnp.bfloat16)
-    queries = query_proj
     query_req, query_begin = request_info(row_ids, req_lengths)
-    queries = queries.reshape(tok_rows, kv_heads, per_group, HD)
-    half_rows = tok_rows // 2
     root = math.sqrt(HD)
-
-    def empty_state():
-        return (
-            jnp.full((half_rows, kv_heads, per_group), -1e30, jnp.float32),
-            jnp.zeros((half_rows, kv_heads, per_group), jnp.float32),
-            jnp.zeros((half_rows, kv_heads, per_group, HD), jnp.float32),
-        )
-
-    carry = (empty_state(), empty_state())
-    first_row = jnp.int32(0)
     reqs = req_lengths.shape[0]
     ends_at = jnp.cumsum(req_lengths)
     last_ids = ends_at - 1
@@ -178,68 +150,104 @@
     query_last = jnp.dot(picker, query_proj, preferred_element_type=jnp.float32)
     seq_last = jnp.dot(picker, seq_in, preferred_element_type=jnp.float32)
     extras = jnp.concatenate([query_last, seq_last], axis=1).astype(jnp.bfloat16).reshape(-1)
-    kv_width = 2 * key_rows.shape[1]
-    extra_rows = -(-extras.shape[0] // kv_width)
-    extras = jnp.pad(extras, (0, extra_rows * kv_width - extras.shape[0]))
-    shipped = jnp.concatenate(
-        [key_rows, value_rows, ], axis=1
-    )
-    shipped = jnp.concatenate([shipped, extras.reshape(extra_rows, kv_width)], axis=0)
+    kv_width = key_rows.shape[1]
+    ship_width = 2 * kv_width
+    extra_rows = -(-extras.shape[0] // ship_width)
+    extras = jnp.pad(extras, (0, extra_rows * ship_width - extras.shape[0]))
+    shipped = jnp.concatenate([key_rows, value_rows], axis=1)
+    shipped = jnp.concatenate([shipped, extras.reshape(extra_rows, ship_width)], axis=0)
     gathered = lax.all_gather(shipped, "blk", axis=0, tiled=False)
     blocks = gathered.shape[0]
-    key_part = gathered[:, :tok_rows, : kv_width // 2].reshape(blocks * tok_rows, kv_width // 2)
-    value_part = gathered[:, :tok_rows, kv_width // 2 :].reshape(blocks * tok_rows, kv_width // 2)
-    extras_all = gathered[:, tok_rows:].reshape(blocks, -1)[:, : reqs * (query_last.shape[1] + feat_dev)]
+    q_cols = query_proj.shape[1]
+    extras_all = gathered[:, tok_rows:].reshape(blocks, -1)[:, : reqs * (q_cols + feat_dev)]
     extras_all = jnp.sum(extras_all.astype(jnp.float32).reshape(blocks, reqs, -1), axis=0)
-    query_last = extras_all[:, : query_last.shape[1]].astype(jnp.bfloat16)
-    seq_last = extras_all[:, query_last.shape[1] :]
-    piece_rows = key_part.shape[0]
-    key_ids = jnp.arange(piece_rows, dtype=jnp.int32)
-    key_req, unused_begin = request_info(key_ids, req_lengths)
-    key_part = key_part.reshape(piece_rows, kv_heads, HD)
-    value_part = value_part.reshape(piece_rows, kv_heads, HD)
-    result = []
-    for part_index in range(2):
-        lower = part_index * half_rows
-        sub_ids = row_ids[lower : lower + half_rows]
-        sub_req = query_req[lower : lower + half_rows]
-        sub_queries = queries[lower : lower + half_rows]
-        needed = (jnp.max(sub_ids) >= first_row) & (
-            first_row + piece_rows - 1 >= jnp.min(query_begin[lower : lower + half_rows])
-        )
+    query_last = extras_all[:, :q_cols].astype(jnp.bfloat16)
+    seq_last = extras_all[:, q_cols:]
+    group_queries = [
+        query_proj[:, g * per_group * HD : (g + 1) * per_group * HD].reshape(tok_rows, per_group, HD)
+        for g in range(kv_heads)
+    ]
+    block_index = lax.axis_index("blk")
+    first_begin = query_begin[0]
+
+    def block_step(kb, state):
+        key_first = kb * tok_rows
+        needed = (kb <= block_index) & (key_first + tok_rows - 1 >= first_begin)
 
         def compute(state):
-            return attend(
-                state, sub_queries, sub_ids, sub_req, key_part, value_part, key_ids, key_req, root
-            )
-
-        def keep_state(state):
-            return state
-
-        result.append(lax.cond(needed, compute, keep_state, carry[part_index]))
-    states = tuple(result)
+            piece = lax.dynamic_index_in_dim(gathered, kb, 0, keepdims=False)
+            key_ids = key_first + local_rows
+            key_req, unused = request_info(key_ids, req_lengths)
+            allowed = (key_ids[None, :] <= row_ids[:, None]) & (key_req[None, :] == query_req[:, None])
+            allowed = allowed[:, None, :]
+            new_state = []
+            for g in range(kv_heads):
+                run_max, run_sum, run_acc = state[g]
+                keys_g = piece[:tok_rows, g * HD : (g + 1) * HD]
+                values_g = piece[:tok_rows, kv_width + g * HD : kv_width + (g + 1) * HD]
+                scores = (
+                    jnp.einsum(
+                        "tqd,kd->tqk", group_queries[g], keys_g, preferred_element_type=jnp.float32
+                    )
+                    / root
+                )
+                scores = jnp.where(allowed, scores, -1e30)
+                new_max = jnp.maximum(run_max, jnp.max(scores, axis=-1))
+                weights = jnp.where(allowed, jnp.exp(scores - new_max[..., None]), 0.0)
+                scale = jnp.exp(run_max - new_max)
+                new_sum = run_sum * scale + jnp.sum(weights, axis=-1)
+                new_acc = run_acc * scale[..., None] + jnp.einsum(
+                    "tqk,kd->tqd",
+                    weights.astype(jnp.bfloat16),
+                    values_g,
+                    preferred_element_type=jnp.float32,
+                )
+                new_state.append((new_max, new_sum, new_acc))
+            return tuple(new_state)
+
+        return lax.cond(needed, compute, lambda s: s, state)
+
+    init = tuple(
+        (
+            jnp.full((tok_rows, per_group), -1e30, jnp.float32),
+            jnp.zeros((tok_rows, per_group), jnp.float32),
+            jnp.zeros((tok_rows, per_group, HD), jnp.float32),
+        )
+        for g in range(kv_heads)
+    )
+    final = lax.fori_loop(0, blocks, block_step, init)
     context = jnp.concatenate(
-        [states[0][2] / states[0][1][..., None], states[1][2] / states[1][1][..., None]], axis=0
-    )
-    context = context.astype(jnp.bfloat16).reshape(tok_rows, kv_heads * per_group * HD)
+        [(acc / total[..., None]).reshape(tok_rows, per_group * HD) for unused, total, acc in final],
+        axis=1,
+    ).astype(jnp.bfloat16)
+    all_ids = jnp.arange(blocks * tok_rows, dtype=jnp.int32)
     last_begin = ends_at - req_lengths
-    last_allowed = (key_ids[None, :] >= last_begin[:, None]) & (key_ids[None, :] <= last_ids[:, None])
-    last_allowed = last_allowed[:, None, None, :]
-    last_q = query_last.reshape(reqs, kv_heads, per_group, HD)
-    last_scores = (
-        jnp.einsum("tgqd,kgd->tgqk", last_q, key_part, preferred_element_type=jnp.float32) / root
-    )
-    last_scores = jnp.where(last_allowed, last_scores, -1e30)
-    last_max = jnp.max(last_scores, axis=-1)
-    last_weights = jnp.where(last_allowed, jnp.exp(last_scores - last_max[..., None]), 0.0)
-    last_sum = jnp.sum(last_weights, axis=-1)
-    last_mix = jnp.einsum(
-        "tgqk,kgd->tgqd",
-        last_weights.astype(jnp.bfloat16),
-        value_part,
-        preferred_element_type=jnp.float32,
-    )
-    last_context = (last_mix / last_sum[..., None]).astype(jnp.bfloat16).reshape(reqs, -1)
+    last_allowed = (all_ids[None, :] >= last_begin[:, None]) & (all_ids[None, :] <= last_ids[:, None])
+    last_allowed = last_allowed[:, None, :]
+    last_parts = []
+    for g in range(kv_heads):
+        keys_g = gathered[:, :tok_rows, g * HD : (g + 1) * HD].reshape(blocks * tok_rows, HD)
+        values_g = gathered[:, :tok_rows, kv_width + g * HD : kv_width + (g + 1) * HD].reshape(
+            blocks * tok_rows, HD
+        )
+        last_q = query_last[:, g * per_group * HD : (g + 1) * per_group * HD].reshape(
+            reqs, per_group, HD
+        )
+        last_scores = (
+            jnp.einsum("tqd,kd->tqk", last_q, keys_g, preferred_element_type=jnp.float32) / root
+        )
+        last_scores = jnp.where(last_allowed, last_scores, -1e30)
+        last_max = jnp.max(last_scores, axis=-1)
+        last_weights = jnp.where(last_allowed, jnp.exp(last_scores - last_max[..., None]), 0.0)
+        last_sum = jnp.sum(last_weights, axis=-1)
+        last_mix = jnp.einsum(
+            "tqk,kd->tqd",
+            last_weights.astype(jnp.bfloat16),
+            values_g,
+            preferred_element_type=jnp.float32,
+        )
+        last_parts.append((last_mix / last_sum[..., None]).reshape(reqs, per_group * HD))
+    last_context = jnp.concatenate(last_parts, axis=1).astype(jnp.bfloat16)
     out_rows = jnp.concatenate([context, last_context], axis=0)
     head_sum = lax.psum_scatter(
         jnp.dot(out_rows, w_out, preferred_element_type=jnp.float32).astype(jnp.bfloat16),

time: 356 us -> 364 us (1.022); the launches traced: 350 us -> 363 us
  waiting for transfers between devices: 175 us -> 236 us
  other arithmetic: 36.8 us -> 17.5 us
  matrix products: 56.4 us -> 39.4 us
  local copies, waits for them, and re-layouts: 31.4 us -> 18 us
  loops' own time: 0.37 us -> 5.47 us
    reduce_scatter x1, waiting for transfers between devices: 43.3 us -> 80.9 us  [on_device(): lax.psum_scatter(jnp.dot(out_rows, w_out, preferred_element_type=jnp.floa...]
    all_gather x1 -> x2, waiting for transfers between devices: 32.3 us -> 52 us  [the longest x1 36.2 us: on_device(): text_rows = lax.all_gather(text_embed, 'kv', axis=1, tiled=True)]
    another operation x6, local copies, waits for them, and re-layouts: 17.6 us -> 1.68 us  [the longest x2 10.3 us: on_device(): value_part = value_part.reshape(piece_rows, kv_heads, HD)]
    dot_general x5 -> x7, matrix products: 25.5 us -> 11.6 us  [the longest x2 5.43 us: compute(): jnp.einsum('tqk,kd->tqd', weights.astype(jnp.bfloat16), values_g, preferr...]
    reduce_sum x3 -> x1, other arithmetic: 11.6 us -> 1.06 us  [compute(): new_sum = run_sum * scale + jnp.sum(weights, axis=-1)]
    another operation x2 -> x9, loops' own time: 0.37 us -> 5.47 us  [the longest x1 5.29 us: on_device(): final = lax.fori_loop(0, blocks, block_step, init)]
  transfers between devices with their start and end apart: 4 -> 5, of which waited for: 4 -> 5; matrix products, arithmetic and copies ran while one was open for 3% -> 3% of each run, Pallas kernels for 0% -> 0%
where the time goes in v1:
time: 364 us; the launch traced here: 363 us
  waiting for transfers between devices  236 us (65%)
  matrix products  39.4 us (11%)
  blocking collectives  32.2 us (9%)
  local copies, waits for them, and re-layouts  18 us (5%)
  other arithmetic  17.5 us (5%)
  between operations  14.3 us (4%)
  loops' own time  5.47 us (2%)
    reduce_scatter x1, waiting for transfers between devices, on_device(): lax.psum_scatter(jnp.dot(out_rows, w_out, preferred_element_type=jnp.floa...  80.9 us
    all_gather x1, waiting for transfers between devices, on_device(): gathered = lax.all_gather(shipped, 'blk', axis=0, tiled=False)  74.7 us
    all_gather x1, waiting for transfers between devices, on_device(): text_rows = lax.all_gather(text_embed, 'kv', axis=1, tiled=True)  36.2 us
    psum x1, waiting for transfers between devices, on_device(): lax.psum(head_pooled.astype(jnp.bfloat16), 'kv').astype(jnp.float32)  27.3 us
    pmax x1, blocking collectives, on_device(): max_logit = lax.pmax(local_max, 'blk')  22 us
    all_gather x1, waiting for transfers between devices, on_device(): lax.all_gather(merged.reshape(pictures * merged_max, feat_dev), 'kv', axi...  15.9 us
    psum x1, blocking collectives, on_device(): lax.psum(square_part.astype(jnp.bfloat16), 'kv').astype(jnp.float32)  10.3 us
  transfers between devices with their start and end apart: 5, of which 5 were waited for; matrix products, arithmetic and copies ran while one was open for 3% of the time, Pallas kernels for 0%

profile of v1, /device:TPU:0, one launch (start us, length us, event | category | flops | bytes accessed | tf_op | source)
XLA Modules:
  0.0 363.2 jit_solution(8306512292676467344)
XLA Ops:
  7.3 2.1 convert_reduce_fusion.1
  9.7 0.7 multiply_reduce_fusion
  10.5 2.9 fusion.58
  13.4 0.8 fusion.49
  14.2 0.7 fusion.50
  14.9 1.0 fusion.86
  15.9 0.6 copy.83
  16.6 0.7 dot_general.68
  17.3 1.3 convolution_reduce_fusion
  18.7 0.9 multiply_convert_fusion.1
  19.6 0.9 copy-done.3
  20.5 2.9 reshape.365
  23.4 4.8 %reduce_sum.145 = f32[3,64,1408]{2,1,0:T(8,128)S(1)} reduce(f32[3,64,4,1408]{3,2,1,0:T(4,128)} %reshape.365, f32[]{:T(128)} %constant.105.clone.1), dimensions={2}, to_apply=%region_1.0 | reduce | flops 811008 | bytes 5406724 | tf_op jit(solution)/shard_map/reduce_sum | solution.py:95
  28.2 27.3 %all-reduce.3.cloned.1.call-done = bf16[3,64,1408]{2,1,0:T(8,128)(2,1)} async-done(((bf16[3,64,1408]{2,1,0:T(8,128)(2,1)}), bf16[3,64,1408]{2,1,0:T(8,128)(2,1)}) %all-reduce.3.cloned.1.call-update) | async-done | bytes 540688 | tf_op jit(solution)/shard_map/psum | solution.py:94
  55.5 3.5 fusion.73
  59.1 0.7 all-gather.7.cloned.1.call-update
  60.7 0.5 multiply_cosine_fusion
  61.3 1.6 fusion.72
  63.1 15.9 %all-gather.5.cloned.1.call-done = bf16[192,4096]{1,0:T(8,128)(2,1)} async-done(((bf16[192,1024]{1,0:T(8,128)(2,1)}), bf16[192,4096]{1,0:T(8,128)(2,1)}) %all-gather.5.cloned.1.call-update) | async-done | bytes 1572880 | tf_op jit(solution)/shard_map/all_gather | solution.py:113
  79.0 36.2 %all-gather.7.cloned.1.call-done = bf16[512,4096]{1,0:T(8,128)(2,1)} async-done(((bf16[512,1024]{1,0:T(8,128)(2,1)}), bf16[512,4096]{1,0:T(8,128)(2,1)}) %all-gather.7.cloned.1.call-update) | async-done | bytes 4194320 | tf_op jit(solution)/shard_map/all_gather | solution.py:66
  115.2 4.5 %fusion.30 = (f32[512]{0:T(512)S(1)}, bf16[512,4096]{1,0:T(8,128)(2,1)S(1)}) fusion(bf16[512,4096]{1,0:T(8,128)(2,1)} %all-gather.7.cloned.1.call-done, bf16[192,4096]{1,0:T(8,128)(2,1)} %all-gather.5.cloned.1.call-done, s32[192]{0:T(256)S(1)} %select_n.59, pred[512]{0:T(512)(128)(4,1)S(1)} %fusion.98), kind=kOutput, calls=%fused_computation.47 | convolution fusion | flops 815889920 | bytes 9964800 | tf_op jit(solution)/shard_map/dot_general | solution.py:116
  119.7 2.6 fusion.42
  122.4 2.6 fusion.76
  125.9 1.0 copy.87
  128.2 74.7 %all-gather.9.cloned.1.call-done = bf16[4288,512]{1,0:T(8,128)(2,1)} async-done(((bf16[536,512]{1,0:T(8,128)(2,1)}), bf16[4288,512]{1,0:T(8,128)(2,1)}) %all-gather.9.cloned.1.call-update) | async-done | bytes 4390928 | tf_op jit(solution)/shard_map/all_gather | solution.py:159
  202.9 4.4 %fusion.120 = (bf16[8,512,128]{2,1,0:T(8,128)(2,1)}, bf16[8,512,128]{2,1,0:T(8,128)(2,1)}, bf16[8,512,128]{2,1,0:T(8,128)(2,1)}, bf16[8,512,128]{2,1,0:T(8,128)(2,1)}) fusion(bf16[8,536,512]{2,1,0:T(8,128)(2,1)} %bitcast.156), kind=kLoop, calls=%fused_computation.185 | loop fusion | bytes 8388608 | tf_op jit(solution)/shard_map/slice | solution.py:229
  207.3 1.0 convert_reduce_fusion.2
  208.2 0.8 broadcast.241
  209.1 0.8 broadcast.241.clone
  209.9 14.9 %while.28 = (s32[]{:T(128)}, f32[512,2]{0,1:T(2,128)S(1)}, f32[512,2]{0,1:T(2,128)S(1)}, f32[512,2,128]{2,0,1:T(8,128)}, f32[512,2]{0,1:T(2,128)S(1)}, /*index=5...) while((s32[]{:T(128)}, f32[512,2]{0,1:T(2,128)S(1)}, ...), condition=%wide.region_21.22_spmd.clone, body=%wide.region_12.21_spmd.clone.sunk | while | flops 551830080 | bytes 20388432 | solution.py:218
  210.6 9.5 %conditional.3 = ((f32[512,2]{0,1:T(2,128)S(1)}, f32[512,2]{0,1:T(2,128)S(1)}, f32[512,2,128]{2,0,1:T(8,128)}, f32[512,2]{0,1:T(2,128)S(1)}, f32[512,2]{0,1:T(2,128)S(1)}, /*index=5*/f32[512,2,128]{2,0,1:T(8,128)})) conditional(s32[]{:T(128)} %convert_element_type.269, (f32[512,2]{0,1:T(2,128)S(1)}, f32[512,2]{0,1:T(2,128)S(1)}, ...), branch_computations={%region_13.13_spmd, %region_14.20_spmd} | conditional | flops 551830080 | bytes 20385994 | solution.py:208
  210.6 1.1 dynamic-slice_bitcast_fusion
  212.7 0.8 fusion.5
  213.5 1.1 fusion.9
  214.6 2.7 convolution_add_fusion
  217.3 2.7 convolution_add_fusion.1
  224.8 1.3 copy.90
  226.1 1.2 copy.91
  227.4 1.9 fusion.123
  229.4 1.8 fusion.122
  232.0 6.6 %convolution_convert_fusion = bf16[520,4096]{1,0:T(8,128)(2,1)} fusion(bf16[512,4096]{1,0:T(8,128)(2,1)} %param.30, bf16[8,512]{0,1:T(8,128)(2,1)S(1)} %copy.92, bf16[512,256]{0,1:T(8,128)(2,1)S(1)} %bitcast.170, bf16[512,256]{0,1:T(8,128)(2,1)S(1)} %bitcast.171), kind=kOutput, calls=%fused_computation.50 | convolution fusion | flops 2184765440 | bytes 8986624 | tf_op jit(solution)/shard_map/dot_general | solution.py:253
  238.7 80.9 %reduce-scatter.2.cloned.1.call-done = bf16[520,1024]{1,0:T(8,128)(2,1)} async-done(((bf16[520,4096]{1,0:T(8,128)(2,1)}), bf16[520,1024]{1,0:T(8,128)(2,1)}) %reduce-scatter.2.cloned.1.call-update) | async-done | bytes 1064976 | tf_op jit(solution)/shard_map/reduce_scatter | solution.py:252
  319.5 1.6 convert_element_type.169
  321.3 1.3 fusion.57
  323.0 0.6 convolution_convert_fusion.3
  323.6 10.3 %all-reduce = (bf16[8]{0:T(256)(128)(2,1)S(1)}, bf16[8,1024]{1,0:T(8,128)(2,1)S(1)}) all-reduce(bf16[8]{0:T(256)(128)(2,1)S(1)} %get-tuple-element.768, bf16[8,1024]{1,0:T(8,128)(2,1)S(1)} %convolution_convert_fusion.3), channel_id=1, replica_groups=mesh['kv'=4,'blk'=8] {'kv'}, use_global_device_ids=true, to_apply=%region_29.30 | all-reduce | flops 8200 | bytes 32800 | tf_op jit(solution)/shard_map/psum | solution.py:267
  333.9 0.8 multiply_reduce_fusion.1
  334.7 22.0 %pmax.7 = f32[8]{0:T(128)} all-reduce(f32[8]{0:T(128)S(1)} %get-tuple-element.787), channel_id=1, replica_groups=mesh['kv'=4,'blk'=8] {'blk'}, use_global_device_ids=true, to_apply=%region_32.33 | all-reduce | flops 8 | bytes 64 | tf_op jit(solution)/shard_map/pmax | solution.py:272
  (117 shorter events, 6.4 us)
Async XLA Ops:
  7.2 3.3 copy-start
  7.2 3.2 copy-start.11
  7.2 3.3 copy-start.18
  7.2 48.3 %all-reduce.3.cloned.1.call-start = ((), (), s32[]{:S(2)}) async-start(), calls=%async_computation.1 | async-start | bytes 1081344 | tf_op jit(solution)/shard_map/psum | solution.py:94
  7.2 2.4 copy-start.2
  15.9 1.4 copy-start.16
  18.7 1.8 copy-start.3
  19.6 59.5 %all-gather.5.cloned.1.call-start = ((), (), s32[]{:S(2)}) async-start(), calls=%async_computation.2 | async-start | bytes 1966080 | tf_op jit(solution)/shard_map/all_gather | solution.py:113
  28.2 31.9 %copy-start.12 = (s32[3]{0:T(128)S(1)}, s32[3]{0:T(128)}, u32[]{:S(2)}) copy-start(s32[3]{0:T(128)} %param.21) | copy-start | bytes 40
  28.2 32.0 %copy-start.13 = (s32[8]{0:T(128)S(1)}, s32[8]{0:T(128)}, u32[]{:S(2)}) copy-start(s32[8]{0:T(128)} %param.31) | copy-start | bytes 100
  28.2 33.1 %copy-start.9 = (bf16[512,1024]{1,0:T(8,128)(2,1)S(1)}, bf16[512,1024]{1,0:T(8,128)(2,1)}, u32[]{:S(2)}) copy-start(bf16[512,1024]{1,0:T(8,128)(2,1)} %param.26) | copy-start | bytes 3145732
  59.1 56.1 %all-gather.7.cloned.1.call-start = ((), (), s32[]{:S(2)}) async-start(), calls=%async_computation.3 | async-start | bytes 5242880 | tf_op jit(solution)/shard_map/all_gather | solution.py:66
  59.8 143.1 %all-gather.9.cloned.1.call-start = ((), (), s32[]{:S(2)}) async-start(), calls=%async_computation.5 | async-start | bytes 4939776 | tf_op jit(solution)/shard_map/all_gather | solution.py:159
  62.8 56.8 %copy-start.4 = (bf16[512,1024]{1,0:T(8,128)(2,1)}, bf16[512,1024]{1,0:T(8,128)(2,1)S(1)}, u32[]{:S(2)}) copy-start(bf16[512,1024]{1,0:T(8,128)(2,1)S(1)} %fusion.72) | copy-start | bytes 3145732
  63.1 56.5 %copy-start.17 = (f32[4096]{0:T(1024)S(1)}, f32[4096]{0:T(1024)}, u32[]{:S(2)}) copy-start(f32[4096]{0:T(1024)} %param.27) | copy-start | bytes 49156
  115.2 4.5 %copy-start.14 = (bf16[4096,2,256]{2,1,0:T(2,128)(2,1)S(1)}, bf16[4096,2,256]{2,1,0:T(2,128)(2,1)}, u32[]{:S(2)}) copy-start(bf16[4096,2,256]{2,1,0:T(2,128)(2,1)} %param.29) | copy-start | bytes 12582916
  119.7 2.7 copy-start.15
  126.9 192.6 %reduce-scatter.2.cloned.1.call-start = ((), (), s32[]{:S(2)}) async-start(), calls=%async_computation.4 | async-start | bytes 5324800 | tf_op jit(solution)/shard_map/reduce_scatter | solution.py:252
  224.8 6.4 %copy-start.7 = (bf16[8,512,128]{2,1,0:T(8,128)(2,1)S(1)}, bf16[8,512,128]{2,1,0:T(8,128)(2,1)}, u32[]{:S(2)}) copy-start(bf16[8,512,128]{2,1,0:T(8,128)(2,1)} %get-tuple-element.776) | copy-start | bytes 3145732
  227.4 4.1 %copy-start.6 = (bf16[8,512,128]{2,1,0:T(8,128)(2,1)S(1)}, bf16[8,512,128]{2,1,0:T(8,128)(2,1)}, u32[]{:S(2)}) copy-start(bf16[8,512,128]{2,1,0:T(8,128)(2,1)} %get-tuple-element.774) | copy-start | bytes 3145732
  319.5 1.7 copy-start.5
  321.1 1.9 copy-start.8
  321.1 1.8 copy-start.10
  321.3 35.4 %copy-start.1 = (bf16[1408,3,352]{0,2,1:T(8,128)(2,1)S(1)}, bf16[1408,3,352]{0,2,1:T(8,128)(2,1)}, u32[]{:S(2)}) copy-start(bf16[1408,3,352]{0,2,1:T(8,128)(2,1)} %param.23) | copy-start | bytes 8921092
Sparse Core Ops, SparseCore 0:
  19.7 35.7 all-reduce.2
  59.2 19.7 all-gather.4
  80.7 34.4 all-gather.6
  127.0 75.8 all-gather.8
  238.8 80.7 reduce-scatter.1

commit v2 on v1

--- a/solution.py
+++ b/solution.py
@@ -1,8 +1,11 @@
+import functools
 import math
 
 import jax
 import jax.numpy as jnp
 from jax import lax
+from jax.experimental import pallas as pl
+from jax.experimental.pallas import tpu as pltpu
 from jax.sharding import PartitionSpec as P
 
 VHD = 88
@@ -39,6 +42,74 @@
     choose = request_id[:, None] == jnp.arange(req_lengths.shape[0], dtype=jnp.int32)[None, :]
     request_begin = jnp.sum(jnp.where(choose, starts_at[None, :], 0), axis=1)
     return (request_id, request_begin)
+
+
+def flash_kernel(needed_ref, q_ref, k_ref, v_ref, qid_ref, qreq_ref, kid_ref, kreq_ref, o_ref,
+                 max_ref, sum_ref, acc_ref, *, root):
+    kb = pl.program_id(1)
+
+    @pl.when(kb == 0)
+    def _():
+        max_ref[...] = jnp.full(max_ref.shape, -1e30, jnp.float32)
+        sum_ref[...] = jnp.zeros(sum_ref.shape, jnp.float32)
+        acc_ref[...] = jnp.zeros(acc_ref.shape, jnp.float32)
+
+    @pl.when(needed_ref[kb] != 0)
+    def _():
+        scores = lax.dot_general(
+            q_ref[...], k_ref[...], (((1,), (1,)), ((), ())), preferred_element_type=jnp.float32
+        ) / root
+        allowed = (kid_ref[...] <= qid_ref[...]) & (kreq_ref[...] == qreq_ref[...])
+        scores = jnp.where(allowed, scores, -1e30)
+        old_max = max_ref[...]
+        new_max = jnp.maximum(old_max, jnp.max(scores, axis=1, keepdims=True))
+        weights = jnp.where(allowed, jnp.exp(scores - new_max), 0.0)
+        scale = jnp.exp(old_max - new_max)
+        sum_ref[...] = sum_ref[...] * scale + jnp.sum(weights, axis=1, keepdims=True)
+        acc_ref[...] = acc_ref[...] * scale + jnp.dot(
+            weights.astype(jnp.bfloat16), v_ref[...], preferred_element_type=jnp.float32
+        )
+        max_ref[...] = new_max
+
+    @pl.when(kb == pl.num_programs(1) - 1)
+    def _():
+        o_ref[...] = (acc_ref[...] / sum_ref[...]).astype(o_ref.dtype)
+
+
+def flash_attention(needed, grouped_q, gathered, q_ids, q_req, k_ids, k_req, groups, tok_rows, root):
+    blocks = gathered.shape[0]
+    group_rows = grouped_q.shape[1]
+    grid_spec = pltpu.PrefetchScalarGridSpec(
+        num_scalar_prefetch=1,
+        grid=(groups, blocks),
+        in_specs=[
+            pl.BlockSpec((None, group_rows, HD), lambda g, kb, n: (g, 0, 0)),
+            pl.BlockSpec((None, tok_rows, HD), lambda g, kb, n: (kb, 0, g)),
+            pl.BlockSpec((None, tok_rows, HD), lambda g, kb, n: (kb, 0, groups + g)),
+            pl.BlockSpec((group_rows, 1), lambda g, kb, n: (0, 0)),
+            pl.BlockSpec((group_rows, 1), lambda g, kb, n: (0, 0)),
+            pl.BlockSpec((None, 1, tok_rows), lambda g, kb, n: (kb, 0, 0)),
+            pl.BlockSpec((None, 1, tok_rows), lambda g, kb, n: (kb, 0, 0)),
+        ],
+        out_specs=pl.BlockSpec((None, group_rows, HD), lambda g, kb, n: (g, 0, 0)),
+        scratch_shapes=[
+            pltpu.VMEM((group_rows, 1), jnp.float32),
+            pltpu.VMEM((group_rows, 1), jnp.float32),
+            pltpu.VMEM((group_rows, HD), jnp.float32),
+        ],
+    )
+    flops = 4 * groups * blocks * group_rows * tok_rows * HD
+    return pl.pallas_call(
+        functools.partial(flash_kernel, root=root),
+        grid_spec=grid_spec,
+        out_shape=jax.ShapeDtypeStruct((groups, group_rows, HD), jnp.bfloat16),
+        compiler_params=pltpu.CompilerParams(dimension_semantics=("arbitrary", "arbitrary")),
+        cost_estimate=pl.CostEstimate(
+            flops=flops,
+            transcendentals=groups * blocks * group_rows * tok_rows,
+            bytes_accessed=2 * groups * blocks * tok_rows * HD * 2 + 4 * groups * group_rows * HD,
+        ),
+    )(needed, grouped_q, gathered, gathered, q_ids, q_req, k_ids, k_req)
 
 
 def on_device(
@@ -163,63 +234,28 @@
     extras_all = jnp.sum(extras_all.astype(jnp.float32).reshape(blocks, reqs, -1), axis=0)
     query_last = extras_all[:, :q_cols].astype(jnp.bfloat16)
     seq_last = extras_all[:, q_cols:]
-    group_queries = [
-        query_proj[:, g * per_group * HD : (g + 1) * per_group * HD].reshape(tok_rows, per_group, HD)
-        for g in range(kv_heads)
-    ]
     block_index = lax.axis_index("blk")
     first_begin = query_begin[0]
-
-    def block_step(kb, state):
-        key_first = kb * tok_rows
-        needed = (kb <= block_index) & (key_first + tok_rows - 1 >= first_begin)
-
-        def compute(state):
-            piece = lax.dynamic_index_in_dim(gathered, kb, 0, keepdims=False)
-            key_ids = key_first + local_rows
-            key_req, unused = request_info(key_ids, req_lengths)
-            allowed = (key_ids[None, :] <= row_ids[:, None]) & (key_req[None, :] == query_req[:, None])
-            allowed = allowed[:, None, :]
-            new_state = []
-            for g in range(kv_heads):
-                run_max, run_sum, run_acc = state[g]
-                keys_g = piece[:tok_rows, g * HD : (g + 1) * HD]
-                values_g = piece[:tok_rows, kv_width + g * HD : kv_width + (g + 1) * HD]
-                scores = (
-                    jnp.einsum(
-                        "tqd,kd->tqk", group_queries[g], keys_g, preferred_element_type=jnp.float32
-                    )
-                    / root
-                )
-                scores = jnp.where(allowed, scores, -1e30)
-                new_max = jnp.maximum(run_max, jnp.max(scores, axis=-1))
-                weights = jnp.where(allowed, jnp.exp(scores - new_max[..., None]), 0.0)
-                scale = jnp.exp(run_max - new_max)
-                new_sum = run_sum * scale + jnp.sum(weights, axis=-1)
-                new_acc = run_acc * scale[..., None] + jnp.einsum(
-                    "tqk,kd->tqd",
-                    weights.astype(jnp.bfloat16),
-                    values_g,
-                    preferred_element_type=jnp.float32,
-                )
-                new_state.append((new_max, new_sum, new_acc))
-            return tuple(new_state)
-
-        return lax.cond(needed, compute, lambda s: s, state)
-
-    init = tuple(
-        (
-            jnp.full((tok_rows, per_group), -1e30, jnp.float32),
-            jnp.zeros((tok_rows, per_group), jnp.float32),
-            jnp.zeros((tok_rows, per_group, HD), jnp.float32),
-        )
-        for g in range(kv_heads)
-    )
-    final = lax.fori_loop(0, blocks, block_step, init)
-    context = jnp.concatenate(
-        [(acc / total[..., None]).reshape(tok_rows, per_group * HD) for unused, total, acc in final],
-        axis=1,
-    ).astype(jnp.bfloat16)
+    block_ids = jnp.arange(blocks, dtype=jnp.int32)
+    needed = (
+        (block_ids <= block_index) & (block_ids * tok_rows + tok_rows - 1 >= first_begin)
+    ).astype(jnp.int32)
+    group_rows = tok_rows * per_group
+    grouped_q = jnp.transpose(
+        query_proj.reshape(tok_rows, kv_heads, per_group, HD), (1, 0, 2, 3)
+    ).reshape(kv_heads, group_rows, HD)
+    q_ids = jnp.repeat(row_ids, per_group)[:, None]
+    q_req = jnp.repeat(query_req, per_group)[:, None]
+    all_ids = jnp.arange(blocks * tok_rows, dtype=jnp.int32)
+    all_req, unused = request_info(all_ids, req_lengths)
+    k_ids = all_ids.reshape(blocks, 1, tok_rows)
+    k_req = all_req.reshape(blocks, 1, tok_rows)
+    context = flash_attention(
+        needed, grouped_q, gathered, q_ids, q_req, k_ids, k_req, kv_heads, tok_rows, root
+    )
+    context = jnp.transpose(
+        context.reshape(kv_heads, tok_rows, per_group, HD), (1, 0, 2, 3)
+    ).reshape(tok_rows, kv_heads * per_group * HD)
     all_ids = jnp.arange(blocks * tok_rows, dtype=jnp.int32)
     last_begin = ends_at - req_lengths
     last_allowed = (all_ids[None, :] >= last_begin[:, None]) & (all_ids[None, :] <= last_ids[:, None])

time: 364 us -> 335 us (0.920)
  waiting for transfers between devices: 236 us -> 204 us
  Pallas kernels: 0 us -> 14.2 us
  loops' own time: 5.47 us -> 0 us
  matrix products: 39.4 us -> 34.1 us
    reduce_scatter x1, waiting for transfers between devices: 80.9 us -> 54.1 us  [on_device(): lax.psum_scatter(jnp.dot(out_rows, w_out, preferred_element_type=jnp.floa...]
    pallas_call x0 -> x1, Pallas kernels: none -> 14.2 us  [flash_attention(): pl.pallas_call(functools.partial(flash_kernel, root=root), grid_spec=grid...]
    dot_general x4 -> x0, matrix products: 6.64 us -> none  [the longest x2 5.43 us: compute(): jnp.einsum('tqk,kd->tqd', weights.astype(jnp.bfloat16), values_g, preferr...]
    another operation x9 -> x0, loops' own time: 5.47 us -> none  [the longest x1 5.29 us: on_device(): final = lax.fori_loop(0, blocks, block_step, init)]
    all_gather x1, waiting for transfers between devices: 74.7 us -> 69.2 us  [on_device(): gathered = lax.all_gather(shipped, 'blk', axis=0, tiled=False)]
  transfers between devices with their start and end apart: 5 -> 5, of which waited for: 5 -> 5; matrix products, arithmetic and copies ran while one was open for 3% -> 5% of each run, Pallas kernels for 0% -> 0%
where the time goes in v2:
time: 335 us
  waiting for transfers between devices  204 us (61%)
  matrix products  34.1 us (10%)
  blocking collectives  32.2 us (10%)
  other arithmetic  19.7 us (6%)
  local copies, waits for them, and re-layouts  15.3 us (5%)
  Pallas kernels  14.2 us (4%)
  between operations  14.2 us (4%)
    all_gather x1, waiting for transfers between devices, on_device(): gathered = lax.all_gather(shipped, 'blk', axis=0, tiled=False)  69.2 us
    reduce_scatter x1, waiting for transfers between devices, on_device(): lax.psum_scatter(jnp.dot(out_rows, w_out, preferred_element_type=jnp.floa...  54.1 us
    all_gather x1, waiting for transfers between devices, on_device(): text_rows = lax.all_gather(text_embed, 'kv', axis=1, tiled=True)  36.2 us
    psum x1, waiting for transfers between devices, on_device(): lax.psum(head_pooled.astype(jnp.bfloat16), 'kv').astype(jnp.float32)  28.1 us
    pmax x1, blocking collectives, on_device(): max_logit = lax.pmax(local_max, 'blk')  22 us
    all_gather x1, waiting for transfers between devices, on_device(): lax.all_gather(merged.reshape(pictures * merged_max, feat_dev), 'kv', axi...  15.9 us
    pallas_call x1, Pallas kernels, flash_attention(): pl.pallas_call(functools.partial(flash_kernel, root=root), grid_spec=grid...  14.2 us
    psum x1, blocking collectives, on_device(): lax.psum(square_part.astype(jnp.bfloat16), 'kv').astype(jnp.float32)  10.3 us
  transfers between devices with their start and end apart: 5, of which 5 were waited for; matrix products, arithmetic and copies ran while one was open for 5% of the time, Pallas kernels for 0%

profile of v2, /device:TPU:0, one launch (start us, length us, event | category | flops | bytes accessed | tf_op | source)
XLA Modules:
  0.0 334.7 jit_solution(10346251914535737079)
XLA Ops:
  7.3 2.1 convert_reduce_fusion
  9.4 0.3 copy-done.2
  9.7 0.7 multiply_reduce_fusion
  10.5 2.9 fusion.30
  13.4 0.8 fusion.21
  14.2 0.7 fusion.22
  14.9 1.0 fusion.58
  15.9 0.6 copy.69
  16.6 0.7 dot_general.56
  17.3 2.7 convolution_reduce_fusion
  20.1 0.9 multiply_convert_fusion.1
  21.0 2.9 reshape.315
  23.9 4.8 %reduce_sum.127 = f32[3,64,1408]{2,1,0:T(8,128)S(1)} reduce(f32[3,64,4,1408]{3,2,1,0:T(4,128)} %reshape.315, f32[]{:T(128)} %constant.52.clone.1), dimensions={2}, to_apply=%region_1.0 | reduce | flops 811008 | bytes 5406724 | tf_op jit(solution)/shard_map/reduce_sum | solution.py:166
  28.8 28.1 %all-reduce.3.cloned.1.call-done = bf16[3,64,1408]{2,1,0:T(8,128)(2,1)} async-done(((bf16[3,64,1408]{2,1,0:T(8,128)(2,1)}), bf16[3,64,1408]{2,1,0:T(8,128)(2,1)}) %all-reduce.3.cloned.1.call-update) | async-done | bytes 540688 | tf_op jit(solution)/shard_map/psum | solution.py:165
  56.9 3.5 %fusion.45 = bf16[3,64,1024]{2,1,0:T(8,128)(2,1)} fusion(bf16[1408,1024]{1,0:T(8,128)(2,1)} %param.21, bf16[3,64,1408]{2,1,0:T(8,128)(2,1)} %all-reduce.3.cloned.1.call-done, f32[3,64,1408]{2,1,0:T(8,128)S(1)} %reduce_sum.127), kind=kOutput, calls=%fused_computation.51 | convolution fusion | flops 554926080 | bytes 4898816 | tf_op jit(solution)/shard_map/pmd,de->pme/dot_general | solution.py:168
  60.5 0.7 all-gather.7.cloned.1.call-update
  62.1 0.5 multiply_cosine_fusion
  62.7 1.6 fusion.44
  64.2 0.3 convolution_convert_fusion.4
  64.5 15.9 %all-gather.5.cloned.1.call-done = bf16[192,4096]{1,0:T(8,128)(2,1)} async-done(((bf16[192,1024]{1,0:T(8,128)(2,1)}), bf16[192,4096]{1,0:T(8,128)(2,1)}) %all-gather.5.cloned.1.call-update) | async-done | bytes 1572880 | tf_op jit(solution)/shard_map/all_gather | solution.py:184
  80.4 36.2 %all-gather.7.cloned.1.call-done = bf16[512,4096]{1,0:T(8,128)(2,1)} async-done(((bf16[512,1024]{1,0:T(8,128)(2,1)}), bf16[512,4096]{1,0:T(8,128)(2,1)}) %all-gather.7.cloned.1.call-update) | async-done | bytes 4194320 | tf_op jit(solution)/shard_map/all_gather | solution.py:137
  116.6 4.5 %fusion.2 = (f32[512]{0:T(512)S(1)}, bf16[512,4096]{1,0:T(8,128)(2,1)S(1)}) fusion(bf16[512,4096]{1,0:T(8,128)(2,1)} %all-gather.7.cloned.1.call-done, bf16[192,4096]{1,0:T(8,128)(2,1)} %all-gather.5.cloned.1.call-done, s32[192]{0:T(256)S(1)} %select_n.42, pred[512]{0:T(512)(128)(4,1)S(1)} %fusion.68), kind=kOutput, calls=%fused_computation.4 | convolution fusion | flops 815889920 | bytes 9964800 | tf_op jit(solution)/shard_map/dot_general | solution.py:187
  121.1 2.6 fusion.14
  123.8 2.6 fusion.49
  127.3 1.0 copy.74
  128.3 0.3 reduce-scatter.2.cloned.1.call-start
  128.6 0.5 slice.76
  129.2 1.0 broadcast_in_dim_reshape.10.qreq_ref
  130.3 1.0 broadcast_in_dim_reshape.9.qid_ref
  131.3 1.2 and_convert_fusion.needed_ref
  132.5 0.6 multiply_add_fusion.kid_ref
  133.1 0.7 convert_reduce_fusion.2
  134.0 1.1 copy.71
  135.1 69.2 %all-gather.9.cloned.1.call-done = bf16[4288,512]{1,0:T(8,128)(2,1)} async-done(((bf16[536,512]{1,0:T(8,128)(2,1)}), bf16[4288,512]{1,0:T(8,128)(2,1)}) %all-gather.9.cloned.1.call-update) | async-done | bytes 4390928 | tf_op jit(solution)/shard_map/all_gather | solution.py:230
  204.3 4.0 %fusion.90 = (bf16[8,512,128]{2,1,0:T(8,128)(2,1)}, bf16[8,512,128]{2,1,0:T(8,128)(2,1)S(1)}, bf16[8,512,128]{2,1,0:T(8,128)(2,1)}, bf16[8,512,128]{2,1,0:T(8,128)(2,1)S(1)}) fusion(bf16[8,536,512]{2,1,0:T(8,128)(2,1)} %bitcast.120), kind=kLoop, calls=%fused_computation.143 | loop fusion | bytes 8388608 | tf_op jit(solution)/shard_map/slice | solution.py:265
  208.3 1.0 convert_reduce_fusion.1
  209.3 14.2 %shard_map.166 = bf16[2,1024,128]{2,1,0:T(8,128)(2,1)} custom-call(s32[8]{0:T(128)} %and_convert_fusion.needed_ref, bf16[2,1024,128]{2,1,0:T(8,128)(2,1)} %bitcast.137, bf16[8,536,512]{2,1,0:T(8,128)(2,1)} %bitcast.122, bf16[8,536,512]{2,1,0:T(8,128)(2,1)} %bitcast.123, s32[1024,1]{1,0:T(8,128)} %broadcast_in_dim_reshape.9.qid_ref, ...), custom_call_target="tpu_custom_call" | custom-call | flops 4294967296 | bytes 5242880 | tf_op jit(solution)/shard_map/pallas_call | solution.py:102
  223.5 1.3 copy.77
  224.9 1.8 fusion.92
  226.7 1.8 fusion.91
  229.2 6.6 %convolution_convert_fusion = bf16[520,4096]{1,0:T(8,128)(2,1)} fusion(bf16[512,4096]{1,0:T(8,128)(2,1)} %param.26, bf16[8,512]{0,1:T(8,128)(2,1)S(1)} %copy.78, bf16[512,512]{0,1:T(8,128)(2,1)S(1)} %bitcast.130), kind=kOutput, calls=%fused_computation.7 | convolution fusion | flops 2184232960 | bytes 8986624 | tf_op jit(solution)/shard_map/dot_general | solution.py:289
  235.9 54.1 %reduce-scatter.2.cloned.1.call-done = bf16[520,1024]{1,0:T(8,128)(2,1)} async-done(((bf16[520,4096]{1,0:T(8,128)(2,1)}), bf16[520,1024]{1,0:T(8,128)(2,1)}) %reduce-scatter.2.cloned.1.call-update) | async-done | bytes 1064976 | tf_op jit(solution)/shard_map/reduce_scatter | solution.py:288
  290.0 1.6 convert_element_type.155
  291.8 2.7 fusion.29
  294.5 0.6 convolution_convert_fusion.3
  295.1 10.3 %all-reduce = (bf16[8]{0:T(256)(128)(2,1)S(1)}, bf16[8,1024]{1,0:T(8,128)(2,1)S(1)}) all-reduce(bf16[8]{0:T(256)(128)(2,1)S(1)} %get-tuple-element.5, bf16[8,1024]{1,0:T(8,128)(2,1)S(1)} %convolution_convert_fusion.3), channel_id=1, replica_groups=mesh['kv'=4,'blk'=8] {'kv'}, use_global_device_ids=true, to_apply=%region_20.21 | all-reduce | flops 8200 | bytes 32800 | tf_op jit(solution)/shard_map/psum | solution.py:303
  305.4 0.8 multiply_reduce_fusion.1
  306.2 22.0 %pmax.7 = f32[8]{0:T(128)} all-reduce(f32[8]{0:T(128)S(1)} %get-tuple-element.19), channel_id=1, replica_groups=mesh['kv'=4,'blk'=8] {'blk'}, use_global_device_ids=true, to_apply=%region_23.24 | all-reduce | flops 8 | bytes 64 | tf_op jit(solution)/shard_map/pmax | solution.py:308
  (75 shorter events, 3.3 us)
Async XLA Ops:
  7.2 3.3 copy-start
  7.2 3.2 copy-start.8
  7.2 3.3 copy-start.14
  7.2 49.7 %all-reduce.3.cloned.1.call-start = ((), (), s32[]{:S(2)}) async-start(), calls=%async_computation.1 | async-start | bytes 1081344 | tf_op jit(solution)/shard_map/psum | solution.py:165
  7.2 2.4 copy-start.2
  17.3 3.7 %copy-start.3 = (bf16[3,256,1408]{2,1,0:T(8,128)(2,1)S(1)}, bf16[3,256,1408]{2,1,0:T(8,128)(2,1)}, u32[]{:S(2)}) copy-start(bf16[3,256,1408]{2,1,0:T(8,128)(2,1)} %param.15) | copy-start | bytes 6488068
  20.9 59.5 %all-gather.5.cloned.1.call-start = ((), (), s32[]{:S(2)}) async-start(), calls=%async_computation.2 | async-start | bytes 1966080 | tf_op jit(solution)/shard_map/all_gather | solution.py:184
  28.7 32.7 %copy-start.9 = (s32[3]{0:T(128)S(1)}, s32[3]{0:T(128)}, u32[]{:S(2)}) copy-start(s32[3]{0:T(128)} %param.17) | copy-start | bytes 40
  28.7 32.8 %copy-start.10 = (s32[8]{0:T(128)S(1)}, s32[8]{0:T(128)}, u32[]{:S(2)}) copy-start(s32[8]{0:T(128)} %param.27) | copy-start | bytes 100
  28.8 33.9 %copy-start.6 = (bf16[512,1024]{1,0:T(8,128)(2,1)S(1)}, bf16[512,1024]{1,0:T(8,128)(2,1)}, u32[]{:S(2)}) copy-start(bf16[512,1024]{1,0:T(8,128)(2,1)} %param.22) | copy-start | bytes 3145732
  60.5 56.1 %all-gather.7.cloned.1.call-start = ((), (), s32[]{:S(2)}) async-start(), calls=%async_computation.3 | async-start | bytes 5242880 | tf_op jit(solution)/shard_map/all_gather | solution.py:137
  61.2 143.1 %all-gather.9.cloned.1.call-start = ((), (), s32[]{:S(2)}) async-start(), calls=%async_computation.5 | async-start | bytes 4939776 | tf_op jit(solution)/shard_map/all_gather | solution.py:230
  64.2 56.8 %copy-start.4 = (bf16[512,1024]{1,0:T(8,128)(2,1)}, bf16[512,1024]{1,0:T(8,128)(2,1)S(1)}, u32[]{:S(2)}) copy-start(bf16[512,1024]{1,0:T(8,128)(2,1)S(1)} %fusion.44) | copy-start | bytes 3145732
  64.5 56.5 %copy-start.13 = (f32[4096]{0:T(1024)S(1)}, f32[4096]{0:T(1024)}, u32[]{:S(2)}) copy-start(f32[4096]{0:T(1024)} %param.23) | copy-start | bytes 49156
  116.6 4.5 %copy-start.11 = (bf16[4096,2,256]{2,1,0:T(2,128)(2,1)S(1)}, bf16[4096,2,256]{2,1,0:T(2,128)(2,1)}, u32[]{:S(2)}) copy-start(bf16[4096,2,256]{2,1,0:T(2,128)(2,1)} %param.25) | copy-start | bytes 12582916
  121.1 2.7 copy-start.12
  128.3 161.7 %reduce-scatter.2.cloned.1.call-start = ((), (), s32[]{:S(2)}) async-start(), calls=%async_computation.4 | async-start | bytes 5324800 | tf_op jit(solution)/shard_map/reduce_scatter | solution.py:288
  235.9 58.6 %copy-start.7 = (f32[1024]{0:T(1024)S(1)}, f32[1024]{0:T(1024)}, u32[]{:S(2)}) copy-start(f32[1024]{0:T(1024)} %param.28) | copy-start | bytes 12292
  290.0 4.5 %copy-start.5 = (bf16[1024,1024]{1,0:T(8,128)(2,1)S(1)}, bf16[1024,1024]{1,0:T(8,128)(2,1)}, u32[]{:S(2)}) copy-start(bf16[1024,1024]{1,0:T(8,128)(2,1)} %param.29) | copy-start | bytes 6291460
  291.6 36.5 %copy-start.1 = (bf16[1408,3,352]{0,2,1:T(8,128)(2,1)S(1)}, bf16[1408,3,352]{0,2,1:T(8,128)(2,1)}, u32[]{:S(2)}) copy-start(bf16[1408,3,352]{0,2,1:T(8,128)(2,1)} %param.19) | copy-start | bytes 8921092
Sparse Core Ops, SparseCore 0:
  21.1 35.7 all-reduce.2
  60.6 19.7 all-gather.4
  82.1 34.4 all-gather.6
  128.5 75.8 all-gather.8
  236.0 53.9 reduce-scatter.1

commit v3 on v2

--- a/solution.py
+++ b/solution.py
@@ -110,6 +110,19 @@
             bytes_accessed=2 * groups * blocks * tok_rows * HD * 2 + 4 * groups * group_rows * HD,
         ),
     )(needed, grouped_q, gathered, gathered, q_ids, q_req, k_ids, k_req)
+
+
+def gather_by_permutes(local, count):
+    me = lax.axis_index("kv")
+    pieces = [local]
+    for shift in range(1, count):
+        pieces.append(
+            lax.ppermute(local, "kv", perm=[(i, (i + shift) % count) for i in range(count)])
+        )
+    stacked = jnp.stack(pieces)
+    order = (me - jnp.arange(count, dtype=jnp.int32)) % count
+    ordered = jnp.take(stacked, order, axis=0)
+    return jnp.concatenate([ordered[j] for j in range(count)], axis=1)
 
 
 def on_device(
@@ -134,7 +147,8 @@
     vis_cols = vis_qkv.shape[2]
     vis_heads = vis_cols // VHD
     tok_rows, feat_dev = text_embed.shape
-    text_rows = lax.all_gather(text_embed, "kv", axis=1, tiled=True)
+    kv_count = D // text_embed.shape[1]
+    text_rows = gather_by_permutes(text_embed, kv_count)
     inputs = patches.astype(jnp.float32)
     normed = layer_norm(inputs, vis_gain).astype(jnp.bfloat16)
     packed = jnp.einsum(

time: 335 us -> 305 us (0.910)
  waiting for transfers between devices: 204 us -> 157 us
  local copies, waits for them, and re-layouts: 15.3 us -> 22 us
  other arithmetic: 19.7 us -> 25.9 us
  starting transfers between devices: 0.6 us -> 5.02 us
    all_gather x1 -> x0, waiting for transfers between devices: 36.2 us -> none  [on_device(): text_rows = lax.all_gather(text_embed, 'kv', axis=1, tiled=True)]
    all_gather x1, waiting for transfers between devices: 15.9 us -> 4.15 us  [on_device(): lax.all_gather(merged.reshape(pictures * merged_max, feat_dev), 'kv', axi...]
    gather x0 -> x1, local copies, waits for them, and re-layouts: none -> 5.28 us  [gather_by_permutes(): ordered = jnp.take(stacked, order, axis=0)]
    ppermute x0 -> x3, starting transfers between devices: none -> 4.46 us  [gather_by_permutes(): lax.ppermute(local, 'kv', perm=[(i, (i + shift) % count) for i in range(c...]
    another operation x4 -> x5, other arithmetic: 0.45 us -> 4.13 us  [the longest x1 3.68 us: gather_by_permutes(): stacked = jnp.stack(pieces)]
  transfers between devices with their start and end apart: 5 -> 7, of which waited for: 5 -> 4; matrix products, arithmetic and copies ran while one was open for 5% -> 16% of each run, Pallas kernels for 0% -> 0%
where the time goes in v3:
time: 305 us; the launch traced here: 304 us
  waiting for transfers between devices  157 us (51%)
  matrix products  33.8 us (11%)
  blocking collectives  32.2 us (11%)
  other arithmetic  25.9 us (8%)
  local copies, waits for them, and re-layouts  22 us (7%)
  Pallas kernels  14.3 us (5%)
  between operations  14.2 us (5%)
  starting transfers between devices  5.02 us (2%)
    all_gather x1, waiting for transfers between devices, on_device(): gathered = lax.all_gather(shipped, 'blk', axis=0, tiled=False)  69.2 us
    reduce_scatter x1, waiting for transfers between devices, on_device(): lax.psum_scatter(jnp.dot(out_rows, w_out, preferred_element_type=jnp.floa...  54.1 us
    psum x1, waiting for transfers between devices, on_device(): lax.psum(head_pooled.astype(jnp.bfloat16), 'kv').astype(jnp.float32)  28.9 us
    pmax x1, blocking collectives, on_device(): max_logit = lax.pmax(local_max, 'blk')  22 us
    pallas_call x1, Pallas kernels, flash_attention(): pl.pallas_call(functools.partial(flash_kernel, root=root), grid_spec=grid...  14.3 us
    psum x1, blocking collectives, on_device(): lax.psum(square_part.astype(jnp.bfloat16), 'kv').astype(jnp.float32)  10.3 us
    dot_general x1, matrix products, on_device(): jnp.dot(out_rows, w_out, preferred_element_type=jnp.float32)  6.58 us
  transfers between devices with their start and end apart: 7, of which 4 were waited for; matrix products, arithmetic and copies ran while one was open for 16% of the time, Pallas kernels for 0%

profile of v3, /device:TPU:0, one launch (start us, length us, event | category | flops | bytes accessed | tf_op | source)
XLA Modules:
  0.0 303.9 jit_solution(8225508284757985822)
XLA Ops:
  7.8 2.6 collective-permute-start.1
  10.3 1.4 collective-permute-start.2
  11.7 2.0 convert_reduce_fusion
  13.7 0.7 multiply_reduce_fusion
  14.5 2.9 fusion.30
  17.4 0.8 fusion.21
  18.2 0.7 fusion.22
  19.0 1.0 fusion.58
  20.0 0.6 copy.69
  20.6 0.7 dot_general.56
  21.4 2.7 convolution_reduce_fusion
  24.1 0.9 multiply_convert_fusion.1
  25.5 2.9 reshape.369
  28.5 4.8 %reduce_sum.127 = f32[3,64,1408]{2,1,0:T(8,128)S(1)} reduce(f32[3,64,4,1408]{3,2,1,0:T(4,128)} %reshape.369, f32[]{:T(128)} %constant.81.clone.1), dimensions={2}, to_apply=%region_1.2 | reduce | flops 811008 | bytes 5406724 | tf_op jit(solution)/shard_map/reduce_sum | solution.py:180
  33.5 28.9 %all-reduce.3.cloned.1.call-done = bf16[3,64,1408]{2,1,0:T(8,128)(2,1)} async-done(((bf16[3,64,1408]{2,1,0:T(8,128)(2,1)}), bf16[3,64,1408]{2,1,0:T(8,128)(2,1)}) %all-reduce.3.cloned.1.call-update) | async-done | bytes 540688 | tf_op jit(solution)/shard_map/psum | solution.py:179
  62.4 3.5 %fusion.45 = bf16[3,64,1024]{2,1,0:T(8,128)(2,1)} fusion(bf16[1408,1024]{1,0:T(8,128)(2,1)} %param.21, bf16[3,64,1408]{2,1,0:T(8,128)(2,1)} %all-reduce.3.cloned.1.call-done, f32[3,64,1408]{2,1,0:T(8,128)S(1)} %reduce_sum.127), kind=kOutput, calls=%fused_computation.54 | convolution fusion | flops 554926080 | bytes 4898816 | tf_op jit(solution)/shard_map/pmd,de->pme/dot_general | solution.py:182
  66.3 0.5 multiply_cosine_fusion
  66.8 1.6 fusion.44
  68.7 3.7 %pad_maximum_fusion = bf16[4,512,1024]{2,1,0:T(8,128)(2,1)} fusion(bf16[1,512,1024]{2,1,0:T(8,128)(2,1)} %bitcast.21, bf16[1,512,1024]{2,1,0:T(8,128)(2,1)} %bitcast.20, bf16[1,512,1024]{2,1,0:T(8,128)(2,1)} %bitcast.19, bf16[1,512,1024]{2,1,0:T(8,128)(2,1)S(1)} %bitcast.151), kind=kLoop, calls=%fused_computation.23 | loop fusion | flops 6291456 | bytes 8388608 | tf_op jit(solution)/shard_map/stack | solution.py:122
  72.4 5.3 %gather_fusion = bf16[4,512,1024]{2,1,0:T(8,128)(2,1)} fusion(bf16[4,512,1024]{2,1,0:T(8,128)(2,1)} %pad_maximum_fusion, s32[1024]{0:T(1024)S(1)} %pad_clamp_fusion), kind=kCustom, calls=%fused_computation | custom fusion | bytes 8388624 | tf_op jit(solution)/shard_map/jit(_take)/gather | solution.py:124
  77.7 2.7 broadcast_select_fusion
  80.3 1.8 slice_bitcast_fusion.3
  82.1 4.1 %all-gather.4.cloned.1.call-done = bf16[192,4096]{1,0:T(8,128)(2,1)} async-done(((bf16[192,1024]{1,0:T(8,128)(2,1)}), bf16[192,4096]{1,0:T(8,128)(2,1)}) %all-gather.4.cloned.1.call-update) | async-done | bytes 1572880 | tf_op jit(solution)/shard_map/all_gather | solution.py:198
  86.3 4.2 %fusion.2 = (f32[512]{0:T(512)S(1)}, bf16[512,4096]{1,0:T(8,128)(2,1)S(1)}) fusion(bf16[512,1024]{1,0:T(8,128)(2,1)S(1)} %get-tuple-element.12, bf16[512,1024]{1,0:T(8,128)(2,1)} %get-tuple-element.13, bf16[512,1024]{1,0:T(8,128)(2,1)} %get-tuple-element.14, bf16[512,1024]{1,0:T(8,128)(2,1)S(1)} %get-tuple-element.11, ...), kind=kOutput, calls=%fused_computation.5 | convolution fusion | flops 832667136 | bytes 9964800 | tf_op jit(solution)/shard_map/dot_general | solution.py:201
  90.5 2.6 fusion.14
  93.2 2.6 fusion.49
  96.7 1.0 copy.74
  98.6 1.0 broadcast_in_dim_reshape.10.qreq_ref
  99.8 0.9 broadcast_in_dim_reshape.9.qid_ref
  100.7 1.2 and_convert_fusion.needed_ref
  101.9 0.6 multiply_add_fusion.kid_ref
  102.5 0.7 convert_reduce_fusion.2
  103.4 1.1 copy.71
  104.5 69.2 %all-gather.6.cloned.1.call-done = bf16[4288,512]{1,0:T(8,128)(2,1)} async-done(((bf16[536,512]{1,0:T(8,128)(2,1)}), bf16[4288,512]{1,0:T(8,128)(2,1)}) %all-gather.6.cloned.1.call-update) | async-done | bytes 4390928 | tf_op jit(solution)/shard_map/all_gather | solution.py:244
  173.7 3.9 %fusion.93 = (bf16[8,512,128]{2,1,0:T(8,128)(2,1)}, bf16[8,512,128]{2,1,0:T(8,128)(2,1)S(1)}, bf16[8,512,128]{2,1,0:T(8,128)(2,1)}, bf16[8,512,128]{2,1,0:T(8,128)(2,1)S(1)}) fusion(bf16[8,536,512]{2,1,0:T(8,128)(2,1)} %bitcast.134), kind=kLoop, calls=%fused_computation.163 | loop fusion | bytes 8388608 | tf_op jit(solution)/shard_map/slice | solution.py:279
  177.7 1.0 convert_reduce_fusion.1
  178.6 14.3 %shard_map.166 = bf16[2,1024,128]{2,1,0:T(8,128)(2,1)} custom-call(s32[8]{0:T(128)} %and_convert_fusion.needed_ref, bf16[2,1024,128]{2,1,0:T(8,128)(2,1)} %bitcast.152, bf16[8,536,512]{2,1,0:T(8,128)(2,1)} %bitcast.136, bf16[8,536,512]{2,1,0:T(8,128)(2,1)} %bitcast.137, s32[1024,1]{1,0:T(8,128)} %broadcast_in_dim_reshape.9.qid_ref, ...), custom_call_target="tpu_custom_call" | custom-call | flops 4294967296 | bytes 5242880 | tf_op jit(solution)/shard_map/pallas_call | solution.py:102
  192.9 1.3 copy.77
  194.2 1.8 fusion.95
  196.1 1.8 fusion.94
  198.6 6.6 %convolution_convert_fusion = bf16[520,4096]{1,0:T(8,128)(2,1)} fusion(bf16[512,4096]{1,0:T(8,128)(2,1)} %param.26, bf16[8,512]{0,1:T(8,128)(2,1)S(1)} %copy.78, bf16[512,512]{0,1:T(8,128)(2,1)S(1)} %bitcast.144), kind=kOutput, calls=%fused_computation.8 | convolution fusion | flops 2184232960 | bytes 8986624 | tf_op jit(solution)/shard_map/dot_general | solution.py:303
  205.2 54.1 %reduce-scatter.2.cloned.1.call-done = bf16[520,1024]{1,0:T(8,128)(2,1)} async-done(((bf16[520,4096]{1,0:T(8,128)(2,1)}), bf16[520,1024]{1,0:T(8,128)(2,1)}) %reduce-scatter.2.cloned.1.call-update) | async-done | bytes 1064976 | tf_op jit(solution)/shard_map/reduce_scatter | solution.py:302
  259.3 1.6 convert_element_type.155
  261.1 2.6 fusion.29
  263.7 0.6 convolution_convert_fusion.3
  264.3 10.3 %all-reduce = (bf16[8]{0:T(256)(128)(2,1)S(1)}, bf16[8,1024]{1,0:T(8,128)(2,1)S(1)}) all-reduce(bf16[8]{0:T(256)(128)(2,1)S(1)} %get-tuple-element.5, bf16[8,1024]{1,0:T(8,128)(2,1)S(1)} %convolution_convert_fusion.3), channel_id=1, replica_groups=mesh['kv'=4,'blk'=8] {'kv'}, use_global_device_ids=true, to_apply=%region_20.21 | all-reduce | flops 8200 | bytes 32800 | tf_op jit(solution)/shard_map/psum | solution.py:317
  274.6 0.8 multiply_reduce_fusion.1
  275.4 22.0 %pmax.7 = f32[8]{0:T(128)} all-reduce(f32[8]{0:T(128)S(1)} %get-tuple-element.23), channel_id=1, replica_groups=mesh['kv'=4,'blk'=8] {'blk'}, use_global_device_ids=true, to_apply=%region_23.24 | all-reduce | flops 8 | bytes 64 | tf_op jit(solution)/shard_map/pmax | solution.py:322
  (85 shorter events, 4.9 us)
Async XLA Ops:
  7.2 7.4 %copy-start = (bf16[1408,3,352]{0,2,1:T(8,128)(2,1)S(1)}, bf16[1408,3,352]{0,2,1:T(8,128)(2,1)}, u32[]{:S(2)}) copy-start(bf16[1408,3,352]{0,2,1:T(8,128)(2,1)} %param.19) | copy-start | bytes 8921092
  7.2 7.2 %copy-start.8 = (s32[3,2]{0,1:T(2,128)S(1)}, s32[3,2]{0,1:T(2,128)}, u32[]{:S(2)}) copy-start(s32[3,2]{0,1:T(2,128)} %param.16) | copy-start | bytes 76
  7.2 7.3 %copy-start.14 = (f32[1408]{0:T(1024)S(1)}, f32[1408]{0:T(1024)}, u32[]{:S(2)}) copy-start(f32[1408]{0:T(1024)} %param.18) | copy-start | bytes 16900
  7.2 55.2 %all-reduce.3.cloned.1.call-start = ((), (), s32[]{:S(2)}) async-start(), calls=%async_computation.1 | async-start | bytes 1081344 | tf_op jit(solution)/shard_map/psum | solution.py:179
  7.2 6.4 %copy-start.2 = (bf16[3,256,1408]{2,1,0:T(8,128)(2,1)S(1)}, bf16[3,256,1408]{2,1,0:T(8,128)(2,1)}, u32[]{:S(2)}) copy-start(bf16[3,256,1408]{2,1,0:T(8,128)(2,1)} %param.15) | copy-start | bytes 6488068
  7.3 61.4 %collective-permute-start = (bf16[512,1024]{1,0:T(8,128)(2,1)}, bf16[512,1024]{1,0:T(8,128)(2,1)}, u32[]{:S(2)}, u32[]{:S(2)}) collective-permute-start(bf16[512,1024]{1,0:T(8,128)(2,1)} %param.22), channel_id=1, source_target_pairs={{0,8},{8,16},{16,24},{24,0},{1,9},{9,17},{17,25},{25,1},{2,10},{10... | collective-permute-start | bytes 3145736 | tf_op jit(solution)/shard_map/ppermute | solution.py:120
  7.8 60.9 %collective-permute-start.1 = (bf16[512,1024]{1,0:T(8,128)(2,1)}, bf16[512,1024]{1,0:T(8,128)(2,1)}, u32[]{:S(2)}, u32[]{:S(2)}) collective-permute-start(bf16[512,1024]{1,0:T(8,128)(2,1)} %param.22), channel_id=1, source_target_pairs={{0,16},{8,24},{16,0},{24,8},{1,17},{9,25},{17,1},{25,9},{2,18},{10... | collective-permute-start | bytes 3145736 | tf_op jit(solution)/shard_map/ppermute | solution.py:120
  10.3 58.3 %collective-permute-start.2 = (bf16[512,1024]{1,0:T(8,128)(2,1)}, bf16[512,1024]{1,0:T(8,128)(2,1)}, u32[]{:S(2)}, u32[]{:S(2)}) collective-permute-start(bf16[512,1024]{1,0:T(8,128)(2,1)} %param.22), channel_id=1, source_target_pairs={{0,24},{8,0},{16,8},{24,16},{1,25},{9,1},{17,9},{25,17},{2,26},{10... | collective-permute-start | bytes 3145736 | tf_op jit(solution)/shard_map/ppermute | solution.py:120
  21.3 3.8 %copy-start.10 = (s32[8]{0:T(128)S(1)}, s32[8]{0:T(128)}, u32[]{:S(2)}) copy-start(s32[8]{0:T(128)} %param.27) | copy-start | bytes 100
  21.4 4.0 %copy-start.9 = (s32[3]{0:T(128)S(1)}, s32[3]{0:T(128)}, u32[]{:S(2)}) copy-start(s32[3]{0:T(128)} %param.17) | copy-start | bytes 40
  21.4 4.1 %copy-start.3 = (bf16[3,256,1408]{2,1,0:T(8,128)(2,1)S(1)}, bf16[3,256,1408]{2,1,0:T(8,128)(2,1)}, u32[]{:S(2)}) copy-start(bf16[3,256,1408]{2,1,0:T(8,128)(2,1)} %param.15) | copy-start | bytes 6488068
  25.0 61.2 %all-gather.4.cloned.1.call-start = ((), (), s32[]{:S(2)}) async-start(), calls=%async_computation.2 | async-start | bytes 1966080 | tf_op jit(solution)/shard_map/all_gather | solution.py:198
  33.3 33.5 %copy-start.6 = (bf16[512,1024]{1,0:T(8,128)(2,1)S(1)}, bf16[512,1024]{1,0:T(8,128)(2,1)}, u32[]{:S(2)}) copy-start(bf16[512,1024]{1,0:T(8,128)(2,1)} %param.22) | copy-start | bytes 3145732
  66.0 107.7 %all-gather.6.cloned.1.call-start = ((), (), s32[]{:S(2)}) async-start(), calls=%async_computation.4 | async-start | bytes 4939776 | tf_op jit(solution)/shard_map/all_gather | solution.py:244
  68.4 4.0 %copy-start.4 = (bf16[512,1024]{1,0:T(8,128)(2,1)}, bf16[512,1024]{1,0:T(8,128)(2,1)S(1)}, u32[]{:S(2)}) copy-start(bf16[512,1024]{1,0:T(8,128)(2,1)S(1)} %fusion.44) | copy-start | bytes 3145732
  86.2 4.2 %copy-start.11 = (bf16[4096,2,256]{2,1,0:T(2,128)(2,1)S(1)}, bf16[4096,2,256]{2,1,0:T(2,128)(2,1)}, u32[]{:S(2)}) copy-start(bf16[4096,2,256]{2,1,0:T(2,128)(2,1)} %param.25) | copy-start | bytes 12582916
  86.3 4.2 %copy-start.13 = (f32[4096]{0:T(1024)S(1)}, f32[4096]{0:T(1024)}, u32[]{:S(2)}) copy-start(f32[4096]{0:T(1024)} %param.23) | copy-start | bytes 49156
  90.5 2.7 copy-start.12
  97.7 161.6 %reduce-scatter.2.cloned.1.call-start = ((), (), s32[]{:S(2)}) async-start(), calls=%async_computation.3 | async-start | bytes 5324800 | tf_op jit(solution)/shard_map/reduce_scatter | solution.py:302
  205.2 58.5 %copy-start.7 = (f32[1024]{0:T(1024)S(1)}, f32[1024]{0:T(1024)}, u32[]{:S(2)}) copy-start(f32[1024]{0:T(1024)} %param.28) | copy-start | bytes 12292
  259.3 4.4 %copy-start.5 = (bf16[1024,1024]{1,0:T(8,128)(2,1)S(1)}, bf16[1024,1024]{1,0:T(8,128)(2,1)}, u32[]{:S(2)}) copy-start(bf16[1024,1024]{1,0:T(8,128)(2,1)} %param.29) | copy-start | bytes 6291460
  259.3 38.0 %copy-start.1 = (bf16[1408,3,352]{0,2,1:T(8,128)(2,1)S(1)}, bf16[1408,3,352]{0,2,1:T(8,128)(2,1)}, u32[]{:S(2)}) copy-start(bf16[1408,3,352]{0,2,1:T(8,128)(2,1)} %param.19) | copy-start | bytes 8921092
Sparse Core Ops, SparseCore 0:
  25.1 37.2 all-reduce.2
  66.1 20.0 all-gather.3
  97.9 75.8 all-gather.5
  205.3 53.9 reduce-scatter.1

commit v4 on v3

--- a/solution.py
+++ b/solution.py
@@ -112,17 +112,31 @@
     )(needed, grouped_q, gathered, gathered, q_ids, q_req, k_ids, k_req)
 
 
-def gather_by_permutes(local, count):
-    me = lax.axis_index("kv")
+def permute_pieces(local, count):
     pieces = [local]
     for shift in range(1, count):
         pieces.append(
             lax.ppermute(local, "kv", perm=[(i, (i + shift) % count) for i in range(count)])
         )
-    stacked = jnp.stack(pieces)
+    return pieces
+
+
+def ordered_sum(pieces, count):
+    me = lax.axis_index("kv")
+    stacked = jnp.stack([piece.astype(jnp.float32) for piece in pieces])
     order = (me - jnp.arange(count, dtype=jnp.int32)) % count
-    ordered = jnp.take(stacked, order, axis=0)
-    return jnp.concatenate([ordered[j] for j in range(count)], axis=1)
+    return jnp.sum(jnp.take(stacked, order, axis=0), axis=0)
+
+
+def tree_max(values, axis, count):
+    if count & (count - 1):
+        return lax.pmax(values, axis)
+    step = 1
+    while step < count:
+        other = lax.ppermute(values, axis, perm=[(i, i ^ step) for i in range(count)])
+        values = jnp.maximum(values, other)
+        step *= 2
+    return values
 
 
 def on_device(
@@ -148,7 +162,7 @@
     vis_heads = vis_cols // VHD
     tok_rows, feat_dev = text_embed.shape
     kv_count = D // text_embed.shape[1]
-    text_rows = gather_by_permutes(text_embed, kv_count)
+    text_pieces = permute_pieces(text_embed, kv_count)
     inputs = patches.astype(jnp.float32)
     normed = layer_norm(inputs, vis_gain).astype(jnp.bfloat16)
     packed = jnp.einsum(
@@ -176,7 +190,7 @@
     )
     head_part = jnp.einsum("pnc,cd->pnd", mixed_rows, vis_out, preferred_element_type=jnp.float32)
     head_pooled = jnp.mean(head_part.reshape(pictures, merged_max, 4, vis_width), axis=2)
-    head_total = lax.psum(head_pooled.astype(jnp.bfloat16), "kv").astype(jnp.float32)
+    head_total = ordered_sum(permute_pieces(head_pooled.astype(jnp.bfloat16), kv_count), kv_count)
     input_pooled = jnp.mean(inputs.reshape(pictures, merged_max, 4, vis_width), axis=2)
     pooled = (input_pooled + head_total).astype(jnp.bfloat16)
     merged = jnp.einsum(
@@ -195,31 +209,52 @@
     )
     is_vision = jnp.any(one_hot, axis=1)
     seq_in = jnp.where(is_vision[:, None], placed.astype(jnp.bfloat16), text_embed)
-    merged_rows = lax.all_gather(
-        merged.reshape(pictures * merged_max, feat_dev), "kv", axis=1, tiled=True
-    )
-    placed_rows = jnp.dot(one_hot.astype(jnp.bfloat16), merged_rows, preferred_element_type=jnp.float32)
-    full_rows = jnp.where(is_vision[:, None], placed_rows.astype(jnp.bfloat16), text_rows)
-    full_float = full_rows.astype(jnp.float32)
-    dec_normed = (
-        full_float
-        * lax.rsqrt(jnp.mean(full_float * full_float, axis=-1, keepdims=True) + 1e-05)
-        * dec_gain
-    ).astype(jnp.bfloat16)
     per_group = QHEADS // KVHEADS
     kv_heads = w_keyval.shape[2] // HD
     row_ids = block_base + local_rows
     request_id, request_begin = request_info(row_ids, req_lengths)
     position = row_ids - request_begin
-    query_proj = jnp.dot(dec_normed, w_query, preferred_element_type=jnp.float32).reshape(
-        tok_rows, kv_heads * per_group, HD
-    )
+    merged_pieces = permute_pieces(merged.reshape(pictures * merged_max, feat_dev), kv_count)
+    one_hot_rows = one_hot.astype(jnp.bfloat16)
+    full_pieces = [
+        jnp.where(
+            is_vision[:, None],
+            jnp.dot(one_hot_rows, merged_piece, preferred_element_type=jnp.float32).astype(
+                jnp.bfloat16
+            ),
+            text_piece,
+        ).astype(jnp.float32)
+        for merged_piece, text_piece in zip(merged_pieces, text_pieces)
+    ]
+    square_sum_rows = sum(jnp.sum(piece * piece, axis=1) for piece in full_pieces)
+    row_scale = lax.rsqrt(square_sum_rows / (kv_count * feat_dev) + 1e-05)[:, None]
+    me_kv = lax.axis_index("kv")
+    query_proj = None
+    key_value = None
+    for shift, piece in enumerate(full_pieces):
+        chunk = ((me_kv - shift) % kv_count) * feat_dev
+        normed_piece = (
+            piece * row_scale * lax.dynamic_slice_in_dim(dec_gain, chunk, feat_dev)
+        ).astype(jnp.bfloat16)
+        q_term = jnp.dot(
+            normed_piece,
+            lax.dynamic_slice_in_dim(w_query, chunk, feat_dev, 0),
+            preferred_element_type=jnp.float32,
+        )
+        kv_term = jnp.einsum(
+            "td,dce->tce",
+            normed_piece,
+            lax.dynamic_slice_in_dim(w_keyval, chunk, feat_dev, 0),
+            preferred_element_type=jnp.float32,
+        )
+        query_proj = q_term if query_proj is None else query_proj + q_term
+        key_value = kv_term if key_value is None else key_value + kv_term
+    query_proj = query_proj.reshape(tok_rows, kv_heads * per_group, HD)
     query_proj = (
         rotate(query_proj, position)
         .astype(jnp.bfloat16)
         .reshape(tok_rows, kv_heads * per_group * HD)
     )
-    key_value = jnp.einsum("td,dce->tce", dec_normed, w_keyval, preferred_element_type=jnp.float32)
     key_rows = (
         rotate(key_value[:, 0].reshape(tok_rows, kv_heads, HD), position)
         .astype(jnp.bfloat16)
@@ -312,14 +347,16 @@
     logit_part = lax.dot_general(
         scaled, table, (((1,), (1,)), ((), ())), preferred_element_type=jnp.float32
     )
-    logit_sum, square_sum = (
-        lax.psum(logit_part.astype(jnp.bfloat16), "kv").astype(jnp.float32),
-        lax.psum(square_part.astype(jnp.bfloat16), "kv").astype(jnp.float32),
-    )
+    packed_sums = ordered_sum(
+        permute_pieces(jnp.concatenate([logit_part, square_part[:, None]], axis=1), kv_count),
+        kv_count,
+    )
+    logit_sum = packed_sums[:, :-1]
+    square_sum = packed_sums[:, -1]
     inv_rms = lax.rsqrt(square_sum / D + 1e-05)
     last_norm = (chosen * inv_rms[:, None] * final_gain).astype(jnp.bfloat16)
     local_max = jnp.max(inv_rms[:, None] * logit_sum, axis=-1)
-    max_logit = lax.pmax(local_max, "blk")
+    max_logit = tree_max(local_max, "blk", blocks)
     return (hidden, last_norm, max_logit)
 
 

time: 305 us -> 320 us (1.049)
  blocking collectives: 32.2 us -> 0 us
  waiting for transfers between devices: 157 us -> 179 us
  starting transfers between devices: 5.02 us -> 15.9 us
  local copies, waits for them, and re-layouts: 22 us -> 31 us
    ppermute x3 -> x15, waiting for transfers between devices: 0.01 us -> 53.9 us  [the longest x12 47.7 us: permute_pieces(): lax.ppermute(local, 'kv', perm=[(i, (i + shift) % count) for i in range(c...]
    psum x1 -> x0, waiting for transfers between devices: 28.9 us -> none  [on_device(): lax.psum(head_pooled.astype(jnp.bfloat16), 'kv').astype(jnp.float32)]
    pmax x1 -> x0, blocking collectives: 22 us -> none  [on_device(): max_logit = lax.pmax(local_max, 'blk')]
    ppermute x3 -> x15, starting transfers between devices: 4.46 us -> 15.6 us  [the longest x12 10.2 us: permute_pieces(): lax.ppermute(local, 'kv', perm=[(i, (i + shift) % count) for i in range(c...]
    psum x1 -> x0, blocking collectives: 10.3 us -> none  [on_device(): lax.psum(square_part.astype(jnp.bfloat16), 'kv').astype(jnp.float32)]
    dynamic_slice x0 -> x2, local copies, waits for them, and re-layouts: none -> 5.77 us  [the longest x1 5.75 us: on_device(): lax.dynamic_slice_in_dim(w_keyval, chunk, feat_dev, 0)]
    unnamed x30 -> x44, local copies, waits for them, and re-layouts: 0.08 us -> 4.32 us
    all_gather x1 -> x0, waiting for transfers between devices: 4.15 us -> none  [on_device(): lax.all_gather(merged.reshape(pictures * merged_max, feat_dev), 'kv', axi...]
  transfers between devices with their start and end apart: 7 -> 17, of which waited for: 4 -> 10; matrix products, arithmetic and copies ran while one was open for 16% -> 13% of each run, Pallas kernels for 0% -> 0%
where the time goes in v4:
time: 320 us; the launch traced here: 319 us
  waiting for transfers between devices  179 us (56%)
  matrix products  35.3 us (11%)
  local copies, waits for them, and re-layouts  31 us (10%)
  other arithmetic  28.3 us (9%)
  starting transfers between devices  15.9 us (5%)
  between operations  14.8 us (5%)
  Pallas kernels  14.2 us (4%)
    all_gather x1, waiting for transfers between devices, on_device(): gathered = lax.all_gather(shipped, 'blk', axis=0, tiled=False)  71.3 us
    reduce_scatter x1, waiting for transfers between devices, on_device(): lax.psum_scatter(jnp.dot(out_rows, w_out, preferred_element_type=jnp.floa...  54.2 us
    ppermute x12, waiting for transfers between devices, permute_pieces(): lax.ppermute(local, 'kv', perm=[(i, (i + shift) % count) for i in range(c...  47.7 us
    pallas_call x1, Pallas kernels, flash_attention(): pl.pallas_call(functools.partial(flash_kernel, root=root), grid_spec=grid...  14.2 us
    ppermute x12, starting transfers between devices, permute_pieces(): lax.ppermute(local, 'kv', perm=[(i, (i + shift) % count) for i in range(c...  10.2 us
    dot_general x1, matrix products, on_device(): jnp.dot(out_rows, w_out, preferred_element_type=jnp.float32)  6.57 us
  transfers between devices with their start and end apart: 17, of which 10 were waited for; matrix products, arithmetic and copies ran while one was open for 13% of the time, Pallas kernels for 0%

profile of v4, /device:TPU:0, one launch (start us, length us, event | category | flops | bytes accessed | tf_op | source)
XLA Modules:
  0.0 318.9 jit_solution(13372600767265419828)
XLA Ops:
  8.2 2.5 convert_reduce_fusion
  11.4 2.9 fusion.35
  15.9 1.0 fusion.63
  18.3 1.3 convolution_reduce_fusion
  19.6 1.0 multiply_convert_fusion.1
  20.6 2.4 collective-permute-start.2
  23.8 1.5 collective-permute-start.8
  25.3 1.5 collective-permute-start.6
  27.6 5.8 %constant_dynamic-slice_fusion = (bf16[1024,2,256]{2,1,0:T(2,128)(2,1)}, bf16[1024,2,256]{2,1,0:T(2,128)(2,1)}, bf16[1024,2,256]{2,1,0:T(2,128)(2,1)}, bf16[1024,2,256]{2,1,0:T(2,128)(2,1)}) fusion(bf16[4096,2,256]{2,1,0:T(2,128)(2,1)} %param.25, s32[]{:T(128)S(6)} %select_n.151, s32[]{:T(128)S(6)} %select_n.149, s32[]{:T(128)S(6)} %select_n.147, ...), kind=kLoop, calls=%fused_computation.184 | loop fusion | bytes 8388624 | tf_op jit(solution)/shard_map/dynamic_slice | solution.py:247
  33.9 2.9 reshape.395
  36.8 4.9 %reduce_sum.172 = f32[3,64,1408]{2,1,0:T(8,128)S(1)} reduce(f32[3,64,4,1408]{3,2,1,0:T(4,128)} %reshape.395, f32[]{:T(128)} %constant.122.clone.1), dimensions={2}, to_apply=%region_1.0 | reduce | flops 811008 | bytes 5406724 | tf_op jit(solution)/shard_map/reduce_sum | solution.py:194
  41.9 6.7 %collective-permute-done.1 = bf16[3,64,1408]{2,1,0:T(8,128)(2,1)} collective-permute-done((bf16[3,64,1408]{2,1,0:T(8,128)(2,1)}, bf16[3,64,1408]{2,1,0:T(8,128)(2,1)}, u32[]{:S(2)}, u32[]{:S(2)}) %collective-permute-start.1) | collective-permute-done | bytes 540704 | tf_op jit(solution)/shard_map/ppermute | solution.py:119
  48.6 3.7 %maximum_convert_fusion = f32[4,3,64,1408]{3,2,1,0:T(8,128)} fusion(bf16[1,3,64,1408]{3,2,1,0:T(8,128)(2,1)} %bitcast.16, bf16[1,3,64,1408]{3,2,1,0:T(8,128)(2,1)} %bitcast.15, bf16[1,3,64,1408]{3,2,1,0:T(8,128)(2,1)} %bitcast.14, bf16[1,3,64,1408]{3,2,1,0:T(8,128)(2,1)S(1)} %fusion.150), kind=kLoop, calls=%fused_computation.38 | loop fusion | flops 4325376 | bytes 6488064 | tf_op jit(solution)/shard_map/stack | solution.py:126
  52.3 5.1 %gather_fusion = f32[4,3,64,1408]{3,2,1,0:T(8,128)} fusion(f32[4,3,64,1408]{3,2,1,0:T(8,128)} %maximum_convert_fusion, s32[1024]{0:T(1024)S(1)} %pad_clamp_fusion), kind=kCustom, calls=%fused_computation | custom fusion | bytes 8650768 | tf_op jit(solution)/shard_map/jit(_take)/gather | solution.py:128
  57.3 2.9 select_reduce_fusion
  61.4 1.6 collective-permute-start.5
  63.0 2.0 fusion.31
  65.2 35.5 %collective-permute-done.7 = bf16[192,1024]{1,0:T(8,128)(2,1)S(1)} collective-permute-done((bf16[192,1024]{1,0:T(8,128)(2,1)S(1)}, bf16[192,1024]{1,0:T(8,128)(2,1)S(1)}, u32[]{:S(2)}, u32[]{:S(2)}) %collective-permute-start.7) | collective-permute-done | bytes 393248 | tf_op jit(solution)/shard_map/ppermute | solution.py:119
  101.5 2.0 fusion.28
  103.4 4.7 %collective-permute-done.5 = bf16[192,1024]{1,0:T(8,128)(2,1)S(1)} collective-permute-done((bf16[192,1024]{1,0:T(8,128)(2,1)S(1)}, bf16[192,1024]{1,0:T(8,128)(2,1)S(1)}, u32[]{:S(2)}, u32[]{:S(2)}) %collective-permute-start.5) | collective-permute-done | bytes 393248 | tf_op jit(solution)/shard_map/ppermute | solution.py:119
  108.1 2.0 fusion.25
  110.1 2.0 fusion.22
  116.8 0.9 copy-done.11
  123.2 1.0 copy.95
  125.2 1.0 broadcast_in_dim_reshape.9.qid_ref
  126.2 1.0 broadcast_in_dim_reshape.10.qreq_ref
  127.2 1.2 and_convert_fusion.needed_ref
  129.9 1.1 copy.89
  131.0 71.3 %all-gather.3.cloned.1.call-done = bf16[4288,512]{1,0:T(8,128)(2,1)} async-done(((bf16[536,512]{1,0:T(8,128)(2,1)}), bf16[4288,512]{1,0:T(8,128)(2,1)}) %all-gather.3.cloned.1.call-update) | async-done | bytes 4390928 | tf_op jit(solution)/shard_map/all_gather | solution.py:279
  202.3 3.9 %fusion.132 = (bf16[8,512,128]{2,1,0:T(8,128)(2,1)}, bf16[8,512,128]{2,1,0:T(8,128)(2,1)S(1)}, bf16[8,512,128]{2,1,0:T(8,128)(2,1)}, bf16[8,512,128]{2,1,0:T(8,128)(2,1)S(1)}) fusion(bf16[8,536,512]{2,1,0:T(8,128)(2,1)} %bitcast.143), kind=kLoop, calls=%fused_computation.213 | loop fusion | bytes 8388608 | tf_op jit(solution)/shard_map/slice | solution.py:314
  206.3 1.0 convert_reduce_fusion.1
  207.3 1.8 fusion.134
  209.1 1.8 fusion.135
  211.6 14.2 %shard_map.166 = bf16[2,1024,128]{2,1,0:T(8,128)(2,1)} custom-call(s32[8]{0:T(128)} %and_convert_fusion.needed_ref, bf16[2,1024,128]{2,1,0:T(8,128)(2,1)} %bitcast.158, bf16[8,536,512]{2,1,0:T(8,128)(2,1)} %bitcast.145, bf16[8,536,512]{2,1,0:T(8,128)(2,1)} %bitcast.146, s32[1024,1]{1,0:T(8,128)} %broadcast_in_dim_reshape.9.qid_ref, ...), custom_call_target="tpu_custom_call" | custom-call | flops 4294967296 | bytes 5242880 | tf_op jit(solution)/shard_map/pallas_call | solution.py:102
  225.9 1.3 copy.98
  227.2 6.6 %convolution_convert_fusion = bf16[520,4096]{1,0:T(8,128)(2,1)} fusion(bf16[512,4096]{1,0:T(8,128)(2,1)} %param.26, bf16[8,512]{0,1:T(8,128)(2,1)S(1)} %copy.99, bf16[512,512]{0,1:T(8,128)(2,1)S(1)} %bitcast.154), kind=kOutput, calls=%fused_computation.4 | convolution fusion | flops 2184232960 | bytes 8986624 | tf_op jit(solution)/shard_map/dot_general | solution.py:338
  233.8 54.2 %reduce-scatter.2.cloned.1.call-done = bf16[520,1024]{1,0:T(8,128)(2,1)} async-done(((bf16[520,4096]{1,0:T(8,128)(2,1)}), bf16[520,1024]{1,0:T(8,128)(2,1)}) %reduce-scatter.2.cloned.1.call-update) | async-done | bytes 1064976 | tf_op jit(solution)/shard_map/reduce_scatter | solution.py:337
  287.9 1.5 convert_element_type.192
  289.4 1.3 copy-done.4
  291.0 2.4 fusion.110
  293.5 1.5 collective-permute-start.10
  294.9 2.5 fusion.34
  299.9 1.5 collective-permute-start.12
  301.4 2.1 collective-permute-done.12
  303.5 1.5 collective-permute-start.13
  305.0 2.1 collective-permute-done.13
  307.1 2.4 collective-permute-start.14
  309.5 2.0 collective-permute-done.14
  (134 shorter events, 25.4 us)
Async XLA Ops:
  7.2 4.2 %copy-start = (bf16[1408,3,352]{0,2,1:T(8,128)(2,1)S(1)}, bf16[1408,3,352]{0,2,1:T(8,128)(2,1)}, u32[]{:S(2)}) copy-start(bf16[1408,3,352]{0,2,1:T(8,128)(2,1)} %param.19) | copy-start | bytes 8921092
  7.2 195.2 %all-gather.3.cloned.1.call-start = ((), (), s32[]{:S(2)}) async-start(), calls=%async_computation.2 | async-start | bytes 4939776 | tf_op jit(solution)/shard_map/all_gather | solution.py:279
  7.2 3.4 %copy-start.2 = (bf16[3,256,1408]{2,1,0:T(8,128)(2,1)S(1)}, bf16[3,256,1408]{2,1,0:T(8,128)(2,1)}, u32[]{:S(2)}) copy-start(bf16[3,256,1408]{2,1,0:T(8,128)(2,1)} %param.15) | copy-start | bytes 6488068
  8.2 3.2 %copy-start.21 = (f32[1408]{0:T(1024)S(1)}, f32[1408]{0:T(1024)}, u32[]{:S(2)}) copy-start(f32[1408]{0:T(1024)} %param.18) | copy-start | bytes 16900
  16.8 1.4 copy-start.20
  18.2 8.6 %copy-start.18 = (s32[3]{0:T(128)S(1)}, s32[3]{0:T(128)}, u32[]{:S(2)}) copy-start(s32[3]{0:T(128)} %param.17) | copy-start | bytes 40
  18.3 8.9 %copy-start.19 = (s32[8]{0:T(128)S(1)}, s32[8]{0:T(128)}, u32[]{:S(2)}) copy-start(s32[8]{0:T(128)} %param.27) | copy-start | bytes 100
  18.3 9.3 %copy-start.17 = (f32[4096]{0:T(1024)S(1)}, f32[4096]{0:T(1024)}, u32[]{:S(2)}) copy-start(f32[4096]{0:T(1024)} %param.23) | copy-start | bytes 49156
  19.6 8.0 %copy-start.6 = (f32[3,64,1408]{2,1,0:T(8,128)}, f32[3,64,1408]{2,1,0:T(8,128)S(1)}, u32[]{:S(2)}) copy-start(f32[3,64,1408]{2,1,0:T(8,128)S(1)} %convolution_reduce_fusion) | copy-start | bytes 3244036
  20.6 21.2 %collective-permute-start.2 = (bf16[3,64,1408]{2,1,0:T(8,128)(2,1)}, bf16[3,64,1408]{2,1,0:T(8,128)(2,1)}, u32[]{:S(2)}, u32[]{:S(2)}) collective-permute-start(bf16[3,64,1408]{2,1,0:T(8,128)(2,1)} %multiply_convert_fusion.1), channel_id=1, source_target_pairs={{0,24},{8,0},{16,8},{24,16},{1,25},{9,1},{17,9},{25,17},{2,26},{10... | collective-permute-start | bytes 1622024 | tf_op jit(solution)/shard_map/ppermute | solution.py:119
  23.0 25.6 %collective-permute-start.1 = (bf16[3,64,1408]{2,1,0:T(8,128)(2,1)}, bf16[3,64,1408]{2,1,0:T(8,128)(2,1)}, u32[]{:S(2)}, u32[]{:S(2)}) collective-permute-start(bf16[3,64,1408]{2,1,0:T(8,128)(2,1)} %multiply_convert_fusion.1), channel_id=1, source_target_pairs={{0,16},{8,24},{16,0},{24,8},{1,17},{9,25},{17,1},{25,9},{2,18},{10... | collective-permute-start | bytes 1622024 | tf_op jit(solution)/shard_map/ppermute | solution.py:119
  23.5 25.0 %collective-permute-start = (bf16[3,64,1408]{2,1,0:T(8,128)(2,1)}, bf16[3,64,1408]{2,1,0:T(8,128)(2,1)}, u32[]{:S(2)}, u32[]{:S(2)}) collective-permute-start(bf16[3,64,1408]{2,1,0:T(8,128)(2,1)} %multiply_convert_fusion.1), channel_id=1, source_target_pairs={{0,8},{8,16},{16,24},{24,0},{1,9},{9,17},{17,25},{25,1},{2,10},{10... | collective-permute-start | bytes 1622024 | tf_op jit(solution)/shard_map/ppermute | solution.py:119
  23.8 77.7 %collective-permute-start.8 = (bf16[512,1024]{1,0:T(8,128)(2,1)}, bf16[512,1024]{1,0:T(8,128)(2,1)}, u32[]{:S(2)}, u32[]{:S(2)}) collective-permute-start(bf16[512,1024]{1,0:T(8,128)(2,1)} %param.22), channel_id=1, source_target_pairs={{0,24},{8,0},{16,8},{24,16},{1,25},{9,1},{17,9},{25,17},{2,26},{10... | collective-permute-start | bytes 3145736 | tf_op jit(solution)/shard_map/ppermute | solution.py:119
  25.3 82.8 %collective-permute-start.6 = (bf16[512,1024]{1,0:T(8,128)(2,1)}, bf16[512,1024]{1,0:T(8,128)(2,1)}, u32[]{:S(2)}, u32[]{:S(2)}) collective-permute-start(bf16[512,1024]{1,0:T(8,128)(2,1)} %param.22), channel_id=1, source_target_pairs={{0,16},{8,24},{16,0},{24,8},{1,17},{9,25},{17,1},{25,9},{2,18},{10... | collective-permute-start | bytes 3145736 | tf_op jit(solution)/shard_map/ppermute | solution.py:119
  27.6 6.3 %copy-start.3 = (bf16[3,256,1408]{2,1,0:T(8,128)(2,1)S(1)}, bf16[3,256,1408]{2,1,0:T(8,128)(2,1)}, u32[]{:S(2)}) copy-start(bf16[3,256,1408]{2,1,0:T(8,128)(2,1)} %param.15) | copy-start | bytes 6488068
  36.8 4.9 %copy-start.7 = (f32[3,64,1408]{2,1,0:T(8,128)S(1)}, f32[3,64,1408]{2,1,0:T(8,128)}, u32[]{:S(2)}) copy-start(f32[3,64,1408]{2,1,0:T(8,128)} %copy-done.6) | copy-start | bytes 3244036
  41.8 68.3 %collective-permute-start.4 = (bf16[512,1024]{1,0:T(8,128)(2,1)}, bf16[512,1024]{1,0:T(8,128)(2,1)}, u32[]{:S(2)}, u32[]{:S(2)}) collective-permute-start(bf16[512,1024]{1,0:T(8,128)(2,1)} %param.22), channel_id=1, source_target_pairs={{0,8},{8,16},{16,24},{24,0},{1,9},{9,17},{17,25},{25,1},{2,10},{10... | collective-permute-start | bytes 3145736 | tf_op jit(solution)/shard_map/ppermute | solution.py:119
  57.3 3.1 copy-start.9
  61.3 39.4 %collective-permute-start.7 = (bf16[192,1024]{1,0:T(8,128)(2,1)S(1)}, bf16[192,1024]{1,0:T(8,128)(2,1)S(1)}, u32[]{:S(2)}, u32[]{:S(2)}) collective-permute-start(bf16[192,1024]{1,0:T(8,128)(2,1)S(1)} %bitcast.160), channel_id=1, source_target_pairs={{0,24},{8,0},{16,8},{24,16},{1,25},{9,1},{17,9},{25,17},{2,26},{10... | collective-permute-start | bytes 1179656 | tf_op jit(solution)/shard_map/ppermute | solution.py:119
  61.4 46.8 %collective-permute-start.5 = (bf16[192,1024]{1,0:T(8,128)(2,1)S(1)}, bf16[192,1024]{1,0:T(8,128)(2,1)S(1)}, u32[]{:S(2)}, u32[]{:S(2)}) collective-permute-start(bf16[192,1024]{1,0:T(8,128)(2,1)S(1)} %bitcast.161), channel_id=1, source_target_pairs={{0,16},{8,24},{16,0},{24,8},{1,17},{9,25},{17,1},{25,9},{2,18},{10... | collective-permute-start | bytes 1179656 | tf_op jit(solution)/shard_map/ppermute | solution.py:119
  64.9 51.8 %copy-start.8 = (bf16[512,1024]{1,0:T(8,128)(2,1)}, bf16[512,1024]{1,0:T(8,128)(2,1)S(1)}, u32[]{:S(2)}) copy-start(bf16[512,1024]{1,0:T(8,128)(2,1)S(1)} %get-tuple-element.39) | copy-start | bytes 3145732
  100.7 9.4 %collective-permute-start.3 = (bf16[192,1024]{1,0:T(8,128)(2,1)S(1)}, bf16[192,1024]{1,0:T(8,128)(2,1)S(1)}, u32[]{:S(2)}, u32[]{:S(2)}) collective-permute-start(bf16[192,1024]{1,0:T(8,128)(2,1)S(1)} %bitcast.163), channel_id=1, source_target_pairs={{0,8},{8,16},{16,24},{24,0},{1,9},{9,17},{17,25},{25,1},{2,10},{10... | collective-permute-start | bytes 1179656 | tf_op jit(solution)/shard_map/ppermute | solution.py:119
  110.1 2.1 copy-start.15
  112.2 1.2 copy-start.14
  113.4 1.2 copy-start.13
  114.6 1.2 copy-start.12
  115.8 2.6 copy-start.10
  116.7 1.0 copy-start.11
  121.9 1.0 slice-start
  124.2 163.7 %reduce-scatter.2.cloned.1.call-start = ((), (), s32[]{:S(2)}) async-start(), calls=%async_computation.1 | async-start | bytes 5324800 | tf_op jit(solution)/shard_map/reduce_scatter | solution.py:337
  233.8 57.2 %copy-start.16 = (f32[1024]{0:T(1024)S(1)}, f32[1024]{0:T(1024)}, u32[]{:S(2)}) copy-start(f32[1024]{0:T(1024)} %param.28) | copy-start | bytes 12292
  289.4 1.4 copy-start.4
  291.0 4.0 %copy-start.5 = (f32[520,1024]{1,0:T(8,128)S(1)}, f32[520,1024]{1,0:T(8,128)}, u32[]{:S(2)}) copy-start(f32[520,1024]{1,0:T(8,128)} %copy-done.4) | copy-start | bytes 6389764
  293.4 18.6 %copy-start.1 = (bf16[1408,3,352]{0,2,1:T(8,128)(2,1)S(1)}, bf16[1408,3,352]{0,2,1:T(8,128)(2,1)}, u32[]{:S(2)}) copy-start(bf16[1408,3,352]{0,2,1:T(8,128)(2,1)} %param.19) | copy-start | bytes 8921092
  293.4 4.1 %collective-permute-start.11 = (f32[8,1025]{1,0:T(8,128)S(1)}, f32[8,1025]{1,0:T(8,128)S(1)}, u32[]{:S(2)}, u32[]{:S(2)}) collective-permute-start(f32[8,1025]{1,0:T(8,128)S(1)} %get-tuple-element.18), channel_id=1, source_target_pairs={{0,24},{8,0},{16,8},{24,16},{1,25},{9,1},{17,9},{25,17},{2,26},{10... | collective-permute-start | bytes 98408 | tf_op jit(solution)/shard_map/ppermute | solution.py:119
  293.5 4.2 %collective-permute-start.10 = (f32[8,1025]{1,0:T(8,128)S(1)}, f32[8,1025]{1,0:T(8,128)S(1)}, u32[]{:S(2)}, u32[]{:S(2)}) collective-permute-start(f32[8,1025]{1,0:T(8,128)S(1)} %get-tuple-element.18), channel_id=1, source_target_pairs={{0,16},{8,24},{16,0},{24,8},{1,17},{9,25},{17,1},{25,9},{2,18},{10... | collective-permute-start | bytes 98408 | tf_op jit(solution)/shard_map/ppermute | solution.py:119
  294.9 3.4 %collective-permute-start.9 = (f32[8,1025]{1,0:T(8,128)S(1)}, f32[8,1025]{1,0:T(8,128)S(1)}, u32[]{:S(2)}, u32[]{:S(2)}) collective-permute-start(f32[8,1025]{1,0:T(8,128)S(1)} %get-tuple-element.18), channel_id=1, source_target_pairs={{0,8},{8,16},{16,24},{24,0},{1,9},{9,17},{17,25},{25,1},{2,10},{10... | collective-permute-start | bytes 98408 | tf_op jit(solution)/shard_map/ppermute | solution.py:119
  299.9 3.6 %collective-permute-start.12 = (f32[8]{0:T(128)S(1)}, f32[8]{0:T(128)S(1)}, u32[]{:S(2)}, u32[]{:S(2)}) collective-permute-start(f32[8]{0:T(128)S(1)} %get-tuple-element.27), channel_id=1, source_target_pairs={{0,1},{1,0},{2,3},{3,2},{4,5},{5,4},{6,7},{7,6},{8,9},{9,8},{10,11... | collective-permute-start | bytes 104 | tf_op jit(solution)/shard_map/ppermute | solution.py:136
  303.5 3.5 %collective-permute-start.13 = (f32[8]{0:T(128)S(1)}, f32[8]{0:T(128)S(1)}, u32[]{:S(2)}, u32[]{:S(2)}) collective-permute-start(f32[8]{0:T(128)S(1)} %max.9), channel_id=1, source_target_pairs={{0,2},{1,3},{2,0},{3,1},{4,6},{5,7},{6,4},{7,5},{8,10},{9,11},{10,... | collective-permute-start | bytes 104 | tf_op jit(solution)/shard_map/ppermute | solution.py:136
  307.1 4.4 %collective-permute-start.14 = (f32[8]{0:T(128)S(1)}, f32[8]{0:T(128)S(1)}, u32[]{:S(2)}, u32[]{:S(2)}) collective-permute-start(f32[8]{0:T(128)S(1)} %max.10), channel_id=1, source_target_pairs={{0,4},{1,5},{2,6},{3,7},{4,0},{5,1},{6,2},{7,3},{8,12},{9,13},{10,... | collective-permute-start | bytes 104 | tf_op jit(solution)/shard_map/ppermute | solution.py:136
Sparse Core Ops, SparseCore 0:
  124.3 77.9 all-gather.2
  233.9 53.9 reduce-scatter.1

commit v5 on v3

--- a/solution.py
+++ b/solution.py
@@ -123,6 +123,33 @@
     order = (me - jnp.arange(count, dtype=jnp.int32)) % count
     ordered = jnp.take(stacked, order, axis=0)
     return jnp.concatenate([ordered[j] for j in range(count)], axis=1)
+
+
+def permute_pieces(local, count):
+    pieces = [local]
+    for shift in range(1, count):
+        pieces.append(
+            lax.ppermute(local, "kv", perm=[(i, (i + shift) % count) for i in range(count)])
+        )
+    return pieces
+
+
+def ordered_sum(pieces, count):
+    me = lax.axis_index("kv")
+    stacked = jnp.stack([piece.astype(jnp.float32) for piece in pieces])
+    order = (me - jnp.arange(count, dtype=jnp.int32)) % count
+    return jnp.sum(jnp.take(stacked, order, axis=0), axis=0)
+
+
+def tree_max(values, axis, count):
+    if count & (count - 1):
+        return lax.pmax(values, axis)
+    step = 1
+    while step < count:
+        other = lax.ppermute(values, axis, perm=[(i, i ^ step) for i in range(count)])
+        values = jnp.maximum(values, other)
+        step *= 2
+    return values
 
 
 def on_device(
@@ -312,14 +339,16 @@
     logit_part = lax.dot_general(
         scaled, table, (((1,), (1,)), ((), ())), preferred_element_type=jnp.float32
     )
-    logit_sum, square_sum = (
-        lax.psum(logit_part.astype(jnp.bfloat16), "kv").astype(jnp.float32),
-        lax.psum(square_part.astype(jnp.bfloat16), "kv").astype(jnp.float32),
-    )
+    packed_sums = ordered_sum(
+        permute_pieces(jnp.concatenate([logit_part, square_part[:, None]], axis=1), kv_count),
+        kv_count,
+    )
+    logit_sum = packed_sums[:, :-1]
+    square_sum = packed_sums[:, -1]
     inv_rms = lax.rsqrt(square_sum / D + 1e-05)
     last_norm = (chosen * inv_rms[:, None] * final_gain).astype(jnp.bfloat16)
     local_max = jnp.max(inv_rms[:, None] * logit_sum, axis=-1)
-    max_logit = lax.pmax(local_max, "blk")
+    max_logit = tree_max(local_max, "blk", blocks)
     return (hidden, last_norm, max_logit)
 
 

time: 305 us -> 290 us (0.951)
  blocking collectives: 32.2 us -> 0 us
  starting transfers between devices: 5.02 us -> 13 us
  waiting for transfers between devices: 157 us -> 162 us
    pmax x1 -> x0, blocking collectives: 22 us -> none  [on_device(): max_logit = lax.pmax(local_max, 'blk')]
    psum x1 -> x0, blocking collectives: 10.3 us -> none  [on_device(): lax.psum(square_part.astype(jnp.bfloat16), 'kv').astype(jnp.float32)]
    ppermute x0 -> x6, starting transfers between devices: none -> 7.97 us  [the longest x3 6.13 us: tree_max(): lax.ppermute(values, axis, perm=[(i, i ^ step) for i in range(count)])]
    ppermute x0 -> x6, waiting for transfers between devices: none -> 5.45 us  [the longest x3 5.44 us: tree_max(): lax.ppermute(values, axis, perm=[(i, i ^ step) for i in range(count)])]
  transfers between devices with their start and end apart: 7 -> 13, of which waited for: 4 -> 7; matrix products, arithmetic and copies ran while one was open for 16% -> 17% of each run, Pallas kernels for 0% -> 0%
where the time goes in v5:
time: 290 us; the launch traced here: 289 us
  waiting for transfers between devices  162 us (56%)
  matrix products  35.6 us (12%)
  other arithmetic  26.4 us (9%)
  local copies, waits for them, and re-layouts  24 us (8%)
  between operations  14.3 us (5%)
  Pallas kernels  14.2 us (5%)
  starting transfers between devices  13 us (4%)
    all_gather x1, waiting for transfers between devices, on_device(): gathered = lax.all_gather(shipped, 'blk', axis=0, tiled=False)  69.2 us
    reduce_scatter x1, waiting for transfers between devices, on_device(): lax.psum_scatter(jnp.dot(out_rows, w_out, preferred_element_type=jnp.floa...  54.1 us
    psum x1, waiting for transfers between devices, on_device(): lax.psum(head_pooled.astype(jnp.bfloat16), 'kv').astype(jnp.float32)  29 us
    pallas_call x1, Pallas kernels, flash_attention(): pl.pallas_call(functools.partial(flash_kernel, root=root), grid_spec=grid...  14.2 us
    dot_general x1, matrix products, on_device(): jnp.dot(out_rows, w_out, preferred_element_type=jnp.float32)  6.58 us
    ppermute x3, starting transfers between devices, tree_max(): lax.ppermute(values, axis, perm=[(i, i ^ step) for i in range(count)])  6.13 us
  transfers between devices with their start and end apart: 13, of which 7 were waited for; matrix products, arithmetic and copies ran while one was open for 17% of the time, Pallas kernels for 0%

profile of v5, /device:TPU:0, one launch (start us, length us, event | category | flops | bytes accessed | tf_op | source)
XLA Modules:
  0.0 289.5 jit_solution(18429602945144745638)
XLA Ops:
  7.8 2.6 collective-permute-start.1
  10.3 1.4 collective-permute-start.2
  11.7 2.0 convert_reduce_fusion
  14.5 2.9 fusion.30
  17.4 0.8 fusion.21
  18.2 0.7 fusion.22
  19.0 1.0 fusion.58
  21.4 2.7 convolution_reduce_fusion
  24.1 0.9 multiply_convert_fusion.1
  25.5 2.9 %reshape.368 = f32[3,64,4,1408]{3,2,1,0:T(4,128)} reshape(bf16[3,256,1408]{2,1,0:T(8,128)(2,1)S(1)} %copy-done.3) | data formatting | bytes 6488064 | tf_op jit(solution)/shard_map/reshape | solution.py:207
  28.5 4.8 %reduce_sum.136 = f32[3,64,1408]{2,1,0:T(8,128)S(1)} reduce(f32[3,64,4,1408]{3,2,1,0:T(4,128)} %reshape.368, f32[]{:T(128)} %constant.96.clone.1), dimensions={2}, to_apply=%region_1.2 | reduce | flops 811008 | bytes 5406724 | tf_op jit(solution)/shard_map/reduce_sum | solution.py:207
  33.5 29.0 %all-reduce.2.cloned.1.call-done = bf16[3,64,1408]{2,1,0:T(8,128)(2,1)} async-done(((bf16[3,64,1408]{2,1,0:T(8,128)(2,1)}), bf16[3,64,1408]{2,1,0:T(8,128)(2,1)}) %all-reduce.2.cloned.1.call-update) | async-done | bytes 540688 | tf_op jit(solution)/shard_map/psum | solution.py:206
  62.5 3.5 %fusion.45 = bf16[3,64,1024]{2,1,0:T(8,128)(2,1)} fusion(bf16[1408,1024]{1,0:T(8,128)(2,1)} %param.21, bf16[3,64,1408]{2,1,0:T(8,128)(2,1)} %all-reduce.2.cloned.1.call-done, f32[3,64,1408]{2,1,0:T(8,128)S(1)} %reduce_sum.136), kind=kOutput, calls=%fused_computation.55 | convolution fusion | flops 554926080 | bytes 4898816 | tf_op jit(solution)/shard_map/pmd,de->pme/dot_general | solution.py:209
  66.9 1.6 fusion.44
  68.7 3.7 %pad_maximum_fusion = bf16[4,512,1024]{2,1,0:T(8,128)(2,1)} fusion(bf16[1,512,1024]{2,1,0:T(8,128)(2,1)} %bitcast.21, bf16[1,512,1024]{2,1,0:T(8,128)(2,1)} %bitcast.20, bf16[1,512,1024]{2,1,0:T(8,128)(2,1)} %bitcast.19, bf16[1,512,1024]{2,1,0:T(8,128)(2,1)S(1)} %bitcast.157), kind=kLoop, calls=%fused_computation.24 | loop fusion | flops 6291456 | bytes 8388608 | tf_op jit(solution)/shard_map/stack | solution.py:122
  72.4 5.3 %gather_fusion = bf16[4,512,1024]{2,1,0:T(8,128)(2,1)} fusion(bf16[4,512,1024]{2,1,0:T(8,128)(2,1)} %pad_maximum_fusion, s32[1024]{0:T(1024)S(1)} %pad_clamp_fusion), kind=kCustom, calls=%fused_computation | custom fusion | bytes 8388624 | tf_op jit(solution)/shard_map/jit(_take)/gather | solution.py:124
  77.7 2.7 broadcast_select_fusion
  80.4 1.8 slice_bitcast_fusion.3
  82.1 4.2 %all-gather.4.cloned.1.call-done = bf16[192,4096]{1,0:T(8,128)(2,1)} async-done(((bf16[192,1024]{1,0:T(8,128)(2,1)}), bf16[192,4096]{1,0:T(8,128)(2,1)}) %all-gather.4.cloned.1.call-update) | async-done | bytes 1572880 | tf_op jit(solution)/shard_map/all_gather | solution.py:225
  86.3 4.2 %fusion.2 = (f32[512]{0:T(512)S(1)}, bf16[512,4096]{1,0:T(8,128)(2,1)S(1)}) fusion(bf16[512,1024]{1,0:T(8,128)(2,1)S(1)} %get-tuple-element.10, bf16[512,1024]{1,0:T(8,128)(2,1)} %get-tuple-element.11, bf16[512,1024]{1,0:T(8,128)(2,1)} %get-tuple-element.12, bf16[512,1024]{1,0:T(8,128)(2,1)S(1)} %get-tuple-element.9, ...), kind=kOutput, calls=%fused_computation.6 | convolution fusion | flops 832667136 | bytes 9964800 | tf_op jit(solution)/shard_map/dot_general | solution.py:228
  90.6 2.6 fusion.14
  93.3 2.6 fusion.49
  96.7 1.0 copy.78
  98.7 1.0 broadcast_in_dim_reshape.10.qreq_ref
  99.8 0.9 broadcast_in_dim_reshape.9.qid_ref
  100.8 1.2 and_convert_fusion.needed_ref
  103.5 1.1 copy.75
  104.6 69.2 %all-gather.6.cloned.1.call-done = bf16[4288,512]{1,0:T(8,128)(2,1)} async-done(((bf16[536,512]{1,0:T(8,128)(2,1)}), bf16[4288,512]{1,0:T(8,128)(2,1)}) %all-gather.6.cloned.1.call-update) | async-done | bytes 4390928 | tf_op jit(solution)/shard_map/all_gather | solution.py:271
  173.8 3.9 %fusion.99 = (bf16[8,512,128]{2,1,0:T(8,128)(2,1)}, bf16[8,512,128]{2,1,0:T(8,128)(2,1)S(1)}, bf16[8,512,128]{2,1,0:T(8,128)(2,1)}, bf16[8,512,128]{2,1,0:T(8,128)(2,1)S(1)}) fusion(bf16[8,536,512]{2,1,0:T(8,128)(2,1)} %bitcast.140), kind=kLoop, calls=%fused_computation.172 | loop fusion | bytes 8388608 | tf_op jit(solution)/shard_map/slice | solution.py:306
  177.7 1.0 convert_reduce_fusion.1
  178.7 14.2 %shard_map.166 = bf16[2,1024,128]{2,1,0:T(8,128)(2,1)} custom-call(s32[8]{0:T(128)} %and_convert_fusion.needed_ref, bf16[2,1024,128]{2,1,0:T(8,128)(2,1)} %bitcast.158, bf16[8,536,512]{2,1,0:T(8,128)(2,1)} %bitcast.142, bf16[8,536,512]{2,1,0:T(8,128)(2,1)} %bitcast.143, s32[1024,1]{1,0:T(8,128)} %broadcast_in_dim_reshape.9.qid_ref, ...), custom_call_target="tpu_custom_call" | custom-call | flops 4294967296 | bytes 5242880 | tf_op jit(solution)/shard_map/pallas_call | solution.py:102
  192.9 1.3 copy.81
  194.3 1.8 fusion.101
  196.1 1.8 fusion.100
  198.6 6.6 %convolution_convert_fusion = bf16[520,4096]{1,0:T(8,128)(2,1)} fusion(bf16[512,4096]{1,0:T(8,128)(2,1)} %param.26, bf16[8,512]{0,1:T(8,128)(2,1)S(1)} %copy.82, bf16[512,512]{0,1:T(8,128)(2,1)S(1)} %bitcast.150), kind=kOutput, calls=%fused_computation.9 | convolution fusion | flops 2184232960 | bytes 8986624 | tf_op jit(solution)/shard_map/dot_general | solution.py:330
  205.2 54.1 %reduce-scatter.2.cloned.1.call-done = bf16[520,1024]{1,0:T(8,128)(2,1)} async-done(((bf16[520,4096]{1,0:T(8,128)(2,1)}), bf16[520,1024]{1,0:T(8,128)(2,1)}) %reduce-scatter.2.cloned.1.call-update) | async-done | bytes 1064976 | tf_op jit(solution)/shard_map/reduce_scatter | solution.py:329
  259.4 1.5 convert_element_type.143
  260.9 1.3 copy-done.4
  262.4 2.4 fusion.81
  265.3 1.4 collective-permute-start.5
  266.7 2.5 fusion.29
  270.0 0.8 fusion.79
  270.8 1.8 collective-permute-start.6
  272.6 1.8 collective-permute-done.6
  274.4 1.7 collective-permute-start.7
  276.2 1.8 collective-permute-done.7
  278.0 2.6 collective-permute-start.8
  280.6 1.8 collective-permute-done.8
  (105 shorter events, 10.7 us)
Async XLA Ops:
  7.2 7.4 %copy-start = (bf16[1408,3,352]{0,2,1:T(8,128)(2,1)S(1)}, bf16[1408,3,352]{0,2,1:T(8,128)(2,1)}, u32[]{:S(2)}) copy-start(bf16[1408,3,352]{0,2,1:T(8,128)(2,1)} %param.19) | copy-start | bytes 8921092
  7.2 7.2 %copy-start.9 = (s32[3,2]{0,1:T(2,128)S(1)}, s32[3,2]{0,1:T(2,128)}, u32[]{:S(2)}) copy-start(s32[3,2]{0,1:T(2,128)} %param.16) | copy-start | bytes 76
  7.2 7.3 %copy-start.15 = (f32[1408]{0:T(1024)S(1)}, f32[1408]{0:T(1024)}, u32[]{:S(2)}) copy-start(f32[1408]{0:T(1024)} %param.18) | copy-start | bytes 16900
  7.2 55.3 %all-reduce.2.cloned.1.call-start = ((), (), s32[]{:S(2)}) async-start(), calls=%async_computation.1 | async-start | bytes 1081344 | tf_op jit(solution)/shard_map/psum | solution.py:206
  7.2 6.4 %copy-start.2 = (bf16[3,256,1408]{2,1,0:T(8,128)(2,1)S(1)}, bf16[3,256,1408]{2,1,0:T(8,128)(2,1)}, u32[]{:S(2)}) copy-start(bf16[3,256,1408]{2,1,0:T(8,128)(2,1)} %param.15) | copy-start | bytes 6488068
  7.3 61.5 %collective-permute-start = (bf16[512,1024]{1,0:T(8,128)(2,1)}, bf16[512,1024]{1,0:T(8,128)(2,1)}, u32[]{:S(2)}, u32[]{:S(2)}) collective-permute-start(bf16[512,1024]{1,0:T(8,128)(2,1)} %param.22), channel_id=1, source_target_pairs={{0,8},{8,16},{16,24},{24,0},{1,9},{9,17},{17,25},{25,1},{2,10},{10... | collective-permute-start | bytes 3145736 | tf_op jit(solution)/shard_map/ppermute | solution.py:120
  7.8 61.0 %collective-permute-start.1 = (bf16[512,1024]{1,0:T(8,128)(2,1)}, bf16[512,1024]{1,0:T(8,128)(2,1)}, u32[]{:S(2)}, u32[]{:S(2)}) collective-permute-start(bf16[512,1024]{1,0:T(8,128)(2,1)} %param.22), channel_id=1, source_target_pairs={{0,16},{8,24},{16,0},{24,8},{1,17},{9,25},{17,1},{25,9},{2,18},{10... | collective-permute-start | bytes 3145736 | tf_op jit(solution)/shard_map/ppermute | solution.py:120
  10.3 58.4 %collective-permute-start.2 = (bf16[512,1024]{1,0:T(8,128)(2,1)}, bf16[512,1024]{1,0:T(8,128)(2,1)}, u32[]{:S(2)}, u32[]{:S(2)}) collective-permute-start(bf16[512,1024]{1,0:T(8,128)(2,1)} %param.22), channel_id=1, source_target_pairs={{0,24},{8,0},{16,8},{24,16},{1,25},{9,1},{17,9},{25,17},{2,26},{10... | collective-permute-start | bytes 3145736 | tf_op jit(solution)/shard_map/ppermute | solution.py:120
  21.3 3.8 %copy-start.11 = (s32[8]{0:T(128)S(1)}, s32[8]{0:T(128)}, u32[]{:S(2)}) copy-start(s32[8]{0:T(128)} %param.27) | copy-start | bytes 100
  21.4 4.0 %copy-start.10 = (s32[3]{0:T(128)S(1)}, s32[3]{0:T(128)}, u32[]{:S(2)}) copy-start(s32[3]{0:T(128)} %param.17) | copy-start | bytes 40
  21.4 4.1 %copy-start.3 = (bf16[3,256,1408]{2,1,0:T(8,128)(2,1)S(1)}, bf16[3,256,1408]{2,1,0:T(8,128)(2,1)}, u32[]{:S(2)}) copy-start(bf16[3,256,1408]{2,1,0:T(8,128)(2,1)} %param.15) | copy-start | bytes 6488068
  25.0 61.3 %all-gather.4.cloned.1.call-start = ((), (), s32[]{:S(2)}) async-start(), calls=%async_computation.2 | async-start | bytes 1966080 | tf_op jit(solution)/shard_map/all_gather | solution.py:225
  33.3 33.6 %copy-start.7 = (bf16[512,1024]{1,0:T(8,128)(2,1)S(1)}, bf16[512,1024]{1,0:T(8,128)(2,1)}, u32[]{:S(2)}) copy-start(bf16[512,1024]{1,0:T(8,128)(2,1)} %param.22) | copy-start | bytes 3145732
  66.0 107.8 %all-gather.6.cloned.1.call-start = ((), (), s32[]{:S(2)}) async-start(), calls=%async_computation.4 | async-start | bytes 4939776 | tf_op jit(solution)/shard_map/all_gather | solution.py:271
  68.4 4.0 %copy-start.6 = (bf16[512,1024]{1,0:T(8,128)(2,1)}, bf16[512,1024]{1,0:T(8,128)(2,1)S(1)}, u32[]{:S(2)}) copy-start(bf16[512,1024]{1,0:T(8,128)(2,1)S(1)} %fusion.44) | copy-start | bytes 3145732
  86.3 4.2 %copy-start.12 = (bf16[4096,2,256]{2,1,0:T(2,128)(2,1)S(1)}, bf16[4096,2,256]{2,1,0:T(2,128)(2,1)}, u32[]{:S(2)}) copy-start(bf16[4096,2,256]{2,1,0:T(2,128)(2,1)} %param.25) | copy-start | bytes 12582916
  86.3 4.2 %copy-start.14 = (f32[4096]{0:T(1024)S(1)}, f32[4096]{0:T(1024)}, u32[]{:S(2)}) copy-start(f32[4096]{0:T(1024)} %param.23) | copy-start | bytes 49156
  90.6 2.7 copy-start.13
  97.8 161.6 %reduce-scatter.2.cloned.1.call-start = ((), (), s32[]{:S(2)}) async-start(), calls=%async_computation.3 | async-start | bytes 5324800 | tf_op jit(solution)/shard_map/reduce_scatter | solution.py:329
  205.2 57.2 %copy-start.8 = (f32[1024]{0:T(1024)S(1)}, f32[1024]{0:T(1024)}, u32[]{:S(2)}) copy-start(f32[1024]{0:T(1024)} %param.28) | copy-start | bytes 12292
  260.9 1.4 copy-start.4
  262.4 4.3 %copy-start.5 = (f32[520,1024]{1,0:T(8,128)S(1)}, f32[520,1024]{1,0:T(8,128)}, u32[]{:S(2)}) copy-start(f32[520,1024]{1,0:T(8,128)} %copy-done.4) | copy-start | bytes 6389764
  262.4 20.5 %copy-start.1 = (bf16[1408,3,352]{0,2,1:T(8,128)(2,1)S(1)}, bf16[1408,3,352]{0,2,1:T(8,128)(2,1)}, u32[]{:S(2)}) copy-start(bf16[1408,3,352]{0,2,1:T(8,128)(2,1)} %param.19) | copy-start | bytes 8921092
  264.8 4.4 %collective-permute-start.3 = (f32[8,1025]{1,0:T(8,128)S(1)}, f32[8,1025]{1,0:T(8,128)S(1)}, u32[]{:S(2)}, u32[]{:S(2)}) collective-permute-start(f32[8,1025]{1,0:T(8,128)S(1)} %get-tuple-element.18), channel_id=1, source_target_pairs={{0,8},{8,16},{16,24},{24,0},{1,9},{9,17},{17,25},{25,1},{2,10},{10... | collective-permute-start | bytes 98408 | tf_op jit(solution)/shard_map/ppermute | solution.py:132
  264.9 4.3 %collective-permute-start.4 = (f32[8,1025]{1,0:T(8,128)S(1)}, f32[8,1025]{1,0:T(8,128)S(1)}, u32[]{:S(2)}, u32[]{:S(2)}) collective-permute-start(f32[8,1025]{1,0:T(8,128)S(1)} %get-tuple-element.18), channel_id=1, source_target_pairs={{0,16},{8,24},{16,0},{24,8},{1,17},{9,25},{17,1},{25,9},{2,18},{10... | collective-permute-start | bytes 98408 | tf_op jit(solution)/shard_map/ppermute | solution.py:132
  265.3 3.9 %collective-permute-start.5 = (f32[8,1025]{1,0:T(8,128)S(1)}, f32[8,1025]{1,0:T(8,128)S(1)}, u32[]{:S(2)}, u32[]{:S(2)}) collective-permute-start(f32[8,1025]{1,0:T(8,128)S(1)} %get-tuple-element.18), channel_id=1, source_target_pairs={{0,24},{8,0},{16,8},{24,16},{1,25},{9,1},{17,9},{25,17},{2,26},{10... | collective-permute-start | bytes 98408 | tf_op jit(solution)/shard_map/ppermute | solution.py:132
  270.8 3.6 %collective-permute-start.6 = (f32[8]{0:T(128)S(1)}, f32[8]{0:T(128)S(1)}, u32[]{:S(2)}, u32[]{:S(2)}) collective-permute-start(f32[8]{0:T(128)S(1)} %get-tuple-element.23), channel_id=1, source_target_pairs={{0,1},{1,0},{2,3},{3,2},{4,5},{5,4},{6,7},{7,6},{8,9},{9,8},{10,11... | collective-permute-start | bytes 104 | tf_op jit(solution)/shard_map/ppermute | solution.py:149
  274.4 3.5 %collective-permute-start.7 = (f32[8]{0:T(128)S(1)}, f32[8]{0:T(128)S(1)}, u32[]{:S(2)}, u32[]{:S(2)}) collective-permute-start(f32[8]{0:T(128)S(1)} %max.9), channel_id=1, source_target_pairs={{0,2},{1,3},{2,0},{3,1},{4,6},{5,7},{6,4},{7,5},{8,10},{9,11},{10,... | collective-permute-start | bytes 104 | tf_op jit(solution)/shard_map/ppermute | solution.py:149
  278.0 4.4 %collective-permute-start.8 = (f32[8]{0:T(128)S(1)}, f32[8]{0:T(128)S(1)}, u32[]{:S(2)}, u32[]{:S(2)}) collective-permute-start(f32[8]{0:T(128)S(1)} %max.10), channel_id=1, source_target_pairs={{0,4},{1,5},{2,6},{3,7},{4,0},{5,1},{6,2},{7,3},{8,12},{9,13},{10,... | collective-permute-start | bytes 104 | tf_op jit(solution)/shard_map/ppermute | solution.py:149
Sparse Core Ops, SparseCore 0:
  25.1 37.3 all-reduce.1
  66.2 20.1 all-gather.3
  97.9 75.8 all-gather.5
  205.4 53.9 reduce-scatter.1

commit v6 on v5

--- a/solution.py
+++ b/solution.py
@@ -209,6 +209,18 @@
     merged = jnp.einsum(
         "pmd,de->pme", pooled, merge_weight, preferred_element_type=jnp.float32
     ).astype(jnp.bfloat16)
+    me_kv = lax.axis_index("kv")
+    out_source, merged = lax.optimization_barrier((w_out, merged))
+    weight_pieces = [lax.dynamic_slice_in_dim(out_source, me_kv * feat_dev, feat_dev, 1)]
+    for shift in range(1, kv_count):
+        payload = lax.dynamic_slice_in_dim(
+            out_source, ((me_kv + shift) % kv_count) * feat_dev, feat_dev, 1
+        )
+        weight_pieces.append(
+            lax.ppermute(
+                payload, "kv", perm=[(i, (i + shift) % kv_count) for i in range(kv_count)]
+            )
+        )
     block_base = lax.axis_index("blk") * tok_rows
     slot_index = jnp.arange(merged_max, dtype=jnp.int32)
     target = picture_start[:, None] + slot_index[None, :] - block_base
@@ -269,6 +281,12 @@
     shipped = jnp.concatenate([key_rows, value_rows], axis=1)
     shipped = jnp.concatenate([shipped, extras.reshape(extra_rows, ship_width)], axis=0)
     gathered = lax.all_gather(shipped, "blk", axis=0, tiled=False)
+    gathered, weight_pieces = lax.optimization_barrier((gathered, weight_pieces))
+    out_weights = jnp.take(
+        jnp.stack(weight_pieces),
+        (me_kv - jnp.arange(kv_count, dtype=jnp.int32)) % kv_count,
+        axis=0,
+    )
     blocks = gathered.shape[0]
     q_cols = query_proj.shape[1]
     extras_all = gathered[:, tok_rows:].reshape(blocks, -1)[:, : reqs * (q_cols + feat_dev)]
@@ -326,12 +344,11 @@
         last_parts.append((last_mix / last_sum[..., None]).reshape(reqs, per_group * HD))
     last_context = jnp.concatenate(last_parts, axis=1).astype(jnp.bfloat16)
     out_rows = jnp.concatenate([context, last_context], axis=0)
-    head_sum = lax.psum_scatter(
-        jnp.dot(out_rows, w_out, preferred_element_type=jnp.float32).astype(jnp.bfloat16),
-        "kv",
-        scatter_dimension=1,
-        tiled=True,
-    ).astype(jnp.float32)
+    context_all = lax.all_gather(out_rows, "kv", axis=0, tiled=False)
+    group_parts = jnp.einsum(
+        "grc,gcf->grf", context_all, out_weights, preferred_element_type=jnp.float32
+    )
+    head_sum = jnp.sum(group_parts.astype(jnp.bfloat16).astype(jnp.float32), axis=0)
     hidden = (seq_in.astype(jnp.float32) + head_sum[:tok_rows]).astype(jnp.bfloat16)
     chosen = (seq_last + head_sum[tok_rows:]).astype(jnp.bfloat16).astype(jnp.float32)
     square_part = jnp.sum(chosen * chosen, axis=-1)

time: 290 us -> 271 us (0.934)
  waiting for transfers between devices: 162 us -> 126 us
  local copies, waits for them, and re-layouts: 24 us -> 34.8 us
  other arithmetic: 26.4 us -> 30.9 us
    reduce_scatter x1 -> x0, waiting for transfers between devices: 54.1 us -> none  [on_device(): lax.psum_scatter(jnp.dot(out_rows, w_out, preferred_element_type=jnp.floa...]
    all_gather x1, waiting for transfers between devices: 69.2 us -> 24 us  [on_device(): gathered = lax.all_gather(shipped, 'blk', axis=0, tiled=False)]
    ppermute x0 -> x3, waiting for transfers between devices: none -> 39.6 us  [on_device(): lax.ppermute(payload, 'kv', perm=[(i, (i + shift) % kv_count) for i in ra...]
    all_gather x0 -> x1, waiting for transfers between devices: none -> 23.4 us  [on_device(): context_all = lax.all_gather(out_rows, 'kv', axis=0, tiled=False)]
    gather x0 -> x1, local copies, waits for them, and re-layouts: none -> 4.97 us  [on_device(): jnp.take(jnp.stack(weight_pieces), (me_kv - jnp.arange(kv_count, dtype=jn...]
    dynamic_slice x0 -> x1, local copies, waits for them, and re-layouts: none -> 4.01 us  [on_device(): lax.dynamic_slice_in_dim(out_source, (me_kv + shift) % kv_count * feat_de...]
    another operation x4 -> x5, other arithmetic: 0.45 us -> 4.04 us  [the longest x1 3.59 us: on_device(): jnp.stack(weight_pieces)]
  transfers between devices with their start and end apart: 13 -> 16, of which waited for: 7 -> 10; matrix products, arithmetic and copies ran while one was open for 17% -> 24% of each run, Pallas kernels for 0% -> 0%
where the time goes in v6:
time: 271 us; the launch traced here: 270 us
  waiting for transfers between devices  126 us (46%)
  matrix products  35.7 us (13%)
  local copies, waits for them, and re-layouts  34.8 us (13%)
  other arithmetic  30.9 us (11%)
  starting transfers between devices  14.5 us (5%)
  between operations  14.3 us (5%)
  Pallas kernels  14.2 us (5%)
    ppermute x3, waiting for transfers between devices, on_device(): lax.ppermute(payload, 'kv', perm=[(i, (i + shift) % kv_count) for i in ra...  39.6 us
    psum x1, waiting for transfers between devices, on_device(): lax.psum(head_pooled.astype(jnp.bfloat16), 'kv').astype(jnp.float32)  28.7 us
    all_gather x1, waiting for transfers between devices, on_device(): gathered = lax.all_gather(shipped, 'blk', axis=0, tiled=False)  24 us
    all_gather x1, waiting for transfers between devices, on_device(): context_all = lax.all_gather(out_rows, 'kv', axis=0, tiled=False)  23.4 us
    pallas_call x1, Pallas kernels, flash_attention(): pl.pallas_call(functools.partial(flash_kernel, root=root), grid_spec=grid...  14.2 us
    ppermute x3, starting transfers between devices, tree_max(): lax.ppermute(values, axis, perm=[(i, i ^ step) for i in range(count)])  6.1 us
    dot_general x1, matrix products, on_device(): jnp.einsum('grc,gcf->grf', context_all, out_weights, preferred_element_ty...  5.58 us
    ppermute x3, waiting for transfers between devices, tree_max(): lax.ppermute(values, axis, perm=[(i, i ^ step) for i in range(count)])  5.48 us
  transfers between devices with their start and end apart: 16, of which 10 were waited for; matrix products, arithmetic and copies ran while one was open for 24% of the time, Pallas kernels for 0%

profile of v6, /device:TPU:0, one launch (start us, length us, event | category | flops | bytes accessed | tf_op | source)
XLA Modules:
  0.0 270.2 jit_solution(303469139376219134)
XLA Ops:
  7.8 2.6 collective-permute-start.1
  10.3 1.4 collective-permute-start.2
  11.7 2.0 convert_reduce_fusion.1
  13.7 2.3 multiply_reduce_fusion
  16.1 2.9 %fusion.36 = bf16[3,256,3,352]{1,3,2,0:T(8,128)(2,1)S(1)} fusion(bf16[1408,3,352]{0,2,1:T(8,128)(2,1)S(1)} %copy-done, bf16[3,256,1408]{2,1,0:T(8,128)(2,1)S(1)} %copy-done.2, f32[1408]{0:T(1024)S(1)} %copy-done.14, f32[3,256]{1,0:T(4,128)S(1)} %add_rsqrt_fusion, f32[3,256]{1,0:T(4,128)S(1)} %broadcast_multiply_fusion), kind=kOutput, calls=%fused_computation.52 | convolution fusion | flops 2290016256 | bytes 6770176 | tf_op jit(solution)/shard_map/pnd,dce->pnce/dot_general | solution.py:181
  22.2 1.6 dot_general.56
  23.8 2.8 %convolution_reduce_fusion = f32[3,64,1408]{2,1,0:T(8,128)S(1)} fusion(bf16[352,1408]{1,0:T(8,128)(2,1)} %param.22, bf16[3,64,4,352]{3,2,1,0:T(4,128)(2,1)} %dot_general.56), kind=kOutput, calls=%fused_computation.51 | convolution fusion | flops 762077184 | bytes 2613248 | tf_op jit(solution)/shard_map/pnc,cd->pnd/dot_general | solution.py:204
  27.9 2.9 %reshape.373 = f32[3,64,4,1408]{3,2,1,0:T(4,128)} reshape(bf16[3,256,1408]{2,1,0:T(8,128)(2,1)S(1)} %copy-done.3) | data formatting | bytes 6488064 | tf_op jit(solution)/shard_map/reshape | solution.py:207
  30.9 4.9 %reduce_sum.145 = f32[3,64,1408]{2,1,0:T(8,128)S(1)} reduce(f32[3,64,4,1408]{3,2,1,0:T(4,128)} %reshape.373, f32[]{:T(128)} %constant.116.clone.1), dimensions={2}, to_apply=%region_1.2 | reduce | flops 811008 | bytes 5406724 | tf_op jit(solution)/shard_map/reduce_sum | solution.py:207
  36.0 28.7 %all-reduce.2.cloned.1.call-done = bf16[3,64,1408]{2,1,0:T(8,128)(2,1)} async-done(((bf16[3,64,1408]{2,1,0:T(8,128)(2,1)}), bf16[3,64,1408]{2,1,0:T(8,128)(2,1)}) %all-reduce.2.cloned.1.call-update) | async-done | bytes 540688 | tf_op jit(solution)/shard_map/psum | solution.py:206
  64.8 3.5 %fusion.51 = bf16[3,64,1024]{2,1,0:T(8,128)(2,1)} fusion(bf16[1408,1024]{1,0:T(8,128)(2,1)} %param.23, bf16[3,64,1408]{2,1,0:T(8,128)(2,1)} %all-reduce.2.cloned.1.call-done, f32[3,64,1408]{2,1,0:T(8,128)S(1)} %reduce_sum.145), kind=kOutput, calls=%fused_computation.61 | convolution fusion | flops 554926080 | bytes 4898816 | tf_op jit(solution)/shard_map/pmd,de->pme/dot_general | solution.py:209
  69.1 1.6 fusion.50
  71.0 3.7 %pad_maximum_fusion = bf16[4,512,1024]{2,1,0:T(8,128)(2,1)} fusion(bf16[1,512,1024]{2,1,0:T(8,128)(2,1)} %bitcast.21, bf16[1,512,1024]{2,1,0:T(8,128)(2,1)} %bitcast.20, bf16[1,512,1024]{2,1,0:T(8,128)(2,1)} %bitcast.19, bf16[1,512,1024]{2,1,0:T(8,128)(2,1)S(1)} %bitcast.163), kind=kLoop, calls=%fused_computation.25 | loop fusion | flops 6291456 | bytes 8388608 | tf_op jit(solution)/shard_map/stack | solution.py:122
  74.7 5.2 %gather_fusion.1 = bf16[4,512,1024]{2,1,0:T(8,128)(2,1)} fusion(bf16[4,512,1024]{2,1,0:T(8,128)(2,1)} %pad_maximum_fusion, s32[1024]{0:T(1024)S(1)} %pad_clamp_fusion.1), kind=kCustom, calls=%fused_computation.clone | custom fusion | bytes 8388624 | tf_op jit(solution)/shard_map/jit(_take)/gather | solution.py:124
  79.8 2.7 broadcast_select_fusion
  82.5 1.8 slice_bitcast_fusion.3
  84.3 4.5 %all-gather.6.cloned.1.call-done = bf16[192,4096]{1,0:T(8,128)(2,1)} async-done(((bf16[192,1024]{1,0:T(8,128)(2,1)}), bf16[192,4096]{1,0:T(8,128)(2,1)}) %all-gather.6.cloned.1.call-update) | async-done | bytes 1572880 | tf_op jit(solution)/shard_map/all_gather | solution.py:237
  88.7 4.2 %fusion.2 = (f32[512]{0:T(512)S(1)}, bf16[512,4096]{1,0:T(8,128)(2,1)S(1)}) fusion(bf16[512,1024]{1,0:T(8,128)(2,1)S(1)} %get-tuple-element.29, bf16[512,1024]{1,0:T(8,128)(2,1)} %get-tuple-element.30, bf16[512,1024]{1,0:T(8,128)(2,1)} %get-tuple-element.31, bf16[512,1024]{1,0:T(8,128)(2,1)S(1)} %get-tuple-element.28, ...), kind=kOutput, calls=%fused_computation.8 | convolution fusion | flops 832667136 | bytes 9964800 | tf_op jit(solution)/shard_map/dot_general | solution.py:240
  93.0 2.6 fusion.14
  95.7 2.6 fusion.55
  102.1 4.0 %constant_dynamic-slice_fusion = (bf16[512,1024]{1,0:T(8,128)(2,1)}, bf16[512,1024]{1,0:T(8,128)(2,1)}, bf16[512,1024]{1,0:T(8,128)(2,1)}, bf16[512,1024]{1,0:T(8,128)(2,1)S(1)}) fusion(bf16[512,4096]{1,0:T(8,128)(2,1)} %param.28, s32[]{:T(128)S(6)} %select_n.128, s32[]{:T(128)S(6)} %select_n.126, s32[]{:T(128)S(6)} %select_n.124, s32[]{:T(128)S(6)} %select_n.122), kind=kLoop, calls=%fused_computation.162 | loop fusion | bytes 8388624 | tf_op jit(solution)/shard_map/dynamic_slice | solution.py:216
  106.7 1.2 collective-permute-start.5
  107.9 1.2 and_convert_fusion.needed_ref
  111.5 1.1 copy.78
  112.7 18.5 %collective-permute-done.3 = bf16[512,1024]{1,0:T(8,128)(2,1)} collective-permute-done((bf16[512,1024]{1,0:T(8,128)(2,1)}, bf16[512,1024]{1,0:T(8,128)(2,1)}, u32[]{:S(2)}, u32[]{:S(2)}) %collective-permute-start.3) | collective-permute-done | bytes 1048608 | tf_op jit(solution)/shard_map/ppermute | solution.py:220
  131.1 1.6 collective-permute-done.4
  132.7 19.5 %collective-permute-done.5 = bf16[512,1024]{1,0:T(8,128)(2,1)} collective-permute-done((bf16[512,1024]{1,0:T(8,128)(2,1)}, bf16[512,1024]{1,0:T(8,128)(2,1)}, u32[]{:S(2)}, u32[]{:S(2)}) %collective-permute-start.5) | collective-permute-done | bytes 1048608 | tf_op jit(solution)/shard_map/ppermute | solution.py:220
  152.2 24.0 %all-gather.8.cloned.1.call-done = bf16[4288,512]{1,0:T(8,128)(2,1)} async-done(((bf16[536,512]{1,0:T(8,128)(2,1)}), bf16[4288,512]{1,0:T(8,128)(2,1)}) %all-gather.8.cloned.1.call-update) | async-done | bytes 4390928 | tf_op jit(solution)/shard_map/all_gather | solution.py:283
  176.2 4.1 %fusion.102 = (bf16[8,512,128]{2,1,0:T(8,128)(2,1)}, bf16[8,512,128]{2,1,0:T(8,128)(2,1)S(1)}, bf16[8,512,128]{2,1,0:T(8,128)(2,1)}, bf16[8,512,128]{2,1,0:T(8,128)(2,1)}) fusion(bf16[8,536,512]{2,1,0:T(8,128)(2,1)} %bitcast.145), kind=kLoop, calls=%fused_computation.181 | loop fusion | bytes 8388608 | tf_op jit(solution)/shard_map/slice | solution.py:324
  181.2 14.2 %shard_map.166 = bf16[2,1024,128]{2,1,0:T(8,128)(2,1)} custom-call(s32[8]{0:T(128)} %and_convert_fusion.needed_ref, bf16[2,1024,128]{2,1,0:T(8,128)(2,1)} %bitcast.164, bf16[8,536,512]{2,1,0:T(8,128)(2,1)} %bitcast.147, bf16[8,536,512]{2,1,0:T(8,128)(2,1)} %bitcast.148, s32[1024,1]{1,0:T(8,128)} %broadcast_in_dim_reshape.9.qid_ref, ...), custom_call_target="tpu_custom_call" | custom-call | flops 4294967296 | bytes 5242880 | tf_op jit(solution)/shard_map/pallas_call | solution.py:102
  195.5 1.3 copy.84
  196.8 1.8 fusion.104
  198.7 1.8 fusion.103
  200.5 1.5 fusion.60
  203.6 3.6 %pad_maximum_fusion.1 = bf16[4,512,1024]{2,1,0:T(8,128)(2,1)} fusion(bf16[1,512,1024]{2,1,0:T(8,128)(2,1)} %bitcast.57, bf16[1,512,1024]{2,1,0:T(8,128)(2,1)} %bitcast.56, bf16[1,512,1024]{2,1,0:T(8,128)(2,1)} %bitcast.55, bf16[1,512,1024]{2,1,0:T(8,128)(2,1)S(1)} %bitcast.149), kind=kLoop, calls=%fused_computation.26 | loop fusion | flops 6291456 | bytes 8388608 | tf_op jit(solution)/shard_map/stack | solution.py:286
  207.2 5.0 %gather_fusion.2 = bf16[4,512,1024]{2,1,0:T(8,128)(2,1)} fusion(bf16[4,512,1024]{2,1,0:T(8,128)(2,1)} %pad_maximum_fusion.1, s32[1024]{0:T(1024)S(1)} %pad_clamp_fusion.1), kind=kCustom, calls=%fused_computation.1.clone | custom fusion | bytes 8388624 | tf_op jit(solution)/shard_map/jit(_take)/gather | solution.py:285
  212.1 23.4 %all-gather.10.cloned.1.call-done = bf16[2080,512]{1,0:T(8,128)(2,1)} async-done(((bf16[520,512]{1,0:T(8,128)(2,1)}), bf16[2080,512]{1,0:T(8,128)(2,1)}) %all-gather.10.cloned.1.call-update) | async-done | bytes 2129936 | tf_op jit(solution)/shard_map/all_gather | solution.py:347
  235.5 5.6 %convert_reduce_fusion = f32[520,1024]{1,0:T(8,128)S(1)} fusion(bf16[4,520,512]{2,1,0:T(8,128)(2,1)} %bitcast.175, bf16[4,512,1024]{2,1,0:T(8,128)(2,1)} %gather_fusion.2, pred[4]{0:T(512)(128)(4,1)S(1)} %compare_and_fusion), kind=kOutput, calls=%fused_computation.7 | convolution fusion | flops 2188992512 | bytes 8454148 | tf_op jit(solution)/shard_map/grc,gcf->grf/dot_general | solution.py:348
  241.1 1.3 copy-done.5
  242.7 2.2 fusion.84
  245.5 1.2 collective-permute-start.8
  246.8 3.2 %fusion.32 = bf16[512,1024]{1,0:T(8,128)(2,1)} fusion(f32[520,1024]{1,0:T(8,128)} %copy-done.5, bf16[512,1024]{1,0:T(8,128)(2,1)} %copy-done.4), kind=kLoop, calls=%fused_computation.49 | loop fusion | flops 1572864 | bytes 4194304 | tf_op jit(solution)/shard_map/convert_element_type | solution.py:352
  251.6 1.8 collective-permute-start.9
  253.3 1.8 collective-permute-done.9
  255.2 1.7 collective-permute-start.10
  256.9 1.8 collective-permute-done.10
  258.7 2.6 collective-permute-start.11
  261.3 1.8 collective-permute-done.11
  (115 shorter events, 18.7 us)
Async XLA Ops:
  7.2 9.0 %copy-start = (bf16[1408,3,352]{0,2,1:T(8,128)(2,1)S(1)}, bf16[1408,3,352]{0,2,1:T(8,128)(2,1)}, u32[]{:S(2)}) copy-start(bf16[1408,3,352]{0,2,1:T(8,128)(2,1)} %param.21) | copy-start | bytes 8921092
  7.2 8.8 %copy-start.8 = (s32[3,2]{0,1:T(2,128)S(1)}, s32[3,2]{0,1:T(2,128)}, u32[]{:S(2)}) copy-start(s32[3,2]{0,1:T(2,128)} %param.18) | copy-start | bytes 76
  7.2 8.9 %copy-start.14 = (f32[1408]{0:T(1024)S(1)}, f32[1408]{0:T(1024)}, u32[]{:S(2)}) copy-start(f32[1408]{0:T(1024)} %param.20) | copy-start | bytes 16900
  7.2 57.5 %all-reduce.2.cloned.1.call-start = ((), (), s32[]{:S(2)}) async-start(), calls=%async_computation | async-start | bytes 1081344 | tf_op jit(solution)/shard_map/psum | solution.py:206
  7.2 8.9 %copy-start.2 = (bf16[3,256,1408]{2,1,0:T(8,128)(2,1)S(1)}, bf16[3,256,1408]{2,1,0:T(8,128)(2,1)}, u32[]{:S(2)}) copy-start(bf16[3,256,1408]{2,1,0:T(8,128)(2,1)} %param.17) | copy-start | bytes 6488068
  7.3 63.7 %collective-permute-start = (bf16[512,1024]{1,0:T(8,128)(2,1)}, bf16[512,1024]{1,0:T(8,128)(2,1)}, u32[]{:S(2)}, u32[]{:S(2)}) collective-permute-start(bf16[512,1024]{1,0:T(8,128)(2,1)} %param.24), channel_id=1, source_target_pairs={{0,8},{8,16},{16,24},{24,0},{1,9},{9,17},{17,25},{25,1},{2,10},{10... | collective-permute-start | bytes 3145736 | tf_op jit(solution)/shard_map/ppermute | solution.py:120
  7.8 63.2 %collective-permute-start.1 = (bf16[512,1024]{1,0:T(8,128)(2,1)}, bf16[512,1024]{1,0:T(8,128)(2,1)}, u32[]{:S(2)}, u32[]{:S(2)}) collective-permute-start(bf16[512,1024]{1,0:T(8,128)(2,1)} %param.24), channel_id=1, source_target_pairs={{0,16},{8,24},{16,0},{24,8},{1,17},{9,25},{17,1},{25,9},{2,18},{10... | collective-permute-start | bytes 3145736 | tf_op jit(solution)/shard_map/ppermute | solution.py:120
  10.3 60.7 %collective-permute-start.2 = (bf16[512,1024]{1,0:T(8,128)(2,1)}, bf16[512,1024]{1,0:T(8,128)(2,1)}, u32[]{:S(2)}, u32[]{:S(2)}) collective-permute-start(bf16[512,1024]{1,0:T(8,128)(2,1)} %param.24), channel_id=1, source_target_pairs={{0,24},{8,0},{16,8},{24,16},{1,25},{9,1},{17,9},{25,17},{2,26},{10... | collective-permute-start | bytes 3145736 | tf_op jit(solution)/shard_map/ppermute | solution.py:120
  22.2 5.4 %copy-start.10 = (s32[8]{0:T(128)S(1)}, s32[8]{0:T(128)}, u32[]{:S(2)}) copy-start(s32[8]{0:T(128)} %param.29) | copy-start | bytes 100
  22.2 5.5 %copy-start.9 = (s32[3]{0:T(128)S(1)}, s32[3]{0:T(128)}, u32[]{:S(2)}) copy-start(s32[3]{0:T(128)} %param.19) | copy-start | bytes 40
  22.2 5.7 %copy-start.3 = (bf16[3,256,1408]{2,1,0:T(8,128)(2,1)S(1)}, bf16[3,256,1408]{2,1,0:T(8,128)(2,1)}, u32[]{:S(2)}) copy-start(bf16[3,256,1408]{2,1,0:T(8,128)(2,1)} %param.17) | copy-start | bytes 6488068
  27.5 61.3 %all-gather.6.cloned.1.call-start = ((), (), s32[]{:S(2)}) async-start(), calls=%async_computation.1 | async-start | bytes 1966080 | tf_op jit(solution)/shard_map/all_gather | solution.py:237
  30.9 38.2 %copy-start.6 = (bf16[512,1024]{1,0:T(8,128)(2,1)S(1)}, bf16[512,1024]{1,0:T(8,128)(2,1)}, u32[]{:S(2)}) copy-start(bf16[512,1024]{1,0:T(8,128)(2,1)} %param.24) | copy-start | bytes 3145732
  68.3 107.9 %all-gather.8.cloned.1.call-start = ((), (), s32[]{:S(2)}) async-start(), calls=%async_computation.2 | async-start | bytes 4939776 | tf_op jit(solution)/shard_map/all_gather | solution.py:283
  70.7 4.0 %copy-start.4 = (bf16[512,1024]{1,0:T(8,128)(2,1)}, bf16[512,1024]{1,0:T(8,128)(2,1)S(1)}, u32[]{:S(2)}) copy-start(bf16[512,1024]{1,0:T(8,128)(2,1)S(1)} %fusion.50) | copy-start | bytes 3145732
  88.7 4.2 %copy-start.11 = (bf16[4096,2,256]{2,1,0:T(2,128)(2,1)S(1)}, bf16[4096,2,256]{2,1,0:T(2,128)(2,1)}, u32[]{:S(2)}) copy-start(bf16[4096,2,256]{2,1,0:T(2,128)(2,1)} %param.27) | copy-start | bytes 12582916
  88.7 4.2 %copy-start.13 = (f32[4096]{0:T(1024)S(1)}, f32[4096]{0:T(1024)}, u32[]{:S(2)}) copy-start(f32[4096]{0:T(1024)} %param.25) | copy-start | bytes 49156
  93.0 2.7 %copy-start.12 = (bf16[4096,512]{1,0:T(8,128)(2,1)S(1)}, bf16[4096,512]{1,0:T(8,128)(2,1)}, u32[]{:S(2)}) copy-start(bf16[4096,512]{1,0:T(8,128)(2,1)} %param.26) | copy-start | bytes 12582916
  100.2 135.3 %all-gather.10.cloned.1.call-start = ((), (), s32[]{:S(2)}) async-start(), calls=%async_computation.3 | async-start | bytes 2662400 | tf_op jit(solution)/shard_map/all_gather | solution.py:347
  106.1 25.0 %collective-permute-start.3 = (bf16[512,1024]{1,0:T(8,128)(2,1)}, bf16[512,1024]{1,0:T(8,128)(2,1)}, u32[]{:S(2)}, u32[]{:S(2)}) collective-permute-start(bf16[512,1024]{1,0:T(8,128)(2,1)} %get-tuple-element.26), channel_id=1, source_target_pairs={{0,8},{8,16},{16,24},{24,0},{1,9},{9,17},{17,25},{25,1},{2,10},{10... | collective-permute-start | bytes 3145736 | tf_op jit(solution)/shard_map/ppermute | solution.py:220
  106.4 26.3 %collective-permute-start.4 = (bf16[512,1024]{1,0:T(8,128)(2,1)}, bf16[512,1024]{1,0:T(8,128)(2,1)}, u32[]{:S(2)}, u32[]{:S(2)}) collective-permute-start(bf16[512,1024]{1,0:T(8,128)(2,1)} %get-tuple-element.25), channel_id=1, source_target_pairs={{0,16},{8,24},{16,0},{24,8},{1,17},{9,25},{17,1},{25,9},{2,18},{10... | collective-permute-start | bytes 3145736 | tf_op jit(solution)/shard_map/ppermute | solution.py:220
  106.7 45.5 %collective-permute-start.5 = (bf16[512,1024]{1,0:T(8,128)(2,1)}, bf16[512,1024]{1,0:T(8,128)(2,1)}, u32[]{:S(2)}, u32[]{:S(2)}) collective-permute-start(bf16[512,1024]{1,0:T(8,128)(2,1)} %get-tuple-element.24), channel_id=1, source_target_pairs={{0,24},{8,0},{16,8},{24,16},{1,25},{9,1},{17,9},{25,17},{2,26},{10... | collective-permute-start | bytes 3145736 | tf_op jit(solution)/shard_map/ppermute | solution.py:220
  235.5 7.2 %copy-start.7 = (f32[1024]{0:T(1024)S(1)}, f32[1024]{0:T(1024)}, u32[]{:S(2)}) copy-start(f32[1024]{0:T(1024)} %param.30) | copy-start | bytes 12292
  235.5 28.1 %copy-start.1 = (bf16[1408,3,352]{0,2,1:T(8,128)(2,1)S(1)}, bf16[1408,3,352]{0,2,1:T(8,128)(2,1)}, u32[]{:S(2)}) copy-start(bf16[1408,3,352]{0,2,1:T(8,128)(2,1)} %param.21) | copy-start | bytes 8921092
  241.1 1.4 copy-start.5
  244.9 5.0 %collective-permute-start.6 = (f32[8,1025]{1,0:T(8,128)S(1)}, f32[8,1025]{1,0:T(8,128)S(1)}, u32[]{:S(2)}, u32[]{:S(2)}) collective-permute-start(f32[8,1025]{1,0:T(8,128)S(1)} %get-tuple-element.37), channel_id=1, source_target_pairs={{0,8},{8,16},{16,24},{24,0},{1,9},{9,17},{17,25},{25,1},{2,10},{10... | collective-permute-start | bytes 98408 | tf_op jit(solution)/shard_map/ppermute | solution.py:132
  245.2 4.7 %collective-permute-start.7 = (f32[8,1025]{1,0:T(8,128)S(1)}, f32[8,1025]{1,0:T(8,128)S(1)}, u32[]{:S(2)}, u32[]{:S(2)}) collective-permute-start(f32[8,1025]{1,0:T(8,128)S(1)} %get-tuple-element.37), channel_id=1, source_target_pairs={{0,16},{8,24},{16,0},{24,8},{1,17},{9,25},{17,1},{25,9},{2,18},{10... | collective-permute-start | bytes 98408 | tf_op jit(solution)/shard_map/ppermute | solution.py:132
  245.5 4.4 %collective-permute-start.8 = (f32[8,1025]{1,0:T(8,128)S(1)}, f32[8,1025]{1,0:T(8,128)S(1)}, u32[]{:S(2)}, u32[]{:S(2)}) collective-permute-start(f32[8,1025]{1,0:T(8,128)S(1)} %get-tuple-element.37), channel_id=1, source_target_pairs={{0,24},{8,0},{16,8},{24,16},{1,25},{9,1},{17,9},{25,17},{2,26},{10... | collective-permute-start | bytes 98408 | tf_op jit(solution)/shard_map/ppermute | solution.py:132
  251.6 3.6 %collective-permute-start.9 = (f32[8]{0:T(128)S(1)}, f32[8]{0:T(128)S(1)}, u32[]{:S(2)}, u32[]{:S(2)}) collective-permute-start(f32[8]{0:T(128)S(1)} %get-tuple-element.42), channel_id=1, source_target_pairs={{0,1},{1,0},{2,3},{3,2},{4,5},{5,4},{6,7},{7,6},{8,9},{9,8},{10,11... | collective-permute-start | bytes 104 | tf_op jit(solution)/shard_map/ppermute | solution.py:149
  255.2 3.5 %collective-permute-start.10 = (f32[8]{0:T(128)S(1)}, f32[8]{0:T(128)S(1)}, u32[]{:S(2)}, u32[]{:S(2)}) collective-permute-start(f32[8]{0:T(128)S(1)} %max.9), channel_id=1, source_target_pairs={{0,2},{1,3},{2,0},{3,1},{4,6},{5,7},{6,4},{7,5},{8,10},{9,11},{10,... | collective-permute-start | bytes 104 | tf_op jit(solution)/shard_map/ppermute | solution.py:149
  258.7 4.4 %collective-permute-start.11 = (f32[8]{0:T(128)S(1)}, f32[8]{0:T(128)S(1)}, u32[]{:S(2)}, u32[]{:S(2)}) collective-permute-start(f32[8]{0:T(128)S(1)} %max.10), channel_id=1, source_target_pairs={{0,4},{1,5},{2,6},{3,7},{4,0},{5,1},{6,2},{7,3},{8,12},{9,13},{10,... | collective-permute-start | bytes 104 | tf_op jit(solution)/shard_map/ppermute | solution.py:149
Sparse Core Ops, SparseCore 0:
  27.6 37.1 all-reduce.1
  68.4 20.2 all-gather.5
  100.3 75.8 all-gather.7
  203.7 31.8 all-gather.9

commit v7 on v6

--- a/solution.py
+++ b/solution.py
@@ -282,11 +282,6 @@
     shipped = jnp.concatenate([shipped, extras.reshape(extra_rows, ship_width)], axis=0)
     gathered = lax.all_gather(shipped, "blk", axis=0, tiled=False)
     gathered, weight_pieces = lax.optimization_barrier((gathered, weight_pieces))
-    out_weights = jnp.take(
-        jnp.stack(weight_pieces),
-        (me_kv - jnp.arange(kv_count, dtype=jnp.int32)) % kv_count,
-        axis=0,
-    )
     blocks = gathered.shape[0]
     q_cols = query_proj.shape[1]
     extras_all = gathered[:, tok_rows:].reshape(blocks, -1)[:, : reqs * (q_cols + feat_dev)]
@@ -345,10 +340,14 @@
     last_context = jnp.concatenate(last_parts, axis=1).astype(jnp.bfloat16)
     out_rows = jnp.concatenate([context, last_context], axis=0)
     context_all = lax.all_gather(out_rows, "kv", axis=0, tiled=False)
-    group_parts = jnp.einsum(
-        "grc,gcf->grf", context_all, out_weights, preferred_element_type=jnp.float32
-    )
-    head_sum = jnp.sum(group_parts.astype(jnp.bfloat16).astype(jnp.float32), axis=0)
+    head_sum = None
+    for shift, piece in enumerate(weight_pieces):
+        source = lax.dynamic_index_in_dim(
+            context_all, (me_kv - shift) % kv_count, 0, keepdims=False
+        )
+        part = jnp.dot(source, piece, preferred_element_type=jnp.float32)
+        part = part.astype(jnp.bfloat16).astype(jnp.float32)
+        head_sum = part if head_sum is None else head_sum + part
     hidden = (seq_in.astype(jnp.float32) + head_sum[:tok_rows]).astype(jnp.bfloat16)
     chosen = (seq_last + head_sum[tok_rows:]).astype(jnp.bfloat16).astype(jnp.float32)
     square_part = jnp.sum(chosen * chosen, axis=-1)

time: 271 us -> 269 us (level)
  waiting for transfers between devices: 126 us -> 134 us
  other arithmetic: 30.9 us -> 24.9 us
  local copies, waits for them, and re-layouts: 34.8 us -> 29 us
    all_gather x1, waiting for transfers between devices: 23.4 us -> 31.9 us  [on_device(): context_all = lax.all_gather(out_rows, 'kv', axis=0, tiled=False)]
    gather x1 -> x0, local copies, waits for them, and re-layouts: 4.97 us -> none  [on_device(): jnp.take(jnp.stack(weight_pieces), (me_kv - jnp.arange(kv_count, dtype=jn...]
    another operation x5 -> x4, other arithmetic: 4.04 us -> 0.45 us  [the longest x1 3.59 us: on_device(): jnp.stack(weight_pieces)]
    dot_general x1 -> x4, matrix products: 5.58 us -> 8.02 us  [on_device(): part = jnp.dot(source, piece, preferred_element_type=jnp.float32)]
  transfers between devices with their start and end apart: 16 -> 16, of which waited for: 10 -> 10; matrix products, arithmetic and copies ran while one was open for 24% -> 20% of each run, Pallas kernels for 0% -> 0%
where the time goes in v7:
time: 269 us
  waiting for transfers between devices  134 us (50%)
  matrix products  37 us (14%)
  local copies, waits for them, and re-layouts  29 us (11%)
  other arithmetic  24.9 us (9%)
  starting transfers between devices  14.6 us (5%)
  between operations  14.4 us (5%)
  Pallas kernels  14.2 us (5%)
    ppermute x3, waiting for transfers between devices, on_device(): lax.ppermute(payload, 'kv', perm=[(i, (i + shift) % kv_count) for i in ra...  39.5 us
    all_gather x1, waiting for transfers between devices, on_device(): context_all = lax.all_gather(out_rows, 'kv', axis=0, tiled=False)  31.9 us
    psum x1, waiting for transfers between devices, on_device(): lax.psum(head_pooled.astype(jnp.bfloat16), 'kv').astype(jnp.float32)  29 us
    all_gather x1, waiting for transfers between devices, on_device(): gathered = lax.all_gather(shipped, 'blk', axis=0, tiled=False)  24.1 us
    pallas_call x1, Pallas kernels, flash_attention(): pl.pallas_call(functools.partial(flash_kernel, root=root), grid_spec=grid...  14.2 us
    dot_general x4, matrix products, on_device(): part = jnp.dot(source, piece, preferred_element_type=jnp.float32)  8.02 us
    ppermute x3, starting transfers between devices, tree_max(): lax.ppermute(values, axis, perm=[(i, i ^ step) for i in range(count)])  6.13 us
    ppermute x3, waiting for transfers between devices, tree_max(): lax.ppermute(values, axis, perm=[(i, i ^ step) for i in range(count)])  5.44 us
  transfers between devices with their start and end apart: 16, of which 10 were waited for; matrix products, arithmetic and copies ran while one was open for 20% of the time, Pallas kernels for 0%

profile of v7, /device:TPU:0, one launch (start us, length us, event | category | flops | bytes accessed | tf_op | source)
XLA Modules:
  0.0 268.5 jit_solution(4367086177824807446)
XLA Ops:
  7.8 2.6 collective-permute-start.1
  10.3 1.4 collective-permute-start.2
  11.7 2.0 convert_reduce_fusion
  14.5 2.9 %fusion.30 = bf16[3,256,3,352]{1,3,2,0:T(8,128)(2,1)S(1)} fusion(bf16[1408,3,352]{0,2,1:T(8,128)(2,1)S(1)} %copy-done, bf16[3,256,1408]{2,1,0:T(8,128)(2,1)S(1)} %copy-done.2, f32[1408]{0:T(1024)S(1)} %copy-done.17, f32[3,256]{1,0:T(4,128)S(1)} %add_rsqrt_fusion, f32[3,256]{1,0:T(4,128)S(1)} %broadcast_multiply_fusion), kind=kOutput, calls=%fused_computation.46 | convolution fusion | flops 2290016256 | bytes 6770176 | tf_op jit(solution)/shard_map/pnd,dce->pnce/dot_general | solution.py:181
  21.4 2.7 %convolution_reduce_fusion = f32[3,64,1408]{2,1,0:T(8,128)S(1)} fusion(bf16[352,1408]{1,0:T(8,128)(2,1)} %param.20, bf16[3,64,4,352]{3,2,1,0:T(4,128)(2,1)S(1)} %dot_general.65), kind=kOutput, calls=%fused_computation.45 | convolution fusion | flops 762077184 | bytes 2613248 | tf_op jit(solution)/shard_map/pnc,cd->pnd/dot_general | solution.py:204
  25.5 2.9 %reshape.368 = f32[3,64,4,1408]{3,2,1,0:T(4,128)} reshape(bf16[3,256,1408]{2,1,0:T(8,128)(2,1)S(1)} %copy-done.3) | data formatting | bytes 6488064 | tf_op jit(solution)/shard_map/reshape | solution.py:207
  28.5 4.8 %reduce_sum.136 = f32[3,64,1408]{2,1,0:T(8,128)S(1)} reduce(f32[3,64,4,1408]{3,2,1,0:T(4,128)} %reshape.368, f32[]{:T(128)} %constant.144.clone.1), dimensions={2}, to_apply=%region_1.2 | reduce | flops 811008 | bytes 5406724 | tf_op jit(solution)/shard_map/reduce_sum | solution.py:207
  33.5 29.0 %all-reduce.2.cloned.1.call-done = bf16[3,64,1408]{2,1,0:T(8,128)(2,1)} async-done(((bf16[3,64,1408]{2,1,0:T(8,128)(2,1)}), bf16[3,64,1408]{2,1,0:T(8,128)(2,1)}) %all-reduce.2.cloned.1.call-update) | async-done | bytes 540688 | tf_op jit(solution)/shard_map/psum | solution.py:206
  62.5 3.5 %fusion.45 = bf16[3,64,1024]{2,1,0:T(8,128)(2,1)} fusion(bf16[1408,1024]{1,0:T(8,128)(2,1)} %param.21, bf16[3,64,1408]{2,1,0:T(8,128)(2,1)} %all-reduce.2.cloned.1.call-done, f32[3,64,1408]{2,1,0:T(8,128)S(1)} %reduce_sum.136), kind=kOutput, calls=%fused_computation.59 | convolution fusion | flops 554926080 | bytes 4898816 | tf_op jit(solution)/shard_map/pmd,de->pme/dot_general | solution.py:209
  66.9 1.6 fusion.44
  68.7 3.7 %pad_maximum_fusion = bf16[4,512,1024]{2,1,0:T(8,128)(2,1)} fusion(bf16[1,512,1024]{2,1,0:T(8,128)(2,1)} %bitcast.21, bf16[1,512,1024]{2,1,0:T(8,128)(2,1)} %bitcast.20, bf16[1,512,1024]{2,1,0:T(8,128)(2,1)} %bitcast.19, bf16[1,512,1024]{2,1,0:T(8,128)(2,1)S(1)} %bitcast.173), kind=kLoop, calls=%fused_computation.23 | loop fusion | flops 6291456 | bytes 8388608 | tf_op jit(solution)/shard_map/stack | solution.py:122
  72.4 5.3 %gather_fusion = bf16[4,512,1024]{2,1,0:T(8,128)(2,1)} fusion(bf16[4,512,1024]{2,1,0:T(8,128)(2,1)} %pad_maximum_fusion, s32[1024]{0:T(1024)S(1)} %pad_clamp_fusion), kind=kCustom, calls=%fused_computation | custom fusion | bytes 8388624 | tf_op jit(solution)/shard_map/jit(_take)/gather | solution.py:124
  77.7 2.7 broadcast_select_fusion
  80.4 1.8 slice_bitcast_fusion.3
  82.1 4.2 %all-gather.6.cloned.1.call-done = bf16[192,4096]{1,0:T(8,128)(2,1)} async-done(((bf16[192,1024]{1,0:T(8,128)(2,1)}), bf16[192,4096]{1,0:T(8,128)(2,1)}) %all-gather.6.cloned.1.call-update) | async-done | bytes 1572880 | tf_op jit(solution)/shard_map/all_gather | solution.py:237
  86.3 4.2 %fusion.2 = (f32[512]{0:T(512)S(1)}, bf16[512,4096]{1,0:T(8,128)(2,1)S(1)}) fusion(bf16[512,1024]{1,0:T(8,128)(2,1)S(1)} %get-tuple-element.28, bf16[512,1024]{1,0:T(8,128)(2,1)} %get-tuple-element.29, bf16[512,1024]{1,0:T(8,128)(2,1)} %get-tuple-element.30, bf16[512,1024]{1,0:T(8,128)(2,1)S(1)} %get-tuple-element.27, ...), kind=kOutput, calls=%fused_computation.6 | convolution fusion | flops 832667136 | bytes 9964800 | tf_op jit(solution)/shard_map/dot_general | solution.py:240
  90.6 2.6 fusion.14
  93.3 2.6 fusion.49
  96.7 1.0 copy.80
  99.7 3.9 %constant_dynamic-slice_fusion = (bf16[512,1024]{1,0:T(8,128)(2,1)S(1)}, bf16[512,1024]{1,0:T(8,128)(2,1)}, bf16[512,1024]{1,0:T(8,128)(2,1)}, bf16[512,1024]{1,0:T(8,128)(2,1)}) fusion(bf16[512,4096]{1,0:T(8,128)(2,1)} %param.26, s32[]{:T(128)S(6)} %select_n.159, s32[]{:T(128)S(6)} %select_n.157, s32[]{:T(128)S(6)} %select_n.155, s32[]{:T(128)S(6)} %select_n.153), kind=kLoop, calls=%fused_computation.162 | loop fusion | bytes 8388624 | tf_op jit(solution)/shard_map/dynamic_slice | solution.py:216
  104.2 1.2 collective-permute-start.5
  105.5 1.2 and_convert_fusion.needed_ref
  109.0 1.1 copy.77
  110.1 18.6 %collective-permute-done.3 = bf16[512,1024]{1,0:T(8,128)(2,1)} collective-permute-done((bf16[512,1024]{1,0:T(8,128)(2,1)}, bf16[512,1024]{1,0:T(8,128)(2,1)}, u32[]{:S(2)}, u32[]{:S(2)}) %collective-permute-start.3) | collective-permute-done | bytes 1048608 | tf_op jit(solution)/shard_map/ppermute | solution.py:220
  128.7 1.6 collective-permute-done.4
  130.2 19.4 %collective-permute-done.5 = bf16[512,1024]{1,0:T(8,128)(2,1)} collective-permute-done((bf16[512,1024]{1,0:T(8,128)(2,1)S(1)}, bf16[512,1024]{1,0:T(8,128)(2,1)}, u32[]{:S(2)}, u32[]{:S(2)}) %collective-permute-start.5) | collective-permute-done | bytes 1048608 | tf_op jit(solution)/shard_map/ppermute | solution.py:220
  149.7 24.1 %all-gather.8.cloned.1.call-done = bf16[4288,512]{1,0:T(8,128)(2,1)} async-done(((bf16[536,512]{1,0:T(8,128)(2,1)}), bf16[4288,512]{1,0:T(8,128)(2,1)}) %all-gather.8.cloned.1.call-update) | async-done | bytes 4390928 | tf_op jit(solution)/shard_map/all_gather | solution.py:283
  173.8 4.0 %fusion.107 = (bf16[8,512,128]{2,1,0:T(8,128)(2,1)}, bf16[8,512,128]{2,1,0:T(8,128)(2,1)S(1)}, bf16[8,512,128]{2,1,0:T(8,128)(2,1)}, bf16[8,512,128]{2,1,0:T(8,128)(2,1)S(1)}) fusion(bf16[8,536,512]{2,1,0:T(8,128)(2,1)} %bitcast.156), kind=kLoop, calls=%fused_computation.189 | loop fusion | bytes 8388608 | tf_op jit(solution)/shard_map/slice | solution.py:319
  178.8 14.2 %shard_map.166 = bf16[2,1024,128]{2,1,0:T(8,128)(2,1)} custom-call(s32[8]{0:T(128)} %and_convert_fusion.needed_ref, bf16[2,1024,128]{2,1,0:T(8,128)(2,1)} %bitcast.174, bf16[8,536,512]{2,1,0:T(8,128)(2,1)} %bitcast.158, bf16[8,536,512]{2,1,0:T(8,128)(2,1)} %bitcast.159, s32[1024,1]{1,0:T(8,128)} %broadcast_in_dim_reshape.9.qid_ref, ...), custom_call_target="tpu_custom_call" | custom-call | flops 4294967296 | bytes 5242880 | tf_op jit(solution)/shard_map/pallas_call | solution.py:102
  193.0 1.3 copy.83
  194.4 1.8 fusion.109
  196.2 1.8 fusion.108
  198.8 1.0 copy.85
  199.9 31.9 %all-gather.10.cloned.1.call-done = bf16[2080,512]{1,0:T(8,128)(2,1)} async-done(((bf16[520,512]{1,0:T(8,128)(2,1)}), bf16[2080,512]{1,0:T(8,128)(2,1)}) %all-gather.10.cloned.1.call-update) | async-done | bytes 2129936 | tf_op jit(solution)/shard_map/all_gather | solution.py:342
  231.8 1.9 convolution_convert_fusion.4
  233.7 2.1 convolution_convert_fusion.3
  235.9 2.0 convolution_convert_fusion.2
  237.9 2.0 convert_add_fusion
  239.9 1.3 copy-done.4
  241.5 2.4 fusion.86
  244.5 1.2 collective-permute-start.8
  245.7 2.5 fusion.29
  249.9 1.8 collective-permute-start.9
  251.6 1.8 collective-permute-done.9
  253.5 1.7 collective-permute-start.10
  255.2 1.8 collective-permute-done.10
  257.0 2.6 collective-permute-start.11
  259.7 1.8 collective-permute-done.11
  (120 shorter events, 18.3 us)
Async XLA Ops:
  7.2 7.4 %copy-start = (bf16[1408,3,352]{0,2,1:T(8,128)(2,1)S(1)}, bf16[1408,3,352]{0,2,1:T(8,128)(2,1)}, u32[]{:S(2)}) copy-start(bf16[1408,3,352]{0,2,1:T(8,128)(2,1)} %param.19) | copy-start | bytes 8921092
  7.2 7.2 %copy-start.11 = (s32[3,2]{0,1:T(2,128)S(1)}, s32[3,2]{0,1:T(2,128)}, u32[]{:S(2)}) copy-start(s32[3,2]{0,1:T(2,128)} %param.16) | copy-start | bytes 76
  7.2 7.3 %copy-start.17 = (f32[1408]{0:T(1024)S(1)}, f32[1408]{0:T(1024)}, u32[]{:S(2)}) copy-start(f32[1408]{0:T(1024)} %param.18) | copy-start | bytes 16900
  7.2 55.3 %all-reduce.2.cloned.1.call-start = ((), (), s32[]{:S(2)}) async-start(), calls=%async_computation | async-start | bytes 1081344 | tf_op jit(solution)/shard_map/psum | solution.py:206
  7.2 6.4 %copy-start.2 = (bf16[3,256,1408]{2,1,0:T(8,128)(2,1)S(1)}, bf16[3,256,1408]{2,1,0:T(8,128)(2,1)}, u32[]{:S(2)}) copy-start(bf16[3,256,1408]{2,1,0:T(8,128)(2,1)} %param.15) | copy-start | bytes 6488068
  7.3 61.5 %collective-permute-start = (bf16[512,1024]{1,0:T(8,128)(2,1)}, bf16[512,1024]{1,0:T(8,128)(2,1)}, u32[]{:S(2)}, u32[]{:S(2)}) collective-permute-start(bf16[512,1024]{1,0:T(8,128)(2,1)} %param.22), channel_id=1, source_target_pairs={{0,8},{8,16},{16,24},{24,0},{1,9},{9,17},{17,25},{25,1},{2,10},{10... | collective-permute-start | bytes 3145736 | tf_op jit(solution)/shard_map/ppermute | solution.py:120
  7.8 61.0 %collective-permute-start.1 = (bf16[512,1024]{1,0:T(8,128)(2,1)}, bf16[512,1024]{1,0:T(8,128)(2,1)}, u32[]{:S(2)}, u32[]{:S(2)}) collective-permute-start(bf16[512,1024]{1,0:T(8,128)(2,1)} %param.22), channel_id=1, source_target_pairs={{0,16},{8,24},{16,0},{24,8},{1,17},{9,25},{17,1},{25,9},{2,18},{10... | collective-permute-start | bytes 3145736 | tf_op jit(solution)/shard_map/ppermute | solution.py:120
  10.3 58.4 %collective-permute-start.2 = (bf16[512,1024]{1,0:T(8,128)(2,1)}, bf16[512,1024]{1,0:T(8,128)(2,1)}, u32[]{:S(2)}, u32[]{:S(2)}) collective-permute-start(bf16[512,1024]{1,0:T(8,128)(2,1)} %param.22), channel_id=1, source_target_pairs={{0,24},{8,0},{16,8},{24,16},{1,25},{9,1},{17,9},{25,17},{2,26},{10... | collective-permute-start | bytes 3145736 | tf_op jit(solution)/shard_map/ppermute | solution.py:120
  21.3 3.8 %copy-start.13 = (s32[8]{0:T(128)S(1)}, s32[8]{0:T(128)}, u32[]{:S(2)}) copy-start(s32[8]{0:T(128)} %param.27) | copy-start | bytes 100
  21.4 4.0 %copy-start.12 = (s32[3]{0:T(128)S(1)}, s32[3]{0:T(128)}, u32[]{:S(2)}) copy-start(s32[3]{0:T(128)} %param.17) | copy-start | bytes 40
  21.4 4.1 %copy-start.3 = (bf16[3,256,1408]{2,1,0:T(8,128)(2,1)S(1)}, bf16[3,256,1408]{2,1,0:T(8,128)(2,1)}, u32[]{:S(2)}) copy-start(bf16[3,256,1408]{2,1,0:T(8,128)(2,1)} %param.15) | copy-start | bytes 6488068
  25.0 61.3 %all-gather.6.cloned.1.call-start = ((), (), s32[]{:S(2)}) async-start(), calls=%async_computation.1 | async-start | bytes 1966080 | tf_op jit(solution)/shard_map/all_gather | solution.py:237
  33.3 33.6 %copy-start.8 = (bf16[512,1024]{1,0:T(8,128)(2,1)S(1)}, bf16[512,1024]{1,0:T(8,128)(2,1)}, u32[]{:S(2)}) copy-start(bf16[512,1024]{1,0:T(8,128)(2,1)} %param.22) | copy-start | bytes 3145732
  66.0 107.8 %all-gather.8.cloned.1.call-start = ((), (), s32[]{:S(2)}) async-start(), calls=%async_computation.2 | async-start | bytes 4939776 | tf_op jit(solution)/shard_map/all_gather | solution.py:283
  68.4 4.0 %copy-start.6 = (bf16[512,1024]{1,0:T(8,128)(2,1)}, bf16[512,1024]{1,0:T(8,128)(2,1)S(1)}, u32[]{:S(2)}) copy-start(bf16[512,1024]{1,0:T(8,128)(2,1)S(1)} %fusion.44) | copy-start | bytes 3145732
  86.3 4.2 %copy-start.14 = (bf16[4096,2,256]{2,1,0:T(2,128)(2,1)S(1)}, bf16[4096,2,256]{2,1,0:T(2,128)(2,1)}, u32[]{:S(2)}) copy-start(bf16[4096,2,256]{2,1,0:T(2,128)(2,1)} %param.25) | copy-start | bytes 12582916
  86.3 4.2 %copy-start.16 = (f32[4096]{0:T(1024)S(1)}, f32[4096]{0:T(1024)}, u32[]{:S(2)}) copy-start(f32[4096]{0:T(1024)} %param.23) | copy-start | bytes 49156
  90.6 2.7 %copy-start.15 = (bf16[4096,512]{1,0:T(8,128)(2,1)S(1)}, bf16[4096,512]{1,0:T(8,128)(2,1)}, u32[]{:S(2)}) copy-start(bf16[4096,512]{1,0:T(8,128)(2,1)} %param.24) | copy-start | bytes 12582916
  97.8 134.0 %all-gather.10.cloned.1.call-start = ((), (), s32[]{:S(2)}) async-start(), calls=%async_computation.3 | async-start | bytes 2662400 | tf_op jit(solution)/shard_map/all_gather | solution.py:342
  103.7 25.0 %collective-permute-start.3 = (bf16[512,1024]{1,0:T(8,128)(2,1)}, bf16[512,1024]{1,0:T(8,128)(2,1)}, u32[]{:S(2)}, u32[]{:S(2)}) collective-permute-start(bf16[512,1024]{1,0:T(8,128)(2,1)} %get-tuple-element.25), channel_id=1, source_target_pairs={{0,8},{8,16},{16,24},{24,0},{1,9},{9,17},{17,25},{25,1},{2,10},{10... | collective-permute-start | bytes 3145736 | tf_op jit(solution)/shard_map/ppermute | solution.py:220
  103.9 26.3 %collective-permute-start.4 = (bf16[512,1024]{1,0:T(8,128)(2,1)}, bf16[512,1024]{1,0:T(8,128)(2,1)}, u32[]{:S(2)}, u32[]{:S(2)}) collective-permute-start(bf16[512,1024]{1,0:T(8,128)(2,1)} %get-tuple-element.24), channel_id=1, source_target_pairs={{0,16},{8,24},{16,0},{24,8},{1,17},{9,25},{17,1},{25,9},{2,18},{10... | collective-permute-start | bytes 3145736 | tf_op jit(solution)/shard_map/ppermute | solution.py:220
  104.2 45.4 %collective-permute-start.5 = (bf16[512,1024]{1,0:T(8,128)(2,1)S(1)}, bf16[512,1024]{1,0:T(8,128)(2,1)}, u32[]{:S(2)}, u32[]{:S(2)}) collective-permute-start(bf16[512,1024]{1,0:T(8,128)(2,1)S(1)} %get-tuple-element.23), channel_id=1, source_target_pairs={{0,24},{8,0},{16,8},{24,16},{1,25},{9,1},{17,9},{25,17},{2,26},{10... | collective-permute-start | bytes 3145736 | tf_op jit(solution)/shard_map/ppermute | solution.py:220
  198.3 33.5 %copy-start.7 = (bf16[512,1024]{1,0:T(8,128)(2,1)S(1)}, bf16[512,1024]{1,0:T(8,128)(2,1)}, u32[]{:S(2)}) copy-start(bf16[512,1024]{1,0:T(8,128)(2,1)} %get-tuple-element.13) | copy-start | bytes 3145732
  231.8 4.1 %copy-start.9 = (bf16[2080,512]{1,0:T(8,128)(2,1)S(1)}, bf16[2080,512]{1,0:T(8,128)(2,1)}, u32[]{:S(2)}) copy-start(bf16[2080,512]{1,0:T(8,128)(2,1)} %all-gather.10.cloned.1.call-done) | copy-start | bytes 6389764
  237.9 3.6 %copy-start.10 = (f32[1024]{0:T(1024)S(1)}, f32[1024]{0:T(1024)}, u32[]{:S(2)}) copy-start(f32[1024]{0:T(1024)} %param.28) | copy-start | bytes 12292
  239.9 1.4 copy-start.4
  241.5 4.3 %copy-start.5 = (f32[520,1024]{1,0:T(8,128)S(1)}, f32[520,1024]{1,0:T(8,128)}, u32[]{:S(2)}) copy-start(f32[520,1024]{1,0:T(8,128)} %copy-done.4) | copy-start | bytes 6389764
  241.5 20.5 %copy-start.1 = (bf16[1408,3,352]{0,2,1:T(8,128)(2,1)S(1)}, bf16[1408,3,352]{0,2,1:T(8,128)(2,1)}, u32[]{:S(2)}) copy-start(bf16[1408,3,352]{0,2,1:T(8,128)(2,1)} %param.19) | copy-start | bytes 8921092
  243.9 4.4 %collective-permute-start.6 = (f32[8,1025]{1,0:T(8,128)S(1)}, f32[8,1025]{1,0:T(8,128)S(1)}, u32[]{:S(2)}, u32[]{:S(2)}) collective-permute-start(f32[8,1025]{1,0:T(8,128)S(1)} %get-tuple-element.36), channel_id=1, source_target_pairs={{0,8},{8,16},{16,24},{24,0},{1,9},{9,17},{17,25},{25,1},{2,10},{10... | collective-permute-start | bytes 98408 | tf_op jit(solution)/shard_map/ppermute | solution.py:132
  244.2 4.1 %collective-permute-start.7 = (f32[8,1025]{1,0:T(8,128)S(1)}, f32[8,1025]{1,0:T(8,128)S(1)}, u32[]{:S(2)}, u32[]{:S(2)}) collective-permute-start(f32[8,1025]{1,0:T(8,128)S(1)} %get-tuple-element.36), channel_id=1, source_target_pairs={{0,16},{8,24},{16,0},{24,8},{1,17},{9,25},{17,1},{25,9},{2,18},{10... | collective-permute-start | bytes 98408 | tf_op jit(solution)/shard_map/ppermute | solution.py:132
  244.5 3.8 %collective-permute-start.8 = (f32[8,1025]{1,0:T(8,128)S(1)}, f32[8,1025]{1,0:T(8,128)S(1)}, u32[]{:S(2)}, u32[]{:S(2)}) collective-permute-start(f32[8,1025]{1,0:T(8,128)S(1)} %get-tuple-element.36), channel_id=1, source_target_pairs={{0,24},{8,0},{16,8},{24,16},{1,25},{9,1},{17,9},{25,17},{2,26},{10... | collective-permute-start | bytes 98408 | tf_op jit(solution)/shard_map/ppermute | solution.py:132
  249.9 3.6 %collective-permute-start.9 = (f32[8]{0:T(128)S(1)}, f32[8]{0:T(128)S(1)}, u32[]{:S(2)}, u32[]{:S(2)}) collective-permute-start(f32[8]{0:T(128)S(1)} %get-tuple-element.41), channel_id=1, source_target_pairs={{0,1},{1,0},{2,3},{3,2},{4,5},{5,4},{6,7},{7,6},{8,9},{9,8},{10,11... | collective-permute-start | bytes 104 | tf_op jit(solution)/shard_map/ppermute | solution.py:149
  253.5 3.5 %collective-permute-start.10 = (f32[8]{0:T(128)S(1)}, f32[8]{0:T(128)S(1)}, u32[]{:S(2)}, u32[]{:S(2)}) collective-permute-start(f32[8]{0:T(128)S(1)} %max.9), channel_id=1, source_target_pairs={{0,2},{1,3},{2,0},{3,1},{4,6},{5,7},{6,4},{7,5},{8,10},{9,11},{10,... | collective-permute-start | bytes 104 | tf_op jit(solution)/shard_map/ppermute | solution.py:149
  257.0 4.4 %collective-permute-start.11 = (f32[8]{0:T(128)S(1)}, f32[8]{0:T(128)S(1)}, u32[]{:S(2)}, u32[]{:S(2)}) collective-permute-start(f32[8]{0:T(128)S(1)} %max.10), channel_id=1, source_target_pairs={{0,4},{1,5},{2,6},{3,7},{4,0},{5,1},{6,2},{7,3},{8,12},{9,13},{10,... | collective-permute-start | bytes 104 | tf_op jit(solution)/shard_map/ppermute | solution.py:149
Sparse Core Ops, SparseCore 0:
  25.1 37.3 all-reduce.1
  66.2 20.1 all-gather.5
  97.9 75.8 all-gather.7
  200.0 31.8 all-gather.9

commit v8 on v7

--- a/solution.py
+++ b/solution.py
@@ -54,22 +54,32 @@
         sum_ref[...] = jnp.zeros(sum_ref.shape, jnp.float32)
         acc_ref[...] = jnp.zeros(acc_ref.shape, jnp.float32)
 
-    @pl.when(needed_ref[kb] != 0)
-    def _():
+    def accumulate(masked):
         scores = lax.dot_general(
             q_ref[...], k_ref[...], (((1,), (1,)), ((), ())), preferred_element_type=jnp.float32
         ) / root
-        allowed = (kid_ref[...] <= qid_ref[...]) & (kreq_ref[...] == qreq_ref[...])
-        scores = jnp.where(allowed, scores, -1e30)
+        if masked:
+            allowed = (kid_ref[...] <= qid_ref[...]) & (kreq_ref[...] == qreq_ref[...])
+            scores = jnp.where(allowed, scores, -1e30)
         old_max = max_ref[...]
         new_max = jnp.maximum(old_max, jnp.max(scores, axis=1, keepdims=True))
-        weights = jnp.where(allowed, jnp.exp(scores - new_max), 0.0)
+        weights = jnp.exp(scores - new_max)
+        if masked:
+            weights = jnp.where(allowed, weights, 0.0)
         scale = jnp.exp(old_max - new_max)
         sum_ref[...] = sum_ref[...] * scale + jnp.sum(weights, axis=1, keepdims=True)
         acc_ref[...] = acc_ref[...] * scale + jnp.dot(
             weights.astype(jnp.bfloat16), v_ref[...], preferred_element_type=jnp.float32
         )
         max_ref[...] = new_max
+
+    @pl.when(needed_ref[kb] == 1)
+    def _():
+        accumulate(True)
+
+    @pl.when(needed_ref[kb] == 2)
+    def _():
+        accumulate(False)
 
     @pl.when(kb == pl.num_programs(1) - 1)
     def _():
@@ -142,6 +152,14 @@
 
 
 def tree_max(values, axis, count):
+    if count <= 8:
+        result = values
+        for shift in range(1, count):
+            result = jnp.maximum(
+                result,
+                lax.ppermute(values, axis, perm=[(i, (i + shift) % count) for i in range(count)]),
+            )
+        return result
     if count & (count - 1):
         return lax.pmax(values, axis)
     step = 1
@@ -302,6 +320,9 @@
     q_req = jnp.repeat(query_req, per_group)[:, None]
     all_ids = jnp.arange(blocks * tok_rows, dtype=jnp.int32)
     all_req, unused = request_info(all_ids, req_lengths)
+    block_first_req = all_req.reshape(blocks, tok_rows)[:, 0]
+    full = (block_ids < block_index) & (block_first_req == query_req[tok_rows - 1])
+    needed = jnp.where(full, 2, needed)
     k_ids = all_ids.reshape(blocks, 1, tok_rows)
     k_req = all_req.reshape(blocks, 1, tok_rows)
     context = flash_attention(

time: 269 us -> 276 us (1.026)
  starting transfers between devices: 14.6 us -> 19.9 us
    ppermute x3 -> x7, starting transfers between devices: 6.13 us -> 11.5 us  [tree_max(): lax.ppermute(values, axis, perm=[(i, (i + shift) % count) for i in range(...]
    ppermute x3 -> x7, waiting for transfers between devices: 5.44 us -> 5.66 us  [tree_max(): lax.ppermute(values, axis, perm=[(i, (i + shift) % count) for i in range(...]
  transfers between devices with their start and end apart: 16 -> 20, of which waited for: 10 -> 10; matrix products, arithmetic and copies ran while one was open for 20% -> 20% of each run, Pallas kernels for 0% -> 0%
where the time goes in v8:
time: 276 us; the launch traced here: 275 us
  waiting for transfers between devices  135 us (49%)
  matrix products  37 us (13%)
  local copies, waits for them, and re-layouts  29.6 us (11%)
  other arithmetic  25.1 us (9%)
  starting transfers between devices  19.9 us (7%)
  between operations  14.5 us (5%)
  Pallas kernels  14.3 us (5%)
    ppermute x3, waiting for transfers between devices, on_device(): lax.ppermute(payload, 'kv', perm=[(i, (i + shift) % kv_count) for i in ra...  40.1 us
    all_gather x1, waiting for transfers between devices, on_device(): context_all = lax.all_gather(out_rows, 'kv', axis=0, tiled=False)  32.8 us
    psum x1, waiting for transfers between devices, on_device(): lax.psum(head_pooled.astype(jnp.bfloat16), 'kv').astype(jnp.float32)  29 us
    all_gather x1, waiting for transfers between devices, on_device(): gathered = lax.all_gather(shipped, 'blk', axis=0, tiled=False)  22.8 us
    pallas_call x1, Pallas kernels, flash_attention(): pl.pallas_call(functools.partial(flash_kernel, root=root), grid_spec=grid...  14.3 us
    ppermute x7, starting transfers between devices, tree_max(): lax.ppermute(values, axis, perm=[(i, (i + shift) % count) for i in range(...  11.5 us
    dot_general x4, matrix products, on_device(): part = jnp.dot(source, piece, preferred_element_type=jnp.float32)  8.03 us
    ppermute x7, waiting for transfers between devices, tree_max(): lax.ppermute(values, axis, perm=[(i, (i + shift) % count) for i in range(...  5.66 us
  transfers between devices with their start and end apart: 20, of which 10 were waited for; matrix products, arithmetic and copies ran while one was open for 20% of the time, Pallas kernels for 0%

profile of v8, /device:TPU:0, one launch (start us, length us, event | category | flops | bytes accessed | tf_op | source)
XLA Modules:
  0.0 275.0 jit_solution(2495277746903822635)
XLA Ops:
  7.8 2.6 collective-permute-start.1
  10.3 1.4 collective-permute-start.2
  11.7 2.0 convert_reduce_fusion
  14.5 2.9 %fusion.30 = bf16[3,256,3,352]{1,3,2,0:T(8,128)(2,1)S(1)} fusion(bf16[1408,3,352]{0,2,1:T(8,128)(2,1)S(1)} %copy-done, bf16[3,256,1408]{2,1,0:T(8,128)(2,1)S(1)} %copy-done.2, f32[1408]{0:T(1024)S(1)} %copy-done.18, f32[3,256]{1,0:T(4,128)S(1)} %add_rsqrt_fusion, f32[3,256]{1,0:T(4,128)S(1)} %broadcast_multiply_fusion), kind=kOutput, calls=%fused_computation.46 | convolution fusion | flops 2290016256 | bytes 6770176 | tf_op jit(solution)/shard_map/pnd,dce->pnce/dot_general | solution.py:199
  21.4 2.7 convolution_reduce_fusion
  25.5 2.9 %reshape.373 = f32[3,64,4,1408]{3,2,1,0:T(4,128)} reshape(bf16[3,256,1408]{2,1,0:T(8,128)(2,1)S(1)} %copy-done.3) | data formatting | bytes 6488064 | tf_op jit(solution)/shard_map/reshape | solution.py:225
  28.5 4.8 %reduce_sum.136 = f32[3,64,1408]{2,1,0:T(8,128)S(1)} reduce(f32[3,64,4,1408]{3,2,1,0:T(4,128)} %reshape.373, f32[]{:T(128)} %constant.144.clone.1), dimensions={2}, to_apply=%region_1.2 | reduce | flops 811008 | bytes 5406724 | tf_op jit(solution)/shard_map/reduce_sum | solution.py:225
  33.5 29.0 %all-reduce.2.cloned.1.call-done = bf16[3,64,1408]{2,1,0:T(8,128)(2,1)} async-done(((bf16[3,64,1408]{2,1,0:T(8,128)(2,1)}), bf16[3,64,1408]{2,1,0:T(8,128)(2,1)}) %all-reduce.2.cloned.1.call-update) | async-done | bytes 540688 | tf_op jit(solution)/shard_map/psum | solution.py:224
  62.5 3.5 %fusion.45 = bf16[3,64,1024]{2,1,0:T(8,128)(2,1)} fusion(bf16[1408,1024]{1,0:T(8,128)(2,1)} %param.21, bf16[3,64,1408]{2,1,0:T(8,128)(2,1)} %all-reduce.2.cloned.1.call-done, f32[3,64,1408]{2,1,0:T(8,128)S(1)} %reduce_sum.136), kind=kOutput, calls=%fused_computation.59 | convolution fusion | flops 554926080 | bytes 4898816 | tf_op jit(solution)/shard_map/pmd,de->pme/dot_general | solution.py:227
  66.8 1.6 fusion.44
  68.7 3.7 %pad_maximum_fusion = bf16[4,512,1024]{2,1,0:T(8,128)(2,1)} fusion(bf16[1,512,1024]{2,1,0:T(8,128)(2,1)} %bitcast.22, bf16[1,512,1024]{2,1,0:T(8,128)(2,1)} %bitcast.21, bf16[1,512,1024]{2,1,0:T(8,128)(2,1)} %bitcast.20, bf16[1,512,1024]{2,1,0:T(8,128)(2,1)S(1)} %bitcast.174), kind=kLoop, calls=%fused_computation.23 | loop fusion | flops 6291456 | bytes 8388608 | tf_op jit(solution)/shard_map/stack | solution.py:132
  72.4 5.3 %gather_fusion = bf16[4,512,1024]{2,1,0:T(8,128)(2,1)} fusion(bf16[4,512,1024]{2,1,0:T(8,128)(2,1)} %pad_maximum_fusion, s32[1024]{0:T(1024)S(1)} %pad_clamp_fusion), kind=kCustom, calls=%fused_computation | custom fusion | bytes 8388624 | tf_op jit(solution)/shard_map/jit(_take)/gather | solution.py:134
  77.7 2.7 broadcast_select_fusion
  80.3 1.8 slice_bitcast_fusion.3
  82.1 4.2 %all-gather.6.cloned.1.call-done = bf16[192,4096]{1,0:T(8,128)(2,1)} async-done(((bf16[192,1024]{1,0:T(8,128)(2,1)}), bf16[192,4096]{1,0:T(8,128)(2,1)}) %all-gather.6.cloned.1.call-update) | async-done | bytes 1572880 | tf_op jit(solution)/shard_map/all_gather | solution.py:255
  86.3 4.2 %fusion.2 = (f32[512]{0:T(512)S(1)}, bf16[512,4096]{1,0:T(8,128)(2,1)S(1)}) fusion(bf16[512,1024]{1,0:T(8,128)(2,1)S(1)} %get-tuple-element.28, bf16[512,1024]{1,0:T(8,128)(2,1)} %get-tuple-element.29, bf16[512,1024]{1,0:T(8,128)(2,1)} %get-tuple-element.30, bf16[512,1024]{1,0:T(8,128)(2,1)S(1)} %get-tuple-element.27, ...), kind=kOutput, calls=%fused_computation.6 | convolution fusion | flops 832667136 | bytes 9964800 | tf_op jit(solution)/shard_map/dot_general | solution.py:258
  90.5 2.6 fusion.14
  93.3 2.6 fusion.49
  99.9 1.2 and_select_fusion.2.needed_ref
  101.0 3.9 %constant_dynamic-slice_fusion = (bf16[512,1024]{1,0:T(8,128)(2,1)S(1)}, bf16[512,1024]{1,0:T(8,128)(2,1)}, bf16[512,1024]{1,0:T(8,128)(2,1)}, bf16[512,1024]{1,0:T(8,128)(2,1)}) fusion(bf16[512,4096]{1,0:T(8,128)(2,1)} %param.26, s32[]{:T(128)S(6)} %select_n.164, s32[]{:T(128)S(6)} %select_n.162, s32[]{:T(128)S(6)} %select_n.160, s32[]{:T(128)S(6)} %select_n.158), kind=kLoop, calls=%fused_computation.165 | loop fusion | bytes 8388624 | tf_op jit(solution)/shard_map/dynamic_slice | solution.py:234
  105.5 1.2 collective-permute-start.5
  109.7 1.1 copy.77
  110.8 19.1 %collective-permute-done.3 = bf16[512,1024]{1,0:T(8,128)(2,1)} collective-permute-done((bf16[512,1024]{1,0:T(8,128)(2,1)}, bf16[512,1024]{1,0:T(8,128)(2,1)}, u32[]{:S(2)}, u32[]{:S(2)}) %collective-permute-start.3) | collective-permute-done | bytes 1048608 | tf_op jit(solution)/shard_map/ppermute | solution.py:238
  130.0 1.6 collective-permute-done.4
  131.5 19.4 %collective-permute-done.5 = bf16[512,1024]{1,0:T(8,128)(2,1)} collective-permute-done((bf16[512,1024]{1,0:T(8,128)(2,1)S(1)}, bf16[512,1024]{1,0:T(8,128)(2,1)}, u32[]{:S(2)}, u32[]{:S(2)}) %collective-permute-start.5) | collective-permute-done | bytes 1048608 | tf_op jit(solution)/shard_map/ppermute | solution.py:238
  151.0 22.8 %all-gather.8.cloned.1.call-done = bf16[4288,512]{1,0:T(8,128)(2,1)} async-done(((bf16[536,512]{1,0:T(8,128)(2,1)}), bf16[4288,512]{1,0:T(8,128)(2,1)}) %all-gather.8.cloned.1.call-update) | async-done | bytes 4390928 | tf_op jit(solution)/shard_map/all_gather | solution.py:301
  173.8 4.0 %fusion.108 = (bf16[8,512,128]{2,1,0:T(8,128)(2,1)}, bf16[8,512,128]{2,1,0:T(8,128)(2,1)S(1)}, bf16[8,512,128]{2,1,0:T(8,128)(2,1)}, bf16[8,512,128]{2,1,0:T(8,128)(2,1)S(1)}) fusion(bf16[8,536,512]{2,1,0:T(8,128)(2,1)} %bitcast.157), kind=kLoop, calls=%fused_computation.193 | loop fusion | bytes 8388608 | tf_op jit(solution)/shard_map/slice | solution.py:340
  178.8 14.3 %shard_map.166 = bf16[2,1024,128]{2,1,0:T(8,128)(2,1)} custom-call(s32[8]{0:T(128)} %and_select_fusion.2.needed_ref, bf16[2,1024,128]{2,1,0:T(8,128)(2,1)} %bitcast.175, bf16[8,536,512]{2,1,0:T(8,128)(2,1)} %bitcast.159, bf16[8,536,512]{2,1,0:T(8,128)(2,1)} %bitcast.160, s32[1024,1]{1,0:T(8,128)} %broadcast_in_dim_reshape.9.qid_ref, ...), custom_call_target="tpu_custom_call" | custom-call | flops 4294967296 | bytes 5242880 | tf_op jit(solution)/shard_map/pallas_call | solution.py:112
  193.0 1.3 copy.83
  194.4 1.8 fusion.110
  196.2 1.8 fusion.109
  199.9 32.8 %all-gather.10.cloned.1.call-done = bf16[2080,512]{1,0:T(8,128)(2,1)} async-done(((bf16[520,512]{1,0:T(8,128)(2,1)}), bf16[2080,512]{1,0:T(8,128)(2,1)}) %all-gather.10.cloned.1.call-update) | async-done | bytes 2129936 | tf_op jit(solution)/shard_map/all_gather | solution.py:363
  232.8 1.9 convolution_convert_fusion.4
  234.7 2.1 convolution_convert_fusion.3
  236.8 2.0 convolution_convert_fusion.2
  238.8 2.0 convert_add_fusion
  240.8 1.3 copy-done.4
  242.4 2.4 fusion.86
  245.4 1.3 collective-permute-start.8
  246.7 2.5 fusion.29
  250.8 1.8 collective-permute-start.10
  252.6 2.4 collective-permute-start.11
  255.0 1.4 collective-permute-start.12
  256.4 2.4 collective-permute-start.13
  258.8 1.4 collective-permute-start.14
  260.3 1.4 collective-permute-start.15
  262.4 1.4 collective-permute-done.15
  263.8 4.1 %collective-permute-done.9 = f32[8]{0:T(128)S(1)} collective-permute-done((f32[8]{0:T(128)S(1)}, f32[8]{0:T(128)S(1)}, u32[]{:S(2)}, u32[]{:S(2)}) %collective-permute-start.9) | collective-permute-done | bytes 64 | tf_op jit(solution)/shard_map/ppermute | solution.py:160
  (131 shorter events, 21.8 us)
Async XLA Ops:
  7.2 7.4 %copy-start = (bf16[1408,3,352]{0,2,1:T(8,128)(2,1)S(1)}, bf16[1408,3,352]{0,2,1:T(8,128)(2,1)}, u32[]{:S(2)}) copy-start(bf16[1408,3,352]{0,2,1:T(8,128)(2,1)} %param.19) | copy-start | bytes 8921092
  7.2 7.2 %copy-start.12 = (s32[3,2]{0,1:T(2,128)S(1)}, s32[3,2]{0,1:T(2,128)}, u32[]{:S(2)}) copy-start(s32[3,2]{0,1:T(2,128)} %param.16) | copy-start | bytes 76
  7.2 7.3 %copy-start.18 = (f32[1408]{0:T(1024)S(1)}, f32[1408]{0:T(1024)}, u32[]{:S(2)}) copy-start(f32[1408]{0:T(1024)} %param.18) | copy-start | bytes 16900
  7.2 55.2 %all-reduce.2.cloned.1.call-start = ((), (), s32[]{:S(2)}) async-start(), calls=%async_computation | async-start | bytes 1081344 | tf_op jit(solution)/shard_map/psum | solution.py:224
  7.2 6.4 %copy-start.2 = (bf16[3,256,1408]{2,1,0:T(8,128)(2,1)S(1)}, bf16[3,256,1408]{2,1,0:T(8,128)(2,1)}, u32[]{:S(2)}) copy-start(bf16[3,256,1408]{2,1,0:T(8,128)(2,1)} %param.15) | copy-start | bytes 6488068
  7.3 61.4 %collective-permute-start = (bf16[512,1024]{1,0:T(8,128)(2,1)}, bf16[512,1024]{1,0:T(8,128)(2,1)}, u32[]{:S(2)}, u32[]{:S(2)}) collective-permute-start(bf16[512,1024]{1,0:T(8,128)(2,1)} %param.22), channel_id=1, source_target_pairs={{0,8},{8,16},{16,24},{24,0},{1,9},{9,17},{17,25},{25,1},{2,10},{10... | collective-permute-start | bytes 3145736 | tf_op jit(solution)/shard_map/ppermute | solution.py:130
  7.8 60.9 %collective-permute-start.1 = (bf16[512,1024]{1,0:T(8,128)(2,1)}, bf16[512,1024]{1,0:T(8,128)(2,1)}, u32[]{:S(2)}, u32[]{:S(2)}) collective-permute-start(bf16[512,1024]{1,0:T(8,128)(2,1)} %param.22), channel_id=1, source_target_pairs={{0,16},{8,24},{16,0},{24,8},{1,17},{9,25},{17,1},{25,9},{2,18},{10... | collective-permute-start | bytes 3145736 | tf_op jit(solution)/shard_map/ppermute | solution.py:130
  10.3 58.4 %collective-permute-start.2 = (bf16[512,1024]{1,0:T(8,128)(2,1)}, bf16[512,1024]{1,0:T(8,128)(2,1)}, u32[]{:S(2)}, u32[]{:S(2)}) collective-permute-start(bf16[512,1024]{1,0:T(8,128)(2,1)} %param.22), channel_id=1, source_target_pairs={{0,24},{8,0},{16,8},{24,16},{1,25},{9,1},{17,9},{25,17},{2,26},{10... | collective-permute-start | bytes 3145736 | tf_op jit(solution)/shard_map/ppermute | solution.py:130
  21.3 3.8 %copy-start.14 = (s32[8]{0:T(128)S(1)}, s32[8]{0:T(128)}, u32[]{:S(2)}) copy-start(s32[8]{0:T(128)} %param.27) | copy-start | bytes 100
  21.4 4.0 %copy-start.13 = (s32[3]{0:T(128)S(1)}, s32[3]{0:T(128)}, u32[]{:S(2)}) copy-start(s32[3]{0:T(128)} %param.17) | copy-start | bytes 40
  21.4 4.1 %copy-start.3 = (bf16[3,256,1408]{2,1,0:T(8,128)(2,1)S(1)}, bf16[3,256,1408]{2,1,0:T(8,128)(2,1)}, u32[]{:S(2)}) copy-start(bf16[3,256,1408]{2,1,0:T(8,128)(2,1)} %param.15) | copy-start | bytes 6488068
  25.0 61.3 %all-gather.6.cloned.1.call-start = ((), (), s32[]{:S(2)}) async-start(), calls=%async_computation.1 | async-start | bytes 1966080 | tf_op jit(solution)/shard_map/all_gather | solution.py:255
  33.3 33.6 %copy-start.8 = (bf16[512,1024]{1,0:T(8,128)(2,1)S(1)}, bf16[512,1024]{1,0:T(8,128)(2,1)}, u32[]{:S(2)}) copy-start(bf16[512,1024]{1,0:T(8,128)(2,1)} %param.22) | copy-start | bytes 3145732
  66.0 107.8 %all-gather.8.cloned.1.call-start = ((), (), s32[]{:S(2)}) async-start(), calls=%async_computation.2 | async-start | bytes 4939776 | tf_op jit(solution)/shard_map/all_gather | solution.py:301
  68.4 4.0 %copy-start.6 = (bf16[512,1024]{1,0:T(8,128)(2,1)}, bf16[512,1024]{1,0:T(8,128)(2,1)S(1)}, u32[]{:S(2)}) copy-start(bf16[512,1024]{1,0:T(8,128)(2,1)S(1)} %fusion.44) | copy-start | bytes 3145732
  86.3 4.2 %copy-start.15 = (bf16[4096,2,256]{2,1,0:T(2,128)(2,1)S(1)}, bf16[4096,2,256]{2,1,0:T(2,128)(2,1)}, u32[]{:S(2)}) copy-start(bf16[4096,2,256]{2,1,0:T(2,128)(2,1)} %param.25) | copy-start | bytes 12582916
  86.3 4.2 %copy-start.17 = (f32[4096]{0:T(1024)S(1)}, f32[4096]{0:T(1024)}, u32[]{:S(2)}) copy-start(f32[4096]{0:T(1024)} %param.23) | copy-start | bytes 49156
  90.5 2.7 copy-start.16
  97.8 135.0 %all-gather.10.cloned.1.call-start = ((), (), s32[]{:S(2)}) async-start(), calls=%async_computation.3 | async-start | bytes 2662400 | tf_op jit(solution)/shard_map/all_gather | solution.py:363
  99.1 5.9 %copy-start.10 = (s32[4096]{0:T(1024)}, s32[4096]{0:T(1024)S(1)}, u32[]{:S(2)}) copy-start(s32[4096]{0:T(1024)S(1)} %convert_reduce_fusion.2) | copy-start | bytes 49156
  105.0 25.0 %collective-permute-start.3 = (bf16[512,1024]{1,0:T(8,128)(2,1)}, bf16[512,1024]{1,0:T(8,128)(2,1)}, u32[]{:S(2)}, u32[]{:S(2)}) collective-permute-start(bf16[512,1024]{1,0:T(8,128)(2,1)} %get-tuple-element.25), channel_id=1, source_target_pairs={{0,8},{8,16},{16,24},{24,0},{1,9},{9,17},{17,25},{25,1},{2,10},{10... | collective-permute-start | bytes 3145736 | tf_op jit(solution)/shard_map/ppermute | solution.py:238
  105.2 26.3 %collective-permute-start.4 = (bf16[512,1024]{1,0:T(8,128)(2,1)}, bf16[512,1024]{1,0:T(8,128)(2,1)}, u32[]{:S(2)}, u32[]{:S(2)}) collective-permute-start(bf16[512,1024]{1,0:T(8,128)(2,1)} %get-tuple-element.24), channel_id=1, source_target_pairs={{0,16},{8,24},{16,0},{24,8},{1,17},{9,25},{17,1},{25,9},{2,18},{10... | collective-permute-start | bytes 3145736 | tf_op jit(solution)/shard_map/ppermute | solution.py:238
  105.5 45.4 %collective-permute-start.5 = (bf16[512,1024]{1,0:T(8,128)(2,1)S(1)}, bf16[512,1024]{1,0:T(8,128)(2,1)}, u32[]{:S(2)}, u32[]{:S(2)}) collective-permute-start(bf16[512,1024]{1,0:T(8,128)(2,1)S(1)} %get-tuple-element.23), channel_id=1, source_target_pairs={{0,24},{8,0},{16,8},{24,16},{1,25},{9,1},{17,9},{25,17},{2,26},{10... | collective-permute-start | bytes 3145736 | tf_op jit(solution)/shard_map/ppermute | solution.py:238
  198.3 34.5 %copy-start.7 = (bf16[512,1024]{1,0:T(8,128)(2,1)S(1)}, bf16[512,1024]{1,0:T(8,128)(2,1)}, u32[]{:S(2)}) copy-start(bf16[512,1024]{1,0:T(8,128)(2,1)} %get-tuple-element.13) | copy-start | bytes 3145732
  232.7 4.1 %copy-start.9 = (bf16[2080,512]{1,0:T(8,128)(2,1)S(1)}, bf16[2080,512]{1,0:T(8,128)(2,1)}, u32[]{:S(2)}) copy-start(bf16[2080,512]{1,0:T(8,128)(2,1)} %all-gather.10.cloned.1.call-done) | copy-start | bytes 6389764
  238.8 3.6 %copy-start.11 = (f32[1024]{0:T(1024)S(1)}, f32[1024]{0:T(1024)}, u32[]{:S(2)}) copy-start(f32[1024]{0:T(1024)} %param.28) | copy-start | bytes 12292
  240.8 1.4 copy-start.4
  242.4 4.3 %copy-start.5 = (f32[520,1024]{1,0:T(8,128)S(1)}, f32[520,1024]{1,0:T(8,128)}, u32[]{:S(2)}) copy-start(f32[520,1024]{1,0:T(8,128)} %copy-done.4) | copy-start | bytes 6389764
  242.4 26.1 %copy-start.1 = (bf16[1408,3,352]{0,2,1:T(8,128)(2,1)S(1)}, bf16[1408,3,352]{0,2,1:T(8,128)(2,1)}, u32[]{:S(2)}) copy-start(bf16[1408,3,352]{0,2,1:T(8,128)(2,1)} %param.19) | copy-start | bytes 8921092
  244.8 4.4 %collective-permute-start.6 = (f32[8,1025]{1,0:T(8,128)S(1)}, f32[8,1025]{1,0:T(8,128)S(1)}, u32[]{:S(2)}, u32[]{:S(2)}) collective-permute-start(f32[8,1025]{1,0:T(8,128)S(1)} %get-tuple-element.36), channel_id=1, source_target_pairs={{0,8},{8,16},{16,24},{24,0},{1,9},{9,17},{17,25},{25,1},{2,10},{10... | collective-permute-start | bytes 98408 | tf_op jit(solution)/shard_map/ppermute | solution.py:142
  245.1 4.1 %collective-permute-start.7 = (f32[8,1025]{1,0:T(8,128)S(1)}, f32[8,1025]{1,0:T(8,128)S(1)}, u32[]{:S(2)}, u32[]{:S(2)}) collective-permute-start(f32[8,1025]{1,0:T(8,128)S(1)} %get-tuple-element.36), channel_id=1, source_target_pairs={{0,16},{8,24},{16,0},{24,8},{1,17},{9,25},{17,1},{25,9},{2,18},{10... | collective-permute-start | bytes 98408 | tf_op jit(solution)/shard_map/ppermute | solution.py:142
  245.4 3.8 %collective-permute-start.8 = (f32[8,1025]{1,0:T(8,128)S(1)}, f32[8,1025]{1,0:T(8,128)S(1)}, u32[]{:S(2)}, u32[]{:S(2)}) collective-permute-start(f32[8,1025]{1,0:T(8,128)S(1)} %get-tuple-element.36), channel_id=1, source_target_pairs={{0,24},{8,0},{16,8},{24,16},{1,25},{9,1},{17,9},{25,17},{2,26},{10... | collective-permute-start | bytes 98408 | tf_op jit(solution)/shard_map/ppermute | solution.py:142
  250.8 9.5 %collective-permute-start.10 = (f32[8]{0:T(128)S(1)}, f32[8]{0:T(128)S(1)}, u32[]{:S(2)}, u32[]{:S(2)}) collective-permute-start(f32[8]{0:T(128)S(1)} %get-tuple-element.41), channel_id=1, source_target_pairs={{0,2},{1,3},{2,4},{3,5},{4,6},{5,7},{6,0},{7,1},{8,10},{9,11},{10,... | collective-permute-start | bytes 104 | tf_op jit(solution)/shard_map/ppermute | solution.py:160
  252.6 9.1 %collective-permute-start.11 = (f32[8]{0:T(128)S(1)}, f32[8]{0:T(128)S(1)}, u32[]{:S(2)}, u32[]{:S(2)}) collective-permute-start(f32[8]{0:T(128)S(1)} %get-tuple-element.41), channel_id=1, source_target_pairs={{0,3},{1,4},{2,5},{3,6},{4,7},{5,0},{6,1},{7,2},{8,11},{9,12},{10,... | collective-permute-start | bytes 104 | tf_op jit(solution)/shard_map/ppermute | solution.py:160
  255.0 7.3 %collective-permute-start.12 = (f32[8]{0:T(128)S(1)}, f32[8]{0:T(128)S(1)}, u32[]{:S(2)}, u32[]{:S(2)}) collective-permute-start(f32[8]{0:T(128)S(1)} %get-tuple-element.41), channel_id=1, source_target_pairs={{0,4},{1,5},{2,6},{3,7},{4,0},{5,1},{6,2},{7,3},{8,12},{9,13},{10,... | collective-permute-start | bytes 104 | tf_op jit(solution)/shard_map/ppermute | solution.py:160
  256.4 5.9 %collective-permute-start.13 = (f32[8]{0:T(128)S(1)}, f32[8]{0:T(128)S(1)}, u32[]{:S(2)}, u32[]{:S(2)}) collective-permute-start(f32[8]{0:T(128)S(1)} %get-tuple-element.41), channel_id=1, source_target_pairs={{0,5},{1,6},{2,7},{3,0},{4,1},{5,2},{6,3},{7,4},{8,13},{9,14},{10,... | collective-permute-start | bytes 104 | tf_op jit(solution)/shard_map/ppermute | solution.py:160
  258.8 3.5 %collective-permute-start.14 = (f32[8]{0:T(128)S(1)}, f32[8]{0:T(128)S(1)}, u32[]{:S(2)}, u32[]{:S(2)}) collective-permute-start(f32[8]{0:T(128)S(1)} %get-tuple-element.41), channel_id=1, source_target_pairs={{0,6},{1,7},{2,0},{3,1},{4,2},{5,3},{6,4},{7,5},{8,14},{9,15},{10,... | collective-permute-start | bytes 104 | tf_op jit(solution)/shard_map/ppermute | solution.py:160
  260.3 3.5 %collective-permute-start.15 = (f32[8]{0:T(128)S(1)}, f32[8]{0:T(128)S(1)}, u32[]{:S(2)}, u32[]{:S(2)}) collective-permute-start(f32[8]{0:T(128)S(1)} %get-tuple-element.41), channel_id=1, source_target_pairs={{0,7},{1,0},{2,1},{3,2},{4,3},{5,4},{6,5},{7,6},{8,15},{9,8},{10,9... | collective-permute-start | bytes 104 | tf_op jit(solution)/shard_map/ppermute | solution.py:160
  261.7 6.2 %collective-permute-start.9 = (f32[8]{0:T(128)S(1)}, f32[8]{0:T(128)S(1)}, u32[]{:S(2)}, u32[]{:S(2)}) collective-permute-start(f32[8]{0:T(128)S(1)} %get-tuple-element.41), channel_id=1, source_target_pairs={{0,1},{1,2},{2,3},{3,4},{4,5},{5,6},{6,7},{7,0},{8,9},{9,10},{10,1... | collective-permute-start | bytes 104 | tf_op jit(solution)/shard_map/ppermute | solution.py:160
Sparse Core Ops, SparseCore 0:
  25.1 37.2 all-reduce.1
  66.1 20.1 all-gather.5
  97.9 75.8 all-gather.7
  200.0 32.7 all-gather.9

commit v9 on v7

--- a/solution.py
+++ b/solution.py
@@ -203,7 +203,12 @@
     )
     head_part = jnp.einsum("pnc,cd->pnd", mixed_rows, vis_out, preferred_element_type=jnp.float32)
     head_pooled = jnp.mean(head_part.reshape(pictures, merged_max, 4, vis_width), axis=2)
-    head_total = lax.psum(head_pooled.astype(jnp.bfloat16), "kv").astype(jnp.float32)
+    head_total = jnp.sum(
+        lax.all_gather(head_pooled.astype(jnp.bfloat16), "kv", axis=0, tiled=False).astype(
+            jnp.float32
+        ),
+        axis=0,
+    )
     input_pooled = jnp.mean(inputs.reshape(pictures, merged_max, 4, vis_width), axis=2)
     pooled = (input_pooled + head_total).astype(jnp.bfloat16)
     merged = jnp.einsum(

time: 269 us -> 289 us (1.074)
  waiting for transfers between devices: 134 us -> 153 us
    psum x1 -> x0, waiting for transfers between devices: 29 us -> none  [on_device(): lax.psum(head_pooled.astype(jnp.bfloat16), 'kv').astype(jnp.float32)]
    ppermute x3, waiting for transfers between devices: 0.01 us -> 26.5 us  [gather_by_permutes(): lax.ppermute(local, 'kv', perm=[(i, (i + shift) % count) for i in range(c...]
    all_gather x0 -> x1, waiting for transfers between devices: none -> 24.5 us  [on_device(): lax.all_gather(head_pooled.astype(jnp.bfloat16), 'kv', axis=0, tiled=False)]
    all_gather x1, waiting for transfers between devices: 4.17 us -> 0.01 us  [on_device(): lax.all_gather(merged.reshape(pictures * merged_max, feat_dev), 'kv', axi...]
  transfers between devices with their start and end apart: 16 -> 16, of which waited for: 10 -> 10; matrix products, arithmetic and copies ran while one was open for 20% -> 14% of each run, Pallas kernels for 0% -> 0%
where the time goes in v9:
time: 289 us; the launch traced here: 288 us
  waiting for transfers between devices  153 us (53%)
  matrix products  34.3 us (12%)
  local copies, waits for them, and re-layouts  29.5 us (10%)
  other arithmetic  27.6 us (10%)
  starting transfers between devices  14.9 us (5%)
  between operations  14.4 us (5%)
  Pallas kernels  14.2 us (5%)
    ppermute x3, waiting for transfers between devices, on_device(): lax.ppermute(payload, 'kv', perm=[(i, (i + shift) % kv_count) for i in ra...  38.6 us
    all_gather x1, waiting for transfers between devices, on_device(): context_all = lax.all_gather(out_rows, 'kv', axis=0, tiled=False)  31.9 us
    ppermute x3, waiting for transfers between devices, gather_by_permutes(): lax.ppermute(local, 'kv', perm=[(i, (i + shift) % count) for i in range(c...  26.5 us
    all_gather x1, waiting for transfers between devices, on_device(): gathered = lax.all_gather(shipped, 'blk', axis=0, tiled=False)  26.3 us
    all_gather x1, waiting for transfers between devices, on_device(): lax.all_gather(head_pooled.astype(jnp.bfloat16), 'kv', axis=0, tiled=False)  24.5 us
    pallas_call x1, Pallas kernels, flash_attention(): pl.pallas_call(functools.partial(flash_kernel, root=root), grid_spec=grid...  14.2 us
    dot_general x4, matrix products, on_device(): part = jnp.dot(source, piece, preferred_element_type=jnp.float32)  8.02 us
    ppermute x3, starting transfers between devices, tree_max(): lax.ppermute(values, axis, perm=[(i, i ^ step) for i in range(count)])  6.14 us
  transfers between devices with their start and end apart: 16, of which 10 were waited for; matrix products, arithmetic and copies ran while one was open for 14% of the time, Pallas kernels for 0%

profile of v9, /device:TPU:0, one launch (start us, length us, event | category | flops | bytes accessed | tf_op | source)
XLA Modules:
  0.0 288.3 jit_solution(9924948570041860068)
XLA Ops:
  7.3 2.1 convert_reduce_fusion.1
  10.5 2.9 fusion.30
  17.3 2.7 convolution_reduce_fusion
  21.5 2.6 collective-permute-start.1
  24.1 1.4 collective-permute-start.2
  25.5 2.9 reshape.381
  28.5 5.1 %reduce_sum.145 = f32[3,64,1408]{2,1,0:T(8,128)S(1)} reduce(f32[3,64,4,1408]{3,2,1,0:T(4,128)} %reshape.381, f32[]{:T(128)} %constant.144.clone.1), dimensions={2}, to_apply=%region_1.2 | reduce | flops 811008 | bytes 5406724 | tf_op jit(solution)/shard_map/reduce_sum | solution.py:212
  34.0 24.5 %all-gather.10.cloned.1.call-done = bf16[12,64,1408]{2,1,0:T(8,128)(2,1)} async-done(((bf16[3,64,1408]{2,1,0:T(8,128)(2,1)}), bf16[12,64,1408]{2,1,0:T(8,128)(2,1)}) %all-gather.10.cloned.1.call-update) | async-done | bytes 2162704 | tf_op jit(solution)/shard_map/all_gather | solution.py:207
  58.5 2.2 convert_reduce_fusion
  60.9 1.5 fusion.45
  63.2 26.5 %collective-permute-done.2 = bf16[512,1024]{1,0:T(8,128)(2,1)} collective-permute-done((bf16[512,1024]{1,0:T(8,128)(2,1)}, bf16[512,1024]{1,0:T(8,128)(2,1)}, u32[]{:S(2)}, u32[]{:S(2)}) %collective-permute-start.2) | collective-permute-done | bytes 1048608 | tf_op jit(solution)/shard_map/ppermute | solution.py:120
  89.8 3.7 %pad_maximum_fusion = bf16[4,512,1024]{2,1,0:T(8,128)(2,1)} fusion(bf16[1,512,1024]{2,1,0:T(8,128)(2,1)} %bitcast.22, bf16[1,512,1024]{2,1,0:T(8,128)(2,1)} %bitcast.21, bf16[1,512,1024]{2,1,0:T(8,128)(2,1)} %bitcast.20, bf16[1,512,1024]{2,1,0:T(8,128)(2,1)} %bitcast.176), kind=kLoop, calls=%fused_computation.24 | loop fusion | flops 6291456 | bytes 8388608 | tf_op jit(solution)/shard_map/stack | solution.py:122
  93.5 5.0 %gather_fusion = bf16[4,512,1024]{2,1,0:T(8,128)(2,1)} fusion(bf16[4,512,1024]{2,1,0:T(8,128)(2,1)} %pad_maximum_fusion, s32[1024]{0:T(1024)S(1)} %pad_clamp_fusion), kind=kCustom, calls=%fused_computation | custom fusion | bytes 8388624 | tf_op jit(solution)/shard_map/jit(_take)/gather | solution.py:124
  98.5 2.7 broadcast_select_fusion
  101.2 2.1 slice_bitcast_fusion.3
  104.2 4.5 %fusion.2 = (f32[512]{0:T(512)S(1)}, bf16[512,4096]{1,0:T(8,128)(2,1)S(1)}) fusion(bf16[512,1024]{1,0:T(8,128)(2,1)} %get-tuple-element.28, bf16[512,1024]{1,0:T(8,128)(2,1)} %get-tuple-element.29, bf16[512,1024]{1,0:T(8,128)(2,1)} %get-tuple-element.30, bf16[512,1024]{1,0:T(8,128)(2,1)} %get-tuple-element.27, ...), kind=kOutput, calls=%fused_computation.6 | convolution fusion | flops 832667136 | bytes 9964800 | tf_op jit(solution)/shard_map/dot_general | solution.py:245
  108.7 2.6 fusion.14
  111.5 2.6 fusion.49
  114.9 1.1 copy.82
  117.9 4.0 %constant_dynamic-slice_fusion = (bf16[512,1024]{1,0:T(8,128)(2,1)S(1)}, bf16[512,1024]{1,0:T(8,128)(2,1)}, bf16[512,1024]{1,0:T(8,128)(2,1)}, bf16[512,1024]{1,0:T(8,128)(2,1)}) fusion(bf16[512,4096]{1,0:T(8,128)(2,1)} %param.26, s32[]{:T(128)S(6)} %select_n.159, s32[]{:T(128)S(6)} %select_n.157, s32[]{:T(128)S(6)} %select_n.155, s32[]{:T(128)S(6)} %select_n.153), kind=kLoop, calls=%fused_computation.163 | loop fusion | bytes 8388624 | tf_op jit(solution)/shard_map/dynamic_slice | solution.py:221
  121.9 2.3 collective-permute-start.4
  124.2 1.2 and_convert_fusion.needed_ref
  127.7 1.1 copy.79
  128.8 18.4 %collective-permute-done.3 = bf16[512,1024]{1,0:T(8,128)(2,1)} collective-permute-done((bf16[512,1024]{1,0:T(8,128)(2,1)}, bf16[512,1024]{1,0:T(8,128)(2,1)}, u32[]{:S(2)}, u32[]{:S(2)}) %collective-permute-start.3) | collective-permute-done | bytes 1048608 | tf_op jit(solution)/shard_map/ppermute | solution.py:225
  147.2 1.3 collective-permute-done.4
  148.4 19.0 %collective-permute-done.5 = bf16[512,1024]{1,0:T(8,128)(2,1)} collective-permute-done((bf16[512,1024]{1,0:T(8,128)(2,1)S(1)}, bf16[512,1024]{1,0:T(8,128)(2,1)}, u32[]{:S(2)}, u32[]{:S(2)}) %collective-permute-start.5) | collective-permute-done | bytes 1048608 | tf_op jit(solution)/shard_map/ppermute | solution.py:225
  167.4 26.3 %all-gather.12.cloned.1.call-done = bf16[4288,512]{1,0:T(8,128)(2,1)} async-done(((bf16[536,512]{1,0:T(8,128)(2,1)}), bf16[4288,512]{1,0:T(8,128)(2,1)}) %all-gather.12.cloned.1.call-update) | async-done | bytes 4390928 | tf_op jit(solution)/shard_map/all_gather | solution.py:288
  193.7 3.9 %fusion.107 = (bf16[8,512,128]{2,1,0:T(8,128)(2,1)}, bf16[8,512,128]{2,1,0:T(8,128)(2,1)S(1)}, bf16[8,512,128]{2,1,0:T(8,128)(2,1)}, bf16[8,512,128]{2,1,0:T(8,128)(2,1)S(1)}) fusion(bf16[8,536,512]{2,1,0:T(8,128)(2,1)} %bitcast.158), kind=kLoop, calls=%fused_computation.190 | loop fusion | bytes 8388608 | tf_op jit(solution)/shard_map/slice | solution.py:324
  198.5 14.2 %shard_map.166 = bf16[2,1024,128]{2,1,0:T(8,128)(2,1)} custom-call(s32[8]{0:T(128)} %and_convert_fusion.needed_ref, bf16[2,1024,128]{2,1,0:T(8,128)(2,1)} %bitcast.177, bf16[8,536,512]{2,1,0:T(8,128)(2,1)} %bitcast.160, bf16[8,536,512]{2,1,0:T(8,128)(2,1)} %bitcast.161, s32[1024,1]{1,0:T(8,128)} %broadcast_in_dim_reshape.9.qid_ref, ...), custom_call_target="tpu_custom_call" | custom-call | flops 4294967296 | bytes 5242880 | tf_op jit(solution)/shard_map/pallas_call | solution.py:102
  212.8 1.3 copy.85
  214.1 1.8 fusion.109
  216.0 1.8 fusion.108
  218.6 1.0 copy.87
  219.7 31.9 %all-gather.14.cloned.1.call-done = bf16[2080,512]{1,0:T(8,128)(2,1)} async-done(((bf16[520,512]{1,0:T(8,128)(2,1)}), bf16[2080,512]{1,0:T(8,128)(2,1)}) %all-gather.14.cloned.1.call-update) | async-done | bytes 2129936 | tf_op jit(solution)/shard_map/all_gather | solution.py:347
  251.6 1.9 convolution_convert_fusion.4
  253.5 2.1 convolution_convert_fusion.3
  255.7 2.0 convolution_convert_fusion.2
  257.7 2.0 convert_add_fusion
  259.7 1.3 copy-done.4
  261.2 2.4 fusion.86
  264.3 1.2 collective-permute-start.8
  265.5 2.5 fusion.29
  269.6 1.8 collective-permute-start.9
  271.4 1.8 collective-permute-done.9
  273.2 1.7 collective-permute-start.10
  275.0 1.8 collective-permute-done.10
  276.8 2.6 collective-permute-start.11
  279.4 1.8 collective-permute-done.11
  (125 shorter events, 18.7 us)
Async XLA Ops:
  7.2 3.3 %copy-start = (bf16[1408,3,352]{0,2,1:T(8,128)(2,1)S(1)}, bf16[1408,3,352]{0,2,1:T(8,128)(2,1)}, u32[]{:S(2)}) copy-start(bf16[1408,3,352]{0,2,1:T(8,128)(2,1)} %param.19) | copy-start | bytes 8921092
  7.2 3.2 %copy-start.13 = (s32[3,2]{0,1:T(2,128)S(1)}, s32[3,2]{0,1:T(2,128)}, u32[]{:S(2)}) copy-start(s32[3,2]{0,1:T(2,128)} %param.16) | copy-start | bytes 76
  7.2 3.3 %copy-start.19 = (f32[1408]{0:T(1024)S(1)}, f32[1408]{0:T(1024)}, u32[]{:S(2)}) copy-start(f32[1408]{0:T(1024)} %param.18) | copy-start | bytes 16900
  7.2 51.3 %all-gather.10.cloned.1.call-start = ((), (), s32[]{:S(2)}) async-start(), calls=%async_computation.1 | async-start | bytes 2703360 | tf_op jit(solution)/shard_map/all_gather | solution.py:207
  7.2 2.4 copy-start.2
  17.3 8.2 %copy-start.3 = (bf16[3,256,1408]{2,1,0:T(8,128)(2,1)S(1)}, bf16[3,256,1408]{2,1,0:T(8,128)(2,1)}, u32[]{:S(2)}) copy-start(bf16[3,256,1408]{2,1,0:T(8,128)(2,1)} %param.15) | copy-start | bytes 6488068
  20.9 7.4 %copy-start.14 = (s32[3]{0:T(128)S(1)}, s32[3]{0:T(128)}, u32[]{:S(2)}) copy-start(s32[3]{0:T(128)} %param.17) | copy-start | bytes 40
  21.0 83.2 %all-gather.8.cloned.1.call-start = ((), (), s32[]{:S(2)}) async-start(), calls=%async_computation | async-start | bytes 1966080 | tf_op jit(solution)/shard_map/all_gather | solution.py:242
  21.0 42.2 %collective-permute-start = (bf16[512,1024]{1,0:T(8,128)(2,1)}, bf16[512,1024]{1,0:T(8,128)(2,1)}, u32[]{:S(2)}, u32[]{:S(2)}) collective-permute-start(bf16[512,1024]{1,0:T(8,128)(2,1)} %param.22), channel_id=1, source_target_pairs={{0,8},{8,16},{16,24},{24,0},{1,9},{9,17},{17,25},{25,1},{2,10},{10... | collective-permute-start | bytes 3145736 | tf_op jit(solution)/shard_map/ppermute | solution.py:120
  21.5 41.7 %collective-permute-start.1 = (bf16[512,1024]{1,0:T(8,128)(2,1)}, bf16[512,1024]{1,0:T(8,128)(2,1)}, u32[]{:S(2)}, u32[]{:S(2)}) collective-permute-start(bf16[512,1024]{1,0:T(8,128)(2,1)} %param.22), channel_id=1, source_target_pairs={{0,16},{8,24},{16,0},{24,8},{1,17},{9,25},{17,1},{25,9},{2,18},{10... | collective-permute-start | bytes 3145736 | tf_op jit(solution)/shard_map/ppermute | solution.py:120
  24.1 65.7 %collective-permute-start.2 = (bf16[512,1024]{1,0:T(8,128)(2,1)}, bf16[512,1024]{1,0:T(8,128)(2,1)}, u32[]{:S(2)}, u32[]{:S(2)}) collective-permute-start(bf16[512,1024]{1,0:T(8,128)(2,1)} %param.22), channel_id=1, source_target_pairs={{0,24},{8,0},{16,8},{24,16},{1,25},{9,1},{17,9},{25,17},{2,26},{10... | collective-permute-start | bytes 3145736 | tf_op jit(solution)/shard_map/ppermute | solution.py:120
  28.3 5.2 %copy-start.15 = (s32[8]{0:T(128)S(1)}, s32[8]{0:T(128)}, u32[]{:S(2)}) copy-start(s32[8]{0:T(128)} %param.27) | copy-start | bytes 100
  58.5 2.5 copy-start.7
  62.5 131.2 %all-gather.12.cloned.1.call-start = ((), (), s32[]{:S(2)}) async-start(), calls=%async_computation.2 | async-start | bytes 4939776 | tf_op jit(solution)/shard_map/all_gather | solution.py:288
  101.1 2.1 copy-start.8
  101.2 2.1 copy-start.10
  103.9 4.8 %copy-start.6 = (bf16[512,1024]{1,0:T(8,128)(2,1)}, bf16[512,1024]{1,0:T(8,128)(2,1)S(1)}, u32[]{:S(2)}) copy-start(bf16[512,1024]{1,0:T(8,128)(2,1)S(1)} %fusion.44) | copy-start | bytes 3145732
  104.2 4.5 %copy-start.16 = (bf16[4096,2,256]{2,1,0:T(2,128)(2,1)S(1)}, bf16[4096,2,256]{2,1,0:T(2,128)(2,1)}, u32[]{:S(2)}) copy-start(bf16[4096,2,256]{2,1,0:T(2,128)(2,1)} %param.25) | copy-start | bytes 12582916
  104.2 4.5 %copy-start.18 = (f32[4096]{0:T(1024)S(1)}, f32[4096]{0:T(1024)}, u32[]{:S(2)}) copy-start(f32[4096]{0:T(1024)} %param.23) | copy-start | bytes 49156
  108.7 2.7 copy-start.17
  116.0 135.6 %all-gather.14.cloned.1.call-start = ((), (), s32[]{:S(2)}) async-start(), calls=%async_computation.3 | async-start | bytes 2662400 | tf_op jit(solution)/shard_map/all_gather | solution.py:347
  121.9 25.3 %collective-permute-start.3 = (bf16[512,1024]{1,0:T(8,128)(2,1)}, bf16[512,1024]{1,0:T(8,128)(2,1)}, u32[]{:S(2)}, u32[]{:S(2)}) collective-permute-start(bf16[512,1024]{1,0:T(8,128)(2,1)} %get-tuple-element.25), channel_id=1, source_target_pairs={{0,8},{8,16},{16,24},{24,0},{1,9},{9,17},{17,25},{25,1},{2,10},{10... | collective-permute-start | bytes 3145736 | tf_op jit(solution)/shard_map/ppermute | solution.py:225
  121.9 26.6 %collective-permute-start.4 = (bf16[512,1024]{1,0:T(8,128)(2,1)}, bf16[512,1024]{1,0:T(8,128)(2,1)}, u32[]{:S(2)}, u32[]{:S(2)}) collective-permute-start(bf16[512,1024]{1,0:T(8,128)(2,1)} %get-tuple-element.24), channel_id=1, source_target_pairs={{0,16},{8,24},{16,0},{24,8},{1,17},{9,25},{17,1},{25,9},{2,18},{10... | collective-permute-start | bytes 3145736 | tf_op jit(solution)/shard_map/ppermute | solution.py:225
  124.2 43.2 %collective-permute-start.5 = (bf16[512,1024]{1,0:T(8,128)(2,1)S(1)}, bf16[512,1024]{1,0:T(8,128)(2,1)}, u32[]{:S(2)}, u32[]{:S(2)}) collective-permute-start(bf16[512,1024]{1,0:T(8,128)(2,1)S(1)} %get-tuple-element.23), channel_id=1, source_target_pairs={{0,24},{8,0},{16,8},{24,16},{1,25},{9,1},{17,9},{25,17},{2,26},{10... | collective-permute-start | bytes 3145736 | tf_op jit(solution)/shard_map/ppermute | solution.py:225
  218.1 33.5 %copy-start.9 = (bf16[512,1024]{1,0:T(8,128)(2,1)S(1)}, bf16[512,1024]{1,0:T(8,128)(2,1)}, u32[]{:S(2)}) copy-start(bf16[512,1024]{1,0:T(8,128)(2,1)} %get-tuple-element.13) | copy-start | bytes 3145732
  251.6 4.1 %copy-start.11 = (bf16[2080,512]{1,0:T(8,128)(2,1)S(1)}, bf16[2080,512]{1,0:T(8,128)(2,1)}, u32[]{:S(2)}) copy-start(bf16[2080,512]{1,0:T(8,128)(2,1)} %all-gather.14.cloned.1.call-done) | copy-start | bytes 6389764
  257.6 3.6 %copy-start.12 = (f32[1024]{0:T(1024)S(1)}, f32[1024]{0:T(1024)}, u32[]{:S(2)}) copy-start(f32[1024]{0:T(1024)} %param.28) | copy-start | bytes 12292
  259.7 1.4 copy-start.4
  261.2 4.3 %copy-start.5 = (f32[520,1024]{1,0:T(8,128)S(1)}, f32[520,1024]{1,0:T(8,128)}, u32[]{:S(2)}) copy-start(f32[520,1024]{1,0:T(8,128)} %copy-done.4) | copy-start | bytes 6389764
  261.2 20.5 %copy-start.1 = (bf16[1408,3,352]{0,2,1:T(8,128)(2,1)S(1)}, bf16[1408,3,352]{0,2,1:T(8,128)(2,1)}, u32[]{:S(2)}) copy-start(bf16[1408,3,352]{0,2,1:T(8,128)(2,1)} %param.19) | copy-start | bytes 8921092
  263.7 4.4 %collective-permute-start.6 = (f32[8,1025]{1,0:T(8,128)S(1)}, f32[8,1025]{1,0:T(8,128)S(1)}, u32[]{:S(2)}, u32[]{:S(2)}) collective-permute-start(f32[8,1025]{1,0:T(8,128)S(1)} %get-tuple-element.36), channel_id=1, source_target_pairs={{0,8},{8,16},{16,24},{24,0},{1,9},{9,17},{17,25},{25,1},{2,10},{10... | collective-permute-start | bytes 98408 | tf_op jit(solution)/shard_map/ppermute | solution.py:132
  264.0 4.1 %collective-permute-start.7 = (f32[8,1025]{1,0:T(8,128)S(1)}, f32[8,1025]{1,0:T(8,128)S(1)}, u32[]{:S(2)}, u32[]{:S(2)}) collective-permute-start(f32[8,1025]{1,0:T(8,128)S(1)} %get-tuple-element.36), channel_id=1, source_target_pairs={{0,16},{8,24},{16,0},{24,8},{1,17},{9,25},{17,1},{25,9},{2,18},{10... | collective-permute-start | bytes 98408 | tf_op jit(solution)/shard_map/ppermute | solution.py:132
  264.3 3.8 %collective-permute-start.8 = (f32[8,1025]{1,0:T(8,128)S(1)}, f32[8,1025]{1,0:T(8,128)S(1)}, u32[]{:S(2)}, u32[]{:S(2)}) collective-permute-start(f32[8,1025]{1,0:T(8,128)S(1)} %get-tuple-element.36), channel_id=1, source_target_pairs={{0,24},{8,0},{16,8},{24,16},{1,25},{9,1},{17,9},{25,17},{2,26},{10... | collective-permute-start | bytes 98408 | tf_op jit(solution)/shard_map/ppermute | solution.py:132
  269.6 3.6 %collective-permute-start.9 = (f32[8]{0:T(128)S(1)}, f32[8]{0:T(128)S(1)}, u32[]{:S(2)}, u32[]{:S(2)}) collective-permute-start(f32[8]{0:T(128)S(1)} %get-tuple-element.41), channel_id=1, source_target_pairs={{0,1},{1,0},{2,3},{3,2},{4,5},{5,4},{6,7},{7,6},{8,9},{9,8},{10,11... | collective-permute-start | bytes 104 | tf_op jit(solution)/shard_map/ppermute | solution.py:149
  273.2 3.5 %collective-permute-start.10 = (f32[8]{0:T(128)S(1)}, f32[8]{0:T(128)S(1)}, u32[]{:S(2)}, u32[]{:S(2)}) collective-permute-start(f32[8]{0:T(128)S(1)} %max.9), channel_id=1, source_target_pairs={{0,2},{1,3},{2,0},{3,1},{4,6},{5,7},{6,4},{7,5},{8,10},{9,11},{10,... | collective-permute-start | bytes 104 | tf_op jit(solution)/shard_map/ppermute | solution.py:149
  276.8 4.4 %collective-permute-start.11 = (f32[8]{0:T(128)S(1)}, f32[8]{0:T(128)S(1)}, u32[]{:S(2)}, u32[]{:S(2)}) collective-permute-start(f32[8]{0:T(128)S(1)} %max.10), channel_id=1, source_target_pairs={{0,4},{1,5},{2,6},{3,7},{4,0},{5,1},{6,2},{7,3},{8,12},{9,13},{10,... | collective-permute-start | bytes 104 | tf_op jit(solution)/shard_map/ppermute | solution.py:149
Sparse Core Ops, SparseCore 0:
  21.1 37.3 all-gather.9
  62.6 28.0 all-gather.7
  116.1 77.5 all-gather.11
  219.7 31.8 all-gather.13

commit v10 on v7

--- a/solution.py
+++ b/solution.py
@@ -341,15 +341,19 @@
     out_rows = jnp.concatenate([context, last_context], axis=0)
     context_all = lax.all_gather(out_rows, "kv", axis=0, tiled=False)
     head_sum = None
+    last_sum = None
     for shift, piece in enumerate(weight_pieces):
         source = lax.dynamic_index_in_dim(
             context_all, (me_kv - shift) % kv_count, 0, keepdims=False
         )
-        part = jnp.dot(source, piece, preferred_element_type=jnp.float32)
+        part = jnp.dot(source[:tok_rows], piece, preferred_element_type=jnp.float32)
         part = part.astype(jnp.bfloat16).astype(jnp.float32)
         head_sum = part if head_sum is None else head_sum + part
-    hidden = (seq_in.astype(jnp.float32) + head_sum[:tok_rows]).astype(jnp.bfloat16)
-    chosen = (seq_last + head_sum[tok_rows:]).astype(jnp.bfloat16).astype(jnp.float32)
+        last_part = jnp.dot(source[tok_rows:], piece, preferred_element_type=jnp.float32)
+        last_part = last_part.astype(jnp.bfloat16).astype(jnp.float32)
+        last_sum = last_part if last_sum is None else last_sum + last_part
+    hidden = (seq_in.astype(jnp.float32) + head_sum).astype(jnp.bfloat16)
+    chosen = (seq_last + last_sum).astype(jnp.bfloat16).astype(jnp.float32)
     square_part = jnp.sum(chosen * chosen, axis=-1)
     scaled = (chosen * final_gain).astype(jnp.bfloat16)
     logit_part = lax.dot_general(

time: 269 us -> 274 us (1.019)
  matrix products: 37 us -> 45.1 us
    dot_general x4 -> x8, matrix products: 8.02 us -> 15.1 us  [the longest x4 9.54 us: on_device(): part = jnp.dot(source[:tok_rows], piece, preferred_element_type=jnp.float32)]
  transfers between devices with their start and end apart: 16 -> 16, of which waited for: 10 -> 10; matrix products, arithmetic and copies ran while one was open for 20% -> 22% of each run, Pallas kernels for 0% -> 0%
where the time goes in v10:
time: 274 us; the launch traced here: 273 us
  waiting for transfers between devices  134 us (49%)
  matrix products  45.1 us (16%)
  local copies, waits for them, and re-layouts  27.8 us (10%)
  other arithmetic  22.3 us (8%)
  starting transfers between devices  14.6 us (5%)
  between operations  14.4 us (5%)
  Pallas kernels  14.2 us (5%)
    ppermute x3, waiting for transfers between devices, on_device(): lax.ppermute(payload, 'kv', perm=[(i, (i + shift) % kv_count) for i in ra...  39.6 us
    all_gather x1, waiting for transfers between devices, on_device(): context_all = lax.all_gather(out_rows, 'kv', axis=0, tiled=False)  31.9 us
    psum x1, waiting for transfers between devices, on_device(): lax.psum(head_pooled.astype(jnp.bfloat16), 'kv').astype(jnp.float32)  29 us
    all_gather x1, waiting for transfers between devices, on_device(): gathered = lax.all_gather(shipped, 'blk', axis=0, tiled=False)  24 us
    pallas_call x1, Pallas kernels, flash_attention(): pl.pallas_call(functools.partial(flash_kernel, root=root), grid_spec=grid...  14.2 us
    dot_general x4, matrix products, on_device(): part = jnp.dot(source[:tok_rows], piece, preferred_element_type=jnp.float32)  9.54 us
    ppermute x3, starting transfers between devices, tree_max(): lax.ppermute(values, axis, perm=[(i, i ^ step) for i in range(count)])  6.15 us
    dot_general x4, matrix products, on_device(): jnp.dot(source[tok_rows:], piece, preferred_element_type=jnp.float32)  5.54 us
  transfers between devices with their start and end apart: 16, of which 10 were waited for; matrix products, arithmetic and copies ran while one was open for 22% of the time, Pallas kernels for 0%

profile of v10, /device:TPU:0, one launch (start us, length us, event | category | flops | bytes accessed | tf_op | source)
XLA Modules:
  0.0 272.7 jit_solution(5825978715319171979)
XLA Ops:
  7.8 2.6 collective-permute-start.1
  10.3 1.4 collective-permute-start.2
  11.7 2.0 convert_reduce_fusion
  14.5 2.9 %fusion.29 = bf16[3,256,3,352]{1,3,2,0:T(8,128)(2,1)S(1)} fusion(bf16[1408,3,352]{0,2,1:T(8,128)(2,1)S(1)} %copy-done, bf16[3,256,1408]{2,1,0:T(8,128)(2,1)S(1)} %copy-done.2, f32[1408]{0:T(1024)S(1)} %copy-done.14, f32[3,256]{1,0:T(4,128)S(1)} %add_rsqrt_fusion, f32[3,256]{1,0:T(4,128)S(1)} %broadcast_multiply_fusion), kind=kOutput, calls=%fused_computation.44 | convolution fusion | flops 2290016256 | bytes 6770176 | tf_op jit(solution)/shard_map/pnd,dce->pnce/dot_general | solution.py:181
  21.4 2.7 %convolution_reduce_fusion = f32[3,64,1408]{2,1,0:T(8,128)S(1)} fusion(bf16[352,1408]{1,0:T(8,128)(2,1)} %param.20, bf16[3,64,4,352]{3,2,1,0:T(4,128)(2,1)S(1)} %dot_general.77), kind=kOutput, calls=%fused_computation.43 | convolution fusion | flops 762077184 | bytes 2613248 | tf_op jit(solution)/shard_map/pnc,cd->pnd/dot_general | solution.py:204
  25.5 2.9 %reshape.376 = f32[3,64,4,1408]{3,2,1,0:T(4,128)} reshape(bf16[3,256,1408]{2,1,0:T(8,128)(2,1)S(1)} %copy-done.3) | data formatting | bytes 6488064 | tf_op jit(solution)/shard_map/reshape | solution.py:207
  28.5 4.8 %reduce_sum.136 = f32[3,64,1408]{2,1,0:T(8,128)S(1)} reduce(f32[3,64,4,1408]{3,2,1,0:T(4,128)} %reshape.376, f32[]{:T(128)} %constant.144.clone.1), dimensions={2}, to_apply=%region_1.2 | reduce | flops 811008 | bytes 5406724 | tf_op jit(solution)/shard_map/reduce_sum | solution.py:207
  33.5 29.0 %all-reduce.2.cloned.1.call-done = bf16[3,64,1408]{2,1,0:T(8,128)(2,1)} async-done(((bf16[3,64,1408]{2,1,0:T(8,128)(2,1)}), bf16[3,64,1408]{2,1,0:T(8,128)(2,1)}) %all-reduce.2.cloned.1.call-update) | async-done | bytes 540688 | tf_op jit(solution)/shard_map/psum | solution.py:206
  62.5 3.5 %fusion.44 = bf16[3,64,1024]{2,1,0:T(8,128)(2,1)} fusion(bf16[1408,1024]{1,0:T(8,128)(2,1)} %param.21, bf16[3,64,1408]{2,1,0:T(8,128)(2,1)} %all-reduce.2.cloned.1.call-done, f32[3,64,1408]{2,1,0:T(8,128)S(1)} %reduce_sum.136), kind=kOutput, calls=%fused_computation.57 | convolution fusion | flops 554926080 | bytes 4898816 | tf_op jit(solution)/shard_map/pmd,de->pme/dot_general | solution.py:209
  66.9 1.6 fusion.43
  68.7 3.7 %pad_maximum_fusion = bf16[4,512,1024]{2,1,0:T(8,128)(2,1)} fusion(bf16[1,512,1024]{2,1,0:T(8,128)(2,1)} %bitcast.21, bf16[1,512,1024]{2,1,0:T(8,128)(2,1)} %bitcast.20, bf16[1,512,1024]{2,1,0:T(8,128)(2,1)} %bitcast.19, bf16[1,512,1024]{2,1,0:T(8,128)(2,1)S(1)} %bitcast.191), kind=kLoop, calls=%fused_computation.23 | loop fusion | flops 6291456 | bytes 8388608 | tf_op jit(solution)/shard_map/stack | solution.py:122
  72.4 5.3 %gather_fusion = bf16[4,512,1024]{2,1,0:T(8,128)(2,1)} fusion(bf16[4,512,1024]{2,1,0:T(8,128)(2,1)} %pad_maximum_fusion, s32[1024]{0:T(1024)S(1)} %pad_clamp_fusion), kind=kCustom, calls=%fused_computation | custom fusion | bytes 8388624 | tf_op jit(solution)/shard_map/jit(_take)/gather | solution.py:124
  77.7 2.7 broadcast_select_fusion
  80.4 1.8 slice_bitcast_fusion.3
  82.1 4.2 %all-gather.6.cloned.1.call-done = bf16[192,4096]{1,0:T(8,128)(2,1)} async-done(((bf16[192,1024]{1,0:T(8,128)(2,1)}), bf16[192,4096]{1,0:T(8,128)(2,1)}) %all-gather.6.cloned.1.call-update) | async-done | bytes 1572880 | tf_op jit(solution)/shard_map/all_gather | solution.py:237
  86.3 4.2 %fusion.2 = (f32[512]{0:T(512)S(1)}, bf16[512,4096]{1,0:T(8,128)(2,1)S(1)}) fusion(bf16[512,1024]{1,0:T(8,128)(2,1)S(1)} %get-tuple-element.26, bf16[512,1024]{1,0:T(8,128)(2,1)} %get-tuple-element.27, bf16[512,1024]{1,0:T(8,128)(2,1)} %get-tuple-element.28, bf16[512,1024]{1,0:T(8,128)(2,1)S(1)} %get-tuple-element.25, ...), kind=kOutput, calls=%fused_computation.6 | convolution fusion | flops 832667136 | bytes 9964800 | tf_op jit(solution)/shard_map/dot_general | solution.py:240
  90.6 2.6 fusion.14
  93.3 2.6 fusion.48
  99.7 4.0 %constant_dynamic-slice_fusion = (bf16[512,1024]{1,0:T(8,128)(2,1)}, bf16[512,1024]{1,0:T(8,128)(2,1)}, bf16[512,1024]{1,0:T(8,128)(2,1)}, bf16[512,1024]{1,0:T(8,128)(2,1)S(1)}) fusion(bf16[512,4096]{1,0:T(8,128)(2,1)} %param.26, s32[]{:T(128)S(6)} %select_n.159, s32[]{:T(128)S(6)} %select_n.157, s32[]{:T(128)S(6)} %select_n.155, s32[]{:T(128)S(6)} %select_n.153), kind=kLoop, calls=%fused_computation.165 | loop fusion | bytes 8388624 | tf_op jit(solution)/shard_map/dynamic_slice | solution.py:216
  104.3 1.2 collective-permute-start.5
  105.5 1.2 and_convert_fusion.needed_ref
  109.1 1.1 copy.77
  110.2 18.6 %collective-permute-done.3 = bf16[512,1024]{1,0:T(8,128)(2,1)} collective-permute-done((bf16[512,1024]{1,0:T(8,128)(2,1)}, bf16[512,1024]{1,0:T(8,128)(2,1)}, u32[]{:S(2)}, u32[]{:S(2)}) %collective-permute-start.3) | collective-permute-done | bytes 1048608 | tf_op jit(solution)/shard_map/ppermute | solution.py:220
  128.7 1.6 collective-permute-done.4
  130.3 19.5 %collective-permute-done.5 = bf16[512,1024]{1,0:T(8,128)(2,1)} collective-permute-done((bf16[512,1024]{1,0:T(8,128)(2,1)}, bf16[512,1024]{1,0:T(8,128)(2,1)}, u32[]{:S(2)}, u32[]{:S(2)}) %collective-permute-start.5) | collective-permute-done | bytes 1048608 | tf_op jit(solution)/shard_map/ppermute | solution.py:220
  149.8 24.0 %all-gather.8.cloned.1.call-done = bf16[4288,512]{1,0:T(8,128)(2,1)} async-done(((bf16[536,512]{1,0:T(8,128)(2,1)}), bf16[4288,512]{1,0:T(8,128)(2,1)}) %all-gather.8.cloned.1.call-update) | async-done | bytes 4390928 | tf_op jit(solution)/shard_map/all_gather | solution.py:283
  173.8 4.1 %fusion.105 = (bf16[8,512,128]{2,1,0:T(8,128)(2,1)}, bf16[8,512,128]{2,1,0:T(8,128)(2,1)S(1)}, bf16[8,512,128]{2,1,0:T(8,128)(2,1)}, bf16[8,512,128]{2,1,0:T(8,128)(2,1)}) fusion(bf16[8,536,512]{2,1,0:T(8,128)(2,1)} %bitcast.174), kind=kLoop, calls=%fused_computation.199 | loop fusion | bytes 8388608 | tf_op jit(solution)/shard_map/slice | solution.py:319
  178.8 14.2 %shard_map.166 = bf16[2,1024,128]{2,1,0:T(8,128)(2,1)} custom-call(s32[8]{0:T(128)} %and_convert_fusion.needed_ref, bf16[2,1024,128]{2,1,0:T(8,128)(2,1)} %bitcast.192, bf16[8,536,512]{2,1,0:T(8,128)(2,1)} %bitcast.176, bf16[8,536,512]{2,1,0:T(8,128)(2,1)} %bitcast.177, s32[1024,1]{1,0:T(8,128)} %broadcast_in_dim_reshape.9.qid_ref, ...), custom_call_target="tpu_custom_call" | custom-call | flops 4294967296 | bytes 5242880 | tf_op jit(solution)/shard_map/pallas_call | solution.py:102
  193.1 1.3 copy.83
  194.4 1.8 fusion.107
  196.3 1.8 fusion.106
  198.1 1.5 fusion.63
  201.2 31.9 %all-gather.10.cloned.1.call-done = bf16[2080,512]{1,0:T(8,128)(2,1)} async-done(((bf16[520,512]{1,0:T(8,128)(2,1)}), bf16[2080,512]{1,0:T(8,128)(2,1)}) %all-gather.10.cloned.1.call-update) | async-done | bytes 2129936 | tf_op jit(solution)/shard_map/all_gather | solution.py:342
  234.1 1.5 fusion.58
  235.5 1.5 fusion.56
  237.0 1.6 multiply_reduce_fusion.1
  238.7 2.2 fusion.82
  241.6 1.2 collective-permute-start.8
  242.8 1.8 convolution_convert_fusion.5
  244.6 2.2 convolution_convert_fusion.4
  246.8 2.2 convolution_convert_fusion.3
  249.1 3.3 %add_convert_fusion = bf16[512,1024]{1,0:T(8,128)(2,1)} fusion(bf16[512,1024]{1,0:T(8,128)(2,1)S(1)} %convolution_convert_fusion.3, bf16[512,1024]{1,0:T(8,128)(2,1)S(1)} %convolution_convert_fusion.4, bf16[512,1024]{1,0:T(8,128)(2,1)S(1)} %convolution_convert_fusion.5, bf16[512,1024]{1,0:T(8,128)(2,1)S(1)} %copy-done.5, ...), kind=kOutput, calls=%fused_computation.42 | convolution fusion | flops 542638080 | bytes 6815748 | tf_op jit(solution)/shard_map/dot_general | solution.py:349
  254.0 1.8 collective-permute-start.9
  255.8 1.8 collective-permute-done.9
  257.6 1.7 collective-permute-start.10
  259.4 1.8 collective-permute-done.10
  261.2 2.6 collective-permute-start.11
  263.8 1.8 collective-permute-done.11
  (116 shorter events, 21.0 us)
Async XLA Ops:
  7.2 7.4 %copy-start = (bf16[1408,3,352]{0,2,1:T(8,128)(2,1)S(1)}, bf16[1408,3,352]{0,2,1:T(8,128)(2,1)}, u32[]{:S(2)}) copy-start(bf16[1408,3,352]{0,2,1:T(8,128)(2,1)} %param.19) | copy-start | bytes 8921092
  7.2 7.2 %copy-start.8 = (s32[3,2]{0,1:T(2,128)S(1)}, s32[3,2]{0,1:T(2,128)}, u32[]{:S(2)}) copy-start(s32[3,2]{0,1:T(2,128)} %param.16) | copy-start | bytes 76
  7.2 7.3 %copy-start.14 = (f32[1408]{0:T(1024)S(1)}, f32[1408]{0:T(1024)}, u32[]{:S(2)}) copy-start(f32[1408]{0:T(1024)} %param.18) | copy-start | bytes 16900
  7.2 55.3 %all-reduce.2.cloned.1.call-start = ((), (), s32[]{:S(2)}) async-start(), calls=%async_computation | async-start | bytes 1081344 | tf_op jit(solution)/shard_map/psum | solution.py:206
  7.2 6.4 %copy-start.2 = (bf16[3,256,1408]{2,1,0:T(8,128)(2,1)S(1)}, bf16[3,256,1408]{2,1,0:T(8,128)(2,1)}, u32[]{:S(2)}) copy-start(bf16[3,256,1408]{2,1,0:T(8,128)(2,1)} %param.15) | copy-start | bytes 6488068
  7.3 61.5 %collective-permute-start = (bf16[512,1024]{1,0:T(8,128)(2,1)}, bf16[512,1024]{1,0:T(8,128)(2,1)}, u32[]{:S(2)}, u32[]{:S(2)}) collective-permute-start(bf16[512,1024]{1,0:T(8,128)(2,1)} %param.22), channel_id=1, source_target_pairs={{0,8},{8,16},{16,24},{24,0},{1,9},{9,17},{17,25},{25,1},{2,10},{10... | collective-permute-start | bytes 3145736 | tf_op jit(solution)/shard_map/ppermute | solution.py:120
  7.8 61.0 %collective-permute-start.1 = (bf16[512,1024]{1,0:T(8,128)(2,1)}, bf16[512,1024]{1,0:T(8,128)(2,1)}, u32[]{:S(2)}, u32[]{:S(2)}) collective-permute-start(bf16[512,1024]{1,0:T(8,128)(2,1)} %param.22), channel_id=1, source_target_pairs={{0,16},{8,24},{16,0},{24,8},{1,17},{9,25},{17,1},{25,9},{2,18},{10... | collective-permute-start | bytes 3145736 | tf_op jit(solution)/shard_map/ppermute | solution.py:120
  10.3 58.4 %collective-permute-start.2 = (bf16[512,1024]{1,0:T(8,128)(2,1)}, bf16[512,1024]{1,0:T(8,128)(2,1)}, u32[]{:S(2)}, u32[]{:S(2)}) collective-permute-start(bf16[512,1024]{1,0:T(8,128)(2,1)} %param.22), channel_id=1, source_target_pairs={{0,24},{8,0},{16,8},{24,16},{1,25},{9,1},{17,9},{25,17},{2,26},{10... | collective-permute-start | bytes 3145736 | tf_op jit(solution)/shard_map/ppermute | solution.py:120
  21.3 3.8 %copy-start.10 = (s32[8]{0:T(128)S(1)}, s32[8]{0:T(128)}, u32[]{:S(2)}) copy-start(s32[8]{0:T(128)} %param.27) | copy-start | bytes 100
  21.4 4.0 %copy-start.9 = (s32[3]{0:T(128)S(1)}, s32[3]{0:T(128)}, u32[]{:S(2)}) copy-start(s32[3]{0:T(128)} %param.17) | copy-start | bytes 40
  21.4 4.1 %copy-start.3 = (bf16[3,256,1408]{2,1,0:T(8,128)(2,1)S(1)}, bf16[3,256,1408]{2,1,0:T(8,128)(2,1)}, u32[]{:S(2)}) copy-start(bf16[3,256,1408]{2,1,0:T(8,128)(2,1)} %param.15) | copy-start | bytes 6488068
  25.0 61.3 %all-gather.6.cloned.1.call-start = ((), (), s32[]{:S(2)}) async-start(), calls=%async_computation.1 | async-start | bytes 1966080 | tf_op jit(solution)/shard_map/all_gather | solution.py:237
  33.3 33.6 %copy-start.6 = (bf16[512,1024]{1,0:T(8,128)(2,1)S(1)}, bf16[512,1024]{1,0:T(8,128)(2,1)}, u32[]{:S(2)}) copy-start(bf16[512,1024]{1,0:T(8,128)(2,1)} %param.22) | copy-start | bytes 3145732
  66.0 107.8 %all-gather.8.cloned.1.call-start = ((), (), s32[]{:S(2)}) async-start(), calls=%async_computation.2 | async-start | bytes 4939776 | tf_op jit(solution)/shard_map/all_gather | solution.py:283
  68.4 4.0 %copy-start.4 = (bf16[512,1024]{1,0:T(8,128)(2,1)}, bf16[512,1024]{1,0:T(8,128)(2,1)S(1)}, u32[]{:S(2)}) copy-start(bf16[512,1024]{1,0:T(8,128)(2,1)S(1)} %fusion.43) | copy-start | bytes 3145732
  86.3 4.2 %copy-start.11 = (bf16[4096,2,256]{2,1,0:T(2,128)(2,1)S(1)}, bf16[4096,2,256]{2,1,0:T(2,128)(2,1)}, u32[]{:S(2)}) copy-start(bf16[4096,2,256]{2,1,0:T(2,128)(2,1)} %param.25) | copy-start | bytes 12582916
  86.3 4.2 %copy-start.13 = (f32[4096]{0:T(1024)S(1)}, f32[4096]{0:T(1024)}, u32[]{:S(2)}) copy-start(f32[4096]{0:T(1024)} %param.23) | copy-start | bytes 49156
  90.6 2.7 %copy-start.12 = (bf16[4096,512]{1,0:T(8,128)(2,1)S(1)}, bf16[4096,512]{1,0:T(8,128)(2,1)}, u32[]{:S(2)}) copy-start(bf16[4096,512]{1,0:T(8,128)(2,1)} %param.24) | copy-start | bytes 12582916
  97.8 135.3 %all-gather.10.cloned.1.call-start = ((), (), s32[]{:S(2)}) async-start(), calls=%async_computation.3 | async-start | bytes 2662400 | tf_op jit(solution)/shard_map/all_gather | solution.py:342
  103.7 25.0 %collective-permute-start.3 = (bf16[512,1024]{1,0:T(8,128)(2,1)}, bf16[512,1024]{1,0:T(8,128)(2,1)}, u32[]{:S(2)}, u32[]{:S(2)}) collective-permute-start(bf16[512,1024]{1,0:T(8,128)(2,1)} %get-tuple-element.23), channel_id=1, source_target_pairs={{0,8},{8,16},{16,24},{24,0},{1,9},{9,17},{17,25},{25,1},{2,10},{10... | collective-permute-start | bytes 3145736 | tf_op jit(solution)/shard_map/ppermute | solution.py:220
  104.0 26.3 %collective-permute-start.4 = (bf16[512,1024]{1,0:T(8,128)(2,1)}, bf16[512,1024]{1,0:T(8,128)(2,1)}, u32[]{:S(2)}, u32[]{:S(2)}) collective-permute-start(bf16[512,1024]{1,0:T(8,128)(2,1)} %get-tuple-element.22), channel_id=1, source_target_pairs={{0,16},{8,24},{16,0},{24,8},{1,17},{9,25},{17,1},{25,9},{2,18},{10... | collective-permute-start | bytes 3145736 | tf_op jit(solution)/shard_map/ppermute | solution.py:220
  104.3 45.5 %collective-permute-start.5 = (bf16[512,1024]{1,0:T(8,128)(2,1)}, bf16[512,1024]{1,0:T(8,128)(2,1)}, u32[]{:S(2)}, u32[]{:S(2)}) collective-permute-start(bf16[512,1024]{1,0:T(8,128)(2,1)} %get-tuple-element.21), channel_id=1, source_target_pairs={{0,24},{8,0},{16,8},{24,16},{1,25},{9,1},{17,9},{25,17},{2,26},{10... | collective-permute-start | bytes 3145736 | tf_op jit(solution)/shard_map/ppermute | solution.py:220
  200.1 38.7 %copy-start.7 = (f32[1024]{0:T(1024)S(1)}, f32[1024]{0:T(1024)}, u32[]{:S(2)}) copy-start(f32[1024]{0:T(1024)} %param.28) | copy-start | bytes 12292
  241.0 11.4 %collective-permute-start.6 = (f32[8,1025]{1,0:T(8,128)S(1)}, f32[8,1025]{1,0:T(8,128)S(1)}, u32[]{:S(2)}, u32[]{:S(2)}) collective-permute-start(f32[8,1025]{1,0:T(8,128)S(1)} %get-tuple-element.34), channel_id=1, source_target_pairs={{0,8},{8,16},{16,24},{24,0},{1,9},{9,17},{17,25},{25,1},{2,10},{10... | collective-permute-start | bytes 98408 | tf_op jit(solution)/shard_map/ppermute | solution.py:132
  241.3 11.1 %collective-permute-start.7 = (f32[8,1025]{1,0:T(8,128)S(1)}, f32[8,1025]{1,0:T(8,128)S(1)}, u32[]{:S(2)}, u32[]{:S(2)}) collective-permute-start(f32[8,1025]{1,0:T(8,128)S(1)} %get-tuple-element.34), channel_id=1, source_target_pairs={{0,16},{8,24},{16,0},{24,8},{1,17},{9,25},{17,1},{25,9},{2,18},{10... | collective-permute-start | bytes 98408 | tf_op jit(solution)/shard_map/ppermute | solution.py:132
  241.6 10.8 %collective-permute-start.8 = (f32[8,1025]{1,0:T(8,128)S(1)}, f32[8,1025]{1,0:T(8,128)S(1)}, u32[]{:S(2)}, u32[]{:S(2)}) collective-permute-start(f32[8,1025]{1,0:T(8,128)S(1)} %get-tuple-element.34), channel_id=1, source_target_pairs={{0,24},{8,0},{16,8},{24,16},{1,25},{9,1},{17,9},{25,17},{2,26},{10... | collective-permute-start | bytes 98408 | tf_op jit(solution)/shard_map/ppermute | solution.py:132
  244.6 4.5 %copy-start.5 = (bf16[512,1024]{1,0:T(8,128)(2,1)S(1)}, bf16[512,1024]{1,0:T(8,128)(2,1)}, u32[]{:S(2)}) copy-start(bf16[512,1024]{1,0:T(8,128)(2,1)} %copy-done.4) | copy-start | bytes 3145732
  246.8 19.3 %copy-start.1 = (bf16[1408,3,352]{0,2,1:T(8,128)(2,1)S(1)}, bf16[1408,3,352]{0,2,1:T(8,128)(2,1)}, u32[]{:S(2)}) copy-start(bf16[1408,3,352]{0,2,1:T(8,128)(2,1)} %param.19) | copy-start | bytes 8921092
  254.0 3.6 %collective-permute-start.9 = (f32[8]{0:T(128)S(1)}, f32[8]{0:T(128)S(1)}, u32[]{:S(2)}, u32[]{:S(2)}) collective-permute-start(f32[8]{0:T(128)S(1)} %get-tuple-element.39), channel_id=1, source_target_pairs={{0,1},{1,0},{2,3},{3,2},{4,5},{5,4},{6,7},{7,6},{8,9},{9,8},{10,11... | collective-permute-start | bytes 104 | tf_op jit(solution)/shard_map/ppermute | solution.py:149
  257.6 3.5 %collective-permute-start.10 = (f32[8]{0:T(128)S(1)}, f32[8]{0:T(128)S(1)}, u32[]{:S(2)}, u32[]{:S(2)}) collective-permute-start(f32[8]{0:T(128)S(1)} %max.9), channel_id=1, source_target_pairs={{0,2},{1,3},{2,0},{3,1},{4,6},{5,7},{6,4},{7,5},{8,10},{9,11},{10,... | collective-permute-start | bytes 104 | tf_op jit(solution)/shard_map/ppermute | solution.py:149
  261.2 4.4 %collective-permute-start.11 = (f32[8]{0:T(128)S(1)}, f32[8]{0:T(128)S(1)}, u32[]{:S(2)}, u32[]{:S(2)}) collective-permute-start(f32[8]{0:T(128)S(1)} %max.10), channel_id=1, source_target_pairs={{0,4},{1,5},{2,6},{3,7},{4,0},{5,1},{6,2},{7,3},{8,12},{9,13},{10,... | collective-permute-start | bytes 104 | tf_op jit(solution)/shard_map/ppermute | solution.py:149
Sparse Core Ops, SparseCore 0:
  25.1 37.3 all-reduce.1
  66.2 20.1 all-gather.5
  97.9 75.8 all-gather.7
  201.3 31.8 all-gather.9

commit v11 on v9

--- a/solution.py
+++ b/solution.py
@@ -112,17 +112,34 @@
     )(needed, grouped_q, gathered, gathered, q_ids, q_req, k_ids, k_req)
 
 
-def gather_by_permutes(local, count):
+def kv_exchange(local, count, paired):
     me = lax.axis_index("kv")
-    pieces = [local]
-    for shift in range(1, count):
-        pieces.append(
-            lax.ppermute(local, "kv", perm=[(i, (i + shift) % count) for i in range(count)])
-        )
-    stacked = jnp.stack(pieces)
-    order = (me - jnp.arange(count, dtype=jnp.int32)) % count
-    ordered = jnp.take(stacked, order, axis=0)
-    return jnp.concatenate([ordered[j] for j in range(count)], axis=1)
+    if paired:
+        chips = count // 2
+        chip, core = me // 2, me % 2
+        pieces = [local]
+        for shift in range(1, chips):
+            pieces.append(
+                lax.ppermute(
+                    local,
+                    "kv",
+                    perm=[(i, ((i // 2 + shift) % chips) * 2 + i % 2) for i in range(count)],
+                )
+            )
+        bundle = jnp.stack(pieces)
+        other = lax.ppermute(bundle, "kv", perm=[(i, i ^ 1) for i in range(count)])
+        stacked = jnp.concatenate([bundle, other])
+        source = jnp.arange(count, dtype=jnp.int32)
+        slot = (chip - source // 2) % chips + jnp.where(source % 2 == core, 0, chips)
+    else:
+        pieces = [local]
+        for shift in range(1, count):
+            pieces.append(
+                lax.ppermute(local, "kv", perm=[(i, (i + shift) % count) for i in range(count)])
+            )
+        stacked = jnp.stack(pieces)
+        slot = (me - jnp.arange(count, dtype=jnp.int32)) % count
+    return jnp.take(stacked, slot, axis=0)
 
 
 def permute_pieces(local, count):
@@ -153,6 +170,7 @@
 
 
 def on_device(
+    paired,
     patches,
     merged_grid,
     picture_start,
@@ -175,7 +193,8 @@
     vis_heads = vis_cols // VHD
     tok_rows, feat_dev = text_embed.shape
     kv_count = D // text_embed.shape[1]
-    text_rows = gather_by_permutes(text_embed, kv_count)
+    text_all = kv_exchange(text_embed, kv_count, paired)
+    text_rows = jnp.concatenate([text_all[j] for j in range(kv_count)], axis=1)
     inputs = patches.astype(jnp.float32)
     normed = layer_norm(inputs, vis_gain).astype(jnp.bfloat16)
     packed = jnp.einsum(
@@ -204,9 +223,7 @@
     head_part = jnp.einsum("pnc,cd->pnd", mixed_rows, vis_out, preferred_element_type=jnp.float32)
     head_pooled = jnp.mean(head_part.reshape(pictures, merged_max, 4, vis_width), axis=2)
     head_total = jnp.sum(
-        lax.all_gather(head_pooled.astype(jnp.bfloat16), "kv", axis=0, tiled=False).astype(
-            jnp.float32
-        ),
+        kv_exchange(head_pooled.astype(jnp.bfloat16), kv_count, paired).astype(jnp.float32),
         axis=0,
     )
     input_pooled = jnp.mean(inputs.reshape(pictures, merged_max, 4, vis_width), axis=2)
@@ -239,9 +256,8 @@
     )
     is_vision = jnp.any(one_hot, axis=1)
     seq_in = jnp.where(is_vision[:, None], placed.astype(jnp.bfloat16), text_embed)
-    merged_rows = lax.all_gather(
-        merged.reshape(pictures * merged_max, feat_dev), "kv", axis=1, tiled=True
-    )
+    merged_all = kv_exchange(merged.reshape(pictures * merged_max, feat_dev), kv_count, paired)
+    merged_rows = jnp.concatenate([merged_all[j] for j in range(kv_count)], axis=1)
     placed_rows = jnp.dot(one_hot.astype(jnp.bfloat16), merged_rows, preferred_element_type=jnp.float32)
     full_rows = jnp.where(is_vision[:, None], placed_rows.astype(jnp.bfloat16), text_rows)
     full_float = full_rows.astype(jnp.float32)
@@ -344,7 +360,7 @@
         last_parts.append((last_mix / last_sum[..., None]).reshape(reqs, per_group * HD))
     last_context = jnp.concatenate(last_parts, axis=1).astype(jnp.bfloat16)
     out_rows = jnp.concatenate([context, last_context], axis=0)
-    context_all = lax.all_gather(out_rows, "kv", axis=0, tiled=False)
+    context_all = kv_exchange(out_rows, kv_count, paired)
     head_sum = None
     for shift, piece in enumerate(weight_pieces):
         source = lax.dynamic_index_in_dim(
@@ -391,8 +407,14 @@
         P("kv"),
         P("blk", "kv"),
     )
+    devices = mesh.devices
+    kv_size = devices.shape[0]
+    paired = kv_size % 2 == 0 and all(
+        getattr(devices[2 * a, 0], "coords", None) == getattr(devices[2 * a + 1, 0], "coords", None)
+        for a in range(kv_size // 2)
+    )
     return jax.shard_map(
-        on_device,
+        functools.partial(on_device, bool(paired)),
         mesh=mesh,
         in_specs=placed,
         out_specs=(P("blk", "kv"), P(None, "kv"), P()),

time: 289 us -> 293 us (1.014); the launches traced: 288 us -> 288 us
  waiting for transfers between devices: 153 us -> 115 us
  starting transfers between devices: 14.9 us -> 28.5 us
  other arithmetic: 27.6 us -> 41 us
  local copies, waits for them, and re-layouts: 29.5 us -> 39.5 us
    all_gather x3 -> x0, waiting for transfers between devices: 56.4 us -> none  [the longest x1 31.9 us: on_device(): context_all = lax.all_gather(out_rows, 'kv', axis=0, tiled=False)]
    ppermute x3 -> x8, waiting for transfers between devices: 26.5 us -> 46.6 us  [the longest x4 44 us: kv_exchange(): lax.ppermute(local, 'kv', perm=[(i, (i // 2 + shift) % chips * 2 + i % 2)...]
    ppermute x3, starting transfers between devices: 6.14 us -> 15.9 us  [tree_max(): lax.ppermute(values, axis, perm=[(i, i ^ step) for i in range(count)])]
    concatenate x1 -> x4, other arithmetic: 0.06 us -> 6.78 us  [kv_exchange(): stacked = jnp.concatenate([bundle, other])]
    gather x1 -> x4, local copies, waits for them, and re-layouts: 4.97 us -> 10.9 us  [kv_exchange(): return jnp.take(stacked, slot, axis=0)]
    select_n x2 -> x5, other arithmetic: 2.67 us -> 6.26 us  [the longest x4 6.25 us: kv_exchange(): return jnp.take(stacked, slot, axis=0)]
    ppermute x3 -> x8, starting transfers between devices: 4.45 us -> 6.39 us  [the longest x4 6.31 us: kv_exchange(): lax.ppermute(local, 'kv', perm=[(i, (i // 2 + shift) % chips * 2 + i % 2)...]
  transfers between devices with their start and end apart: 16 -> 18, of which waited for: 10 -> 12; matrix products, arithmetic and copies ran while one was open for 14% -> 15% of each run, Pallas kernels for 0% -> 0%
where the time goes in v11:
time: 293 us; the launch traced here: 288 us
  waiting for transfers between devices  115 us (39%)
  other arithmetic  41 us (14%)
  local copies, waits for them, and re-layouts  39.5 us (13%)
  matrix products  34.4 us (12%)
  starting transfers between devices  28.5 us (10%)
  between operations  15.2 us (5%)
  Pallas kernels  14.2 us (5%)
    ppermute x4, waiting for transfers between devices, kv_exchange(): lax.ppermute(local, 'kv', perm=[(i, (i // 2 + shift) % chips * 2 + i % 2)...  44 us
    ppermute x3, waiting for transfers between devices, on_device(): lax.ppermute(payload, 'kv', perm=[(i, (i + shift) % kv_count) for i in ra...  39.3 us
    all_gather x1, waiting for transfers between devices, on_device(): gathered = lax.all_gather(shipped, 'blk', axis=0, tiled=False)  24.4 us
    ppermute x3, starting transfers between devices, tree_max(): lax.ppermute(values, axis, perm=[(i, i ^ step) for i in range(count)])  15.9 us
    pallas_call x1, Pallas kernels, flash_attention(): pl.pallas_call(functools.partial(flash_kernel, root=root), grid_spec=grid...  14.2 us
    gather x4, local copies, waits for them, and re-layouts, kv_exchange(): return jnp.take(stacked, slot, axis=0)  10.9 us
    concatenate x4, other arithmetic, kv_exchange(): stacked = jnp.concatenate([bundle, other])  6.78 us
    dot_general x4, matrix products, on_device(): part = jnp.dot(source, piece, preferred_element_type=jnp.float32)  6.7 us
  transfers between devices with their start and end apart: 18, of which 12 were waited for; matrix products, arithmetic and copies ran while one was open for 15% of the time, Pallas kernels for 0%

profile of v11, /device:TPU:0, one launch (start us, length us, event | category | flops | bytes accessed | tf_op | source)
XLA Modules:
  0.0 287.6 jit_solution(12939916354302485844)
XLA Ops:
  7.3 2.1 convert_reduce_fusion.1
  10.5 2.9 fusion.30
  20.7 2.9 %collective-permute-start = (bf16[3,64,1408]{2,1,0:T(8,128)(2,1)}, bf16[3,64,1408]{2,1,0:T(8,128)(2,1)S(1)}, u32[]{:S(2)}, u32[]{:S(2)}) collective-permute-start(bf16[3,64,1408]{2,1,0:T(8,128)(2,1)} %multiply_convert_fusion.1), channel_id=1, source_target_pairs={{0,16},{8,24},{16,0},{24,8},{1,17},{9,25},{17,1},{25,9},{2,18},{10... | collective-permute-start | bytes 1622024 | tf_op jit(solution)/shard_map/ppermute | solution.py:123
  25.0 12.0 %collective-permute-done = bf16[3,64,1408]{2,1,0:T(8,128)(2,1)S(1)} collective-permute-done((bf16[3,64,1408]{2,1,0:T(8,128)(2,1)}, bf16[3,64,1408]{2,1,0:T(8,128)(2,1)S(1)}, u32[]{:S(2)}, u32[]{:S(2)}) %collective-permute-start) | collective-permute-done | bytes 540704 | tf_op jit(solution)/shard_map/ppermute | solution.py:123
  38.0 2.9 %reshape.489 = f32[3,64,4,1408]{3,2,1,0:T(4,128)} reshape(bf16[3,256,1408]{2,1,0:T(8,128)(2,1)S(1)} %copy-done.3) | data formatting | bytes 6488064 | tf_op jit(solution)/shard_map/reshape | solution.py:229
  41.1 5.9 %reduce_sum.145 = f32[3,64,1408]{2,1,0:T(8,128)} reduce(f32[3,64,4,1408]{3,2,1,0:T(4,128)} %reshape.489, f32[]{:T(128)} %constant.259.clone.1), dimensions={2}, to_apply=%region_1.2 | reduce | flops 811008 | bytes 5406724 | tf_op jit(solution)/shard_map/reduce_sum | solution.py:229
  47.2 11.5 %collective-permute-done.4 = bf16[512,1024]{1,0:T(8,128)(2,1)} collective-permute-done((bf16[512,1024]{1,0:T(8,128)(2,1)}, bf16[512,1024]{1,0:T(8,128)(2,1)}, u32[]{:S(2)}, u32[]{:S(2)}) %collective-permute-start.4) | collective-permute-done | bytes 1048608 | tf_op jit(solution)/shard_map/ppermute | solution.py:123
  58.7 3.1 %pad_maximum_fusion.3 = bf16[2,512,1024]{2,1,0:T(8,128)(2,1)} fusion(bf16[1,512,1024]{2,1,0:T(8,128)(2,1)} %bitcast.28, bf16[1,512,1024]{2,1,0:T(8,128)(2,1)} %bitcast.27), kind=kLoop, calls=%fused_computation.52 | loop fusion | flops 1048576 | bytes 4194304 | tf_op jit(solution)/shard_map/stack | solution.py:129
  63.3 2.1 gather_fusion
  65.4 2.3 convert_reduce_fusion
  67.7 2.6 fusion.52
  70.3 1.8 collective-permute-start.2
  72.4 9.5 %collective-permute-done.2 = bf16[192,1024]{1,0:T(8,128)(2,1)S(1)} collective-permute-done((bf16[192,1024]{1,0:T(8,128)(2,1)S(1)}, bf16[192,1024]{1,0:T(8,128)(2,1)S(1)}, u32[]{:S(2)}, u32[]{:S(2)}) %collective-permute-start.2) | collective-permute-done | bytes 393248 | tf_op jit(solution)/shard_map/ppermute | solution.py:123
  82.6 1.8 fusion.51
  85.7 1.8 gather_fusion.1
  87.5 1.6 broadcast_select_fusion.2
  90.1 3.7 %pad_maximum_fusion = bf16[4,512,1024]{2,1,0:T(8,128)(2,1)} fusion(bf16[2,512,1024]{2,1,0:T(8,128)(2,1)} %collective-permute-done.5, bf16[1,512,1024]{2,1,0:T(8,128)(2,1)} %bitcast.28, bf16[1,512,1024]{2,1,0:T(8,128)(2,1)} %bitcast.27), kind=kLoop, calls=%fused_computation.27 | loop fusion | flops 4194304 | bytes 8388608 | tf_op jit(solution)/shard_map/concatenate | solution.py:131
  93.8 5.0 %gather_fusion.2 = bf16[4,512,1024]{2,1,0:T(8,128)(2,1)} fusion(bf16[4,512,1024]{2,1,0:T(8,128)(2,1)} %pad_maximum_fusion, s32[1024]{0:T(1024)S(1)} %pad_clamp_fusion.1), kind=kCustom, calls=%fused_computation.2 | custom fusion | bytes 8388624 | tf_op jit(solution)/shard_map/jit(_take)/gather | solution.py:142
  98.7 2.7 broadcast_select_fusion
  102.5 5.2 %fusion.2 = (f32[512]{0:T(512)S(1)}, bf16[512,4096]{1,0:T(8,128)(2,1)S(1)}) fusion(bf16[512,1024]{1,0:T(8,128)(2,1)S(1)} %get-tuple-element.28, bf16[512,1024]{1,0:T(8,128)(2,1)S(1)} %get-tuple-element.29, bf16[512,1024]{1,0:T(8,128)(2,1)S(1)} %get-tuple-element.30, bf16[512,1024]{1,0:T(8,128)(2,1)S(1)} %get-tuple-element.27, ...), kind=kOutput, calls=%fused_computation.9 | convolution fusion | flops 838958592 | bytes 9964800 | tf_op jit(solution)/shard_map/dot_general | solution.py:261
  107.8 2.5 fusion.14
  110.3 2.6 fusion.56
  117.6 3.9 %constant_dynamic-slice_fusion = (bf16[512,1024]{1,0:T(8,128)(2,1)S(1)}, bf16[512,1024]{1,0:T(8,128)(2,1)}, bf16[512,1024]{1,0:T(8,128)(2,1)}, bf16[512,1024]{1,0:T(8,128)(2,1)}) fusion(bf16[512,4096]{1,0:T(8,128)(2,1)} %param.26, s32[]{:T(128)S(6)} %select_n.293, s32[]{:T(128)S(6)} %select_n.291, s32[]{:T(128)S(6)} %select_n.289, s32[]{:T(128)S(6)} %select_n.287), kind=kLoop, calls=%fused_computation.195 | loop fusion | bytes 8388624 | tf_op jit(solution)/shard_map/dynamic_slice | solution.py:238
  122.0 1.7 collective-permute-start.7
  129.6 16.8 %collective-permute-done.6 = bf16[512,1024]{1,0:T(8,128)(2,1)} collective-permute-done((bf16[512,1024]{1,0:T(8,128)(2,1)}, bf16[512,1024]{1,0:T(8,128)(2,1)}, u32[]{:S(2)}, u32[]{:S(2)}) %collective-permute-start.6) | collective-permute-done | bytes 1048608 | tf_op jit(solution)/shard_map/ppermute | solution.py:242
  146.4 1.9 collective-permute-done.7
  148.3 20.6 %collective-permute-done.8 = bf16[512,1024]{1,0:T(8,128)(2,1)} collective-permute-done((bf16[512,1024]{1,0:T(8,128)(2,1)S(1)}, bf16[512,1024]{1,0:T(8,128)(2,1)}, u32[]{:S(2)}, u32[]{:S(2)}) %collective-permute-start.8) | collective-permute-done | bytes 1048608 | tf_op jit(solution)/shard_map/ppermute | solution.py:242
  168.9 24.4 %all-gather.3.cloned.1.call-done = bf16[4288,512]{1,0:T(8,128)(2,1)} async-done(((bf16[536,512]{1,0:T(8,128)(2,1)}), bf16[4288,512]{1,0:T(8,128)(2,1)}) %all-gather.3.cloned.1.call-update) | async-done | bytes 4390928 | tf_op jit(solution)/shard_map/all_gather | solution.py:304
  193.3 3.9 %fusion.123 = (bf16[8,512,128]{2,1,0:T(8,128)(2,1)}, bf16[8,512,128]{2,1,0:T(8,128)(2,1)S(1)}, bf16[8,512,128]{2,1,0:T(8,128)(2,1)}, bf16[8,512,128]{2,1,0:T(8,128)(2,1)S(1)}) fusion(bf16[8,536,512]{2,1,0:T(8,128)(2,1)} %bitcast.172), kind=kLoop, calls=%fused_computation.244 | loop fusion | bytes 8388608 | tf_op jit(solution)/shard_map/slice | solution.py:340
  198.2 14.2 %shard_map.166 = bf16[2,1024,128]{2,1,0:T(8,128)(2,1)} custom-call(s32[8]{0:T(128)} %and_convert_fusion.needed_ref, bf16[2,1024,128]{2,1,0:T(8,128)(2,1)} %bitcast.195, bf16[8,536,512]{2,1,0:T(8,128)(2,1)} %bitcast.174, bf16[8,536,512]{2,1,0:T(8,128)(2,1)} %bitcast.175, s32[1024,1]{1,0:T(8,128)} %broadcast_in_dim_reshape.9.qid_ref, ...), custom_call_target="tpu_custom_call" | custom-call | flops 4294967296 | bytes 5242880 | tf_op jit(solution)/shard_map/pallas_call | solution.py:102
  213.8 1.8 fusion.125
  215.6 1.8 fusion.124
  218.5 1.5 collective-permute-start.9
  220.0 11.1 %collective-permute-done.9 = bf16[520,512]{1,0:T(8,128)(2,1)S(1)} collective-permute-done((bf16[520,512]{1,0:T(8,128)(2,1)S(1)}, bf16[520,512]{1,0:T(8,128)(2,1)S(1)}, u32[]{:S(2)}, u32[]{:S(2)}) %collective-permute-start.9) | collective-permute-done | bytes 532512 | tf_op jit(solution)/shard_map/ppermute | solution.py:123
  233.6 2.5 collective-permute-done.10
  237.5 2.0 gather_fusion.3
  239.6 2.0 broadcast_select_fusion.1
  242.3 2.0 convolution_convert_fusion.3
  244.2 2.0 convolution_convert_fusion.2
  246.2 2.0 convert_add_fusion
  249.8 2.4 fusion.93
  255.2 2.5 fusion.29
  259.4 3.3 %collective-permute-start.14 = (f32[8]{0:T(128)S(1)}, f32[8]{0:T(128)S(1)}, u32[]{:S(2)}, u32[]{:S(2)}) collective-permute-start(f32[8]{0:T(128)S(1)} %get-tuple-element.47), channel_id=1, source_target_pairs={{0,1},{1,0},{2,3},{3,2},{4,5},{5,4},{6,7},{7,6},{8,9},{9,8},{10,11... | collective-permute-start | bytes 104 | tf_op jit(solution)/shard_map/ppermute | solution.py:166
  262.7 1.5 collective-permute-done.14
  264.2 3.6 %collective-permute-start.15 = (f32[8]{0:T(128)S(1)}, f32[8]{0:T(128)S(1)}, u32[]{:S(2)}, u32[]{:S(2)}) collective-permute-start(f32[8]{0:T(128)S(1)} %max.9), channel_id=1, source_target_pairs={{0,2},{1,3},{2,0},{3,1},{4,6},{5,7},{6,4},{7,5},{8,10},{9,11},{10,... | collective-permute-start | bytes 104 | tf_op jit(solution)/shard_map/ppermute | solution.py:166
  267.9 1.5 collective-permute-done.15
  269.4 8.9 %collective-permute-start.16 = (f32[8]{0:T(128)S(1)}, f32[8]{0:T(128)S(1)}, u32[]{:S(2)}, u32[]{:S(2)}) collective-permute-start(f32[8]{0:T(128)S(1)} %max.10), channel_id=1, source_target_pairs={{0,4},{1,5},{2,6},{3,7},{4,0},{5,1},{6,2},{7,3},{8,12},{9,13},{10,... | collective-permute-start | bytes 104 | tf_op jit(solution)/shard_map/ppermute | solution.py:166
  278.3 1.5 collective-permute-done.16
  (152 shorter events, 42.4 us)
Async XLA Ops:
  7.2 3.3 %copy-start = (bf16[1408,3,352]{0,2,1:T(8,128)(2,1)S(1)}, bf16[1408,3,352]{0,2,1:T(8,128)(2,1)}, u32[]{:S(2)}) copy-start(bf16[1408,3,352]{0,2,1:T(8,128)(2,1)} %param.19) | copy-start | bytes 8921092
  7.2 3.2 %copy-start.14 = (s32[3,2]{0,1:T(2,128)S(1)}, s32[3,2]{0,1:T(2,128)}, u32[]{:S(2)}) copy-start(s32[3,2]{0,1:T(2,128)} %param.16) | copy-start | bytes 76
  7.2 3.3 %copy-start.21 = (f32[1408]{0:T(1024)S(1)}, f32[1408]{0:T(1024)}, u32[]{:S(2)}) copy-start(f32[1408]{0:T(1024)} %param.18) | copy-start | bytes 16900
  7.2 186.1 %all-gather.3.cloned.1.call-start = ((), (), s32[]{:S(2)}) async-start(), calls=%async_computation | async-start | bytes 4939776 | tf_op jit(solution)/shard_map/all_gather | solution.py:304
  7.2 2.4 copy-start.2
  15.9 1.6 copy-start.19
  18.8 1.0 copy-start.6
  20.7 17.3 %copy-start.3 = (bf16[3,256,1408]{2,1,0:T(8,128)(2,1)S(1)}, bf16[3,256,1408]{2,1,0:T(8,128)(2,1)}, u32[]{:S(2)}) copy-start(bf16[3,256,1408]{2,1,0:T(8,128)(2,1)} %param.15) | copy-start | bytes 6488068
  20.7 16.2 %collective-permute-start = (bf16[3,64,1408]{2,1,0:T(8,128)(2,1)}, bf16[3,64,1408]{2,1,0:T(8,128)(2,1)S(1)}, u32[]{:S(2)}, u32[]{:S(2)}) collective-permute-start(bf16[3,64,1408]{2,1,0:T(8,128)(2,1)} %multiply_convert_fusion.1), channel_id=1, source_target_pairs={{0,16},{8,24},{16,0},{24,8},{1,17},{9,25},{17,1},{25,9},{2,18},{10... | collective-permute-start | bytes 1622024 | tf_op jit(solution)/shard_map/ppermute | solution.py:123
  23.6 35.1 %collective-permute-start.4 = (bf16[512,1024]{1,0:T(8,128)(2,1)}, bf16[512,1024]{1,0:T(8,128)(2,1)}, u32[]{:S(2)}, u32[]{:S(2)}) collective-permute-start(bf16[512,1024]{1,0:T(8,128)(2,1)} %param.22), channel_id=1, source_target_pairs={{0,16},{8,24},{16,0},{24,8},{1,17},{9,25},{17,1},{25,9},{2,18},{10... | collective-permute-start | bytes 3145736 | tf_op jit(solution)/shard_map/ppermute | solution.py:123
  38.0 23.8 %collective-permute-start.1 = (bf16[2,3,64,1408]{3,2,1,0:T(8,128)(2,1)}, bf16[2,3,64,1408]{3,2,1,0:T(8,128)(2,1)}, u32[]{:S(2)}, u32[]{:S(2)}) collective-permute-start(bf16[2,3,64,1408]{3,2,1,0:T(8,128)(2,1)} %pad_maximum_fusion.6), channel_id=1, source_target_pairs={{0,8},{8,0},{16,24},{24,16},{1,9},{9,1},{17,25},{25,17},{2,10},{10... | collective-permute-start | bytes 3244040 | tf_op jit(solution)/shard_map/ppermute | solution.py:130
  38.0 2.9 %copy-start.16 = (s32[8]{0:T(128)S(1)}, s32[8]{0:T(128)}, u32[]{:S(2)}) copy-start(s32[8]{0:T(128)} %param.27) | copy-start | bytes 100
  41.1 6.0 %copy-start.15 = (s32[3]{0:T(128)S(1)}, s32[3]{0:T(128)}, u32[]{:S(2)}) copy-start(s32[3]{0:T(128)} %param.17) | copy-start | bytes 40
  61.8 28.3 %collective-permute-start.5 = (bf16[2,512,1024]{2,1,0:T(8,128)(2,1)}, bf16[2,512,1024]{2,1,0:T(8,128)(2,1)}, u32[]{:S(2)}, u32[]{:S(2)}) collective-permute-start(bf16[2,512,1024]{2,1,0:T(8,128)(2,1)} %pad_maximum_fusion.3), channel_id=1, source_target_pairs={{0,8},{8,0},{16,24},{24,16},{1,9},{9,1},{17,25},{25,17},{2,10},{10... | collective-permute-start | bytes 6291464 | tf_op jit(solution)/shard_map/ppermute | solution.py:130
  65.4 2.3 copy-start.7
  70.3 11.6 %collective-permute-start.2 = (bf16[192,1024]{1,0:T(8,128)(2,1)S(1)}, bf16[192,1024]{1,0:T(8,128)(2,1)S(1)}, u32[]{:S(2)}, u32[]{:S(2)}) collective-permute-start(bf16[192,1024]{1,0:T(8,128)(2,1)S(1)} %bitcast.180), channel_id=1, source_target_pairs={{0,16},{8,24},{16,0},{24,8},{1,17},{9,25},{17,1},{25,9},{2,18},{10... | collective-permute-start | bytes 1179656 | tf_op jit(solution)/shard_map/ppermute | solution.py:123
  82.0 3.5 %collective-permute-start.3 = (bf16[2,192,1024]{2,1,0:T(8,128)(2,1)S(1)}, bf16[2,192,1024]{2,1,0:T(8,128)(2,1)S(1)}, u32[]{:S(2)}, u32[]{:S(2)}) collective-permute-start(bf16[2,192,1024]{2,1,0:T(8,128)(2,1)S(1)} %pad_maximum_fusion.7), channel_id=1, source_target_pairs={{0,8},{8,0},{16,24},{24,16},{1,9},{9,1},{17,25},{25,17},{2,10},{10... | collective-permute-start | bytes 2359304 | tf_op jit(solution)/shard_map/ppermute | solution.py:130
  84.4 1.1 copy-start.8
  101.4 1.0 copy-start.11
  101.4 1.1 copy-start.12
  102.5 5.3 %copy-start.17 = (bf16[4096,2,256]{2,1,0:T(2,128)(2,1)S(1)}, bf16[4096,2,256]{2,1,0:T(2,128)(2,1)}, u32[]{:S(2)}) copy-start(bf16[4096,2,256]{2,1,0:T(2,128)(2,1)} %param.25) | copy-start | bytes 12582916
  102.5 5.3 %copy-start.20 = (f32[4096]{0:T(1024)S(1)}, f32[4096]{0:T(1024)}, u32[]{:S(2)}) copy-start(f32[4096]{0:T(1024)} %param.23) | copy-start | bytes 49156
  107.8 2.5 copy-start.18
  110.3 2.7 copy-start.9
  112.9 1.0 slice-start
  121.5 24.9 %collective-permute-start.6 = (bf16[512,1024]{1,0:T(8,128)(2,1)}, bf16[512,1024]{1,0:T(8,128)(2,1)}, u32[]{:S(2)}, u32[]{:S(2)}) collective-permute-start(bf16[512,1024]{1,0:T(8,128)(2,1)} %get-tuple-element.25), channel_id=1, source_target_pairs={{0,8},{8,16},{16,24},{24,0},{1,9},{9,17},{17,25},{25,1},{2,10},{10... | collective-permute-start | bytes 3145736 | tf_op jit(solution)/shard_map/ppermute | solution.py:242
  122.0 26.3 %collective-permute-start.7 = (bf16[512,1024]{1,0:T(8,128)(2,1)}, bf16[512,1024]{1,0:T(8,128)(2,1)}, u32[]{:S(2)}, u32[]{:S(2)}) collective-permute-start(bf16[512,1024]{1,0:T(8,128)(2,1)} %get-tuple-element.24), channel_id=1, source_target_pairs={{0,16},{8,24},{16,0},{24,8},{1,17},{9,25},{17,1},{25,9},{2,18},{10... | collective-permute-start | bytes 3145736 | tf_op jit(solution)/shard_map/ppermute | solution.py:242
  123.7 45.2 %collective-permute-start.8 = (bf16[512,1024]{1,0:T(8,128)(2,1)S(1)}, bf16[512,1024]{1,0:T(8,128)(2,1)}, u32[]{:S(2)}, u32[]{:S(2)}) collective-permute-start(bf16[512,1024]{1,0:T(8,128)(2,1)S(1)} %get-tuple-element.23), channel_id=1, source_target_pairs={{0,24},{8,0},{16,8},{24,16},{1,25},{9,1},{17,9},{25,17},{2,26},{10... | collective-permute-start | bytes 3145736 | tf_op jit(solution)/shard_map/ppermute | solution.py:242
  218.5 12.7 %collective-permute-start.9 = (bf16[520,512]{1,0:T(8,128)(2,1)S(1)}, bf16[520,512]{1,0:T(8,128)(2,1)S(1)}, u32[]{:S(2)}, u32[]{:S(2)}) collective-permute-start(bf16[520,512]{1,0:T(8,128)(2,1)S(1)} %copy.90), channel_id=1, source_target_pairs={{0,16},{8,24},{16,0},{24,8},{1,17},{9,25},{17,1},{25,9},{2,18},{10... | collective-permute-start | bytes 1597448 | tf_op jit(solution)/shard_map/ppermute | solution.py:123
  233.1 3.0 %collective-permute-start.10 = (bf16[2,520,512]{2,1,0:T(8,128)(2,1)}, bf16[2,520,512]{2,1,0:T(8,128)(2,1)}, u32[]{:S(2)}, u32[]{:S(2)}) collective-permute-start(bf16[2,520,512]{2,1,0:T(8,128)(2,1)} %copy.92), channel_id=1, source_target_pairs={{0,8},{8,0},{16,24},{24,16},{1,9},{9,1},{17,25},{25,17},{2,10},{10... | collective-permute-start | bytes 3194888 | tf_op jit(solution)/shard_map/ppermute | solution.py:130
  239.6 2.0 copy-start.10
  246.2 3.6 %copy-start.13 = (f32[1024]{0:T(1024)S(1)}, f32[1024]{0:T(1024)}, u32[]{:S(2)}) copy-start(f32[1024]{0:T(1024)} %param.28) | copy-start | bytes 12292
  248.3 1.4 copy-start.4
  249.8 5.4 %copy-start.5 = (f32[520,1024]{1,0:T(8,128)S(1)}, f32[520,1024]{1,0:T(8,128)}, u32[]{:S(2)}) copy-start(f32[520,1024]{1,0:T(8,128)} %copy-done.4) | copy-start | bytes 6389764
  252.2 28.1 %copy-start.1 = (bf16[1408,3,352]{0,2,1:T(8,128)(2,1)S(1)}, bf16[1408,3,352]{0,2,1:T(8,128)(2,1)}, u32[]{:S(2)}) copy-start(bf16[1408,3,352]{0,2,1:T(8,128)(2,1)} %param.19) | copy-start | bytes 8921092
  252.3 5.5 %collective-permute-start.11 = (f32[8,1025]{1,0:T(8,128)S(1)}, f32[8,1025]{1,0:T(8,128)S(1)}, u32[]{:S(2)}, u32[]{:S(2)}) collective-permute-start(f32[8,1025]{1,0:T(8,128)S(1)} %get-tuple-element.42), channel_id=1, source_target_pairs={{0,8},{8,16},{16,24},{24,0},{1,9},{9,17},{17,25},{25,1},{2,10},{10... | collective-permute-start | bytes 98408 | tf_op jit(solution)/shard_map/ppermute | solution.py:149
  252.4 5.4 %collective-permute-start.12 = (f32[8,1025]{1,0:T(8,128)S(1)}, f32[8,1025]{1,0:T(8,128)S(1)}, u32[]{:S(2)}, u32[]{:S(2)}) collective-permute-start(f32[8,1025]{1,0:T(8,128)S(1)} %get-tuple-element.42), channel_id=1, source_target_pairs={{0,16},{8,24},{16,0},{24,8},{1,17},{9,25},{17,1},{25,9},{2,18},{10... | collective-permute-start | bytes 98408 | tf_op jit(solution)/shard_map/ppermute | solution.py:149
  253.9 3.9 %collective-permute-start.13 = (f32[8,1025]{1,0:T(8,128)S(1)}, f32[8,1025]{1,0:T(8,128)S(1)}, u32[]{:S(2)}, u32[]{:S(2)}) collective-permute-start(f32[8,1025]{1,0:T(8,128)S(1)} %get-tuple-element.42), channel_id=1, source_target_pairs={{0,24},{8,0},{16,8},{24,16},{1,25},{9,1},{17,9},{25,17},{2,26},{10... | collective-permute-start | bytes 98408 | tf_op jit(solution)/shard_map/ppermute | solution.py:149
  259.4 4.9 %collective-permute-start.14 = (f32[8]{0:T(128)S(1)}, f32[8]{0:T(128)S(1)}, u32[]{:S(2)}, u32[]{:S(2)}) collective-permute-start(f32[8]{0:T(128)S(1)} %get-tuple-element.47), channel_id=1, source_target_pairs={{0,1},{1,0},{2,3},{3,2},{4,5},{5,4},{6,7},{7,6},{8,9},{9,8},{10,11... | collective-permute-start | bytes 104 | tf_op jit(solution)/shard_map/ppermute | solution.py:166
  264.2 5.2 %collective-permute-start.15 = (f32[8]{0:T(128)S(1)}, f32[8]{0:T(128)S(1)}, u32[]{:S(2)}, u32[]{:S(2)}) collective-permute-start(f32[8]{0:T(128)S(1)} %max.9), channel_id=1, source_target_pairs={{0,2},{1,3},{2,0},{3,1},{4,6},{5,7},{6,4},{7,5},{8,10},{9,11},{10,... | collective-permute-start | bytes 104 | tf_op jit(solution)/shard_map/ppermute | solution.py:166
  269.4 10.4 %collective-permute-start.16 = (f32[8]{0:T(128)S(1)}, f32[8]{0:T(128)S(1)}, u32[]{:S(2)}, u32[]{:S(2)}) collective-permute-start(f32[8]{0:T(128)S(1)} %max.10), channel_id=1, source_target_pairs={{0,4},{1,5},{2,6},{3,7},{4,0},{5,1},{6,2},{7,3},{8,12},{9,13},{10,... | collective-permute-start | bytes 104 | tf_op jit(solution)/shard_map/ppermute | solution.py:166
Sparse Core Ops, SparseCore 0:
  115.8 77.4 all-gather.2

commit v12 on v7

--- a/solution.py
+++ b/solution.py
@@ -73,7 +73,12 @@
 
     @pl.when(kb == pl.num_programs(1) - 1)
     def _():
-        o_ref[...] = (acc_ref[...] / sum_ref[...]).astype(o_ref.dtype)
+        rows = o_ref.shape[0]
+        for head in range(o_ref.shape[1] // HD):
+            part = slice(head * rows, (head + 1) * rows)
+            o_ref[:, head * HD : (head + 1) * HD] = (acc_ref[part, :] / sum_ref[part, :]).astype(
+                o_ref.dtype
+            )
 
 
 def flash_attention(needed, grouped_q, gathered, q_ids, q_req, k_ids, k_req, groups, tok_rows, root):
@@ -91,7 +96,7 @@
             pl.BlockSpec((None, 1, tok_rows), lambda g, kb, n: (kb, 0, 0)),
             pl.BlockSpec((None, 1, tok_rows), lambda g, kb, n: (kb, 0, 0)),
         ],
-        out_specs=pl.BlockSpec((None, group_rows, HD), lambda g, kb, n: (g, 0, 0)),
+        out_specs=pl.BlockSpec((tok_rows, group_rows // tok_rows * HD), lambda g, kb, n: (0, g)),
         scratch_shapes=[
             pltpu.VMEM((group_rows, 1), jnp.float32),
             pltpu.VMEM((group_rows, 1), jnp.float32),
@@ -102,7 +107,7 @@
     return pl.pallas_call(
         functools.partial(flash_kernel, root=root),
         grid_spec=grid_spec,
-        out_shape=jax.ShapeDtypeStruct((groups, group_rows, HD), jnp.bfloat16),
+        out_shape=jax.ShapeDtypeStruct((tok_rows, groups * group_rows // tok_rows * HD), jnp.bfloat16),
         compiler_params=pltpu.CompilerParams(dimension_semantics=("arbitrary", "arbitrary")),
         cost_estimate=pl.CostEstimate(
             flops=flops,
@@ -296,10 +301,10 @@
     ).astype(jnp.int32)
     group_rows = tok_rows * per_group
     grouped_q = jnp.transpose(
-        query_proj.reshape(tok_rows, kv_heads, per_group, HD), (1, 0, 2, 3)
+        query_proj.reshape(tok_rows, kv_heads, per_group, HD), (1, 2, 0, 3)
     ).reshape(kv_heads, group_rows, HD)
-    q_ids = jnp.repeat(row_ids, per_group)[:, None]
-    q_req = jnp.repeat(query_req, per_group)[:, None]
+    q_ids = jnp.tile(row_ids, per_group)[:, None]
+    q_req = jnp.tile(query_req, per_group)[:, None]
     all_ids = jnp.arange(blocks * tok_rows, dtype=jnp.int32)
     all_req, unused = request_info(all_ids, req_lengths)
     k_ids = all_ids.reshape(blocks, 1, tok_rows)
@@ -307,9 +312,6 @@
     context = flash_attention(
         needed, grouped_q, gathered, q_ids, q_req, k_ids, k_req, kv_heads, tok_rows, root
     )
-    context = jnp.transpose(
-        context.reshape(kv_heads, tok_rows, per_group, HD), (1, 0, 2, 3)
-    ).reshape(tok_rows, kv_heads * per_group * HD)
     all_ids = jnp.arange(blocks * tok_rows, dtype=jnp.int32)
     last_begin = ends_at - req_lengths
     last_allowed = (all_ids[None, :] >= last_begin[:, None]) & (all_ids[None, :] <= last_ids[:, None])

time: 269 us -> 269 us (level)
  local copies, waits for them, and re-layouts: 29 us -> 25.9 us
  other arithmetic: 24.9 us -> 27.8 us
where the time goes in v12:
time: 269 us; the launch traced here: 268 us
  waiting for transfers between devices  134 us (50%)
  matrix products  37 us (14%)
  other arithmetic  27.8 us (10%)
  local copies, waits for them, and re-layouts  25.9 us (10%)
  starting transfers between devices  14.5 us (5%)
  Pallas kernels  14.4 us (5%)
  between operations  14.4 us (5%)
    ppermute x3, waiting for transfers between devices, on_device(): lax.ppermute(payload, 'kv', perm=[(i, (i + shift) % kv_count) for i in ra...  39.1 us
    all_gather x1, waiting for transfers between devices, on_device(): context_all = lax.all_gather(out_rows, 'kv', axis=0, tiled=False)  31.9 us
    psum x1, waiting for transfers between devices, on_device(): lax.psum(head_pooled.astype(jnp.bfloat16), 'kv').astype(jnp.float32)  29 us
    all_gather x1, waiting for transfers between devices, on_device(): gathered = lax.all_gather(shipped, 'blk', axis=0, tiled=False)  24.1 us
    pallas_call x1, Pallas kernels, flash_attention(): pl.pallas_call(functools.partial(flash_kernel, root=root), grid_spec=grid...  14.4 us
    dot_general x4, matrix products, on_device(): part = jnp.dot(source, piece, preferred_element_type=jnp.float32)  8.03 us
    ppermute x3, starting transfers between devices, tree_max(): lax.ppermute(values, axis, perm=[(i, i ^ step) for i in range(count)])  6.09 us
    ppermute x3, waiting for transfers between devices, tree_max(): lax.ppermute(values, axis, perm=[(i, i ^ step) for i in range(count)])  5.48 us
  transfers between devices with their start and end apart: 16, of which 10 were waited for; matrix products, arithmetic and copies ran while one was open for 20% of the time, Pallas kernels for 0%

profile of v12, /device:TPU:0, one launch (start us, length us, event | category | flops | bytes accessed | tf_op | source)
XLA Modules:
  0.0 268.0 jit_solution(7805504700800627862)
XLA Ops:
  7.8 2.6 collective-permute-start.1
  10.3 1.4 collective-permute-start.2
  11.7 2.0 convert_reduce_fusion
  14.5 2.9 %fusion.30 = bf16[3,256,3,352]{1,3,2,0:T(8,128)(2,1)S(1)} fusion(bf16[1408,3,352]{0,2,1:T(8,128)(2,1)S(1)} %copy-done, bf16[3,256,1408]{2,1,0:T(8,128)(2,1)S(1)} %copy-done.2, f32[1408]{0:T(1024)S(1)} %copy-done.17, f32[3,256]{1,0:T(4,128)S(1)} %add_rsqrt_fusion, f32[3,256]{1,0:T(4,128)S(1)} %broadcast_multiply_fusion), kind=kOutput, calls=%fused_computation.46 | convolution fusion | flops 2290016256 | bytes 6770176 | tf_op jit(solution)/shard_map/pnd,dce->pnce/dot_general | solution.py:186
  21.4 2.7 %convolution_reduce_fusion = f32[3,64,1408]{2,1,0:T(8,128)S(1)} fusion(bf16[352,1408]{1,0:T(8,128)(2,1)} %param.20, bf16[3,64,4,352]{3,2,1,0:T(4,128)(2,1)S(1)} %dot_general.65), kind=kOutput, calls=%fused_computation.45 | convolution fusion | flops 762077184 | bytes 2613248 | tf_op jit(solution)/shard_map/pnc,cd->pnd/dot_general | solution.py:209
  25.5 2.9 %reshape.367 = f32[3,64,4,1408]{3,2,1,0:T(4,128)} reshape(bf16[3,256,1408]{2,1,0:T(8,128)(2,1)S(1)} %copy-done.3) | data formatting | bytes 6488064 | tf_op jit(solution)/shard_map/reshape | solution.py:212
  28.5 4.8 %reduce_sum.136 = f32[3,64,1408]{2,1,0:T(8,128)S(1)} reduce(f32[3,64,4,1408]{3,2,1,0:T(4,128)} %reshape.367, f32[]{:T(128)} %constant.144.clone.1), dimensions={2}, to_apply=%region_1.2 | reduce | flops 811008 | bytes 5406724 | tf_op jit(solution)/shard_map/reduce_sum | solution.py:212
  33.5 29.0 %all-reduce.2.cloned.1.call-done = bf16[3,64,1408]{2,1,0:T(8,128)(2,1)} async-done(((bf16[3,64,1408]{2,1,0:T(8,128)(2,1)}), bf16[3,64,1408]{2,1,0:T(8,128)(2,1)}) %all-reduce.2.cloned.1.call-update) | async-done | bytes 540688 | tf_op jit(solution)/shard_map/psum | solution.py:211
  62.5 3.5 %fusion.45 = bf16[3,64,1024]{2,1,0:T(8,128)(2,1)} fusion(bf16[1408,1024]{1,0:T(8,128)(2,1)} %param.21, bf16[3,64,1408]{2,1,0:T(8,128)(2,1)} %all-reduce.2.cloned.1.call-done, f32[3,64,1408]{2,1,0:T(8,128)S(1)} %reduce_sum.136), kind=kOutput, calls=%fused_computation.59 | convolution fusion | flops 554926080 | bytes 4898816 | tf_op jit(solution)/shard_map/pmd,de->pme/dot_general | solution.py:214
  66.9 1.6 fusion.44
  68.7 3.7 %pad_maximum_fusion = bf16[4,512,1024]{2,1,0:T(8,128)(2,1)} fusion(bf16[1,512,1024]{2,1,0:T(8,128)(2,1)} %bitcast.21, bf16[1,512,1024]{2,1,0:T(8,128)(2,1)} %bitcast.20, bf16[1,512,1024]{2,1,0:T(8,128)(2,1)} %bitcast.19, bf16[1,512,1024]{2,1,0:T(8,128)(2,1)S(1)} %bitcast.178), kind=kLoop, calls=%fused_computation.23 | loop fusion | flops 6291456 | bytes 8388608 | tf_op jit(solution)/shard_map/stack | solution.py:127
  72.4 5.3 %gather_fusion = bf16[4,512,1024]{2,1,0:T(8,128)(2,1)} fusion(bf16[4,512,1024]{2,1,0:T(8,128)(2,1)} %pad_maximum_fusion, s32[1024]{0:T(1024)S(1)} %pad_clamp_fusion), kind=kCustom, calls=%fused_computation | custom fusion | bytes 8388624 | tf_op jit(solution)/shard_map/jit(_take)/gather | solution.py:129
  77.7 2.7 broadcast_select_fusion
  80.4 1.8 slice_bitcast_fusion.3
  82.1 4.2 %all-gather.6.cloned.1.call-done = bf16[192,4096]{1,0:T(8,128)(2,1)} async-done(((bf16[192,1024]{1,0:T(8,128)(2,1)}), bf16[192,4096]{1,0:T(8,128)(2,1)}) %all-gather.6.cloned.1.call-update) | async-done | bytes 1572880 | tf_op jit(solution)/shard_map/all_gather | solution.py:242
  86.3 4.2 %fusion.2 = (f32[512]{0:T(512)S(1)}, bf16[512,4096]{1,0:T(8,128)(2,1)S(1)}) fusion(bf16[512,1024]{1,0:T(8,128)(2,1)S(1)} %get-tuple-element.28, bf16[512,1024]{1,0:T(8,128)(2,1)} %get-tuple-element.29, bf16[512,1024]{1,0:T(8,128)(2,1)} %get-tuple-element.30, bf16[512,1024]{1,0:T(8,128)(2,1)S(1)} %get-tuple-element.27, ...), kind=kOutput, calls=%fused_computation.6 | convolution fusion | flops 832667136 | bytes 9964800 | tf_op jit(solution)/shard_map/dot_general | solution.py:245
  90.6 2.6 fusion.14
  93.3 2.6 fusion.49
  96.7 1.0 copy.64
  99.7 3.9 %constant_dynamic-slice_fusion = (bf16[512,1024]{1,0:T(8,128)(2,1)S(1)}, bf16[512,1024]{1,0:T(8,128)(2,1)}, bf16[512,1024]{1,0:T(8,128)(2,1)}, bf16[512,1024]{1,0:T(8,128)(2,1)}) fusion(bf16[512,4096]{1,0:T(8,128)(2,1)} %param.26, s32[]{:T(128)S(6)} %select_n.159, s32[]{:T(128)S(6)} %select_n.157, s32[]{:T(128)S(6)} %select_n.155, s32[]{:T(128)S(6)} %select_n.153), kind=kLoop, calls=%fused_computation.163 | loop fusion | bytes 8388624 | tf_op jit(solution)/shard_map/dynamic_slice | solution.py:221
  104.2 1.2 collective-permute-start.5
  105.5 1.2 and_convert_fusion.needed_ref
  106.7 1.1 copy.77
  109.4 1.1 pad_maximum_fusion.2
  110.5 18.1 %collective-permute-done.3 = bf16[512,1024]{1,0:T(8,128)(2,1)} collective-permute-done((bf16[512,1024]{1,0:T(8,128)(2,1)}, bf16[512,1024]{1,0:T(8,128)(2,1)}, u32[]{:S(2)}, u32[]{:S(2)}) %collective-permute-start.3) | collective-permute-done | bytes 1048608 | tf_op jit(solution)/shard_map/ppermute | solution.py:225
  128.7 1.6 collective-permute-done.4
  130.2 19.4 %collective-permute-done.5 = bf16[512,1024]{1,0:T(8,128)(2,1)} collective-permute-done((bf16[512,1024]{1,0:T(8,128)(2,1)S(1)}, bf16[512,1024]{1,0:T(8,128)(2,1)}, u32[]{:S(2)}, u32[]{:S(2)}) %collective-permute-start.5) | collective-permute-done | bytes 1048608 | tf_op jit(solution)/shard_map/ppermute | solution.py:225
  149.7 24.1 %all-gather.8.cloned.1.call-done = bf16[4288,512]{1,0:T(8,128)(2,1)} async-done(((bf16[536,512]{1,0:T(8,128)(2,1)}), bf16[4288,512]{1,0:T(8,128)(2,1)}) %all-gather.8.cloned.1.call-update) | async-done | bytes 4390928 | tf_op jit(solution)/shard_map/all_gather | solution.py:288
  173.8 4.0 %fusion.107 = (bf16[8,512,128]{2,1,0:T(8,128)(2,1)}, bf16[8,512,128]{2,1,0:T(8,128)(2,1)S(1)}, bf16[8,512,128]{2,1,0:T(8,128)(2,1)}, bf16[8,512,128]{2,1,0:T(8,128)(2,1)S(1)}) fusion(bf16[8,536,512]{2,1,0:T(8,128)(2,1)} %bitcast.162), kind=kLoop, calls=%fused_computation.190 | loop fusion | bytes 8388608 | tf_op jit(solution)/shard_map/slice | solution.py:321
  178.8 1.8 fusion.109
  180.7 1.8 fusion.108
  183.0 14.4 %shard_map.166 = bf16[512,512]{1,0:T(8,128)(2,1)} custom-call(s32[8]{0:T(128)} %and_convert_fusion.needed_ref, bf16[2,1024,128]{2,1,0:T(8,128)(2,1)} %bitcast.179, bf16[8,536,512]{2,1,0:T(8,128)(2,1)} %bitcast.164, bf16[8,536,512]{2,1,0:T(8,128)(2,1)} %bitcast.165, s32[1024,1]{1,0:T(8,128)} %bitcast.181, s32[1024,1]{1,0:T(8,128)} %bitcast.180, ...), custom_call_target="tpu_custom_call" | custom-call | flops 4294967296 | bytes 5242880 | tf_op jit(solution)/shard_map/pallas_call | solution.py:107
  197.4 1.9 maximum_maximum_fusion
  199.4 31.9 %all-gather.10.cloned.1.call-done = bf16[2080,512]{1,0:T(8,128)(2,1)} async-done(((bf16[520,512]{1,0:T(8,128)(2,1)}), bf16[2080,512]{1,0:T(8,128)(2,1)}) %all-gather.10.cloned.1.call-update) | async-done | bytes 2129936 | tf_op jit(solution)/shard_map/all_gather | solution.py:344
  231.3 1.9 convolution_convert_fusion.4
  233.2 2.1 convolution_convert_fusion.3
  235.3 2.0 convolution_convert_fusion.2
  237.3 2.0 convert_add_fusion
  239.4 1.3 copy-done.4
  240.9 2.4 fusion.86
  243.9 1.2 collective-permute-start.8
  245.2 2.5 fusion.29
  249.3 1.7 collective-permute-start.9
  251.1 1.8 collective-permute-done.9
  252.9 1.7 collective-permute-start.10
  254.6 1.8 collective-permute-done.10
  256.5 2.6 collective-permute-start.11
  259.1 1.8 collective-permute-done.11
  (119 shorter events, 17.5 us)
Async XLA Ops:
  7.2 7.4 %copy-start = (bf16[1408,3,352]{0,2,1:T(8,128)(2,1)S(1)}, bf16[1408,3,352]{0,2,1:T(8,128)(2,1)}, u32[]{:S(2)}) copy-start(bf16[1408,3,352]{0,2,1:T(8,128)(2,1)} %param.19) | copy-start | bytes 8921092
  7.2 7.2 %copy-start.11 = (s32[3,2]{0,1:T(2,128)S(1)}, s32[3,2]{0,1:T(2,128)}, u32[]{:S(2)}) copy-start(s32[3,2]{0,1:T(2,128)} %param.16) | copy-start | bytes 76
  7.2 7.3 %copy-start.17 = (f32[1408]{0:T(1024)S(1)}, f32[1408]{0:T(1024)}, u32[]{:S(2)}) copy-start(f32[1408]{0:T(1024)} %param.18) | copy-start | bytes 16900
  7.2 55.3 %all-reduce.2.cloned.1.call-start = ((), (), s32[]{:S(2)}) async-start(), calls=%async_computation | async-start | bytes 1081344 | tf_op jit(solution)/shard_map/psum | solution.py:211
  7.2 6.4 %copy-start.2 = (bf16[3,256,1408]{2,1,0:T(8,128)(2,1)S(1)}, bf16[3,256,1408]{2,1,0:T(8,128)(2,1)}, u32[]{:S(2)}) copy-start(bf16[3,256,1408]{2,1,0:T(8,128)(2,1)} %param.15) | copy-start | bytes 6488068
  7.3 61.5 %collective-permute-start = (bf16[512,1024]{1,0:T(8,128)(2,1)}, bf16[512,1024]{1,0:T(8,128)(2,1)}, u32[]{:S(2)}, u32[]{:S(2)}) collective-permute-start(bf16[512,1024]{1,0:T(8,128)(2,1)} %param.22), channel_id=1, source_target_pairs={{0,8},{8,16},{16,24},{24,0},{1,9},{9,17},{17,25},{25,1},{2,10},{10... | collective-permute-start | bytes 3145736 | tf_op jit(solution)/shard_map/ppermute | solution.py:125
  7.8 61.0 %collective-permute-start.1 = (bf16[512,1024]{1,0:T(8,128)(2,1)}, bf16[512,1024]{1,0:T(8,128)(2,1)}, u32[]{:S(2)}, u32[]{:S(2)}) collective-permute-start(bf16[512,1024]{1,0:T(8,128)(2,1)} %param.22), channel_id=1, source_target_pairs={{0,16},{8,24},{16,0},{24,8},{1,17},{9,25},{17,1},{25,9},{2,18},{10... | collective-permute-start | bytes 3145736 | tf_op jit(solution)/shard_map/ppermute | solution.py:125
  10.3 58.4 %collective-permute-start.2 = (bf16[512,1024]{1,0:T(8,128)(2,1)}, bf16[512,1024]{1,0:T(8,128)(2,1)}, u32[]{:S(2)}, u32[]{:S(2)}) collective-permute-start(bf16[512,1024]{1,0:T(8,128)(2,1)} %param.22), channel_id=1, source_target_pairs={{0,24},{8,0},{16,8},{24,16},{1,25},{9,1},{17,9},{25,17},{2,26},{10... | collective-permute-start | bytes 3145736 | tf_op jit(solution)/shard_map/ppermute | solution.py:125
  21.3 3.8 %copy-start.13 = (s32[8]{0:T(128)S(1)}, s32[8]{0:T(128)}, u32[]{:S(2)}) copy-start(s32[8]{0:T(128)} %param.27) | copy-start | bytes 100
  21.4 4.0 %copy-start.12 = (s32[3]{0:T(128)S(1)}, s32[3]{0:T(128)}, u32[]{:S(2)}) copy-start(s32[3]{0:T(128)} %param.17) | copy-start | bytes 40
  21.4 4.1 %copy-start.3 = (bf16[3,256,1408]{2,1,0:T(8,128)(2,1)S(1)}, bf16[3,256,1408]{2,1,0:T(8,128)(2,1)}, u32[]{:S(2)}) copy-start(bf16[3,256,1408]{2,1,0:T(8,128)(2,1)} %param.15) | copy-start | bytes 6488068
  25.0 61.3 %all-gather.6.cloned.1.call-start = ((), (), s32[]{:S(2)}) async-start(), calls=%async_computation.1 | async-start | bytes 1966080 | tf_op jit(solution)/shard_map/all_gather | solution.py:242
  33.3 33.6 %copy-start.8 = (bf16[512,1024]{1,0:T(8,128)(2,1)S(1)}, bf16[512,1024]{1,0:T(8,128)(2,1)}, u32[]{:S(2)}) copy-start(bf16[512,1024]{1,0:T(8,128)(2,1)} %param.22) | copy-start | bytes 3145732
  66.0 107.8 %all-gather.8.cloned.1.call-start = ((), (), s32[]{:S(2)}) async-start(), calls=%async_computation.2 | async-start | bytes 4939776 | tf_op jit(solution)/shard_map/all_gather | solution.py:288
  68.4 4.0 %copy-start.6 = (bf16[512,1024]{1,0:T(8,128)(2,1)}, bf16[512,1024]{1,0:T(8,128)(2,1)S(1)}, u32[]{:S(2)}) copy-start(bf16[512,1024]{1,0:T(8,128)(2,1)S(1)} %fusion.44) | copy-start | bytes 3145732
  86.3 4.2 %copy-start.14 = (bf16[4096,2,256]{2,1,0:T(2,128)(2,1)S(1)}, bf16[4096,2,256]{2,1,0:T(2,128)(2,1)}, u32[]{:S(2)}) copy-start(bf16[4096,2,256]{2,1,0:T(2,128)(2,1)} %param.25) | copy-start | bytes 12582916
  86.3 4.2 %copy-start.16 = (f32[4096]{0:T(1024)S(1)}, f32[4096]{0:T(1024)}, u32[]{:S(2)}) copy-start(f32[4096]{0:T(1024)} %param.23) | copy-start | bytes 49156
  90.6 2.7 %copy-start.15 = (bf16[4096,512]{1,0:T(8,128)(2,1)S(1)}, bf16[4096,512]{1,0:T(8,128)(2,1)}, u32[]{:S(2)}) copy-start(bf16[4096,512]{1,0:T(8,128)(2,1)} %param.24) | copy-start | bytes 12582916
  97.8 133.5 %all-gather.10.cloned.1.call-start = ((), (), s32[]{:S(2)}) async-start(), calls=%async_computation.3 | async-start | bytes 2662400 | tf_op jit(solution)/shard_map/all_gather | solution.py:344
  103.7 25.0 %collective-permute-start.3 = (bf16[512,1024]{1,0:T(8,128)(2,1)}, bf16[512,1024]{1,0:T(8,128)(2,1)}, u32[]{:S(2)}, u32[]{:S(2)}) collective-permute-start(bf16[512,1024]{1,0:T(8,128)(2,1)} %get-tuple-element.25), channel_id=1, source_target_pairs={{0,8},{8,16},{16,24},{24,0},{1,9},{9,17},{17,25},{25,1},{2,10},{10... | collective-permute-start | bytes 3145736 | tf_op jit(solution)/shard_map/ppermute | solution.py:225
  103.9 26.3 %collective-permute-start.4 = (bf16[512,1024]{1,0:T(8,128)(2,1)}, bf16[512,1024]{1,0:T(8,128)(2,1)}, u32[]{:S(2)}, u32[]{:S(2)}) collective-permute-start(bf16[512,1024]{1,0:T(8,128)(2,1)} %get-tuple-element.24), channel_id=1, source_target_pairs={{0,16},{8,24},{16,0},{24,8},{1,17},{9,25},{17,1},{25,9},{2,18},{10... | collective-permute-start | bytes 3145736 | tf_op jit(solution)/shard_map/ppermute | solution.py:225
  104.2 45.4 %collective-permute-start.5 = (bf16[512,1024]{1,0:T(8,128)(2,1)S(1)}, bf16[512,1024]{1,0:T(8,128)(2,1)}, u32[]{:S(2)}, u32[]{:S(2)}) collective-permute-start(bf16[512,1024]{1,0:T(8,128)(2,1)S(1)} %get-tuple-element.23), channel_id=1, source_target_pairs={{0,24},{8,0},{16,8},{24,16},{1,25},{9,1},{17,9},{25,17},{2,26},{10... | collective-permute-start | bytes 3145736 | tf_op jit(solution)/shard_map/ppermute | solution.py:225
  183.0 48.3 %copy-start.7 = (bf16[512,1024]{1,0:T(8,128)(2,1)S(1)}, bf16[512,1024]{1,0:T(8,128)(2,1)}, u32[]{:S(2)}) copy-start(bf16[512,1024]{1,0:T(8,128)(2,1)} %get-tuple-element.13) | copy-start | bytes 3145732
  231.3 4.1 %copy-start.9 = (bf16[2080,512]{1,0:T(8,128)(2,1)S(1)}, bf16[2080,512]{1,0:T(8,128)(2,1)}, u32[]{:S(2)}) copy-start(bf16[2080,512]{1,0:T(8,128)(2,1)} %all-gather.10.cloned.1.call-done) | copy-start | bytes 6389764
  237.3 3.6 %copy-start.10 = (f32[1024]{0:T(1024)S(1)}, f32[1024]{0:T(1024)}, u32[]{:S(2)}) copy-start(f32[1024]{0:T(1024)} %param.28) | copy-start | bytes 12292
  239.4 1.4 copy-start.4
  240.9 4.3 %copy-start.5 = (f32[520,1024]{1,0:T(8,128)S(1)}, f32[520,1024]{1,0:T(8,128)}, u32[]{:S(2)}) copy-start(f32[520,1024]{1,0:T(8,128)} %copy-done.4) | copy-start | bytes 6389764
  240.9 20.5 %copy-start.1 = (bf16[1408,3,352]{0,2,1:T(8,128)(2,1)S(1)}, bf16[1408,3,352]{0,2,1:T(8,128)(2,1)}, u32[]{:S(2)}) copy-start(bf16[1408,3,352]{0,2,1:T(8,128)(2,1)} %param.19) | copy-start | bytes 8921092
  243.3 4.4 %collective-permute-start.6 = (f32[8,1025]{1,0:T(8,128)S(1)}, f32[8,1025]{1,0:T(8,128)S(1)}, u32[]{:S(2)}, u32[]{:S(2)}) collective-permute-start(f32[8,1025]{1,0:T(8,128)S(1)} %get-tuple-element.36), channel_id=1, source_target_pairs={{0,8},{8,16},{16,24},{24,0},{1,9},{9,17},{17,25},{25,1},{2,10},{10... | collective-permute-start | bytes 98408 | tf_op jit(solution)/shard_map/ppermute | solution.py:137
  243.6 4.1 %collective-permute-start.7 = (f32[8,1025]{1,0:T(8,128)S(1)}, f32[8,1025]{1,0:T(8,128)S(1)}, u32[]{:S(2)}, u32[]{:S(2)}) collective-permute-start(f32[8,1025]{1,0:T(8,128)S(1)} %get-tuple-element.36), channel_id=1, source_target_pairs={{0,16},{8,24},{16,0},{24,8},{1,17},{9,25},{17,1},{25,9},{2,18},{10... | collective-permute-start | bytes 98408 | tf_op jit(solution)/shard_map/ppermute | solution.py:137
  243.9 3.8 %collective-permute-start.8 = (f32[8,1025]{1,0:T(8,128)S(1)}, f32[8,1025]{1,0:T(8,128)S(1)}, u32[]{:S(2)}, u32[]{:S(2)}) collective-permute-start(f32[8,1025]{1,0:T(8,128)S(1)} %get-tuple-element.36), channel_id=1, source_target_pairs={{0,24},{8,0},{16,8},{24,16},{1,25},{9,1},{17,9},{25,17},{2,26},{10... | collective-permute-start | bytes 98408 | tf_op jit(solution)/shard_map/ppermute | solution.py:137
  249.3 3.6 %collective-permute-start.9 = (f32[8]{0:T(128)S(1)}, f32[8]{0:T(128)S(1)}, u32[]{:S(2)}, u32[]{:S(2)}) collective-permute-start(f32[8]{0:T(128)S(1)} %get-tuple-element.41), channel_id=1, source_target_pairs={{0,1},{1,0},{2,3},{3,2},{4,5},{5,4},{6,7},{7,6},{8,9},{9,8},{10,11... | collective-permute-start | bytes 104 | tf_op jit(solution)/shard_map/ppermute | solution.py:154
  252.9 3.5 %collective-permute-start.10 = (f32[8]{0:T(128)S(1)}, f32[8]{0:T(128)S(1)}, u32[]{:S(2)}, u32[]{:S(2)}) collective-permute-start(f32[8]{0:T(128)S(1)} %max.9), channel_id=1, source_target_pairs={{0,2},{1,3},{2,0},{3,1},{4,6},{5,7},{6,4},{7,5},{8,10},{9,11},{10,... | collective-permute-start | bytes 104 | tf_op jit(solution)/shard_map/ppermute | solution.py:154
  256.5 4.4 %collective-permute-start.11 = (f32[8]{0:T(128)S(1)}, f32[8]{0:T(128)S(1)}, u32[]{:S(2)}, u32[]{:S(2)}) collective-permute-start(f32[8]{0:T(128)S(1)} %max.10), channel_id=1, source_target_pairs={{0,4},{1,5},{2,6},{3,7},{4,0},{5,1},{6,2},{7,3},{8,12},{9,13},{10,... | collective-permute-start | bytes 104 | tf_op jit(solution)/shard_map/ppermute | solution.py:154
Sparse Core Ops, SparseCore 0:
  25.1 37.3 all-reduce.1
  66.2 20.1 all-gather.5
  97.9 75.8 all-gather.7
  199.4 31.8 all-gather.9

commit v13 on v12

--- a/solution.py
+++ b/solution.py
@@ -44,15 +44,16 @@
     return (request_id, request_begin)
 
 
-def flash_kernel(needed_ref, q_ref, k_ref, v_ref, qid_ref, qreq_ref, kid_ref, kreq_ref, o_ref,
+def flash_kernel(needed_ref, q_ref, k_ref, v_ref, qid_ref, qreq_ref, kid_ref, kreq_ref,
+                 max_in, sum_in, acc_in, o_ref, max_out, sum_out, acc_out,
                  max_ref, sum_ref, acc_ref, *, root):
     kb = pl.program_id(1)
 
     @pl.when(kb == 0)
     def _():
-        max_ref[...] = jnp.full(max_ref.shape, -1e30, jnp.float32)
-        sum_ref[...] = jnp.zeros(sum_ref.shape, jnp.float32)
-        acc_ref[...] = jnp.zeros(acc_ref.shape, jnp.float32)
+        max_ref[...] = max_in[...]
+        sum_ref[...] = sum_in[...]
+        acc_ref[...] = acc_in[...]
 
     @pl.when(needed_ref[kb] != 0)
     def _():
@@ -73,6 +74,9 @@
 
     @pl.when(kb == pl.num_programs(1) - 1)
     def _():
+        max_out[...] = max_ref[...]
+        sum_out[...] = sum_ref[...]
+        acc_out[...] = acc_ref[...]
         rows = o_ref.shape[0]
         for head in range(o_ref.shape[1] // HD):
             part = slice(head * rows, (head + 1) * rows)
@@ -81,40 +85,56 @@
             )
 
 
-def flash_attention(needed, grouped_q, gathered, q_ids, q_req, k_ids, k_req, groups, tok_rows, root):
+def flash_attention(needed, grouped_q, gathered, q_ids, q_req, k_ids, k_req, groups, tok_rows, root,
+                    state, key_rows):
     blocks = gathered.shape[0]
     group_rows = grouped_q.shape[1]
+    state_spec = pl.BlockSpec((None, group_rows, 1), lambda g, kb, n: (g, 0, 0))
+    acc_spec = pl.BlockSpec((None, group_rows, HD), lambda g, kb, n: (g, 0, 0))
     grid_spec = pltpu.PrefetchScalarGridSpec(
         num_scalar_prefetch=1,
         grid=(groups, blocks),
         in_specs=[
             pl.BlockSpec((None, group_rows, HD), lambda g, kb, n: (g, 0, 0)),
-            pl.BlockSpec((None, tok_rows, HD), lambda g, kb, n: (kb, 0, g)),
-            pl.BlockSpec((None, tok_rows, HD), lambda g, kb, n: (kb, 0, groups + g)),
+            pl.BlockSpec((None, key_rows, HD), lambda g, kb, n: (kb, 0, g)),
+            pl.BlockSpec((None, key_rows, HD), lambda g, kb, n: (kb, 0, groups + g)),
             pl.BlockSpec((group_rows, 1), lambda g, kb, n: (0, 0)),
             pl.BlockSpec((group_rows, 1), lambda g, kb, n: (0, 0)),
-            pl.BlockSpec((None, 1, tok_rows), lambda g, kb, n: (kb, 0, 0)),
-            pl.BlockSpec((None, 1, tok_rows), lambda g, kb, n: (kb, 0, 0)),
+            pl.BlockSpec((None, 1, key_rows), lambda g, kb, n: (kb, 0, 0)),
+            pl.BlockSpec((None, 1, key_rows), lambda g, kb, n: (kb, 0, 0)),
+            state_spec,
+            state_spec,
+            acc_spec,
         ],
-        out_specs=pl.BlockSpec((tok_rows, group_rows // tok_rows * HD), lambda g, kb, n: (0, g)),
+        out_specs=[
+            pl.BlockSpec((tok_rows, group_rows // tok_rows * HD), lambda g, kb, n: (0, g)),
+            state_spec,
+            state_spec,
+            acc_spec,
+        ],
         scratch_shapes=[
             pltpu.VMEM((group_rows, 1), jnp.float32),
             pltpu.VMEM((group_rows, 1), jnp.float32),
             pltpu.VMEM((group_rows, HD), jnp.float32),
         ],
     )
-    flops = 4 * groups * blocks * group_rows * tok_rows * HD
+    flops = 4 * groups * blocks * group_rows * key_rows * HD
     return pl.pallas_call(
         functools.partial(flash_kernel, root=root),
         grid_spec=grid_spec,
-        out_shape=jax.ShapeDtypeStruct((tok_rows, groups * group_rows // tok_rows * HD), jnp.bfloat16),
+        out_shape=[
+            jax.ShapeDtypeStruct((tok_rows, groups * group_rows // tok_rows * HD), jnp.bfloat16),
+            jax.ShapeDtypeStruct((groups, group_rows, 1), jnp.float32),
+            jax.ShapeDtypeStruct((groups, group_rows, 1), jnp.float32),
+            jax.ShapeDtypeStruct((groups, group_rows, HD), jnp.float32),
+        ],
         compiler_params=pltpu.CompilerParams(dimension_semantics=("arbitrary", "arbitrary")),
         cost_estimate=pl.CostEstimate(
             flops=flops,
-            transcendentals=groups * blocks * group_rows * tok_rows,
-            bytes_accessed=2 * groups * blocks * tok_rows * HD * 2 + 4 * groups * group_rows * HD,
+            transcendentals=groups * blocks * group_rows * key_rows,
+            bytes_accessed=2 * groups * blocks * key_rows * HD * 2 + 12 * groups * group_rows * HD,
         ),
-    )(needed, grouped_q, gathered, gathered, q_ids, q_req, k_ids, k_req)
+    )(needed, grouped_q, gathered, gathered, q_ids, q_req, k_ids, k_req, *state)
 
 
 def gather_by_permutes(local, count):
@@ -283,20 +303,26 @@
     ship_width = 2 * kv_width
     extra_rows = -(-extras.shape[0] // ship_width)
     extras = jnp.pad(extras, (0, extra_rows * ship_width - extras.shape[0]))
+    half = tok_rows // 2
     shipped = jnp.concatenate([key_rows, value_rows], axis=1)
-    shipped = jnp.concatenate([shipped, extras.reshape(extra_rows, ship_width)], axis=0)
-    gathered = lax.all_gather(shipped, "blk", axis=0, tiled=False)
-    gathered, weight_pieces = lax.optimization_barrier((gathered, weight_pieces))
-    blocks = gathered.shape[0]
+    ship_a = jnp.concatenate([shipped[:half], extras.reshape(extra_rows, ship_width)], axis=0)
+    ship_b = jnp.pad(shipped[half:], ((0, extra_rows), (0, 0)))
+    gathered_a = lax.all_gather(ship_a, "blk", axis=0, tiled=False)
+    gathered_b = lax.all_gather(ship_b, "blk", axis=0, tiled=False)
+    gathered = gathered_a
+    blocks = gathered_a.shape[0]
     q_cols = query_proj.shape[1]
-    extras_all = gathered[:, tok_rows:].reshape(blocks, -1)[:, : reqs * (q_cols + feat_dev)]
+    extras_all = gathered_a[:, half:].reshape(blocks, -1)[:, : reqs * (q_cols + feat_dev)]
     extras_all = jnp.sum(extras_all.astype(jnp.float32).reshape(blocks, reqs, -1), axis=0)
     query_last = extras_all[:, :q_cols].astype(jnp.bfloat16)
     seq_last = extras_all[:, q_cols:]
     block_index = lax.axis_index("blk")
     first_begin = query_begin[0]
     block_ids = jnp.arange(blocks, dtype=jnp.int32)
-    needed = (
+    needed_a = (
+        (block_ids <= block_index) & (block_ids * tok_rows + half - 1 >= first_begin)
+    ).astype(jnp.int32)
+    needed_b = (
         (block_ids <= block_index) & (block_ids * tok_rows + tok_rows - 1 >= first_begin)
     ).astype(jnp.int32)
     group_rows = tok_rows * per_group
@@ -307,11 +333,26 @@
     q_req = jnp.tile(query_req, per_group)[:, None]
     all_ids = jnp.arange(blocks * tok_rows, dtype=jnp.int32)
     all_req, unused = request_info(all_ids, req_lengths)
-    k_ids = all_ids.reshape(blocks, 1, tok_rows)
-    k_req = all_req.reshape(blocks, 1, tok_rows)
-    context = flash_attention(
-        needed, grouped_q, gathered, q_ids, q_req, k_ids, k_req, kv_heads, tok_rows, root
-    )
+    k_ids = all_ids.reshape(blocks, 2, 1, half)
+    k_req = all_req.reshape(blocks, 2, 1, half)
+    start_state = (
+        jnp.full((kv_heads, group_rows, 1), -1e30, jnp.float32),
+        jnp.zeros((kv_heads, group_rows, 1), jnp.float32),
+        jnp.zeros((kv_heads, group_rows, HD), jnp.float32),
+    )
+    outcome = flash_attention(
+        needed_a, grouped_q, gathered_a, q_ids, q_req, k_ids[:, 0], k_req[:, 0], kv_heads,
+        tok_rows, root, start_state, half,
+    )
+    gathered_b, weight_pieces, first_state = lax.optimization_barrier(
+        (gathered_b, weight_pieces, tuple(outcome[1:]))
+    )
+    outcome = flash_attention(
+        needed_b, grouped_q, gathered_b, q_ids, q_req, k_ids[:, 1], k_req[:, 1], kv_heads,
+        tok_rows, root, first_state, half,
+    )
+    context = outcome[0]
+    gathered = jnp.concatenate([gathered_a[:, :half], gathered_b[:, :half]], axis=1)
     all_ids = jnp.arange(blocks * tok_rows, dtype=jnp.int32)
     last_begin = ends_at - req_lengths
     last_allowed = (all_ids[None, :] >= last_begin[:, None]) & (all_ids[None, :] <= last_ids[:, None])

time: 269 us -> 293 us (1.089)
  Pallas kernels: 14.4 us -> 28.6 us
  local copies, waits for them, and re-layouts: 25.9 us -> 30.7 us
  other arithmetic: 27.8 us -> 30.8 us
    all_gather x1 -> x2, waiting for transfers between devices: 24.1 us -> 68.2 us  [the longest x1 36.5 us: on_device(): gathered_a = lax.all_gather(ship_a, 'blk', axis=0, tiled=False)]
    ppermute x3, waiting for transfers between devices: 39.1 us -> 0.01 us  [on_device(): lax.ppermute(payload, 'kv', perm=[(i, (i + shift) % kv_count) for i in ra...]
    pallas_call x1 -> x2, Pallas kernels: 14.4 us -> 28.6 us  [flash_attention(): pl.pallas_call(functools.partial(flash_kernel, root=root), grid_spec=grid...]
    all_gather x1, waiting for transfers between devices: 31.9 us -> 27.6 us  [on_device(): context_all = lax.all_gather(out_rows, 'kv', axis=0, tiled=False)]
    broadcast_in_dim x0 -> x3, local copies, waits for them, and re-layouts: none -> 3.17 us  [the longest x1 1.07 us: on_device(): jnp.zeros((kv_heads, group_rows, 1), jnp.float32)]
  transfers between devices with their start and end apart: 16 -> 17, of which waited for: 10 -> 8; matrix products, arithmetic and copies ran while one was open for 20% -> 22% of each run, Pallas kernels for 0% -> 5%
where the time goes in v13:
time: 293 us; the launch traced here: 292 us
  waiting for transfers between devices  135 us (46%)
  matrix products  37.3 us (13%)
  other arithmetic  30.8 us (11%)
  local copies, waits for them, and re-layouts  30.7 us (10%)
  Pallas kernels  28.6 us (10%)
  starting transfers between devices  15.3 us (5%)
  between operations  14.5 us (5%)
    all_gather x1, waiting for transfers between devices, on_device(): gathered_a = lax.all_gather(ship_a, 'blk', axis=0, tiled=False)  36.5 us
    all_gather x1, waiting for transfers between devices, on_device(): gathered_b = lax.all_gather(ship_b, 'blk', axis=0, tiled=False)  31.8 us
    psum x1, waiting for transfers between devices, on_device(): lax.psum(head_pooled.astype(jnp.bfloat16), 'kv').astype(jnp.float32)  28.7 us
    pallas_call x2, Pallas kernels, flash_attention(): pl.pallas_call(functools.partial(flash_kernel, root=root), grid_spec=grid...  28.6 us
    all_gather x1, waiting for transfers between devices, on_device(): context_all = lax.all_gather(out_rows, 'kv', axis=0, tiled=False)  27.6 us
    dot_general x4, matrix products, on_device(): part = jnp.dot(source, piece, preferred_element_type=jnp.float32)  6.97 us
    ppermute x3, starting transfers between devices, tree_max(): lax.ppermute(values, axis, perm=[(i, i ^ step) for i in range(count)])  6.13 us
  transfers between devices with their start and end apart: 17, of which 8 were waited for; matrix products, arithmetic and copies ran while one was open for 22% of the time, Pallas kernels for 5%

profile of v13, /device:TPU:0, one launch (start us, length us, event | category | flops | bytes accessed | tf_op | source)
XLA Modules:
  0.0 291.6 jit_solution(11998392724407504257)
XLA Ops:
  7.8 2.0 collective-permute-start.2
  9.7 2.2 collective-permute-start.1
  12.8 2.0 convert_reduce_fusion
  15.5 2.9 fusion.30
  22.4 2.7 convolution_reduce_fusion
  26.5 3.0 %reshape.391 = f32[3,64,4,1408]{3,2,1,0:T(4,128)} reshape(bf16[3,256,1408]{2,1,0:T(8,128)(2,1)S(1)} %copy-done.3) | data formatting | bytes 6488064 | tf_op jit(solution)/shard_map/reshape | solution.py:232
  29.6 4.8 %reduce_sum.136 = f32[3,64,1408]{2,1,0:T(8,128)S(1)} reduce(f32[3,64,4,1408]{3,2,1,0:T(4,128)} %reshape.391, f32[]{:T(128)} %constant.152.clone.1), dimensions={2}, to_apply=%region_1.2 | reduce | flops 811008 | bytes 5406724 | tf_op jit(solution)/shard_map/reduce_sum | solution.py:232
  34.6 28.7 %all-reduce.3.cloned.1.call-done = bf16[3,64,1408]{2,1,0:T(8,128)(2,1)} async-done(((bf16[3,64,1408]{2,1,0:T(8,128)(2,1)}), bf16[3,64,1408]{2,1,0:T(8,128)(2,1)}) %all-reduce.3.cloned.1.call-update) | async-done | bytes 540688 | tf_op jit(solution)/shard_map/psum | solution.py:231
  63.3 3.5 %fusion.45 = bf16[3,64,1024]{2,1,0:T(8,128)(2,1)} fusion(bf16[1408,1024]{1,0:T(8,128)(2,1)} %param.21, bf16[3,64,1408]{2,1,0:T(8,128)(2,1)} %all-reduce.3.cloned.1.call-done, f32[3,64,1408]{2,1,0:T(8,128)S(1)} %reduce_sum.136), kind=kOutput, calls=%fused_computation.65 | convolution fusion | flops 554926080 | bytes 4898816 | tf_op jit(solution)/shard_map/pmd,de->pme/dot_general | solution.py:234
  67.7 1.6 fusion.44
  69.6 3.7 %pad_maximum_fusion = bf16[4,512,1024]{2,1,0:T(8,128)(2,1)} fusion(bf16[1,512,1024]{2,1,0:T(8,128)(2,1)} %bitcast.21, bf16[1,512,1024]{2,1,0:T(8,128)(2,1)} %bitcast.20, bf16[1,512,1024]{2,1,0:T(8,128)(2,1)} %bitcast.19, bf16[1,512,1024]{2,1,0:T(8,128)(2,1)S(1)} %bitcast.196), kind=kLoop, calls=%fused_computation.29 | loop fusion | flops 6291456 | bytes 8388608 | tf_op jit(solution)/shard_map/stack | solution.py:147
  73.3 5.2 %gather_fusion = bf16[4,512,1024]{2,1,0:T(8,128)(2,1)} fusion(bf16[4,512,1024]{2,1,0:T(8,128)(2,1)} %pad_maximum_fusion, s32[1024]{0:T(1024)S(1)} %pad_clamp_fusion), kind=kCustom, calls=%fused_computation | custom fusion | bytes 8388624 | tf_op jit(solution)/shard_map/jit(_take)/gather | solution.py:149
  78.5 2.7 broadcast_select_fusion
  81.2 1.8 slice_bitcast_fusion.3
  83.0 4.4 %all-gather.8.cloned.1.call-done = bf16[192,4096]{1,0:T(8,128)(2,1)} async-done(((bf16[192,1024]{1,0:T(8,128)(2,1)}), bf16[192,4096]{1,0:T(8,128)(2,1)}) %all-gather.8.cloned.1.call-update) | async-done | bytes 1572880 | tf_op jit(solution)/shard_map/all_gather | solution.py:262
  87.3 4.2 %fusion.2 = (f32[512]{0:T(512)S(1)}, bf16[512,4096]{1,0:T(8,128)(2,1)S(1)}) fusion(bf16[512,1024]{1,0:T(8,128)(2,1)S(1)} %get-tuple-element.42, bf16[512,1024]{1,0:T(8,128)(2,1)} %get-tuple-element.43, bf16[512,1024]{1,0:T(8,128)(2,1)} %get-tuple-element.44, bf16[512,1024]{1,0:T(8,128)(2,1)S(1)} %get-tuple-element.41, ...), kind=kOutput, calls=%fused_computation.6 | convolution fusion | flops 832667136 | bytes 9964800 | tf_op jit(solution)/shard_map/dot_general | solution.py:265
  91.6 2.6 fusion.14
  94.3 2.6 fusion.49
  102.5 1.2 and_convert_fusion.needed_ref
  103.7 1.2 and_convert_fusion.1.needed_ref
  105.5 4.5 %constant_dynamic-slice_fusion = (bf16[512,1024]{1,0:T(8,128)(2,1)}, bf16[512,1024]{1,0:T(8,128)(2,1)}, bf16[512,1024]{1,0:T(8,128)(2,1)}, bf16[512,1024]{1,0:T(8,128)(2,1)}) fusion(bf16[512,4096]{1,0:T(8,128)(2,1)} %param.26, s32[]{:T(128)S(6)} %select_n.159, s32[]{:T(128)S(6)} %select_n.157, s32[]{:T(128)S(6)} %select_n.155, s32[]{:T(128)S(6)} %select_n.153), kind=kLoop, calls=%fused_computation.184 | loop fusion | bytes 8388624 | tf_op jit(solution)/shard_map/dynamic_slice | solution.py:241
  110.0 1.8 collective-permute-start.4
  112.5 1.1 pad_maximum_fusion.2
  113.6 36.5 %all-gather.12.cloned.1.call-done = bf16[2240,512]{1,0:T(8,128)(2,1)} async-done(((bf16[280,512]{1,0:T(8,128)(2,1)}), bf16[2240,512]{1,0:T(8,128)(2,1)}) %all-gather.12.cloned.1.call-update) | async-done | bytes 2293776 | tf_op jit(solution)/shard_map/all_gather | solution.py:310
  150.1 1.8 slice.174
  156.1 14.3 %shard_map.166 = (bf16[512,512]{1,0:T(8,128)(2,1)}, f32[2,1024,1]{2,1,0:T(8,128)}, f32[2,1024,1]{2,1,0:T(8,128)}, f32[2,1024,128]{2,1,0:T(8,128)}) custom-call(s32[8]{0:T(128)} %and_convert_fusion.needed_ref, bf16[2,1024,128]{2,1,0:T(8,128)(2,1)} %bitcast.177, bf16[8,280,512]{2,1,0:T(8,128)(2,1)} %bitcast.172, bf16[8,280,512]{2,1,0:T(8,128)(2,1)} %bitcast.173, ...), custom_call_target="tpu_custom_call" | custom-call | flops 2147483648 | bytes 5242880 | tf_op jit(solution)/shard_map/pallas_call | solution.py:122
  170.5 31.8 %all-gather.10.cloned.1.call-done = bf16[2240,512]{1,0:T(8,128)(2,1)} async-done(((bf16[280,512]{1,0:T(8,128)(2,1)}), bf16[2240,512]{1,0:T(8,128)(2,1)}) %all-gather.10.cloned.1.call-update) | async-done | bytes 2293776 | tf_op jit(solution)/shard_map/all_gather | solution.py:311
  202.2 1.8 slice.138
  204.0 2.2 fusion.62
  206.3 1.9 fusion.116
  208.2 1.8 fusion.115
  210.0 1.5 fusion.53
  211.8 14.3 %shard_map.167 = (bf16[512,512]{1,0:T(8,128)(2,1)}, f32[2,1024,1]{2,1,0:T(8,128)}, f32[2,1024,1]{2,1,0:T(8,128)}, f32[2,1024,128]{2,1,0:T(8,128)}) custom-call(s32[8]{0:T(128)} %and_convert_fusion.1.needed_ref, bf16[2,1024,128]{2,1,0:T(8,128)(2,1)} %bitcast.178, bf16[8,280,512]{2,1,0:T(8,128)(2,1)} %bitcast.175, bf16[8,280,512]{2,1,0:T(8,128)(2,1)} %bitcast.176, ...), custom_call_target="tpu_custom_call" | custom-call | flops 2147483648 | bytes 5242880 | tf_op jit(solution)/shard_map/pallas_call | solution.py:122
  226.0 1.9 maximum_maximum_fusion
  228.0 27.6 %all-gather.14.cloned.1.call-done = bf16[2080,512]{1,0:T(8,128)(2,1)} async-done(((bf16[520,512]{1,0:T(8,128)(2,1)}), bf16[2080,512]{1,0:T(8,128)(2,1)}) %all-gather.14.cloned.1.call-update) | async-done | bytes 2129936 | tf_op jit(solution)/shard_map/all_gather | solution.py:385
  255.6 2.3 convolution_convert_fusion.2
  257.9 2.0 convolution_convert_fusion.3
  260.7 2.0 convert_add_fusion
  262.7 1.3 copy-done.4
  264.3 2.4 fusion.94
  267.1 1.7 collective-permute-start.8
  268.8 2.5 fusion.29
  272.9 1.8 collective-permute-start.9
  274.7 1.8 collective-permute-done.9
  276.5 1.7 collective-permute-start.10
  278.3 1.8 collective-permute-done.10
  280.1 2.6 collective-permute-start.11
  282.7 1.8 collective-permute-done.11
  (134 shorter events, 23.5 us)
Async XLA Ops:
  7.2 8.4 %copy-start = (bf16[1408,3,352]{0,2,1:T(8,128)(2,1)S(1)}, bf16[1408,3,352]{0,2,1:T(8,128)(2,1)}, u32[]{:S(2)}) copy-start(bf16[1408,3,352]{0,2,1:T(8,128)(2,1)} %param.19) | copy-start | bytes 8921092
  7.2 8.4 %copy-start.17 = (f32[1408]{0:T(1024)S(1)}, f32[1408]{0:T(1024)}, u32[]{:S(2)}) copy-start(f32[1408]{0:T(1024)} %param.18) | copy-start | bytes 16900
  7.2 56.1 %all-reduce.3.cloned.1.call-start = ((), (), s32[]{:S(2)}) async-start(), calls=%async_computation | async-start | bytes 1081344 | tf_op jit(solution)/shard_map/psum | solution.py:231
  7.2 7.6 %copy-start.2 = (bf16[3,256,1408]{2,1,0:T(8,128)(2,1)S(1)}, bf16[3,256,1408]{2,1,0:T(8,128)(2,1)}, u32[]{:S(2)}) copy-start(bf16[3,256,1408]{2,1,0:T(8,128)(2,1)} %param.15) | copy-start | bytes 6488068
  7.2 62.3 %collective-permute-start = (bf16[512,1024]{1,0:T(8,128)(2,1)}, bf16[512,1024]{1,0:T(8,128)(2,1)}, u32[]{:S(2)}, u32[]{:S(2)}) collective-permute-start(bf16[512,1024]{1,0:T(8,128)(2,1)} %param.22), channel_id=1, source_target_pairs={{0,8},{8,16},{16,24},{24,0},{1,9},{9,17},{17,25},{25,1},{2,10},{10... | collective-permute-start | bytes 3145736 | tf_op jit(solution)/shard_map/ppermute | solution.py:145
  7.8 61.8 %collective-permute-start.2 = (bf16[512,1024]{1,0:T(8,128)(2,1)}, bf16[512,1024]{1,0:T(8,128)(2,1)}, u32[]{:S(2)}, u32[]{:S(2)}) collective-permute-start(bf16[512,1024]{1,0:T(8,128)(2,1)} %param.22), channel_id=1, source_target_pairs={{0,24},{8,0},{16,8},{24,16},{1,25},{9,1},{17,9},{25,17},{2,26},{10... | collective-permute-start | bytes 3145736 | tf_op jit(solution)/shard_map/ppermute | solution.py:145
  9.7 59.8 %collective-permute-start.1 = (bf16[512,1024]{1,0:T(8,128)(2,1)}, bf16[512,1024]{1,0:T(8,128)(2,1)}, u32[]{:S(2)}, u32[]{:S(2)}) collective-permute-start(bf16[512,1024]{1,0:T(8,128)(2,1)} %param.22), channel_id=1, source_target_pairs={{0,16},{8,24},{16,0},{24,8},{1,17},{9,25},{17,1},{25,9},{2,18},{10... | collective-permute-start | bytes 3145736 | tf_op jit(solution)/shard_map/ppermute | solution.py:145
  22.4 3.8 %copy-start.13 = (s32[8]{0:T(128)S(1)}, s32[8]{0:T(128)}, u32[]{:S(2)}) copy-start(s32[8]{0:T(128)} %param.27) | copy-start | bytes 100
  22.4 4.0 %copy-start.12 = (s32[3]{0:T(128)S(1)}, s32[3]{0:T(128)}, u32[]{:S(2)}) copy-start(s32[3]{0:T(128)} %param.17) | copy-start | bytes 40
  22.4 4.1 %copy-start.3 = (bf16[3,256,1408]{2,1,0:T(8,128)(2,1)S(1)}, bf16[3,256,1408]{2,1,0:T(8,128)(2,1)}, u32[]{:S(2)}) copy-start(bf16[3,256,1408]{2,1,0:T(8,128)(2,1)} %param.15) | copy-start | bytes 6488068
  26.0 61.3 %all-gather.8.cloned.1.call-start = ((), (), s32[]{:S(2)}) async-start(), calls=%async_computation.1 | async-start | bytes 1966080 | tf_op jit(solution)/shard_map/all_gather | solution.py:262
  34.4 33.3 %copy-start.9 = (bf16[512,1024]{1,0:T(8,128)(2,1)S(1)}, bf16[512,1024]{1,0:T(8,128)(2,1)}, u32[]{:S(2)}) copy-start(bf16[512,1024]{1,0:T(8,128)(2,1)} %param.22) | copy-start | bytes 3145732
  66.9 83.2 %all-gather.12.cloned.1.call-start = ((), (), s32[]{:S(2)}) async-start(), calls=%async_computation.3 | async-start | bytes 2580480 | tf_op jit(solution)/shard_map/all_gather | solution.py:310
  69.3 4.0 %copy-start.6 = (bf16[512,1024]{1,0:T(8,128)(2,1)}, bf16[512,1024]{1,0:T(8,128)(2,1)S(1)}, u32[]{:S(2)}) copy-start(bf16[512,1024]{1,0:T(8,128)(2,1)S(1)} %fusion.44) | copy-start | bytes 3145732
  87.3 4.2 %copy-start.14 = (bf16[4096,2,256]{2,1,0:T(2,128)(2,1)S(1)}, bf16[4096,2,256]{2,1,0:T(2,128)(2,1)}, u32[]{:S(2)}) copy-start(bf16[4096,2,256]{2,1,0:T(2,128)(2,1)} %param.25) | copy-start | bytes 12582916
  87.3 4.2 %copy-start.16 = (f32[4096]{0:T(1024)S(1)}, f32[4096]{0:T(1024)}, u32[]{:S(2)}) copy-start(f32[4096]{0:T(1024)} %param.23) | copy-start | bytes 49156
  91.6 2.7 copy-start.15
  98.6 103.6 %all-gather.10.cloned.1.call-start = ((), (), s32[]{:S(2)}) async-start(), calls=%async_computation.2 | async-start | bytes 2580480 | tf_op jit(solution)/shard_map/all_gather | solution.py:311
  99.6 156.0 %all-gather.14.cloned.1.call-start = ((), (), s32[]{:S(2)}) async-start(), calls=%async_computation.4 | async-start | bytes 2662400 | tf_op jit(solution)/shard_map/all_gather | solution.py:385
  110.0 60.5 %collective-permute-start.5 = (bf16[512,1024]{1,0:T(8,128)(2,1)}, bf16[512,1024]{1,0:T(8,128)(2,1)}, u32[]{:S(2)}, u32[]{:S(2)}) collective-permute-start(bf16[512,1024]{1,0:T(8,128)(2,1)} %get-tuple-element.37), channel_id=1, source_target_pairs={{0,24},{8,0},{16,8},{24,16},{1,25},{9,1},{17,9},{25,17},{2,26},{10... | collective-permute-start | bytes 3145736 | tf_op jit(solution)/shard_map/ppermute | solution.py:245
  110.0 60.4 %collective-permute-start.4 = (bf16[512,1024]{1,0:T(8,128)(2,1)}, bf16[512,1024]{1,0:T(8,128)(2,1)}, u32[]{:S(2)}, u32[]{:S(2)}) collective-permute-start(bf16[512,1024]{1,0:T(8,128)(2,1)} %get-tuple-element.38), channel_id=1, source_target_pairs={{0,16},{8,24},{16,0},{24,8},{1,17},{9,25},{17,1},{25,9},{2,18},{10... | collective-permute-start | bytes 3145736 | tf_op jit(solution)/shard_map/ppermute | solution.py:245
  111.8 58.6 %collective-permute-start.3 = (bf16[512,1024]{1,0:T(8,128)(2,1)}, bf16[512,1024]{1,0:T(8,128)(2,1)}, u32[]{:S(2)}, u32[]{:S(2)}) collective-permute-start(bf16[512,1024]{1,0:T(8,128)(2,1)} %get-tuple-element.39), channel_id=1, source_target_pairs={{0,8},{8,16},{16,24},{24,0},{1,9},{9,17},{17,25},{25,1},{2,10},{10... | collective-permute-start | bytes 3145736 | tf_op jit(solution)/shard_map/ppermute | solution.py:245
  206.3 5.2 %copy-start.7 = (bf16[8,512,128]{2,1,0:T(8,128)(2,1)S(1)}, bf16[8,512,128]{2,1,0:T(8,128)(2,1)}, u32[]{:S(2)}) copy-start(bf16[8,512,128]{2,1,0:T(8,128)(2,1)} %get-tuple-element.34) | copy-start | bytes 3145732
  255.6 2.3 copy-start.10
  255.6 4.2 %copy-start.8 = (bf16[512,1024]{1,0:T(8,128)(2,1)S(1)}, bf16[512,1024]{1,0:T(8,128)(2,1)}, u32[]{:S(2)}) copy-start(bf16[512,1024]{1,0:T(8,128)(2,1)} %get-tuple-element.27) | copy-start | bytes 3145732
  260.6 3.6 %copy-start.11 = (f32[1024]{0:T(1024)S(1)}, f32[1024]{0:T(1024)}, u32[]{:S(2)}) copy-start(f32[1024]{0:T(1024)} %param.28) | copy-start | bytes 12292
  262.7 1.4 copy-start.4
  264.2 4.6 %copy-start.5 = (f32[520,1024]{1,0:T(8,128)S(1)}, f32[520,1024]{1,0:T(8,128)}, u32[]{:S(2)}) copy-start(f32[520,1024]{1,0:T(8,128)} %copy-done.4) | copy-start | bytes 6389764
  264.3 20.8 %copy-start.1 = (bf16[1408,3,352]{0,2,1:T(8,128)(2,1)S(1)}, bf16[1408,3,352]{0,2,1:T(8,128)(2,1)}, u32[]{:S(2)}) copy-start(bf16[1408,3,352]{0,2,1:T(8,128)(2,1)} %param.19) | copy-start | bytes 8921092
  266.7 4.7 %collective-permute-start.7 = (f32[8,1025]{1,0:T(8,128)S(1)}, f32[8,1025]{1,0:T(8,128)S(1)}, u32[]{:S(2)}, u32[]{:S(2)}) collective-permute-start(f32[8,1025]{1,0:T(8,128)S(1)} %get-tuple-element.50), channel_id=1, source_target_pairs={{0,16},{8,24},{16,0},{24,8},{1,17},{9,25},{17,1},{25,9},{2,18},{10... | collective-permute-start | bytes 98408 | tf_op jit(solution)/shard_map/ppermute | solution.py:157
  267.1 4.3 %collective-permute-start.6 = (f32[8,1025]{1,0:T(8,128)S(1)}, f32[8,1025]{1,0:T(8,128)S(1)}, u32[]{:S(2)}, u32[]{:S(2)}) collective-permute-start(f32[8,1025]{1,0:T(8,128)S(1)} %get-tuple-element.50), channel_id=1, source_target_pairs={{0,8},{8,16},{16,24},{24,0},{1,9},{9,17},{17,25},{25,1},{2,10},{10... | collective-permute-start | bytes 98408 | tf_op jit(solution)/shard_map/ppermute | solution.py:157
  267.1 4.3 %collective-permute-start.8 = (f32[8,1025]{1,0:T(8,128)S(1)}, f32[8,1025]{1,0:T(8,128)S(1)}, u32[]{:S(2)}, u32[]{:S(2)}) collective-permute-start(f32[8,1025]{1,0:T(8,128)S(1)} %get-tuple-element.50), channel_id=1, source_target_pairs={{0,24},{8,0},{16,8},{24,16},{1,25},{9,1},{17,9},{25,17},{2,26},{10... | collective-permute-start | bytes 98408 | tf_op jit(solution)/shard_map/ppermute | solution.py:157
  272.9 3.6 %collective-permute-start.9 = (f32[8]{0:T(128)S(1)}, f32[8]{0:T(128)S(1)}, u32[]{:S(2)}, u32[]{:S(2)}) collective-permute-start(f32[8]{0:T(128)S(1)} %get-tuple-element.59), channel_id=1, source_target_pairs={{0,1},{1,0},{2,3},{3,2},{4,5},{5,4},{6,7},{7,6},{8,9},{9,8},{10,11... | collective-permute-start | bytes 104 | tf_op jit(solution)/shard_map/ppermute | solution.py:174
  276.5 3.5 %collective-permute-start.10 = (f32[8]{0:T(128)S(1)}, f32[8]{0:T(128)S(1)}, u32[]{:S(2)}, u32[]{:S(2)}) collective-permute-start(f32[8]{0:T(128)S(1)} %max.9), channel_id=1, source_target_pairs={{0,2},{1,3},{2,0},{3,1},{4,6},{5,7},{6,4},{7,5},{8,10},{9,11},{10,... | collective-permute-start | bytes 104 | tf_op jit(solution)/shard_map/ppermute | solution.py:174
  280.1 4.4 %collective-permute-start.11 = (f32[8]{0:T(128)S(1)}, f32[8]{0:T(128)S(1)}, u32[]{:S(2)}, u32[]{:S(2)}) collective-permute-start(f32[8]{0:T(128)S(1)} %max.10), channel_id=1, source_target_pairs={{0,4},{1,5},{2,6},{3,7},{4,0},{5,1},{6,2},{7,3},{8,12},{9,13},{10,... | collective-permute-start | bytes 104 | tf_op jit(solution)/shard_map/ppermute | solution.py:174
Sparse Core Ops, SparseCore 0:
  26.2 37.1 all-reduce.2
  67.0 20.2 all-gather.7
  98.8 51.2 all-gather.11
  152.4 49.8 all-gather.9
  228.1 27.5 all-gather.13

commit v14 on v12

--- a/solution.py
+++ b/solution.py
@@ -46,7 +46,8 @@
 
 def flash_kernel(needed_ref, q_ref, k_ref, v_ref, qid_ref, qreq_ref, kid_ref, kreq_ref, o_ref,
                  max_ref, sum_ref, acc_ref, *, root):
-    kb = pl.program_id(1)
+    kb = pl.program_id(0)
+    groups = q_ref.shape[0]
 
     @pl.when(kb == 0)
     def _():
@@ -56,51 +57,58 @@
 
     @pl.when(needed_ref[kb] != 0)
     def _():
-        scores = lax.dot_general(
-            q_ref[...], k_ref[...], (((1,), (1,)), ((), ())), preferred_element_type=jnp.float32
-        ) / root
         allowed = (kid_ref[...] <= qid_ref[...]) & (kreq_ref[...] == qreq_ref[...])
-        scores = jnp.where(allowed, scores, -1e30)
-        old_max = max_ref[...]
-        new_max = jnp.maximum(old_max, jnp.max(scores, axis=1, keepdims=True))
-        weights = jnp.where(allowed, jnp.exp(scores - new_max), 0.0)
-        scale = jnp.exp(old_max - new_max)
-        sum_ref[...] = sum_ref[...] * scale + jnp.sum(weights, axis=1, keepdims=True)
-        acc_ref[...] = acc_ref[...] * scale + jnp.dot(
-            weights.astype(jnp.bfloat16), v_ref[...], preferred_element_type=jnp.float32
-        )
-        max_ref[...] = new_max
-
-    @pl.when(kb == pl.num_programs(1) - 1)
+        for g in range(groups):
+            scores = lax.dot_general(
+                q_ref[g], k_ref[:, g * HD : (g + 1) * HD], (((1,), (1,)), ((), ())),
+                preferred_element_type=jnp.float32,
+            ) / root
+            scores = jnp.where(allowed, scores, -1e30)
+            old_max = max_ref[g]
+            new_max = jnp.maximum(old_max, jnp.max(scores, axis=1, keepdims=True))
+            weights = jnp.where(allowed, jnp.exp(scores - new_max), 0.0)
+            scale = jnp.exp(old_max - new_max)
+            sum_ref[g] = sum_ref[g] * scale + jnp.sum(weights, axis=1, keepdims=True)
+            acc_ref[g] = acc_ref[g] * scale + jnp.dot(
+                weights.astype(jnp.bfloat16), v_ref[:, g * HD : (g + 1) * HD],
+                preferred_element_type=jnp.float32,
+            )
+            max_ref[g] = new_max
+
+    @pl.when(kb == pl.num_programs(0) - 1)
     def _():
         rows = o_ref.shape[0]
-        for head in range(o_ref.shape[1] // HD):
-            part = slice(head * rows, (head + 1) * rows)
-            o_ref[:, head * HD : (head + 1) * HD] = (acc_ref[part, :] / sum_ref[part, :]).astype(
-                o_ref.dtype
-            )
+        per_group = q_ref.shape[1] // rows
+        for g in range(groups):
+            for head in range(per_group):
+                part = slice(head * rows, (head + 1) * rows)
+                col = (g * per_group + head) * HD
+                o_ref[:, col : col + HD] = (acc_ref[g, part, :] / sum_ref[g, part, :]).astype(
+                    o_ref.dtype
+                )
 
 
 def flash_attention(needed, grouped_q, gathered, q_ids, q_req, k_ids, k_req, groups, tok_rows, root):
     blocks = gathered.shape[0]
     group_rows = grouped_q.shape[1]
+    width = groups * HD
     grid_spec = pltpu.PrefetchScalarGridSpec(
         num_scalar_prefetch=1,
-        grid=(groups, blocks),
+        grid=(blocks,),
         in_specs=[
-            pl.BlockSpec((None, group_rows, HD), lambda g, kb, n: (g, 0, 0)),
-            pl.BlockSpec((None, tok_rows, HD), lambda g, kb, n: (kb, 0, g)),
-            pl.BlockSpec((None, tok_rows, HD), lambda g, kb, n: (kb, 0, groups + g)),
-            pl.BlockSpec((group_rows, 1), lambda g, kb, n: (0, 0)),
-            pl.BlockSpec((group_rows, 1), lambda g, kb, n: (0, 0)),
-            pl.BlockSpec((None, 1, tok_rows), lambda g, kb, n: (kb, 0, 0)),
-            pl.BlockSpec((None, 1, tok_rows), lambda g, kb, n: (kb, 0, 0)),
+            pl.BlockSpec((groups, group_rows, HD), lambda kb, n: (0, 0, 0)),
+            pl.BlockSpec((None, tok_rows, width), lambda kb, n: (kb, 0, 0)),
+            pl.BlockSpec((None, tok_rows, width), lambda kb, n: (kb, 0, 1)),
+            pl.BlockSpec((group_rows, 1), lambda kb, n: (0, 0)),
+            pl.BlockSpec((group_rows, 1), lambda kb, n: (0, 0)),
+            pl.BlockSpec((None, 1, tok_rows), lambda kb, n: (kb, 0, 0)),
+            pl.BlockSpec((None, 1, tok_rows), lambda kb, n: (kb, 0, 0)),
         ],
-        out_specs=pl.BlockSpec((tok_rows, group_rows // tok_rows * HD), lambda g, kb, n: (0, g)),
+        out_specs=pl.BlockSpec((tok_rows, groups * group_rows // tok_rows * HD), lambda kb, n: (0, 0)),
         scratch_shapes=[
-            pltpu.VMEM((group_rows, 1), jnp.float32),
-            pltpu.VMEM((group_rows, 1), jnp.float32),
-            pltpu.VMEM((group_rows, HD), jnp.float32),
+            pltpu.VMEM((groups, group_rows, 1), jnp.float32),
+            pltpu.VMEM((groups, group_rows, 1), jnp.float32),
+            pltpu.VMEM((groups, group_rows, HD), jnp.float32),
         ],
     )
     flops = 4 * groups * blocks * group_rows * tok_rows * HD
@@ -108,7 +116,7 @@
         functools.partial(flash_kernel, root=root),
         grid_spec=grid_spec,
         out_shape=jax.ShapeDtypeStruct((tok_rows, groups * group_rows // tok_rows * HD), jnp.bfloat16),
-        compiler_params=pltpu.CompilerParams(dimension_semantics=("arbitrary", "arbitrary")),
+        compiler_params=pltpu.CompilerParams(dimension_semantics=("arbitrary",)),
         cost_estimate=pl.CostEstimate(
             flops=flops,
             transcendentals=groups * blocks * group_rows * tok_rows,

time: 269 us -> 264 us (0.981)
  Pallas kernels: 14.4 us -> 10.2 us
    pallas_call x1, Pallas kernels: 14.4 us -> 10.2 us  [flash_attention(): pl.pallas_call(functools.partial(flash_kernel, root=root), grid_spec=grid...]
  transfers between devices with their start and end apart: 16 -> 16, of which waited for: 10 -> 10; matrix products, arithmetic and copies ran while one was open for 20% -> 21% of each run, Pallas kernels for 0% -> 0%
where the time goes in v14:
time: 264 us; the launch traced here: 263 us
  waiting for transfers between devices  133 us (50%)
  matrix products  37 us (14%)
  other arithmetic  27.8 us (11%)
  local copies, waits for them, and re-layouts  25.9 us (10%)
  starting transfers between devices  14.6 us (6%)
  between operations  14.4 us (5%)
  Pallas kernels  10.2 us (4%)
    ppermute x3, waiting for transfers between devices, on_device(): lax.ppermute(payload, 'kv', perm=[(i, (i + shift) % kv_count) for i in ra...  39.1 us
    all_gather x1, waiting for transfers between devices, on_device(): context_all = lax.all_gather(out_rows, 'kv', axis=0, tiled=False)  31.1 us
    psum x1, waiting for transfers between devices, on_device(): lax.psum(head_pooled.astype(jnp.bfloat16), 'kv').astype(jnp.float32)  29 us
    all_gather x1, waiting for transfers between devices, on_device(): gathered = lax.all_gather(shipped, 'blk', axis=0, tiled=False)  24.1 us
    pallas_call x1, Pallas kernels, flash_attention(): pl.pallas_call(functools.partial(flash_kernel, root=root), grid_spec=grid...  10.2 us
    dot_general x4, matrix products, on_device(): part = jnp.dot(source, piece, preferred_element_type=jnp.float32)  8.02 us
    ppermute x3, starting transfers between devices, tree_max(): lax.ppermute(values, axis, perm=[(i, i ^ step) for i in range(count)])  6.16 us
    ppermute x3, waiting for transfers between devices, tree_max(): lax.ppermute(values, axis, perm=[(i, i ^ step) for i in range(count)])  5.41 us
  transfers between devices with their start and end apart: 16, of which 10 were waited for; matrix products, arithmetic and copies ran while one was open for 21% of the time, Pallas kernels for 0%

profile of v14, /device:TPU:0, one launch (start us, length us, event | category | flops | bytes accessed | tf_op | source)
XLA Modules:
  0.0 263.0 jit_solution(9885390661615798574)
XLA Ops:
  7.8 2.6 collective-permute-start.1
  10.3 1.4 collective-permute-start.2
  11.7 2.0 convert_reduce_fusion
  14.5 2.9 %fusion.30 = bf16[3,256,3,352]{1,3,2,0:T(8,128)(2,1)S(1)} fusion(bf16[1408,3,352]{0,2,1:T(8,128)(2,1)S(1)} %copy-done, bf16[3,256,1408]{2,1,0:T(8,128)(2,1)S(1)} %copy-done.2, f32[1408]{0:T(1024)S(1)} %copy-done.17, f32[3,256]{1,0:T(4,128)S(1)} %add_rsqrt_fusion, f32[3,256]{1,0:T(4,128)S(1)} %broadcast_multiply_fusion), kind=kOutput, calls=%fused_computation.46 | convolution fusion | flops 2290016256 | bytes 6770176 | tf_op jit(solution)/shard_map/pnd,dce->pnce/dot_general | solution.py:194
  21.4 2.7 %convolution_reduce_fusion = f32[3,64,1408]{2,1,0:T(8,128)S(1)} fusion(bf16[352,1408]{1,0:T(8,128)(2,1)} %param.20, bf16[3,64,4,352]{3,2,1,0:T(4,128)(2,1)S(1)} %dot_general.65), kind=kOutput, calls=%fused_computation.45 | convolution fusion | flops 762077184 | bytes 2613248 | tf_op jit(solution)/shard_map/pnc,cd->pnd/dot_general | solution.py:217
  25.5 2.9 %reshape.367 = f32[3,64,4,1408]{3,2,1,0:T(4,128)} reshape(bf16[3,256,1408]{2,1,0:T(8,128)(2,1)S(1)} %copy-done.3) | data formatting | bytes 6488064 | tf_op jit(solution)/shard_map/reshape | solution.py:220
  28.5 4.8 %reduce_sum.136 = f32[3,64,1408]{2,1,0:T(8,128)S(1)} reduce(f32[3,64,4,1408]{3,2,1,0:T(4,128)} %reshape.367, f32[]{:T(128)} %constant.144.clone.1), dimensions={2}, to_apply=%region_1.2 | reduce | flops 811008 | bytes 5406724 | tf_op jit(solution)/shard_map/reduce_sum | solution.py:220
  33.5 29.0 %all-reduce.2.cloned.1.call-done = bf16[3,64,1408]{2,1,0:T(8,128)(2,1)} async-done(((bf16[3,64,1408]{2,1,0:T(8,128)(2,1)}), bf16[3,64,1408]{2,1,0:T(8,128)(2,1)}) %all-reduce.2.cloned.1.call-update) | async-done | bytes 540688 | tf_op jit(solution)/shard_map/psum | solution.py:219
  62.5 3.5 %fusion.45 = bf16[3,64,1024]{2,1,0:T(8,128)(2,1)} fusion(bf16[1408,1024]{1,0:T(8,128)(2,1)} %param.21, bf16[3,64,1408]{2,1,0:T(8,128)(2,1)} %all-reduce.2.cloned.1.call-done, f32[3,64,1408]{2,1,0:T(8,128)S(1)} %reduce_sum.136), kind=kOutput, calls=%fused_computation.59 | convolution fusion | flops 554926080 | bytes 4898816 | tf_op jit(solution)/shard_map/pmd,de->pme/dot_general | solution.py:222
  66.9 1.6 fusion.44
  68.7 3.7 %pad_maximum_fusion = bf16[4,512,1024]{2,1,0:T(8,128)(2,1)} fusion(bf16[1,512,1024]{2,1,0:T(8,128)(2,1)} %bitcast.21, bf16[1,512,1024]{2,1,0:T(8,128)(2,1)} %bitcast.20, bf16[1,512,1024]{2,1,0:T(8,128)(2,1)} %bitcast.19, bf16[1,512,1024]{2,1,0:T(8,128)(2,1)S(1)} %bitcast.178), kind=kLoop, calls=%fused_computation.23 | loop fusion | flops 6291456 | bytes 8388608 | tf_op jit(solution)/shard_map/stack | solution.py:135
  72.4 5.3 %gather_fusion = bf16[4,512,1024]{2,1,0:T(8,128)(2,1)} fusion(bf16[4,512,1024]{2,1,0:T(8,128)(2,1)} %pad_maximum_fusion, s32[1024]{0:T(1024)S(1)} %pad_clamp_fusion), kind=kCustom, calls=%fused_computation | custom fusion | bytes 8388624 | tf_op jit(solution)/shard_map/jit(_take)/gather | solution.py:137
  77.7 2.7 %broadcast_select_fusion = bf16[4,512,1024]{2,1,0:T(8,128)(2,1)S(1)} fusion(bf16[4,512,1024]{2,1,0:T(8,128)(2,1)} %gather_fusion, pred[4]{0:T(512)(128)(4,1)S(1)} %compare_and_fusion), kind=kLoop, calls=%fused_computation.27 | loop fusion | flops 2097152 | bytes 8388612 | tf_op jit(solution)/shard_map/jit(_take)/select_n | solution.py:137
  80.4 1.8 slice_bitcast_fusion.3
  82.1 4.2 %all-gather.6.cloned.1.call-done = bf16[192,4096]{1,0:T(8,128)(2,1)} async-done(((bf16[192,1024]{1,0:T(8,128)(2,1)}), bf16[192,4096]{1,0:T(8,128)(2,1)}) %all-gather.6.cloned.1.call-update) | async-done | bytes 1572880 | tf_op jit(solution)/shard_map/all_gather | solution.py:250
  86.3 4.2 %fusion.2 = (f32[512]{0:T(512)S(1)}, bf16[512,4096]{1,0:T(8,128)(2,1)S(1)}) fusion(bf16[512,1024]{1,0:T(8,128)(2,1)S(1)} %get-tuple-element.28, bf16[512,1024]{1,0:T(8,128)(2,1)} %get-tuple-element.29, bf16[512,1024]{1,0:T(8,128)(2,1)} %get-tuple-element.30, bf16[512,1024]{1,0:T(8,128)(2,1)S(1)} %get-tuple-element.27, ...), kind=kOutput, calls=%fused_computation.6 | convolution fusion | flops 832667136 | bytes 9964800 | tf_op jit(solution)/shard_map/dot_general | solution.py:253
  90.6 2.6 %fusion.14 = f32[512,2,256]{0,2,1:T(8,128)S(1)} fusion(bf16[4096,2,256]{2,1,0:T(2,128)(2,1)S(1)} %copy-done.14, bf16[512,4096]{1,0:T(8,128)(2,1)S(1)} %get-tuple-element.49, f32[4096]{0:T(1024)S(1)} %copy-done.16, f32[512]{0:T(512)S(1)} %add_rsqrt_fusion.1), kind=kOutput, calls=%fused_computation.24 | convolution fusion | flops 2155872256 | bytes 9455616 | tf_op jit(solution)/shard_map/td,dce->tce/dot_general | solution.py:274
  93.3 2.6 fusion.49
  96.7 1.0 copy.64
  99.7 3.9 %constant_dynamic-slice_fusion = (bf16[512,1024]{1,0:T(8,128)(2,1)S(1)}, bf16[512,1024]{1,0:T(8,128)(2,1)}, bf16[512,1024]{1,0:T(8,128)(2,1)}, bf16[512,1024]{1,0:T(8,128)(2,1)}) fusion(bf16[512,4096]{1,0:T(8,128)(2,1)} %param.26, s32[]{:T(128)S(6)} %select_n.159, s32[]{:T(128)S(6)} %select_n.157, s32[]{:T(128)S(6)} %select_n.155, s32[]{:T(128)S(6)} %select_n.153), kind=kLoop, calls=%fused_computation.163 | loop fusion | bytes 8388624 | tf_op jit(solution)/shard_map/dynamic_slice | solution.py:229
  104.2 1.2 collective-permute-start.5
  105.5 1.2 and_convert_fusion.needed_ref
  106.7 1.1 copy.77
  109.4 1.1 pad_maximum_fusion.2
  110.5 18.1 %collective-permute-done.3 = bf16[512,1024]{1,0:T(8,128)(2,1)} collective-permute-done((bf16[512,1024]{1,0:T(8,128)(2,1)}, bf16[512,1024]{1,0:T(8,128)(2,1)}, u32[]{:S(2)}, u32[]{:S(2)}) %collective-permute-start.3) | collective-permute-done | bytes 1048608 | tf_op jit(solution)/shard_map/ppermute | solution.py:233
  128.7 1.6 collective-permute-done.4
  130.2 19.4 %collective-permute-done.5 = bf16[512,1024]{1,0:T(8,128)(2,1)} collective-permute-done((bf16[512,1024]{1,0:T(8,128)(2,1)S(1)}, bf16[512,1024]{1,0:T(8,128)(2,1)}, u32[]{:S(2)}, u32[]{:S(2)}) %collective-permute-start.5) | collective-permute-done | bytes 1048608 | tf_op jit(solution)/shard_map/ppermute | solution.py:233
  149.7 24.1 %all-gather.8.cloned.1.call-done = bf16[4288,512]{1,0:T(8,128)(2,1)} async-done(((bf16[536,512]{1,0:T(8,128)(2,1)}), bf16[4288,512]{1,0:T(8,128)(2,1)}) %all-gather.8.cloned.1.call-update) | async-done | bytes 4390928 | tf_op jit(solution)/shard_map/all_gather | solution.py:296
  173.8 4.0 %fusion.107 = (bf16[8,512,128]{2,1,0:T(8,128)(2,1)}, bf16[8,512,128]{2,1,0:T(8,128)(2,1)S(1)}, bf16[8,512,128]{2,1,0:T(8,128)(2,1)}, bf16[8,512,128]{2,1,0:T(8,128)(2,1)S(1)}) fusion(bf16[8,536,512]{2,1,0:T(8,128)(2,1)} %bitcast.162), kind=kLoop, calls=%fused_computation.190 | loop fusion | bytes 8388608 | tf_op jit(solution)/shard_map/slice | solution.py:329
  178.8 1.8 fusion.109
  180.7 1.8 fusion.108
  183.0 10.2 %shard_map.166 = bf16[512,512]{1,0:T(8,128)(2,1)} custom-call(s32[8]{0:T(128)} %and_convert_fusion.needed_ref, bf16[2,1024,128]{2,1,0:T(8,128)(2,1)} %bitcast.179, bf16[8,536,512]{2,1,0:T(8,128)(2,1)} %bitcast.164, bf16[8,536,512]{2,1,0:T(8,128)(2,1)} %bitcast.165, s32[1024,1]{1,0:T(8,128)} %bitcast.181, s32[1024,1]{1,0:T(8,128)} %bitcast.180, ...), custom_call_target="tpu_custom_call" | custom-call | flops 4294967296 | bytes 5242880 | tf_op jit(solution)/shard_map/pallas_call | solution.py:115
  193.2 1.9 maximum_maximum_fusion
  195.2 31.1 %all-gather.10.cloned.1.call-done = bf16[2080,512]{1,0:T(8,128)(2,1)} async-done(((bf16[520,512]{1,0:T(8,128)(2,1)}), bf16[2080,512]{1,0:T(8,128)(2,1)}) %all-gather.10.cloned.1.call-update) | async-done | bytes 2129936 | tf_op jit(solution)/shard_map/all_gather | solution.py:352
  226.3 1.9 convolution_convert_fusion.4
  228.3 2.1 convolution_convert_fusion.3
  230.4 2.0 convolution_convert_fusion.2
  232.4 2.0 convert_add_fusion
  234.4 1.3 copy-done.4
  236.0 2.4 fusion.86
  239.0 1.2 collective-permute-start.8
  240.2 2.5 fusion.29
  244.4 1.8 collective-permute-start.9
  246.1 1.8 collective-permute-done.9
  248.0 1.7 collective-permute-start.10
  249.7 1.8 collective-permute-done.10
  251.5 2.7 %collective-permute-start.11 = (f32[8]{0:T(128)S(1)}, f32[8]{0:T(128)S(1)}, u32[]{:S(2)}, u32[]{:S(2)}) collective-permute-start(f32[8]{0:T(128)S(1)} %max.10), channel_id=1, source_target_pairs={{0,4},{1,5},{2,6},{3,7},{4,0},{5,1},{6,2},{7,3},{8,12},{9,13},{10,... | collective-permute-start | bytes 104 | tf_op jit(solution)/shard_map/ppermute | solution.py:162
  254.2 1.8 collective-permute-done.11
  (119 shorter events, 17.5 us)
Async XLA Ops:
  7.2 7.4 %copy-start = (bf16[1408,3,352]{0,2,1:T(8,128)(2,1)S(1)}, bf16[1408,3,352]{0,2,1:T(8,128)(2,1)}, u32[]{:S(2)}) copy-start(bf16[1408,3,352]{0,2,1:T(8,128)(2,1)} %param.19) | copy-start | bytes 8921092
  7.2 7.2 %copy-start.11 = (s32[3,2]{0,1:T(2,128)S(1)}, s32[3,2]{0,1:T(2,128)}, u32[]{:S(2)}) copy-start(s32[3,2]{0,1:T(2,128)} %param.16) | copy-start | bytes 76
  7.2 7.3 %copy-start.17 = (f32[1408]{0:T(1024)S(1)}, f32[1408]{0:T(1024)}, u32[]{:S(2)}) copy-start(f32[1408]{0:T(1024)} %param.18) | copy-start | bytes 16900
  7.2 55.3 %all-reduce.2.cloned.1.call-start = ((), (), s32[]{:S(2)}) async-start(), calls=%async_computation | async-start | bytes 1081344 | tf_op jit(solution)/shard_map/psum | solution.py:219
  7.2 6.4 %copy-start.2 = (bf16[3,256,1408]{2,1,0:T(8,128)(2,1)S(1)}, bf16[3,256,1408]{2,1,0:T(8,128)(2,1)}, u32[]{:S(2)}) copy-start(bf16[3,256,1408]{2,1,0:T(8,128)(2,1)} %param.15) | copy-start | bytes 6488068
  7.3 61.5 %collective-permute-start = (bf16[512,1024]{1,0:T(8,128)(2,1)}, bf16[512,1024]{1,0:T(8,128)(2,1)}, u32[]{:S(2)}, u32[]{:S(2)}) collective-permute-start(bf16[512,1024]{1,0:T(8,128)(2,1)} %param.22), channel_id=1, source_target_pairs={{0,8},{8,16},{16,24},{24,0},{1,9},{9,17},{17,25},{25,1},{2,10},{10... | collective-permute-start | bytes 3145736 | tf_op jit(solution)/shard_map/ppermute | solution.py:133
  7.8 61.0 %collective-permute-start.1 = (bf16[512,1024]{1,0:T(8,128)(2,1)}, bf16[512,1024]{1,0:T(8,128)(2,1)}, u32[]{:S(2)}, u32[]{:S(2)}) collective-permute-start(bf16[512,1024]{1,0:T(8,128)(2,1)} %param.22), channel_id=1, source_target_pairs={{0,16},{8,24},{16,0},{24,8},{1,17},{9,25},{17,1},{25,9},{2,18},{10... | collective-permute-start | bytes 3145736 | tf_op jit(solution)/shard_map/ppermute | solution.py:133
  10.3 58.4 %collective-permute-start.2 = (bf16[512,1024]{1,0:T(8,128)(2,1)}, bf16[512,1024]{1,0:T(8,128)(2,1)}, u32[]{:S(2)}, u32[]{:S(2)}) collective-permute-start(bf16[512,1024]{1,0:T(8,128)(2,1)} %param.22), channel_id=1, source_target_pairs={{0,24},{8,0},{16,8},{24,16},{1,25},{9,1},{17,9},{25,17},{2,26},{10... | collective-permute-start | bytes 3145736 | tf_op jit(solution)/shard_map/ppermute | solution.py:133
  21.3 3.8 %copy-start.13 = (s32[8]{0:T(128)S(1)}, s32[8]{0:T(128)}, u32[]{:S(2)}) copy-start(s32[8]{0:T(128)} %param.27) | copy-start | bytes 100
  21.4 4.0 %copy-start.12 = (s32[3]{0:T(128)S(1)}, s32[3]{0:T(128)}, u32[]{:S(2)}) copy-start(s32[3]{0:T(128)} %param.17) | copy-start | bytes 40
  21.4 4.1 %copy-start.3 = (bf16[3,256,1408]{2,1,0:T(8,128)(2,1)S(1)}, bf16[3,256,1408]{2,1,0:T(8,128)(2,1)}, u32[]{:S(2)}) copy-start(bf16[3,256,1408]{2,1,0:T(8,128)(2,1)} %param.15) | copy-start | bytes 6488068
  25.0 61.3 %all-gather.6.cloned.1.call-start = ((), (), s32[]{:S(2)}) async-start(), calls=%async_computation.1 | async-start | bytes 1966080 | tf_op jit(solution)/shard_map/all_gather | solution.py:250
  33.3 33.6 %copy-start.8 = (bf16[512,1024]{1,0:T(8,128)(2,1)S(1)}, bf16[512,1024]{1,0:T(8,128)(2,1)}, u32[]{:S(2)}) copy-start(bf16[512,1024]{1,0:T(8,128)(2,1)} %param.22) | copy-start | bytes 3145732
  66.0 107.8 %all-gather.8.cloned.1.call-start = ((), (), s32[]{:S(2)}) async-start(), calls=%async_computation.2 | async-start | bytes 4939776 | tf_op jit(solution)/shard_map/all_gather | solution.py:296
  68.4 4.0 %copy-start.6 = (bf16[512,1024]{1,0:T(8,128)(2,1)}, bf16[512,1024]{1,0:T(8,128)(2,1)S(1)}, u32[]{:S(2)}) copy-start(bf16[512,1024]{1,0:T(8,128)(2,1)S(1)} %fusion.44) | copy-start | bytes 3145732
  86.3 4.2 %copy-start.14 = (bf16[4096,2,256]{2,1,0:T(2,128)(2,1)S(1)}, bf16[4096,2,256]{2,1,0:T(2,128)(2,1)}, u32[]{:S(2)}) copy-start(bf16[4096,2,256]{2,1,0:T(2,128)(2,1)} %param.25) | copy-start | bytes 12582916
  86.3 4.2 %copy-start.16 = (f32[4096]{0:T(1024)S(1)}, f32[4096]{0:T(1024)}, u32[]{:S(2)}) copy-start(f32[4096]{0:T(1024)} %param.23) | copy-start | bytes 49156
  90.6 2.7 %copy-start.15 = (bf16[4096,512]{1,0:T(8,128)(2,1)S(1)}, bf16[4096,512]{1,0:T(8,128)(2,1)}, u32[]{:S(2)}) copy-start(bf16[4096,512]{1,0:T(8,128)(2,1)} %param.24) | copy-start | bytes 12582916
  97.8 128.5 %all-gather.10.cloned.1.call-start = ((), (), s32[]{:S(2)}) async-start(), calls=%async_computation.3 | async-start | bytes 2662400 | tf_op jit(solution)/shard_map/all_gather | solution.py:352
  103.7 25.0 %collective-permute-start.3 = (bf16[512,1024]{1,0:T(8,128)(2,1)}, bf16[512,1024]{1,0:T(8,128)(2,1)}, u32[]{:S(2)}, u32[]{:S(2)}) collective-permute-start(bf16[512,1024]{1,0:T(8,128)(2,1)} %get-tuple-element.25), channel_id=1, source_target_pairs={{0,8},{8,16},{16,24},{24,0},{1,9},{9,17},{17,25},{25,1},{2,10},{10... | collective-permute-start | bytes 3145736 | tf_op jit(solution)/shard_map/ppermute | solution.py:233
  103.9 26.3 %collective-permute-start.4 = (bf16[512,1024]{1,0:T(8,128)(2,1)}, bf16[512,1024]{1,0:T(8,128)(2,1)}, u32[]{:S(2)}, u32[]{:S(2)}) collective-permute-start(bf16[512,1024]{1,0:T(8,128)(2,1)} %get-tuple-element.24), channel_id=1, source_target_pairs={{0,16},{8,24},{16,0},{24,8},{1,17},{9,25},{17,1},{25,9},{2,18},{10... | collective-permute-start | bytes 3145736 | tf_op jit(solution)/shard_map/ppermute | solution.py:233
  104.2 45.4 %collective-permute-start.5 = (bf16[512,1024]{1,0:T(8,128)(2,1)S(1)}, bf16[512,1024]{1,0:T(8,128)(2,1)}, u32[]{:S(2)}, u32[]{:S(2)}) collective-permute-start(bf16[512,1024]{1,0:T(8,128)(2,1)S(1)} %get-tuple-element.23), channel_id=1, source_target_pairs={{0,24},{8,0},{16,8},{24,16},{1,25},{9,1},{17,9},{25,17},{2,26},{10... | collective-permute-start | bytes 3145736 | tf_op jit(solution)/shard_map/ppermute | solution.py:233
  183.0 43.3 %copy-start.7 = (bf16[512,1024]{1,0:T(8,128)(2,1)S(1)}, bf16[512,1024]{1,0:T(8,128)(2,1)}, u32[]{:S(2)}) copy-start(bf16[512,1024]{1,0:T(8,128)(2,1)} %get-tuple-element.13) | copy-start | bytes 3145732
  226.3 4.1 %copy-start.9 = (bf16[2080,512]{1,0:T(8,128)(2,1)S(1)}, bf16[2080,512]{1,0:T(8,128)(2,1)}, u32[]{:S(2)}) copy-start(bf16[2080,512]{1,0:T(8,128)(2,1)} %all-gather.10.cloned.1.call-done) | copy-start | bytes 6389764
  232.4 3.6 %copy-start.10 = (f32[1024]{0:T(1024)S(1)}, f32[1024]{0:T(1024)}, u32[]{:S(2)}) copy-start(f32[1024]{0:T(1024)} %param.28) | copy-start | bytes 12292
  234.4 1.4 copy-start.4
  236.0 4.3 %copy-start.5 = (f32[520,1024]{1,0:T(8,128)S(1)}, f32[520,1024]{1,0:T(8,128)}, u32[]{:S(2)}) copy-start(f32[520,1024]{1,0:T(8,128)} %copy-done.4) | copy-start | bytes 6389764
  236.0 20.5 %copy-start.1 = (bf16[1408,3,352]{0,2,1:T(8,128)(2,1)S(1)}, bf16[1408,3,352]{0,2,1:T(8,128)(2,1)}, u32[]{:S(2)}) copy-start(bf16[1408,3,352]{0,2,1:T(8,128)(2,1)} %param.19) | copy-start | bytes 8921092
  238.4 4.4 %collective-permute-start.6 = (f32[8,1025]{1,0:T(8,128)S(1)}, f32[8,1025]{1,0:T(8,128)S(1)}, u32[]{:S(2)}, u32[]{:S(2)}) collective-permute-start(f32[8,1025]{1,0:T(8,128)S(1)} %get-tuple-element.36), channel_id=1, source_target_pairs={{0,8},{8,16},{16,24},{24,0},{1,9},{9,17},{17,25},{25,1},{2,10},{10... | collective-permute-start | bytes 98408 | tf_op jit(solution)/shard_map/ppermute | solution.py:145
  238.7 4.1 %collective-permute-start.7 = (f32[8,1025]{1,0:T(8,128)S(1)}, f32[8,1025]{1,0:T(8,128)S(1)}, u32[]{:S(2)}, u32[]{:S(2)}) collective-permute-start(f32[8,1025]{1,0:T(8,128)S(1)} %get-tuple-element.36), channel_id=1, source_target_pairs={{0,16},{8,24},{16,0},{24,8},{1,17},{9,25},{17,1},{25,9},{2,18},{10... | collective-permute-start | bytes 98408 | tf_op jit(solution)/shard_map/ppermute | solution.py:145
  239.0 3.8 %collective-permute-start.8 = (f32[8,1025]{1,0:T(8,128)S(1)}, f32[8,1025]{1,0:T(8,128)S(1)}, u32[]{:S(2)}, u32[]{:S(2)}) collective-permute-start(f32[8,1025]{1,0:T(8,128)S(1)} %get-tuple-element.36), channel_id=1, source_target_pairs={{0,24},{8,0},{16,8},{24,16},{1,25},{9,1},{17,9},{25,17},{2,26},{10... | collective-permute-start | bytes 98408 | tf_op jit(solution)/shard_map/ppermute | solution.py:145
  244.4 3.6 %collective-permute-start.9 = (f32[8]{0:T(128)S(1)}, f32[8]{0:T(128)S(1)}, u32[]{:S(2)}, u32[]{:S(2)}) collective-permute-start(f32[8]{0:T(128)S(1)} %get-tuple-element.41), channel_id=1, source_target_pairs={{0,1},{1,0},{2,3},{3,2},{4,5},{5,4},{6,7},{7,6},{8,9},{9,8},{10,11... | collective-permute-start | bytes 104 | tf_op jit(solution)/shard_map/ppermute | solution.py:162
  248.0 3.5 %collective-permute-start.10 = (f32[8]{0:T(128)S(1)}, f32[8]{0:T(128)S(1)}, u32[]{:S(2)}, u32[]{:S(2)}) collective-permute-start(f32[8]{0:T(128)S(1)} %max.9), channel_id=1, source_target_pairs={{0,2},{1,3},{2,0},{3,1},{4,6},{5,7},{6,4},{7,5},{8,10},{9,11},{10,... | collective-permute-start | bytes 104 | tf_op jit(solution)/shard_map/ppermute | solution.py:162
  251.5 4.4 %collective-permute-start.11 = (f32[8]{0:T(128)S(1)}, f32[8]{0:T(128)S(1)}, u32[]{:S(2)}, u32[]{:S(2)}) collective-permute-start(f32[8]{0:T(128)S(1)} %max.10), channel_id=1, source_target_pairs={{0,4},{1,5},{2,6},{3,7},{4,0},{5,1},{6,2},{7,3},{8,12},{9,13},{10,... | collective-permute-start | bytes 104 | tf_op jit(solution)/shard_map/ppermute | solution.py:162
Sparse Core Ops, SparseCore 0:
  25.1 37.3 all-reduce.1
  66.2 20.1 all-gather.5
  97.9 75.8 all-gather.7
  195.2 31.0 all-gather.9

commit v15 on v14

--- a/solution.py
+++ b/solution.py
@@ -55,12 +55,11 @@
         sum_ref[...] = jnp.zeros(sum_ref.shape, jnp.float32)
         acc_ref[...] = jnp.zeros(acc_ref.shape, jnp.float32)
 
-    @pl.when(needed_ref[kb] != 0)
-    def _():
-        allowed = (kid_ref[...] <= qid_ref[...]) & (kreq_ref[...] == qreq_ref[...])
+    def step(j):
+        allowed = (kid_ref[j] <= qid_ref[...]) & (kreq_ref[j] == qreq_ref[...])
         for g in range(groups):
             scores = lax.dot_general(
-                q_ref[g], k_ref[:, g * HD : (g + 1) * HD], (((1,), (1,)), ((), ())),
+                q_ref[g], k_ref[j, :, g * HD : (g + 1) * HD], (((1,), (1,)), ((), ())),
                 preferred_element_type=jnp.float32,
             ) / root
             scores = jnp.where(allowed, scores, -1e30)
@@ -70,10 +69,13 @@
             scale = jnp.exp(old_max - new_max)
             sum_ref[g] = sum_ref[g] * scale + jnp.sum(weights, axis=1, keepdims=True)
             acc_ref[g] = acc_ref[g] * scale + jnp.dot(
-                weights.astype(jnp.bfloat16), v_ref[:, g * HD : (g + 1) * HD],
+                weights.astype(jnp.bfloat16), v_ref[j, :, g * HD : (g + 1) * HD],
                 preferred_element_type=jnp.float32,
             )
             max_ref[g] = new_max
+
+    for j in range(k_ref.shape[0]):
+        pl.when(needed_ref[kb * k_ref.shape[0] + j] != 0)(functools.partial(step, j))
 
     @pl.when(kb == pl.num_programs(0) - 1)
     def _():
@@ -92,17 +94,18 @@
     blocks = gathered.shape[0]
     group_rows = grouped_q.shape[1]
     width = groups * HD
+    pair = 2 if blocks % 2 == 0 else 1
     grid_spec = pltpu.PrefetchScalarGridSpec(
         num_scalar_prefetch=1,
-        grid=(blocks,),
+        grid=(blocks // pair,),
         in_specs=[
             pl.BlockSpec((groups, group_rows, HD), lambda kb, n: (0, 0, 0)),
-            pl.BlockSpec((None, tok_rows, width), lambda kb, n: (kb, 0, 0)),
-            pl.BlockSpec((None, tok_rows, width), lambda kb, n: (kb, 0, 1)),
+            pl.BlockSpec((pair, tok_rows, width), lambda kb, n: (kb, 0, 0)),
+            pl.BlockSpec((pair, tok_rows, width), lambda kb, n: (kb, 0, 1)),
             pl.BlockSpec((group_rows, 1), lambda kb, n: (0, 0)),
             pl.BlockSpec((group_rows, 1), lambda kb, n: (0, 0)),
-            pl.BlockSpec((None, 1, tok_rows), lambda kb, n: (kb, 0, 0)),
-            pl.BlockSpec((None, 1, tok_rows), lambda kb, n: (kb, 0, 0)),
+            pl.BlockSpec((pair, 1, tok_rows), lambda kb, n: (kb, 0, 0)),
+            pl.BlockSpec((pair, 1, tok_rows), lambda kb, n: (kb, 0, 0)),
         ],
         out_specs=pl.BlockSpec((tok_rows, groups * group_rows // tok_rows * HD), lambda kb, n: (0, 0)),
         scratch_shapes=[

time: 264 us -> 263 us (level)
  no operation moved by 1% of the time
where the time goes in v15:
time: 263 us; the launch traced here: 262 us
  waiting for transfers between devices  134 us (51%)
  matrix products  37 us (14%)
  other arithmetic  27.8 us (11%)
  local copies, waits for them, and re-layouts  25.9 us (10%)
  starting transfers between devices  14.6 us (6%)
  between operations  14.4 us (5%)
  Pallas kernels  8.79 us (3%)
    ppermute x3, waiting for transfers between devices, on_device(): lax.ppermute(payload, 'kv', perm=[(i, (i + shift) % kv_count) for i in ra...  39.1 us
    all_gather x1, waiting for transfers between devices, on_device(): context_all = lax.all_gather(out_rows, 'kv', axis=0, tiled=False)  31.8 us
    psum x1, waiting for transfers between devices, on_device(): lax.psum(head_pooled.astype(jnp.bfloat16), 'kv').astype(jnp.float32)  29 us
    all_gather x1, waiting for transfers between devices, on_device(): gathered = lax.all_gather(shipped, 'blk', axis=0, tiled=False)  24.1 us
    pallas_call x1, Pallas kernels, flash_attention(): pl.pallas_call(functools.partial(flash_kernel, root=root), grid_spec=grid...  8.79 us
    dot_general x4, matrix products, on_device(): part = jnp.dot(source, piece, preferred_element_type=jnp.float32)  8.02 us
    ppermute x3, starting transfers between devices, tree_max(): lax.ppermute(values, axis, perm=[(i, i ^ step) for i in range(count)])  6.17 us
    ppermute x3, waiting for transfers between devices, tree_max(): lax.ppermute(values, axis, perm=[(i, i ^ step) for i in range(count)])  5.4 us
  transfers between devices with their start and end apart: 16, of which 10 were waited for; matrix products, arithmetic and copies ran while one was open for 21% of the time, Pallas kernels for 0%

profile of v15, /device:TPU:0, one launch (start us, length us, event | category | flops | bytes accessed | tf_op | source)
XLA Modules:
  0.0 262.2 jit_solution(348799543358624289)
XLA Ops:
  7.8 2.6 collective-permute-start.1
  10.3 1.4 collective-permute-start.2
  11.7 2.0 convert_reduce_fusion
  14.5 2.9 %fusion.30 = bf16[3,256,3,352]{1,3,2,0:T(8,128)(2,1)S(1)} fusion(bf16[1408,3,352]{0,2,1:T(8,128)(2,1)S(1)} %copy-done, bf16[3,256,1408]{2,1,0:T(8,128)(2,1)S(1)} %copy-done.2, f32[1408]{0:T(1024)S(1)} %copy-done.17, f32[3,256]{1,0:T(4,128)S(1)} %add_rsqrt_fusion, f32[3,256]{1,0:T(4,128)S(1)} %broadcast_multiply_fusion), kind=kOutput, calls=%fused_computation.46 | convolution fusion | flops 2290016256 | bytes 6770176 | tf_op jit(solution)/shard_map/pnd,dce->pnce/dot_general | solution.py:197
  21.4 2.7 %convolution_reduce_fusion = f32[3,64,1408]{2,1,0:T(8,128)S(1)} fusion(bf16[352,1408]{1,0:T(8,128)(2,1)} %param.20, bf16[3,64,4,352]{3,2,1,0:T(4,128)(2,1)S(1)} %dot_general.65), kind=kOutput, calls=%fused_computation.45 | convolution fusion | flops 762077184 | bytes 2613248 | tf_op jit(solution)/shard_map/pnc,cd->pnd/dot_general | solution.py:220
  25.5 2.9 %reshape.367 = f32[3,64,4,1408]{3,2,1,0:T(4,128)} reshape(bf16[3,256,1408]{2,1,0:T(8,128)(2,1)S(1)} %copy-done.3) | data formatting | bytes 6488064 | tf_op jit(solution)/shard_map/reshape | solution.py:223
  28.5 4.8 %reduce_sum.136 = f32[3,64,1408]{2,1,0:T(8,128)S(1)} reduce(f32[3,64,4,1408]{3,2,1,0:T(4,128)} %reshape.367, f32[]{:T(128)} %constant.144.clone.1), dimensions={2}, to_apply=%region_1.2 | reduce | flops 811008 | bytes 5406724 | tf_op jit(solution)/shard_map/reduce_sum | solution.py:223
  33.5 29.0 %all-reduce.2.cloned.1.call-done = bf16[3,64,1408]{2,1,0:T(8,128)(2,1)} async-done(((bf16[3,64,1408]{2,1,0:T(8,128)(2,1)}), bf16[3,64,1408]{2,1,0:T(8,128)(2,1)}) %all-reduce.2.cloned.1.call-update) | async-done | bytes 540688 | tf_op jit(solution)/shard_map/psum | solution.py:222
  62.5 3.5 %fusion.45 = bf16[3,64,1024]{2,1,0:T(8,128)(2,1)} fusion(bf16[1408,1024]{1,0:T(8,128)(2,1)} %param.21, bf16[3,64,1408]{2,1,0:T(8,128)(2,1)} %all-reduce.2.cloned.1.call-done, f32[3,64,1408]{2,1,0:T(8,128)S(1)} %reduce_sum.136), kind=kOutput, calls=%fused_computation.59 | convolution fusion | flops 554926080 | bytes 4898816 | tf_op jit(solution)/shard_map/pmd,de->pme/dot_general | solution.py:225
  66.9 1.6 fusion.44
  68.7 3.7 %pad_maximum_fusion = bf16[4,512,1024]{2,1,0:T(8,128)(2,1)} fusion(bf16[1,512,1024]{2,1,0:T(8,128)(2,1)} %bitcast.21, bf16[1,512,1024]{2,1,0:T(8,128)(2,1)} %bitcast.20, bf16[1,512,1024]{2,1,0:T(8,128)(2,1)} %bitcast.19, bf16[1,512,1024]{2,1,0:T(8,128)(2,1)S(1)} %bitcast.178), kind=kLoop, calls=%fused_computation.23 | loop fusion | flops 6291456 | bytes 8388608 | tf_op jit(solution)/shard_map/stack | solution.py:138
  72.4 5.3 %gather_fusion = bf16[4,512,1024]{2,1,0:T(8,128)(2,1)} fusion(bf16[4,512,1024]{2,1,0:T(8,128)(2,1)} %pad_maximum_fusion, s32[1024]{0:T(1024)S(1)} %pad_clamp_fusion), kind=kCustom, calls=%fused_computation | custom fusion | bytes 8388624 | tf_op jit(solution)/shard_map/jit(_take)/gather | solution.py:140
  77.7 2.7 %broadcast_select_fusion = bf16[4,512,1024]{2,1,0:T(8,128)(2,1)S(1)} fusion(bf16[4,512,1024]{2,1,0:T(8,128)(2,1)} %gather_fusion, pred[4]{0:T(512)(128)(4,1)S(1)} %compare_and_fusion), kind=kLoop, calls=%fused_computation.27 | loop fusion | flops 2097152 | bytes 8388612 | tf_op jit(solution)/shard_map/jit(_take)/select_n | solution.py:140
  80.4 1.8 slice_bitcast_fusion.3
  82.1 4.2 %all-gather.6.cloned.1.call-done = bf16[192,4096]{1,0:T(8,128)(2,1)} async-done(((bf16[192,1024]{1,0:T(8,128)(2,1)}), bf16[192,4096]{1,0:T(8,128)(2,1)}) %all-gather.6.cloned.1.call-update) | async-done | bytes 1572880 | tf_op jit(solution)/shard_map/all_gather | solution.py:253
  86.3 4.2 %fusion.2 = (f32[512]{0:T(512)S(1)}, bf16[512,4096]{1,0:T(8,128)(2,1)S(1)}) fusion(bf16[512,1024]{1,0:T(8,128)(2,1)S(1)} %get-tuple-element.28, bf16[512,1024]{1,0:T(8,128)(2,1)} %get-tuple-element.29, bf16[512,1024]{1,0:T(8,128)(2,1)} %get-tuple-element.30, bf16[512,1024]{1,0:T(8,128)(2,1)S(1)} %get-tuple-element.27, ...), kind=kOutput, calls=%fused_computation.6 | convolution fusion | flops 832667136 | bytes 9964800 | tf_op jit(solution)/shard_map/dot_general | solution.py:256
  90.6 2.6 %fusion.14 = f32[512,2,256]{0,2,1:T(8,128)S(1)} fusion(bf16[4096,2,256]{2,1,0:T(2,128)(2,1)S(1)} %copy-done.14, bf16[512,4096]{1,0:T(8,128)(2,1)S(1)} %get-tuple-element.49, f32[4096]{0:T(1024)S(1)} %copy-done.16, f32[512]{0:T(512)S(1)} %add_rsqrt_fusion.1), kind=kOutput, calls=%fused_computation.24 | convolution fusion | flops 2155872256 | bytes 9455616 | tf_op jit(solution)/shard_map/td,dce->tce/dot_general | solution.py:277
  93.3 2.6 fusion.49
  96.7 1.0 copy.64
  99.7 3.9 %constant_dynamic-slice_fusion = (bf16[512,1024]{1,0:T(8,128)(2,1)S(1)}, bf16[512,1024]{1,0:T(8,128)(2,1)}, bf16[512,1024]{1,0:T(8,128)(2,1)}, bf16[512,1024]{1,0:T(8,128)(2,1)}) fusion(bf16[512,4096]{1,0:T(8,128)(2,1)} %param.26, s32[]{:T(128)S(6)} %select_n.159, s32[]{:T(128)S(6)} %select_n.157, s32[]{:T(128)S(6)} %select_n.155, s32[]{:T(128)S(6)} %select_n.153), kind=kLoop, calls=%fused_computation.163 | loop fusion | bytes 8388624 | tf_op jit(solution)/shard_map/dynamic_slice | solution.py:232
  104.2 1.2 collective-permute-start.5
  105.5 1.2 and_convert_fusion.needed_ref
  106.7 1.1 copy.77
  109.4 1.1 pad_maximum_fusion.2
  110.5 18.1 %collective-permute-done.3 = bf16[512,1024]{1,0:T(8,128)(2,1)} collective-permute-done((bf16[512,1024]{1,0:T(8,128)(2,1)}, bf16[512,1024]{1,0:T(8,128)(2,1)}, u32[]{:S(2)}, u32[]{:S(2)}) %collective-permute-start.3) | collective-permute-done | bytes 1048608 | tf_op jit(solution)/shard_map/ppermute | solution.py:236
  128.7 1.6 collective-permute-done.4
  130.2 19.4 %collective-permute-done.5 = bf16[512,1024]{1,0:T(8,128)(2,1)} collective-permute-done((bf16[512,1024]{1,0:T(8,128)(2,1)S(1)}, bf16[512,1024]{1,0:T(8,128)(2,1)}, u32[]{:S(2)}, u32[]{:S(2)}) %collective-permute-start.5) | collective-permute-done | bytes 1048608 | tf_op jit(solution)/shard_map/ppermute | solution.py:236
  149.7 24.1 %all-gather.8.cloned.1.call-done = bf16[4288,512]{1,0:T(8,128)(2,1)} async-done(((bf16[536,512]{1,0:T(8,128)(2,1)}), bf16[4288,512]{1,0:T(8,128)(2,1)}) %all-gather.8.cloned.1.call-update) | async-done | bytes 4390928 | tf_op jit(solution)/shard_map/all_gather | solution.py:299
  173.8 4.0 %fusion.107 = (bf16[8,512,128]{2,1,0:T(8,128)(2,1)}, bf16[8,512,128]{2,1,0:T(8,128)(2,1)S(1)}, bf16[8,512,128]{2,1,0:T(8,128)(2,1)}, bf16[8,512,128]{2,1,0:T(8,128)(2,1)S(1)}) fusion(bf16[8,536,512]{2,1,0:T(8,128)(2,1)} %bitcast.162), kind=kLoop, calls=%fused_computation.190 | loop fusion | bytes 8388608 | tf_op jit(solution)/shard_map/slice | solution.py:332
  178.8 1.8 fusion.109
  180.7 1.8 fusion.108
  183.0 8.8 %shard_map.166 = bf16[512,512]{1,0:T(8,128)(2,1)} custom-call(s32[8]{0:T(128)} %and_convert_fusion.needed_ref, bf16[2,1024,128]{2,1,0:T(8,128)(2,1)} %bitcast.179, bf16[8,536,512]{2,1,0:T(8,128)(2,1)} %bitcast.164, bf16[8,536,512]{2,1,0:T(8,128)(2,1)} %bitcast.165, s32[1024,1]{1,0:T(8,128)} %bitcast.181, s32[1024,1]{1,0:T(8,128)} %bitcast.180, ...), custom_call_target="tpu_custom_call" | custom-call | flops 4294967296 | bytes 5242880 | tf_op jit(solution)/shard_map/pallas_call | solution.py:118
  191.8 1.9 maximum_maximum_fusion
  193.8 31.8 %all-gather.10.cloned.1.call-done = bf16[2080,512]{1,0:T(8,128)(2,1)} async-done(((bf16[520,512]{1,0:T(8,128)(2,1)}), bf16[2080,512]{1,0:T(8,128)(2,1)}) %all-gather.10.cloned.1.call-update) | async-done | bytes 2129936 | tf_op jit(solution)/shard_map/all_gather | solution.py:355
  225.5 1.9 convolution_convert_fusion.4
  227.4 2.1 convolution_convert_fusion.3
  229.6 2.0 convolution_convert_fusion.2
  231.6 2.0 convert_add_fusion
  233.6 1.3 copy-done.4
  235.2 2.4 fusion.86
  238.2 1.2 collective-permute-start.8
  239.4 2.5 fusion.29
  243.6 1.8 collective-permute-start.9
  245.3 1.8 collective-permute-done.9
  247.2 1.7 collective-permute-start.10
  248.9 1.8 collective-permute-done.10
  250.7 2.7 %collective-permute-start.11 = (f32[8]{0:T(128)S(1)}, f32[8]{0:T(128)S(1)}, u32[]{:S(2)}, u32[]{:S(2)}) collective-permute-start(f32[8]{0:T(128)S(1)} %max.10), channel_id=1, source_target_pairs={{0,4},{1,5},{2,6},{3,7},{4,0},{5,1},{6,2},{7,3},{8,12},{9,13},{10,... | collective-permute-start | bytes 104 | tf_op jit(solution)/shard_map/ppermute | solution.py:165
  253.4 1.8 collective-permute-done.11
  (119 shorter events, 17.5 us)
Async XLA Ops:
  7.2 7.4 %copy-start = (bf16[1408,3,352]{0,2,1:T(8,128)(2,1)S(1)}, bf16[1408,3,352]{0,2,1:T(8,128)(2,1)}, u32[]{:S(2)}) copy-start(bf16[1408,3,352]{0,2,1:T(8,128)(2,1)} %param.19) | copy-start | bytes 8921092
  7.2 7.2 %copy-start.11 = (s32[3,2]{0,1:T(2,128)S(1)}, s32[3,2]{0,1:T(2,128)}, u32[]{:S(2)}) copy-start(s32[3,2]{0,1:T(2,128)} %param.16) | copy-start | bytes 76
  7.2 7.3 %copy-start.17 = (f32[1408]{0:T(1024)S(1)}, f32[1408]{0:T(1024)}, u32[]{:S(2)}) copy-start(f32[1408]{0:T(1024)} %param.18) | copy-start | bytes 16900
  7.2 55.3 %all-reduce.2.cloned.1.call-start = ((), (), s32[]{:S(2)}) async-start(), calls=%async_computation | async-start | bytes 1081344 | tf_op jit(solution)/shard_map/psum | solution.py:222
  7.2 6.4 %copy-start.2 = (bf16[3,256,1408]{2,1,0:T(8,128)(2,1)S(1)}, bf16[3,256,1408]{2,1,0:T(8,128)(2,1)}, u32[]{:S(2)}) copy-start(bf16[3,256,1408]{2,1,0:T(8,128)(2,1)} %param.15) | copy-start | bytes 6488068
  7.3 61.5 %collective-permute-start = (bf16[512,1024]{1,0:T(8,128)(2,1)}, bf16[512,1024]{1,0:T(8,128)(2,1)}, u32[]{:S(2)}, u32[]{:S(2)}) collective-permute-start(bf16[512,1024]{1,0:T(8,128)(2,1)} %param.22), channel_id=1, source_target_pairs={{0,8},{8,16},{16,24},{24,0},{1,9},{9,17},{17,25},{25,1},{2,10},{10... | collective-permute-start | bytes 3145736 | tf_op jit(solution)/shard_map/ppermute | solution.py:136
  7.8 61.0 %collective-permute-start.1 = (bf16[512,1024]{1,0:T(8,128)(2,1)}, bf16[512,1024]{1,0:T(8,128)(2,1)}, u32[]{:S(2)}, u32[]{:S(2)}) collective-permute-start(bf16[512,1024]{1,0:T(8,128)(2,1)} %param.22), channel_id=1, source_target_pairs={{0,16},{8,24},{16,0},{24,8},{1,17},{9,25},{17,1},{25,9},{2,18},{10... | collective-permute-start | bytes 3145736 | tf_op jit(solution)/shard_map/ppermute | solution.py:136
  10.3 58.4 %collective-permute-start.2 = (bf16[512,1024]{1,0:T(8,128)(2,1)}, bf16[512,1024]{1,0:T(8,128)(2,1)}, u32[]{:S(2)}, u32[]{:S(2)}) collective-permute-start(bf16[512,1024]{1,0:T(8,128)(2,1)} %param.22), channel_id=1, source_target_pairs={{0,24},{8,0},{16,8},{24,16},{1,25},{9,1},{17,9},{25,17},{2,26},{10... | collective-permute-start | bytes 3145736 | tf_op jit(solution)/shard_map/ppermute | solution.py:136
  21.3 3.8 %copy-start.13 = (s32[8]{0:T(128)S(1)}, s32[8]{0:T(128)}, u32[]{:S(2)}) copy-start(s32[8]{0:T(128)} %param.27) | copy-start | bytes 100
  21.4 4.0 %copy-start.12 = (s32[3]{0:T(128)S(1)}, s32[3]{0:T(128)}, u32[]{:S(2)}) copy-start(s32[3]{0:T(128)} %param.17) | copy-start | bytes 40
  21.4 4.1 %copy-start.3 = (bf16[3,256,1408]{2,1,0:T(8,128)(2,1)S(1)}, bf16[3,256,1408]{2,1,0:T(8,128)(2,1)}, u32[]{:S(2)}) copy-start(bf16[3,256,1408]{2,1,0:T(8,128)(2,1)} %param.15) | copy-start | bytes 6488068
  25.0 61.3 %all-gather.6.cloned.1.call-start = ((), (), s32[]{:S(2)}) async-start(), calls=%async_computation.1 | async-start | bytes 1966080 | tf_op jit(solution)/shard_map/all_gather | solution.py:253
  33.3 33.6 %copy-start.8 = (bf16[512,1024]{1,0:T(8,128)(2,1)S(1)}, bf16[512,1024]{1,0:T(8,128)(2,1)}, u32[]{:S(2)}) copy-start(bf16[512,1024]{1,0:T(8,128)(2,1)} %param.22) | copy-start | bytes 3145732
  66.0 107.8 %all-gather.8.cloned.1.call-start = ((), (), s32[]{:S(2)}) async-start(), calls=%async_computation.2 | async-start | bytes 4939776 | tf_op jit(solution)/shard_map/all_gather | solution.py:299
  68.4 4.0 %copy-start.6 = (bf16[512,1024]{1,0:T(8,128)(2,1)}, bf16[512,1024]{1,0:T(8,128)(2,1)S(1)}, u32[]{:S(2)}) copy-start(bf16[512,1024]{1,0:T(8,128)(2,1)S(1)} %fusion.44) | copy-start | bytes 3145732
  86.3 4.2 %copy-start.14 = (bf16[4096,2,256]{2,1,0:T(2,128)(2,1)S(1)}, bf16[4096,2,256]{2,1,0:T(2,128)(2,1)}, u32[]{:S(2)}) copy-start(bf16[4096,2,256]{2,1,0:T(2,128)(2,1)} %param.25) | copy-start | bytes 12582916
  86.3 4.2 %copy-start.16 = (f32[4096]{0:T(1024)S(1)}, f32[4096]{0:T(1024)}, u32[]{:S(2)}) copy-start(f32[4096]{0:T(1024)} %param.23) | copy-start | bytes 49156
  90.6 2.7 %copy-start.15 = (bf16[4096,512]{1,0:T(8,128)(2,1)S(1)}, bf16[4096,512]{1,0:T(8,128)(2,1)}, u32[]{:S(2)}) copy-start(bf16[4096,512]{1,0:T(8,128)(2,1)} %param.24) | copy-start | bytes 12582916
  97.8 127.7 %all-gather.10.cloned.1.call-start = ((), (), s32[]{:S(2)}) async-start(), calls=%async_computation.3 | async-start | bytes 2662400 | tf_op jit(solution)/shard_map/all_gather | solution.py:355
  103.7 25.0 %collective-permute-start.3 = (bf16[512,1024]{1,0:T(8,128)(2,1)}, bf16[512,1024]{1,0:T(8,128)(2,1)}, u32[]{:S(2)}, u32[]{:S(2)}) collective-permute-start(bf16[512,1024]{1,0:T(8,128)(2,1)} %get-tuple-element.25), channel_id=1, source_target_pairs={{0,8},{8,16},{16,24},{24,0},{1,9},{9,17},{17,25},{25,1},{2,10},{10... | collective-permute-start | bytes 3145736 | tf_op jit(solution)/shard_map/ppermute | solution.py:236
  103.9 26.3 %collective-permute-start.4 = (bf16[512,1024]{1,0:T(8,128)(2,1)}, bf16[512,1024]{1,0:T(8,128)(2,1)}, u32[]{:S(2)}, u32[]{:S(2)}) collective-permute-start(bf16[512,1024]{1,0:T(8,128)(2,1)} %get-tuple-element.24), channel_id=1, source_target_pairs={{0,16},{8,24},{16,0},{24,8},{1,17},{9,25},{17,1},{25,9},{2,18},{10... | collective-permute-start | bytes 3145736 | tf_op jit(solution)/shard_map/ppermute | solution.py:236
  104.2 45.4 %collective-permute-start.5 = (bf16[512,1024]{1,0:T(8,128)(2,1)S(1)}, bf16[512,1024]{1,0:T(8,128)(2,1)}, u32[]{:S(2)}, u32[]{:S(2)}) collective-permute-start(bf16[512,1024]{1,0:T(8,128)(2,1)S(1)} %get-tuple-element.23), channel_id=1, source_target_pairs={{0,24},{8,0},{16,8},{24,16},{1,25},{9,1},{17,9},{25,17},{2,26},{10... | collective-permute-start | bytes 3145736 | tf_op jit(solution)/shard_map/ppermute | solution.py:236
  183.0 42.5 %copy-start.7 = (bf16[512,1024]{1,0:T(8,128)(2,1)S(1)}, bf16[512,1024]{1,0:T(8,128)(2,1)}, u32[]{:S(2)}) copy-start(bf16[512,1024]{1,0:T(8,128)(2,1)} %get-tuple-element.13) | copy-start | bytes 3145732
  225.5 4.1 %copy-start.9 = (bf16[2080,512]{1,0:T(8,128)(2,1)S(1)}, bf16[2080,512]{1,0:T(8,128)(2,1)}, u32[]{:S(2)}) copy-start(bf16[2080,512]{1,0:T(8,128)(2,1)} %all-gather.10.cloned.1.call-done) | copy-start | bytes 6389764
  231.6 3.6 %copy-start.10 = (f32[1024]{0:T(1024)S(1)}, f32[1024]{0:T(1024)}, u32[]{:S(2)}) copy-start(f32[1024]{0:T(1024)} %param.28) | copy-start | bytes 12292
  233.6 1.4 copy-start.4
  235.2 4.3 %copy-start.5 = (f32[520,1024]{1,0:T(8,128)S(1)}, f32[520,1024]{1,0:T(8,128)}, u32[]{:S(2)}) copy-start(f32[520,1024]{1,0:T(8,128)} %copy-done.4) | copy-start | bytes 6389764
  235.2 20.5 %copy-start.1 = (bf16[1408,3,352]{0,2,1:T(8,128)(2,1)S(1)}, bf16[1408,3,352]{0,2,1:T(8,128)(2,1)}, u32[]{:S(2)}) copy-start(bf16[1408,3,352]{0,2,1:T(8,128)(2,1)} %param.19) | copy-start | bytes 8921092
  237.6 4.4 %collective-permute-start.6 = (f32[8,1025]{1,0:T(8,128)S(1)}, f32[8,1025]{1,0:T(8,128)S(1)}, u32[]{:S(2)}, u32[]{:S(2)}) collective-permute-start(f32[8,1025]{1,0:T(8,128)S(1)} %get-tuple-element.36), channel_id=1, source_target_pairs={{0,8},{8,16},{16,24},{24,0},{1,9},{9,17},{17,25},{25,1},{2,10},{10... | collective-permute-start | bytes 98408 | tf_op jit(solution)/shard_map/ppermute | solution.py:148
  237.9 4.1 %collective-permute-start.7 = (f32[8,1025]{1,0:T(8,128)S(1)}, f32[8,1025]{1,0:T(8,128)S(1)}, u32[]{:S(2)}, u32[]{:S(2)}) collective-permute-start(f32[8,1025]{1,0:T(8,128)S(1)} %get-tuple-element.36), channel_id=1, source_target_pairs={{0,16},{8,24},{16,0},{24,8},{1,17},{9,25},{17,1},{25,9},{2,18},{10... | collective-permute-start | bytes 98408 | tf_op jit(solution)/shard_map/ppermute | solution.py:148
  238.2 3.8 %collective-permute-start.8 = (f32[8,1025]{1,0:T(8,128)S(1)}, f32[8,1025]{1,0:T(8,128)S(1)}, u32[]{:S(2)}, u32[]{:S(2)}) collective-permute-start(f32[8,1025]{1,0:T(8,128)S(1)} %get-tuple-element.36), channel_id=1, source_target_pairs={{0,24},{8,0},{16,8},{24,16},{1,25},{9,1},{17,9},{25,17},{2,26},{10... | collective-permute-start | bytes 98408 | tf_op jit(solution)/shard_map/ppermute | solution.py:148
  243.6 3.6 %collective-permute-start.9 = (f32[8]{0:T(128)S(1)}, f32[8]{0:T(128)S(1)}, u32[]{:S(2)}, u32[]{:S(2)}) collective-permute-start(f32[8]{0:T(128)S(1)} %get-tuple-element.41), channel_id=1, source_target_pairs={{0,1},{1,0},{2,3},{3,2},{4,5},{5,4},{6,7},{7,6},{8,9},{9,8},{10,11... | collective-permute-start | bytes 104 | tf_op jit(solution)/shard_map/ppermute | solution.py:165
  247.2 3.5 %collective-permute-start.10 = (f32[8]{0:T(128)S(1)}, f32[8]{0:T(128)S(1)}, u32[]{:S(2)}, u32[]{:S(2)}) collective-permute-start(f32[8]{0:T(128)S(1)} %max.9), channel_id=1, source_target_pairs={{0,2},{1,3},{2,0},{3,1},{4,6},{5,7},{6,4},{7,5},{8,10},{9,11},{10,... | collective-permute-start | bytes 104 | tf_op jit(solution)/shard_map/ppermute | solution.py:165
  250.7 4.4 %collective-permute-start.11 = (f32[8]{0:T(128)S(1)}, f32[8]{0:T(128)S(1)}, u32[]{:S(2)}, u32[]{:S(2)}) collective-permute-start(f32[8]{0:T(128)S(1)} %max.10), channel_id=1, source_target_pairs={{0,4},{1,5},{2,6},{3,7},{4,0},{5,1},{6,2},{7,3},{8,12},{9,13},{10,... | collective-permute-start | bytes 104 | tf_op jit(solution)/shard_map/ppermute | solution.py:165
Sparse Core Ops, SparseCore 0:
  25.1 37.3 all-reduce.1
  66.2 20.1 all-gather.5
  97.9 75.8 all-gather.7
  193.8 31.6 all-gather.9
